TPU v7x, 32 devices: a whole 2x2x4 slice. The times are simulated.
32 devices in a mesh: comp: 2 (over core), gx: 4 (over z), gy: 4 (over y, x).
Axes of the slice: x: 2, y: 2, z: 4, core: 2. Of those that a mesh axis runs over, the one named last changes fastest.
Arguments:
- adjoint_in: float32 [2, 4, 32, 32, 512], P('comp', None, None, 'gx', 'gy'), may hold values from -6 to 6
- u_east: float32 [2, 32, 32, 512], P('comp', None, 'gx', 'gy'), may hold values from -0.4 to 0.4
- u_north: float32 [2, 32, 32, 512], P('comp', None, 'gx', 'gy'), may hold values from -0.4 to 0.4
- diffusivity: float32 [2, 4, 32, 32, 512], P('comp', None, None, 'gx', 'gy'), may hold values from 0.1 to 10
- wet_mask: int32 [2, 32, 512], P('comp', 'gx', 'gy'), may hold values 0 or 1
- dest_tile: int32 [2, 4, 4, 32, 1], P('comp', 'gx', 'gy'), may hold values from 0 to 15; in each aligned block of 32 rows (0 to 31, 32 to 63, ..., all dimensions but the last counted through in order) at most 4 rows name the same one
- src_row: int32 [2, 4, 4, 32], P('comp', 'gx', 'gy'), may hold values from 0 to 7
- dst_row: int32 [2, 4, 4, 32], P('comp', 'gx', 'gy'), may hold values from 0 to 7
- area_weight: float32 [2, 4, 4, 32, 128], P('comp', 'gx', 'gy'), may hold values from 0.2 to 0.8
Outputs:
- adjoint_out: float32 [2, 4, 32, 32, 512], P('comp', None, None, 'gx', 'gy')
Inputs may be any that keep to these rules, and one draw needn't show every extreme that they name: `dest_tile`: among the rows of one device no tile is named more than 4 times, and some device names some tile exactly 4 times.
All inputs are finite; a program needn't handle non-finite values. No bound on the sum of `wet_mask` on one device may be relied on, other than what follows from the above.
Results may differ from a plain program's by a relative error of at most 0.0001.
Values sent between devices are 32-bit elements; how exact they have to be, the bound alone decides.
No kernel may reach another device: no remote copies, remote signals or barrier semaphores. Data moves between devices by JAX's collectives and lax.ppermute only.
A program may use at most 64 MiB of HBM per device.

v0:
```python
import jax
import jax.numpy as jnp
from jax import lax
from jax.sharding import PartitionSpec as P

CAP = 4


diffusion = 0.2


def partner(block, axis, distance):
    count = lax.axis_size(axis)
    route = []
    for low in range(count):
        high = low | 1 << distance
        if high != low and high < count:
            route += [(low, high), (high, low)]
    return lax.ppermute(block, axis, route)


def with_halo(value, sides, width):
    for axis, dim in sides:
        size, length = (lax.axis_size(axis), value.shape[dim])
        up = [(i, (i + 1) % size) for i in range(size - 1)]
        down = [(j, i) for i, j in up]
        last = lax.slice_in_dim(value, length - width, length, axis=dim)
        first = lax.slice_in_dim(value, 0, width, axis=dim)
        before = lax.ppermute(last, axis, up)
        after = lax.ppermute(first, axis, down)
        value = jnp.concatenate([before, value, after], axis=dim)
    return value


def stencil_core(values, east_flux, north_flux):
    centre = values[..., 1:-1, 1:-1]
    laplace = (
        values[..., 2:, 1:-1]
        + values[..., :-2, 1:-1]
        + values[..., 1:-1, 2:]
        + values[..., 1:-1, :-2]
        - 4.0 * centre
    )
    advect = 0.5 * (east_flux[..., :-2, 1:-1] - east_flux[..., 2:, 1:-1]) + 0.5 * (
        north_flux[..., 1:-1, :-2] - north_flux[..., 1:-1, 2:]
    )
    return centre + diffusion * laplace + advect


def column_solve(right_side, coeffs):
    levels = right_side.shape[-3]
    cprime = []
    dprime = []
    for depth_index in range(levels):
        diagonal = 1.0 + jnp.zeros_like(right_side[..., 0, :, :])
        if depth_index < levels - 1:
            diagonal = diagonal + coeffs[..., depth_index, :, :]
        if depth_index > 0:
            coupling_dn = coeffs[..., depth_index - 1, :, :]
            divisor = diagonal + coupling_dn + coupling_dn * cprime[depth_index - 1]
            numerator = right_side[..., depth_index, :, :] + coupling_dn * dprime[depth_index - 1]
        else:
            divisor = diagonal
            numerator = right_side[..., 0, :, :]
        if depth_index < levels - 1:
            cprime.append(-coeffs[..., depth_index, :, :] / divisor)
        dprime.append(numerator / divisor)
    result = [None] * levels
    result[levels - 1] = dprime[levels - 1]
    for depth_index in range(levels - 2, -1, -1):
        result[depth_index] = dprime[depth_index] - cprime[depth_index] * result[depth_index + 1]
    return jnp.stack(result, axis=-3)


def shards(
    adjoint_in, u_east, u_north, diffusivity, wet_mask, dest_tile, src_row, dst_row, area_weight
):
    adjoint = adjoint_in[0]
    fields, levels, rows_x, cols_y = adjoint.shape
    tiles_x = lax.axis_size("gx")
    tiles_y = lax.axis_size("gy")
    tiles = tiles_x * tiles_y
    targets = dest_tile[0, 0, 0, :, 0]
    sources = src_row[0, 0, 0]
    landing = dst_row[0, 0, 0]
    weights = area_weight[0, 0, 0]
    count = targets.shape[0]
    surface_rows = jnp.transpose(adjoint[:, 0], (1, 0, 2)).reshape(rows_x, fields * cols_y)
    pick_table = (sources[:, None] == jnp.arange(rows_x, dtype=jnp.int32)[None, :]).astype(
        jnp.float32
    )
    payload = jnp.dot(
        pick_table,
        surface_rows,
        precision=lax.Precision.HIGHEST,
        preferred_element_type=jnp.float32,
    )
    payload = (payload.reshape(count, fields, cols_y) * weights[:, None, :]).reshape(
        count, fields * cols_y
    )
    order_ids = jnp.arange(count, dtype=jnp.int32)
    earlier = (targets[:, None] == targets[None, :]) & (order_ids[None, :] < order_ids[:, None])
    rank_in = jnp.sum(earlier.astype(jnp.int32), axis=1)
    slot_ids = targets * CAP + rank_in
    placing = slot_ids[:, None] == jnp.arange(tiles * CAP, dtype=jnp.int32)[None, :]
    send_data = jnp.dot(
        placing.astype(jnp.float32).T,
        payload,
        precision=lax.Precision.HIGHEST,
        preferred_element_type=jnp.float32,
    )
    send_rows = jnp.sum(placing.astype(jnp.int32) * (landing + 1)[:, None], axis=0) - 1
    got_data, got_rows = (
        lax.all_to_all(
            send_data.reshape(tiles, CAP, fields * cols_y),
            ("gx", "gy"),
            split_axis=0,
            concat_axis=0,
            tiled=True,
        ),
        lax.all_to_all(
            send_rows.reshape(tiles, CAP), ("gx", "gy"), split_axis=0, concat_axis=0, tiled=True
        ),
    )
    got_data = got_data.reshape(tiles * CAP, fields * cols_y)
    got_rows = got_rows.reshape(tiles * CAP)
    row_table = (got_rows[None, :] == jnp.arange(rows_x, dtype=jnp.int32)[:, None]).astype(
        jnp.float32
    )
    increment = jnp.dot(
        row_table, got_data, precision=lax.Precision.HIGHEST, preferred_element_type=jnp.float32
    )
    arriving = partner(increment, "comp", 0)
    arriving = jnp.transpose(arriving.reshape(rows_x, fields, cols_y), (1, 0, 2))
    adjoint = adjoint.at[:, 0].add(arriving)
    wet = wet_mask[0].astype(jnp.float32)
    east = u_east[0]
    north = u_north[0]
    coeffs = diffusivity[0]
    wet_levels = jnp.broadcast_to(wet[None, None], (1, levels, rows_x, cols_y))
    stacked = jnp.concatenate([adjoint, east[None], north[None], coeffs, wet_levels], axis=0)
    widened = with_halo(stacked, (("gx", 2), ("gy", 3)), 2)
    first = widened[:fields]
    east_wide = widened[fields]
    north_wide = widened[fields + 1]
    coeff_wide = widened[fields + 2 : 2 * fields + 2]
    wet_wide = widened[2 * fields + 2, 0]
    horizontal = stencil_core(first, east_wide[None] * first, north_wide[None] * first)
    middle = column_solve(horizontal, coeff_wide[:, :, 1:-1, 1:-1]) * wet_wide[1:-1, 1:-1]
    east_cycle = east_wide[:, 1:-1, 1:-1]
    north_cycle = north_wide[:, 1:-1, 1:-1]
    horizontal = stencil_core(middle, east_cycle[None] * middle, north_cycle[None] * middle)
    adjoint = column_solve(horizontal, coeffs) * wet
    return adjoint[None]


def solution(mesh):
    placed = (
        P("comp", None, None, "gx", "gy"),
        P("comp", None, "gx", "gy"),
        P("comp", None, "gx", "gy"),
        P("comp", None, None, "gx", "gy"),
        P("comp", "gx", "gy"),
        P("comp", "gx", "gy", None, None),
        P("comp", "gx", "gy", None),
        P("comp", "gx", "gy", None),
        P("comp", "gx", "gy", None, None),
    )
    return jax.shard_map(
        shards,
        mesh=mesh,
        in_specs=placed,
        out_specs=P("comp", None, None, "gx", "gy"),
        check_vma=False,
    )
```

profile of v0, /device:TPU:0, one launch (start us, length us, event | category | flops | bytes accessed | tf_op | source)
XLA Modules:
  0.0 102.6 jit_solution(11250953832032506483)
XLA Ops:
  0.0 0.9 convert_reduce_fusion
  0.9 0.7 multiply_add_fusion.60
  1.6 0.7 add_bitcast_fusion
  2.2 0.1 select_reduce_fusion
  2.3 0.7 sub.1203
  3.0 8.3 %all-to-all-start = ((s32[16,1,4]{2,1,0:T(1,128)}), s32[16,1,4]{2,1,0:T(1,128)S(1)}, u32[]{:S(2)}, u32[]{:S(2)}) async-start(s32[16,1,4]{2,1,0:T(1,128)} %bitcast.4), calls=%async_computation | async-start | bytes 16384 | tf_op jit(solution)/shard_map/all_to_all | solution.py:121
  11.4 1.1 %copy.465 = f32[1,4,32,8,128]{4,3,1,2,0:T(8,128)S(1)} copy(f32[1,4,32,8,128]{4,3,2,1,0:T(8,128)} %param.11) | data formatting | bytes 1048576 | tf_op args[0]
  12.5 0.0 copy-start.9
  12.5 0.0 copy-start.10
  12.5 0.0 copy-start.7
  12.5 1.0 convolution_multiply_fusion
  13.6 0.3 fusion.51
  13.9 0.7 copy.259
  14.6 4.0 %all-to-all-done = s32[16,1,4]{2,1,0:T(1,128)S(1)} async-done(((s32[16,1,4]{2,1,0:T(1,128)}), s32[16,1,4]{2,1,0:T(1,128)S(1)}, u32[]{:S(2)}, u32[]{:S(2)}) %all-to-all-start) | async-done | bytes 288 | tf_op jit(solution)/shard_map/all_to_all | solution.py:121
  18.7 3.5 %all-to-all-start.1 = ((f32[16,4,512]{2,1,0:T(4,128)}), f32[16,4,512]{2,1,0:T(4,128)S(1)}, u32[]{:S(2)}, u32[]{:S(2)}) async-start(f32[16,4,512]{2,1,0:T(4,128)} %copy.259), calls=%async_computation.1 | async-start | bytes 262144 | tf_op jit(solution)/shard_map/all_to_all | solution.py:114
  22.2 0.5 broadcast.2488
  22.7 0.7 reduce.5
  23.4 0.1 eq.84
  23.5 6.5 %all-to-all-done.1 = f32[16,4,512]{2,1,0:T(4,128)S(1)} async-done(((f32[16,4,512]{2,1,0:T(4,128)}), f32[16,4,512]{2,1,0:T(4,128)S(1)}, u32[]{:S(2)}, u32[]{:S(2)}) %all-to-all-start.1) | async-done | bytes 131104 | tf_op jit(solution)/shard_map/all_to_all | solution.py:114
  30.0 0.2 fusion.123
  30.2 0.0 collective-permute-start
  30.2 1.1 %collective-permute-done = f32[8,512]{1,0:T(8,128)S(1)} collective-permute-done((f32[8,512]{1,0:T(8,128)S(1)}, f32[8,512]{1,0:T(8,128)S(1)}, u32[]{:S(2)}, u32[]{:S(2)}) %collective-permute-start) | collective-permute-done | bytes 16416 | tf_op jit(solution)/shard_map/ppermute | solution.py:19
  31.4 0.0 copy-done.9
  31.5 0.2 fusion.186
  31.8 2.7 %collective-permute-start.1 = (f32[11,32,2,128]{3,2,0,1:T(2,128)S(1)}, f32[11,32,2,128]{3,2,0,1:T(2,128)S(1)}, u32[]{:S(2)}, u32[]{:S(2)}) collective-permute-start(f32[11,32,2,128]{3,2,0,1:T(2,128)S(1)} %get-tuple-element.190), channel_id=1, source_target_pairs={{0,4},{4,8},{8,12},{1,5},{5,9},{9,13},{2,6},{6,10},{10,14},{3,7},{... | collective-permute-start | bytes 1081352 | tf_op jit(solution)/shard_map/ppermute | solution.py:29
  34.4 1.3 %collective-permute-start.2 = (f32[11,32,2,128]{3,2,0,1:T(2,128)S(1)}, f32[11,32,2,128]{3,2,0,1:T(2,128)S(1)}, u32[]{:S(2)}, u32[]{:S(2)}) collective-permute-start(f32[11,32,2,128]{3,2,0,1:T(2,128)S(1)} %get-tuple-element.191), channel_id=1, source_target_pairs={{4,0},{8,4},{12,8},{5,1},{9,5},{13,9},{6,2},{10,6},{14,10},{7,3},{... | collective-permute-start | bytes 1081352 | tf_op jit(solution)/shard_map/ppermute | solution.py:30
  35.7 6.7 %collective-permute-done.1 = f32[11,32,2,128]{3,2,0,1:T(2,128)S(1)} collective-permute-done((f32[11,32,2,128]{3,2,0,1:T(2,128)S(1)}, f32[11,32,2,128]{3,2,0,1:T(2,128)S(1)}, u32[]{:S(2)}, u32[]{:S(2)}) %collective-permute-start.1) | collective-permute-done | bytes 360480 | tf_op jit(solution)/shard_map/ppermute | solution.py:29
  42.4 4.1 %collective-permute-done.2 = f32[11,32,2,128]{3,2,0,1:T(2,128)S(1)} collective-permute-done((f32[11,32,2,128]{3,2,0,1:T(2,128)S(1)}, f32[11,32,2,128]{3,2,0,1:T(2,128)S(1)}, u32[]{:S(2)}, u32[]{:S(2)}) %collective-permute-start.2) | collective-permute-done | bytes 360480 | tf_op jit(solution)/shard_map/ppermute | solution.py:30
  46.5 0.0 copy-done.1
  46.5 0.7 copy-done.3
  47.3 0.5 pad_maximum_fusion.1
  47.8 2.5 %fusion.185 = (f32[11,32,12,2]{3,2,0,1:T(8,128)}, f32[11,32,12,2]{3,2,0,1:T(8,128)S(1)}) fusion(f32[11,32,12,128]{3,2,0,1:T(8,128)S(1)} %pad_maximum_fusion.1), kind=kLoop, calls=%fused_computation.517 | loop fusion | bytes 135168 | tf_op jit(solution)/shard_map/slice | solution.py:27
  50.3 3.1 %copy.263 = f32[11,32,12,2]{1,3,2,0:T(2,128)} copy(f32[11,32,12,2]{3,2,0,1:T(8,128)} %get-tuple-element.186) | data formatting | bytes 67584 | tf_op jit(solution)/shard_map/slice | solution.py:27
  53.5 2.5 %collective-permute-start.3 = (f32[11,32,12,2]{1,3,2,0:T(2,128)}, f32[11,32,12,2]{1,3,2,0:T(2,128)S(1)}, u32[]{:S(2)}, u32[]{:S(2)}) collective-permute-start(f32[11,32,12,2]{1,3,2,0:T(2,128)} %copy.263), channel_id=1, source_target_pairs={{0,1},{1,2},{2,3},{4,5},{5,6},{6,7},{8,9},{9,10},{10,11},{12,13},{... | collective-permute-start | bytes 101384 | tf_op jit(solution)/shard_map/ppermute | solution.py:29
  55.9 2.1 %copy.264 = f32[11,32,12,2]{1,3,2,0:T(2,128)} copy(f32[11,32,12,2]{3,2,0,1:T(8,128)S(1)} %get-tuple-element.187) | data formatting | bytes 67584 | tf_op jit(solution)/shard_map/slice | solution.py:28
  58.0 1.5 %collective-permute-start.4 = (f32[11,32,12,2]{1,3,2,0:T(2,128)}, f32[11,32,12,2]{1,3,2,0:T(2,128)S(1)}, u32[]{:S(2)}, u32[]{:S(2)}) collective-permute-start(f32[11,32,12,2]{1,3,2,0:T(2,128)} %copy.264), channel_id=1, source_target_pairs={{1,0},{2,1},{3,2},{5,4},{6,5},{7,6},{9,8},{10,9},{11,10},{13,12},{... | collective-permute-start | bytes 101384 | tf_op jit(solution)/shard_map/ppermute | solution.py:30
  59.5 1.9 %copy.464 = f32[1,4,32,8,128]{4,3,1,2,0:T(8,128)} copy(f32[1,4,32,8,128]{4,3,2,1,0:T(8,128)} %param.14) | data formatting | bytes 1048576 | tf_op args[3]
  61.4 0.0 collective-permute-done.3
  61.4 1.4 %copy.265 = f32[11,32,12,2]{3,2,1,0:T(8,128)S(1)} copy(f32[11,32,12,2]{1,3,2,0:T(2,128)S(1)} %collective-permute-done.3) | data formatting | bytes 67584 | tf_op jit(solution)/shard_map/ppermute | solution.py:29
  62.8 2.3 %collective-permute-done.4 = f32[11,32,12,2]{1,3,2,0:T(2,128)S(1)} collective-permute-done((f32[11,32,12,2]{1,3,2,0:T(2,128)}, f32[11,32,12,2]{1,3,2,0:T(2,128)S(1)}, u32[]{:S(2)}, u32[]{:S(2)}) %collective-permute-start.4) | collective-permute-done | bytes 33824 | tf_op jit(solution)/shard_map/ppermute | solution.py:30
  65.1 2.4 %copy.267 = f32[11,32,12,2]{3,2,1,0:T(8,128)} copy(f32[11,32,12,2]{1,3,2,0:T(2,128)S(1)} %collective-permute-done.4) | data formatting | bytes 67584 | tf_op jit(solution)/shard_map/ppermute | solution.py:30
  67.5 4.4 %pad_maximum_fusion = f32[11,32,12,132]{3,2,1,0:T(8,128)S(1)} fusion(f32[11,32,12,2]{3,2,1,0:T(8,128)} %copy.267, f32[11,32,12,2]{3,2,1,0:T(8,128)S(1)} %copy.265, f32[11,32,2,128]{3,2,0,1:T(2,128)} %copy-done.3, f32[11,32,8,128]{3,2,0,1:T(8,128)} %copy-done.1, f32[11,32,2,128]{3,2,0,1:T(2,128)S(1)} %collective-permute-done.1), kind=kLoop, calls=%fused_computation | loop fusion | flops 2196480 | bytes 4460544 | tf_op jit(solution)/shard_map/concatenate | solution.py:31
  71.9 0.1 slice_bitcast_fusion
  72.0 4.3 %fusion.184 = (f32[4,32,10,130]{3,2,1,0:T(8,128)}, f32[4,32,10,130]{3,2,1,0:T(8,128)}, f32[4,32,10,130]{3,2,1,0:T(8,128)}) fusion(f32[11,32,12,132]{3,2,1,0:T(8,128)S(1)} %pad_maximum_fusion), kind=kLoop, calls=%fused_computation.516 | loop fusion | bytes 3993600 | tf_op jit(solution)/shard_map/slice | solution.py:36
  76.3 1.0 slice.871
  77.3 2.6 %copy_multiply_fusion.1 = (f32[4,32,12,132]{3,2,0,1:T(8,128)}, f32[4,32,12,132]{3,2,0,1:T(8,128)}) fusion(f32[32,12,132]{2,1,0:T(8,128)S(1)} %get-tuple-element.185, f32[32,12,132]{2,1,0:T(8,128)S(1)} %get-tuple-element.184, f32[11,32,12,132]{3,2,1,0:T(8,128)S(1)} %pad_maximum_fusion), kind=kLoop, calls=%fused_computation.20 | loop fusion | flops 405504 | bytes 4767744 | tf_op jit(solution)/shard_map/mul | solution.py:148
  80.0 1.0 %slice.874 = f32[32,10,130]{2,1,0:T(8,128)} slice(f32[32,12,132]{2,1,0:T(8,128)S(1)} %get-tuple-element.184), slice={[0:32], [1:11], [1:131]} | slice | bytes 332800 | tf_op jit(solution)/shard_map/slice | solution.py:151
  81.0 2.5 %copy.271 = f32[11,32,12,2]{3,2,0,1:T(8,128)} copy(f32[11,32,12,2]{1,3,2,0:T(2,128)S(1)} %collective-permute-done.4) | data formatting | bytes 67584 | tf_op jit(solution)/shard_map/ppermute | solution.py:30
  83.5 2.4 %copy.272 = f32[11,32,12,2]{3,2,0,1:T(8,128)} copy(f32[11,32,12,2]{1,3,2,0:T(2,128)S(1)} %collective-permute-done.3) | data formatting | bytes 67584 | tf_op jit(solution)/shard_map/ppermute | solution.py:29
  85.9 8.6 %fusion.2 = f32[4,32,10,130]{3,2,0,1:T(8,128)S(1)} fusion(f32[4,32,12,132]{3,2,0,1:T(8,128)} %get-tuple-element.189, f32[4,32,12,132]{3,2,0,1:T(8,128)} %get-tuple-element.188, f32[11,32,12,2]{3,2,0,1:T(8,128)} %copy.272, f32[11,32,2,128]{3,2,0,1:T(2,128)} %copy-done.3, f32[11,32,8,128]{3,2,0,1:T(8,128)} %copy-done.1, ...), kind=kLoop, calls=%fused_computation.5 | loop fusion | flops 2995200 | bytes 7555072 | tf_op jit(solution)/shard_map/add | solution.py:47
  94.5 1.5 %fusion.18 = (f32[4,1,10,130]{3,2,0,1:T(8,128)S(1)}, f32[4,1,10,130]{3,2,0,1:T(8,128)S(1)}, f32[4,1,10,130]{3,2,0,1:T(8,128)S(1)}, f32[4,1,10,130]{3,2,0,1:T(8,1...) fusion(f32[4,32,10,130]{3,2,0,1:T(8,128)S(1)} %fusion.2, ...), kind=kLoop, calls=%fused_computation.120 | loop fusion | flops 2703744 | bytes 4247872 | tf_op jit(solution)/shard_map/div | solution.py:67
  96.0 0.8 constant_dynamic-update-slice_fusion.36
  97.4 0.1 maximum_bitcast_fusion.30
  97.5 0.1 slice.865
  97.6 0.8 copy-done.8
  98.4 0.5 broadcast_multiply_fusion.1
  99.0 0.5 copy-done.6
  99.5 0.3 broadcast_multiply_fusion
  99.8 0.0 copy-start.5
  99.8 1.0 fusion.10
  100.8 0.0 copy-done.5
  100.8 0.3 fusion.57
  101.1 0.2 constant_dynamic-update-slice_fusion.68
  101.8 0.8 copy.378
  (90 shorter events, 1.0 us)
Async XLA Ops:
  0.0 30.2 %copy-start.11 = (s32[1,8,128]{2,1,0:T(8,128)S(1)}, s32[1,8,128]{2,1,0:T(8,128)}, u32[]{:S(2)}) copy-start(s32[1,8,128]{2,1,0:T(8,128)} %param.15) | copy-start | bytes 12292
  3.0 15.6 %all-to-all-start = ((s32[16,1,4]{2,1,0:T(1,128)}), s32[16,1,4]{2,1,0:T(1,128)S(1)}, u32[]{:S(2)}, u32[]{:S(2)}) async-start(s32[16,1,4]{2,1,0:T(1,128)} %bitcast.4), calls=%async_computation | async-start | bytes 16384 | tf_op jit(solution)/shard_map/all_to_all | solution.py:121
  12.5 18.9 %copy-start.9 = (f32[1,32,8,128]{3,2,1,0:T(8,128)S(1)}, f32[1,32,8,128]{3,2,1,0:T(8,128)}, u32[]{:S(2)}) copy-start(f32[1,32,8,128]{3,2,1,0:T(8,128)} %param.12) | copy-start | bytes 393220
  12.5 18.9 %copy-start.10 = (f32[1,32,8,128]{3,2,1,0:T(8,128)S(1)}, f32[1,32,8,128]{3,2,1,0:T(8,128)}, u32[]{:S(2)}) copy-start(f32[1,32,8,128]{3,2,1,0:T(8,128)} %param.13) | copy-start | bytes 393220
  12.5 18.9 %copy-start.7 = (f32[1,4,32,8,128]{4,3,2,1,0:T(8,128)S(1)}, f32[1,4,32,8,128]{4,3,2,1,0:T(8,128)}, u32[]{:S(2)}) copy-start(f32[1,4,32,8,128]{4,3,2,1,0:T(8,128)} %param.14) | copy-start | bytes 1572868
  18.7 11.3 %all-to-all-start.1 = ((f32[16,4,512]{2,1,0:T(4,128)}), f32[16,4,512]{2,1,0:T(4,128)S(1)}, u32[]{:S(2)}, u32[]{:S(2)}) async-start(f32[16,4,512]{2,1,0:T(4,128)} %copy.259), calls=%async_computation.1 | async-start | bytes 262144 | tf_op jit(solution)/shard_map/all_to_all | solution.py:114
  30.2 1.2 %collective-permute-start = (f32[8,512]{1,0:T(8,128)S(1)}, f32[8,512]{1,0:T(8,128)S(1)}, u32[]{:S(2)}, u32[]{:S(2)}) collective-permute-start(f32[8,512]{1,0:T(8,128)S(1)} %fusion.123), channel_id=1, source_target_pairs={{0,16},{16,0},{1,17},{17,1},{2,18},{18,2},{3,19},{19,3},{4,20},{20... | collective-permute-start | bytes 49160 | tf_op jit(solution)/shard_map/ppermute | solution.py:19
  31.5 15.0 %copy-start.1 = (f32[11,32,8,128]{3,2,0,1:T(8,128)}, f32[11,32,8,128]{3,2,0,1:T(8,128)S(1)}, u32[]{:S(2)}) copy-start(f32[11,32,8,128]{3,2,0,1:T(8,128)S(1)} %constant_dynamic-update-slice_fusion) | copy-start | bytes 4325380
  31.8 10.6 %collective-permute-start.1 = (f32[11,32,2,128]{3,2,0,1:T(2,128)S(1)}, f32[11,32,2,128]{3,2,0,1:T(2,128)S(1)}, u32[]{:S(2)}, u32[]{:S(2)}) collective-permute-start(f32[11,32,2,128]{3,2,0,1:T(2,128)S(1)} %get-tuple-element.190), channel_id=1, source_target_pairs={{0,4},{4,8},{8,12},{1,5},{5,9},{9,13},{2,6},{6,10},{10,14},{3,7},{... | collective-permute-start | bytes 1081352 | tf_op jit(solution)/shard_map/ppermute | solution.py:29
  34.4 12.1 %collective-permute-start.2 = (f32[11,32,2,128]{3,2,0,1:T(2,128)S(1)}, f32[11,32,2,128]{3,2,0,1:T(2,128)S(1)}, u32[]{:S(2)}, u32[]{:S(2)}) collective-permute-start(f32[11,32,2,128]{3,2,0,1:T(2,128)S(1)} %get-tuple-element.191), channel_id=1, source_target_pairs={{4,0},{8,4},{12,8},{5,1},{9,5},{13,9},{6,2},{10,6},{14,10},{7,3},{... | collective-permute-start | bytes 1081352 | tf_op jit(solution)/shard_map/ppermute | solution.py:30
  46.5 0.7 copy-start.3
  53.5 7.9 %collective-permute-start.3 = (f32[11,32,12,2]{1,3,2,0:T(2,128)}, f32[11,32,12,2]{1,3,2,0:T(2,128)S(1)}, u32[]{:S(2)}, u32[]{:S(2)}) collective-permute-start(f32[11,32,12,2]{1,3,2,0:T(2,128)} %copy.263), channel_id=1, source_target_pairs={{0,1},{1,2},{2,3},{4,5},{5,6},{6,7},{8,9},{9,10},{10,11},{12,13},{... | collective-permute-start | bytes 101384 | tf_op jit(solution)/shard_map/ppermute | solution.py:29
  58.0 7.1 %collective-permute-start.4 = (f32[11,32,12,2]{1,3,2,0:T(2,128)}, f32[11,32,12,2]{1,3,2,0:T(2,128)S(1)}, u32[]{:S(2)}, u32[]{:S(2)}) collective-permute-start(f32[11,32,12,2]{1,3,2,0:T(2,128)} %copy.264), channel_id=1, source_target_pairs={{1,0},{2,1},{3,2},{5,4},{6,5},{7,6},{9,8},{10,9},{11,10},{13,12},{... | collective-permute-start | bytes 101384 | tf_op jit(solution)/shard_map/ppermute | solution.py:30
  85.9 8.6 %copy-start = (f32[11,32,12,2]{3,2,1,0:T(8,128)S(1)}, f32[11,32,12,2]{3,2,1,0:T(8,128)}, u32[]{:S(2)}) copy-start(f32[11,32,12,2]{3,2,1,0:T(8,128)} %copy.267) | copy-start | bytes 101380
  85.9 8.6 %copy-start.2 = (f32[11,32,8,128]{3,2,0,1:T(8,128)S(1)}, f32[11,32,8,128]{3,2,0,1:T(8,128)}, u32[]{:S(2)}) copy-start(f32[11,32,8,128]{3,2,0,1:T(8,128)} %copy-done.1) | copy-start | bytes 4325380
  85.9 8.6 %copy-start.4 = (f32[11,32,2,128]{3,2,0,1:T(2,128)S(1)}, f32[11,32,2,128]{3,2,0,1:T(2,128)}, u32[]{:S(2)}) copy-start(f32[11,32,2,128]{3,2,0,1:T(2,128)} %copy-done.3) | copy-start | bytes 1081348
  97.4 1.0 %copy-start.8 = (f32[32,10,130]{2,1,0:T(8,128)S(1)}, f32[32,10,130]{2,1,0:T(8,128)}, u32[]{:S(2)}) copy-start(f32[32,10,130]{2,1,0:T(8,128)} %slice.871) | copy-start | bytes 499204
  98.4 1.0 %copy-start.6 = (f32[32,10,130]{2,1,0:T(8,128)S(1)}, f32[32,10,130]{2,1,0:T(8,128)}, u32[]{:S(2)}) copy-start(f32[32,10,130]{2,1,0:T(8,128)} %slice.874) | copy-start | bytes 499204
  99.8 1.0 %copy-start.5 = (f32[1,4,32,8,128]{4,3,1,2,0:T(8,128)S(1)}, f32[1,4,32,8,128]{4,3,1,2,0:T(8,128)}, u32[]{:S(2)}) copy-start(f32[1,4,32,8,128]{4,3,1,2,0:T(8,128)} %copy.464) | copy-start | bytes 1572868
where the time goes:
time: 103 us
  local copies, waits for them, and re-layouts  31.6 us (31%)
  waiting for transfers between devices  24.8 us (24%)
  other arithmetic  24.3 us (24%)
  starting transfers between devices  19.7 us (19%)
  matrix products  1.43 us (1%)
    add x2, other arithmetic, stencil_core(): return centre + diffusion * laplace + advect  9.58 us
    all_to_all x1, starting transfers between devices, shards(): lax.all_to_all(send_rows.reshape(tiles, CAP), ('gx', 'gy'), split_axis=0,...  8.34 us
    ppermute x2, waiting for transfers between devices, with_halo(): before = lax.ppermute(last, axis, up)  6.66 us
    ppermute x2, waiting for transfers between devices, with_halo(): after = lax.ppermute(first, axis, down)  6.48 us
    all_to_all x1, waiting for transfers between devices, shards(): lax.all_to_all(send_data.reshape(tiles, CAP, fields * cols_y), ('gx', 'gy...  6.47 us
    slice x3, local copies, waits for them, and re-layouts, with_halo(): last = lax.slice_in_dim(value, length - width, length, axis=dim)  5.87 us
    unnamed x61, local copies, waits for them, and re-layouts  5.4 us
    ppermute x2, starting transfers between devices, with_halo(): before = lax.ppermute(last, axis, up)  5.12 us
  transfers between devices with their start and end apart: 7, of which 6 were waited for; matrix products, arithmetic and copies ran while one was open for 10% of the time, Pallas kernels for 0%

commit v1 on v0

v1 whole, which is shorter than its diff:
```python
import jax
import jax.numpy as jnp
from jax import lax
from jax.experimental import pallas as pl
from jax.experimental.pallas import tpu as pltpu
from jax.sharding import PartitionSpec as P

CAP = 4


diffusion = 0.2


def shift(block, axis, step):
    count = lax.axis_size(axis)
    route = [(i, i + step) for i in range(count) if 0 <= i + step < count]
    return lax.ppermute(block, axis, route)


def step_kernel(fields, levels, rows, cols, coupled):
    def kernel(*refs):
        if coupled:
            (a_ref, up_ref, dn_ref, lf_ref, rt_ref, cu_ref, cd_ref, cl_ref, cr_ref, ue_ref, un_ref,
             k_ref, wet_ref, inc_ref, iu_ref, id_ref, il_ref, ir_ref, out_ref, c_ref) = refs
        else:
            (a_ref, up_ref, dn_ref, lf_ref, rt_ref, cu_ref, cd_ref, cl_ref, cr_ref, ue_ref, un_ref,
             k_ref, wet_ref, out_ref, c_ref) = refs
        row = lax.broadcasted_iota(jnp.int32, (rows, cols), 0)
        col = lax.broadcasted_iota(jnp.int32, (rows, cols), 1)
        top = row == 0
        bottom = row == rows - 1
        left = col == 0
        right = col == cols - 1
        cprev = [None] * fields
        dprev = [None] * fields
        for l in range(levels):
            ue = ue_ref[l]
            un = un_ref[l]
            ue_m = jnp.where(top, cu_ref[fields, l], pltpu.roll(ue, 1, 0))
            ue_p = jnp.where(bottom, cd_ref[fields, l], pltpu.roll(ue, rows - 1, 0))
            un_m = jnp.where(left, cl_ref[fields, l], pltpu.roll(un, 1, 1))
            un_p = jnp.where(right, cr_ref[fields, l], pltpu.roll(un, cols - 1, 1))
            for f in range(fields):
                a = a_ref[f, l]
                up = up_ref[f, l]
                dn = dn_ref[f, l]
                lf = lf_ref[f, l]
                rt = rt_ref[f, l]
                if coupled and l == 0:
                    a = a + inc_ref[f]
                    up = up + iu_ref[f]
                    dn = dn + id_ref[f]
                    lf = lf + il_ref[f]
                    rt = rt + ir_ref[f]
                a_im = jnp.where(top, up, pltpu.roll(a, 1, 0))
                a_ip = jnp.where(bottom, dn, pltpu.roll(a, rows - 1, 0))
                a_jm = jnp.where(left, lf, pltpu.roll(a, 1, 1))
                a_jp = jnp.where(right, rt, pltpu.roll(a, cols - 1, 1))
                laplace = a_ip + a_im + a_jp + a_jm - 4.0 * a
                advect = 0.5 * (ue_m * a_im - ue_p * a_ip) + 0.5 * (un_m * a_jm - un_p * a_jp)
                h = a + diffusion * laplace + advect
                if l < levels - 1:
                    kd = k_ref[f, l]
                    diagonal = 1.0 + kd
                else:
                    diagonal = 1.0
                if l > 0:
                    kp = k_ref[f, l - 1]
                    divisor = diagonal + kp + kp * cprev[f]
                    numerator = h + kp * dprev[f]
                else:
                    divisor = diagonal
                    numerator = h
                if l < levels - 1:
                    cprev[f] = -kd / divisor
                    c_ref[f, l] = cprev[f]
                dprev[f] = numerator / divisor
                out_ref[f, l] = dprev[f]
        wet = wet_ref[...]
        for f in range(fields):
            r = dprev[f]
            out_ref[f, levels - 1] = r * wet
            for l in range(levels - 2, -1, -1):
                r = out_ref[f, l] - c_ref[f, l] * r
                out_ref[f, l] = r * wet

    return kernel


def run_step(a, halos, coef_halos, ue, un, coeffs, wet, inc=None):
    fields, levels, rows, cols = a.shape
    coupled = inc is not None
    operands = [a, *halos, *coef_halos, ue, un, coeffs, wet]
    if coupled:
        operands += list(inc)
    return pl.pallas_call(
        step_kernel(fields, levels, rows, cols, coupled),
        out_shape=jax.ShapeDtypeStruct(a.shape, jnp.float32),
        scratch_shapes=[pltpu.VMEM(a.shape, jnp.float32)],
    )(*operands)


def edges(value):
    rows, cols = value.shape[-2:]
    return (
        value[..., rows - 1 : rows, :],
        value[..., 0:1, :],
        value[..., :, cols - 1 : cols],
        value[..., :, 0:1],
    )


def exchange(value):
    last_row, first_row, last_col, first_col = edges(value)
    return (
        shift(last_row, "gx", 1),
        shift(first_row, "gx", -1),
        shift(last_col, "gy", 1),
        shift(first_col, "gy", -1),
    )


def shards(
    adjoint_in, u_east, u_north, diffusivity, wet_mask, dest_tile, src_row, dst_row, area_weight
):
    adjoint = adjoint_in[0]
    fields, levels, rows_x, cols_y = adjoint.shape
    sections = lax.axis_size("comp")
    tiles_x = lax.axis_size("gx")
    tiles_y = lax.axis_size("gy")
    tiles = tiles_x * tiles_y
    east = u_east[0]
    north = u_north[0]
    coeffs = diffusivity[0]
    wet = wet_mask[0].astype(jnp.float32)

    last_row, first_row, last_col, first_col = edges(adjoint)
    e_last, e_first, _, _ = edges(east)
    _, _, n_last, n_first = edges(north)
    start_halos = (
        shift(jnp.concatenate([last_row, e_last[None]], 0), "gx", 1),
        shift(jnp.concatenate([first_row, e_first[None]], 0), "gx", -1),
        shift(jnp.concatenate([last_col, n_last[None]], 0), "gy", 1),
        shift(jnp.concatenate([first_col, n_first[None]], 0), "gy", -1),
    )

    targets = dest_tile[0, 0, 0, :, 0]
    sources = src_row[0, 0, 0]
    landing = dst_row[0, 0, 0]
    weights = area_weight[0, 0, 0]
    count = targets.shape[0]
    surface_rows = jnp.transpose(adjoint[:, 0], (1, 0, 2)).reshape(rows_x, fields * cols_y)
    pick_table = (sources[:, None] == jnp.arange(rows_x, dtype=jnp.int32)[None, :]).astype(
        jnp.float32
    )
    payload = jnp.dot(
        pick_table,
        surface_rows,
        precision=lax.Precision.HIGHEST,
        preferred_element_type=jnp.float32,
    )
    payload = (payload.reshape(count, fields, cols_y) * weights[:, None, :]).reshape(
        count, fields * cols_y
    )
    tag = jnp.broadcast_to((landing + 1).astype(jnp.float32)[:, None], (count, cols_y))
    tagged = jnp.concatenate([payload, tag], axis=1)
    order_ids = jnp.arange(count, dtype=jnp.int32)
    earlier = (targets[:, None] == targets[None, :]) & (order_ids[None, :] < order_ids[:, None])
    rank_in = jnp.sum(earlier.astype(jnp.int32), axis=1)
    slot_ids = targets * CAP + rank_in
    placing = slot_ids[:, None] == jnp.arange(tiles * CAP, dtype=jnp.int32)[None, :]
    send_data = jnp.dot(
        placing.astype(jnp.float32).T,
        tagged,
        precision=lax.Precision.HIGHEST,
        preferred_element_type=jnp.float32,
    )
    width = (fields + 1) * cols_y
    got = lax.all_to_all(
        send_data.reshape(tiles, CAP, width), ("gx", "gy"), split_axis=0, concat_axis=0, tiled=True
    ).reshape(tiles * CAP, width)
    got_rows = got[:, fields * cols_y]
    row_table = (
        got_rows[None, :] == (jnp.arange(rows_x, dtype=jnp.int32) + 1).astype(jnp.float32)[:, None]
    ).astype(jnp.float32)
    increment = jnp.dot(
        row_table,
        got[:, : fields * cols_y],
        precision=lax.Precision.HIGHEST,
        preferred_element_type=jnp.float32,
    )
    increment = jnp.transpose(increment.reshape(rows_x, fields, cols_y), (1, 0, 2))

    def linear(c, x, y):
        return (c * tiles_x + x) * tiles_y + y

    def cross(block, dx, dy):
        route = []
        for c in range(sections):
            for x in range(tiles_x):
                for y in range(tiles_y):
                    if 0 <= x + dx < tiles_x and 0 <= y + dy < tiles_y:
                        route.append((linear(c, x, y), linear(sections - 1 - c, x + dx, y + dy)))
        return lax.ppermute(block, ("comp", "gx", "gy"), route)

    i_last_row, i_first_row, i_last_col, i_first_col = edges(increment)
    inc = (
        cross(increment, 0, 0),
        cross(i_last_row, 1, 0),
        cross(i_first_row, -1, 0),
        cross(i_last_col, 0, 1),
        cross(i_first_col, 0, -1),
    )

    middle = run_step(adjoint, start_halos, start_halos, east, north, coeffs, wet, inc)
    step_halos = exchange(middle)
    result = run_step(middle, step_halos, start_halos, east, north, coeffs, wet)
    return result[None]


def solution(mesh):
    placed = (
        P("comp", None, None, "gx", "gy"),
        P("comp", None, "gx", "gy"),
        P("comp", None, "gx", "gy"),
        P("comp", None, None, "gx", "gy"),
        P("comp", "gx", "gy"),
        P("comp", "gx", "gy", None, None),
        P("comp", "gx", "gy", None),
        P("comp", "gx", "gy", None),
        P("comp", "gx", "gy", None, None),
    )
    return jax.shard_map(
        shards,
        mesh=mesh,
        in_specs=placed,
        out_specs=P("comp", None, None, "gx", "gy"),
        check_vma=False,
    )
```

time: 103 us -> 89.7 us (0.87)
  other arithmetic: 24.3 us -> 0.96 us
  starting transfers between devices: 19.7 us -> 41.9 us
  local copies, waits for them, and re-layouts: 31.6 us -> 11.6 us
  Pallas kernels: 0 us -> 7.61 us
    ppermute x5 -> x13, starting transfers between devices: 7.88 us -> 33.6 us  [the longest x8 22.1 us: shift(): return lax.ppermute(block, axis, route)]
    ppermute x5 -> x13, waiting for transfers between devices: 14.3 us -> 25.1 us  [the longest x8 21.8 us: shift(): return lax.ppermute(block, axis, route)]
    all_to_all x2 -> x1, waiting for transfers between devices: 10.5 us -> 0.01 us  [shards(): lax.all_to_all(send_data.reshape(tiles, CAP, width), ('gx', 'gy'), split_...]
    slice x8 -> x12, local copies, waits for them, and re-layouts: 14.4 us -> 4.05 us  [the longest x6 2.16 us: edges(): value[..., :, 0:1]]
    add x3 -> x0, other arithmetic: 10.2 us -> none  [the longest x2 9.58 us: stencil_core(): return centre + diffusion * laplace + advect]
    pallas_call x0 -> x2, Pallas kernels: none -> 7.61 us  [run_step(): pl.pallas_call(step_kernel(fields, levels, rows, cols, coupled), out_shap...]
    ppermute x4 -> x2, local copies, waits for them, and re-layouts: 8.72 us -> 2.34 us  [shift(): return lax.ppermute(block, axis, route)]
    concatenate x2 -> x4, other arithmetic: 4.92 us -> 0.17 us  [the longest x1 0.08 us: shards(): jnp.concatenate([last_row, e_last[None]], 0)]
  transfers between devices with their start and end apart: 7 -> 14, of which waited for: 6 -> 3; matrix products, arithmetic and copies ran while one was open for 10% -> 8% of each run, Pallas kernels for 0% -> 0%
where the time goes in v1:
time: 89.7 us; the launch traced here: 89 us
  starting transfers between devices  41.9 us (47%)
  waiting for transfers between devices  25.1 us (28%)
  local copies, waits for them, and re-layouts  11.6 us (13%)
  Pallas kernels  7.61 us (8%)
  matrix products  1.53 us (2%)
  other arithmetic  0.96 us (1%)
    ppermute x8, starting transfers between devices, shift(): return lax.ppermute(block, axis, route)  22.1 us
    ppermute x8, waiting for transfers between devices, shift(): return lax.ppermute(block, axis, route)  21.8 us
    ppermute x5, starting transfers between devices, cross(): return lax.ppermute(block, ('comp', 'gx', 'gy'), route)  11.5 us
    all_to_all x1, starting transfers between devices, shards(): lax.all_to_all(send_data.reshape(tiles, CAP, width), ('gx', 'gy'), split_...  8.34 us
    pallas_call x2, Pallas kernels, run_step(): pl.pallas_call(step_kernel(fields, levels, rows, cols, coupled), out_shap...  7.61 us
    unnamed x34, local copies, waits for them, and re-layouts  3.32 us
    ppermute x5, waiting for transfers between devices, cross(): return lax.ppermute(block, ('comp', 'gx', 'gy'), route)  3.28 us
    ppermute x2, local copies, waits for them, and re-layouts, shift(): return lax.ppermute(block, axis, route)  2.34 us
  transfers between devices with their start and end apart: 14, of which 3 were waited for; matrix products, arithmetic and copies ran while one was open for 8% of the time, Pallas kernels for 0%

profile of v1, /device:TPU:0, one launch (start us, length us, event | category | flops | bytes accessed | tf_op | source)
XLA Modules:
  0.0 89.0 jit_solution(7917855816002020966)
XLA Ops:
  0.0 0.7 copy-done.14
  0.7 1.0 %fusion = f32[4,4,8,128]{3,2,1,0:T(8,128)S(1)} fusion(f32[32,128]{1,0:T(8,128)} %bitcast.61, f32[4,32,8,128]{3,2,1,0:T(8,128)} %bitcast.46, s32[32]{0:T(128)S(1)} %bitcast.62), kind=kOutput, calls=%fused_computation.1 | convolution fusion | flops 1589504 | bytes 98432 | tf_op jit(solution)/shard_map/dot_general | solution.py:156
  1.6 0.0 copy-start
  1.7 0.2 convert_reduce_fusion
  1.9 0.1 broadcast_in_dim.31
  2.0 0.3 fusion.2
  2.3 0.7 reshape.47
  3.0 8.3 %all-to-all-start = ((f32[16,4,640]{2,1,0:T(4,128)}), f32[16,4,640]{2,1,0:T(4,128)S(1)}, u32[]{:S(2)}, u32[]{:S(2)}) async-start(f32[16,4,640]{2,1,0:T(4,128)} %reshape.47), calls=%async_computation | async-start | bytes 327680 | tf_op jit(solution)/shard_map/all_to_all | solution.py:179
  11.4 0.2 fusion.17
  11.6 0.3 copy.45
  11.9 0.6 copy-done.1
  12.5 0.1 fusion.19
  12.6 0.1 copy.44
  12.7 3.8 %collective-permute-start.2 = (f32[5,32,8,1]{1,2,3,0:T(8,128)S(1)}, f32[5,32,8,1]{1,2,3,0:T(8,128)S(1)}, u32[]{:S(2)}, u32[]{:S(2)}) collective-permute-start(f32[5,32,8,1]{1,2,3,0:T(8,128)S(1)} %pad_maximum_fusion.2), channel_id=1, source_target_pairs={{0,1},{1,2},{2,3},{4,5},{5,6},{6,7},{8,9},{9,10},{10,11},{12,13},{... | collective-permute-start | bytes 15368 | tf_op jit(solution)/shard_map/ppermute | solution.py:17
  16.6 0.3 copy.47
  16.8 0.1 copy.46
  17.0 1.3 %collective-permute-start.3 = (f32[5,32,8,1]{1,2,3,0:T(8,128)S(1)}, f32[5,32,8,1]{1,2,3,0:T(8,128)S(1)}, u32[]{:S(2)}, u32[]{:S(2)}) collective-permute-start(f32[5,32,8,1]{1,2,3,0:T(8,128)S(1)} %pad_maximum_fusion.3), channel_id=1, source_target_pairs={{1,0},{2,1},{3,2},{5,4},{6,5},{7,6},{9,8},{10,9},{11,10},{13,12},{... | collective-permute-start | bytes 15368 | tf_op jit(solution)/shard_map/ppermute | solution.py:17
  18.3 0.1 fusion.18
  18.4 1.0 %slice_bitcast_fusion.2 = (f32[1,32,1,128]{3,2,1,0:T(1,128)S(1)}, f32[1,32,1,128]{3,2,1,0:T(1,128)S(1)}) fusion(f32[32,8,128]{2,1,0:T(8,128)} %bitcast.55), kind=kLoop, calls=%fused_computation.15 | loop fusion | bytes 65536 | tf_op jit(solution)/shard_map/broadcast_in_dim | solution.py:142
  19.4 0.1 pad_maximum_fusion
  19.5 3.4 %collective-permute-start = (f32[5,32,1,128]{3,2,1,0:T(1,128)S(1)}, f32[5,32,1,128]{3,2,1,0:T(1,128)S(1)}, u32[]{:S(2)}, u32[]{:S(2)}) collective-permute-start(f32[5,32,1,128]{3,2,1,0:T(1,128)S(1)} %pad_maximum_fusion), channel_id=1, source_target_pairs={{0,4},{4,8},{8,12},{1,5},{5,9},{9,13},{2,6},{6,10},{10,14},{3,7},{... | collective-permute-start | bytes 245768 | tf_op jit(solution)/shard_map/ppermute | solution.py:17
  22.8 0.0 copy-start.11
  22.9 0.1 pad_maximum_fusion.1
  22.9 1.3 %collective-permute-start.1 = (f32[5,32,1,128]{3,2,1,0:T(1,128)S(1)}, f32[5,32,1,128]{3,2,1,0:T(1,128)S(1)}, u32[]{:S(2)}, u32[]{:S(2)}) collective-permute-start(f32[5,32,1,128]{3,2,1,0:T(1,128)S(1)} %pad_maximum_fusion.1), channel_id=1, source_target_pairs={{4,0},{8,4},{12,8},{5,1},{9,5},{13,9},{6,2},{10,6},{14,10},{7,3},{... | collective-permute-start | bytes 245768 | tf_op jit(solution)/shard_map/ppermute | solution.py:17
  24.2 0.6 convert_bitcast_fusion.refs_12_
  24.8 0.0 collective-permute-done.2
  24.9 1.1 %copy.49.refs_3_.refs_7_ = f32[5,32,8,1]{3,2,1,0:T(8,128)} copy(f32[5,32,8,1]{1,2,3,0:T(8,128)S(1)} %collective-permute-done.2) | data formatting | bytes 10240 | tf_op jit(solution)/shard_map/ppermute | solution.py:17
  26.0 0.0 all-to-all-done
  26.0 0.1 reshape.48
  26.1 0.1 slice_reduce_fusion
  26.2 0.2 convolution_bitcast_fusion
  26.4 0.1 collective-permute-start.4
  26.5 4.6 %collective-permute-start.5 = (f32[4,1,128]{2,1,0:T(1,128)S(1)}, f32[4,1,128]{2,1,0:T(1,128)S(1)}, u32[]{:S(2)}, u32[]{:S(2)}) collective-permute-start(f32[4,1,128]{2,1,0:T(1,128)S(1)} %get-tuple-element.20), channel_id=1, source_target_pairs={{0,20},{1,21},{2,22},{3,23},{4,24},{5,25},{6,26},{7,27},{8,28},{9,... | collective-permute-start | bytes 6152 | tf_op jit(solution)/shard_map/ppermute | solution.py:204
  31.1 0.0 collective-permute-done.3
  31.1 1.3 %collective-permute-start.6 = (f32[4,1,128]{2,1,0:T(1,128)S(1)}, f32[4,1,128]{2,1,0:T(1,128)S(1)}, u32[]{:S(2)}, u32[]{:S(2)}) collective-permute-start(f32[4,1,128]{2,1,0:T(1,128)S(1)} %get-tuple-element.19), channel_id=1, source_target_pairs={{4,16},{5,17},{6,18},{7,19},{8,20},{9,21},{10,22},{11,23},{12,24},... | collective-permute-start | bytes 6152 | tf_op jit(solution)/shard_map/ppermute | solution.py:204
  32.4 0.1 fusion.20
  32.5 0.0 collective-permute-done.refs_1_.refs_5_
  32.5 4.2 %collective-permute-start.7 = (f32[4,8,1]{2,1,0:T(8,128)S(1)}, f32[4,8,1]{2,1,0:T(8,128)S(1)}, u32[]{:S(2)}, u32[]{:S(2)}) collective-permute-start(f32[4,8,1]{2,1,0:T(8,128)S(1)} %get-tuple-element.18), channel_id=1, source_target_pairs={{0,17},{1,18},{2,19},{4,21},{5,22},{6,23},{8,25},{9,26},{10,27},{1... | collective-permute-start | bytes 392 | tf_op jit(solution)/shard_map/ppermute | solution.py:204
  36.7 0.0 collective-permute-done.1.refs_2_.refs_6_
  36.7 1.3 %collective-permute-start.8 = (f32[4,8,1]{2,1,0:T(8,128)S(1)}, f32[4,8,1]{2,1,0:T(8,128)S(1)}, u32[]{:S(2)}, u32[]{:S(2)}) collective-permute-start(f32[4,8,1]{2,1,0:T(8,128)S(1)} %get-tuple-element.17), channel_id=1, source_target_pairs={{1,16},{2,17},{3,18},{5,20},{6,21},{7,22},{9,24},{10,25},{11,26},{... | collective-permute-start | bytes 392 | tf_op jit(solution)/shard_map/ppermute | solution.py:204
  38.0 1.2 %copy.50.refs_4_.refs_8_ = f32[5,32,8,1]{3,2,1,0:T(8,128)} copy(f32[5,32,8,1]{1,2,3,0:T(8,128)S(1)} %collective-permute-done.3) | data formatting | bytes 10240 | tf_op jit(solution)/shard_map/ppermute | solution.py:17
  39.2 0.0 collective-permute-done.7.refs_16_
  39.2 3.3 %collective-permute-done.8.refs_17_ = f32[4,8,1]{2,1,0:T(8,128)S(1)} collective-permute-done((f32[4,8,1]{2,1,0:T(8,128)S(1)}, f32[4,8,1]{2,1,0:T(8,128)S(1)}, u32[]{:S(2)}, u32[]{:S(2)}) %collective-permute-start.8) | collective-permute-done | bytes 160 | tf_op jit(solution)/shard_map/ppermute | solution.py:204
  42.5 0.0 collective-permute-done.5.refs_14_
  42.5 0.0 collective-permute-done.6.refs_15_
  42.5 0.0 collective-permute-done.4.refs_13_
  42.5 0.0 copy-start.8
  42.5 0.5 copy-done.10
  43.1 0.0 copy-done.13
  43.1 0.0 copy-done.8
  43.1 3.9 %shard_map.91.refs_0_ = f32[4,32,8,128]{3,2,1,0:T(8,128)} custom-call(f32[4,32,8,128]{3,2,1,0:T(8,128)} %bitcast.47, f32[5,32,1,128]{3,2,1,0:T(1,128)} %copy-done.2, f32[5,32,1,128]{3,2,1,0:T(1,128)} %copy-done.3, f32[5,32,8,1]{3,2,1,0:T(8,128)} %copy.49.refs_3_.refs_7_, f32[5,32,8,1]{3,2,1,0:T(8,128)} %copy.50.refs_4_.refs_8_, f32[5,32,1,128]{3,2,1,0:T(1,128)} %copy-done.2, ...), custom_call_target="tpu_custom_call" | custom-call | tf_op jit(solution)/shard_map/pallas_call | solution.py:96
  47.0 1.3 %fusion.16 = (f32[4,32,1,128]{3,2,1,0:T(1,128)S(1)}, f32[4,32,1,128]{3,2,1,0:T(1,128)S(1)}) fusion(f32[4,32,8,128]{3,2,1,0:T(8,128)} %shard_map.91.refs_0_), kind=kLoop, calls=%fused_computation.34 | loop fusion | bytes 262144 | tf_op jit(solution)/shard_map/slice | solution.py:107
  48.3 1.3 %collective-permute-start.10 = (f32[4,32,1,128]{3,2,1,0:T(1,128)S(1)}, f32[4,32,1,128]{3,2,1,0:T(1,128)S(1)}, u32[]{:S(2)}, u32[]{:S(2)}) collective-permute-start(f32[4,32,1,128]{3,2,1,0:T(1,128)S(1)} %get-tuple-element.7), channel_id=1, source_target_pairs={{4,0},{8,4},{12,8},{5,1},{9,5},{13,9},{6,2},{10,6},{14,10},{7,3},{... | collective-permute-start | bytes 196616 | tf_op jit(solution)/shard_map/ppermute | solution.py:17
  49.6 4.8 %collective-permute-start.9 = (f32[4,32,1,128]{3,2,1,0:T(1,128)S(1)}, f32[4,32,1,128]{3,2,1,0:T(1,128)S(1)}, u32[]{:S(2)}, u32[]{:S(2)}) collective-permute-start(f32[4,32,1,128]{3,2,1,0:T(1,128)S(1)} %get-tuple-element.8), channel_id=1, source_target_pairs={{0,4},{4,8},{8,12},{1,5},{5,9},{9,13},{2,6},{6,10},{10,14},{3,7},{... | collective-permute-start | bytes 196616 | tf_op jit(solution)/shard_map/ppermute | solution.py:17
  54.4 1.4 %fusion.15 = (f32[4,32,8,1]{3,2,1,0:T(8,128)S(1)}, f32[4,32,8,1]{3,2,1,0:T(8,128)S(1)}) fusion(f32[4,32,8,128]{3,2,1,0:T(8,128)} %shard_map.91.refs_0_), kind=kLoop, calls=%fused_computation.33 | loop fusion | bytes 16384 | tf_op jit(solution)/shard_map/slice | solution.py:109
  55.8 4.9 %collective-permute-start.11 = (f32[4,32,8,1]{3,2,1,0:T(8,128)S(1)}, f32[4,32,8,1]{3,2,1,0:T(8,128)S(1)}, u32[]{:S(2)}, u32[]{:S(2)}) collective-permute-start(f32[4,32,8,1]{3,2,1,0:T(8,128)S(1)} %get-tuple-element.6), channel_id=1, source_target_pairs={{0,1},{1,2},{2,3},{4,5},{5,6},{6,7},{8,9},{9,10},{10,11},{12,13},{... | collective-permute-start | bytes 12296 | tf_op jit(solution)/shard_map/ppermute | solution.py:17
  60.8 1.3 %collective-permute-start.12 = (f32[4,32,8,1]{3,2,1,0:T(8,128)S(1)}, f32[4,32,8,1]{3,2,1,0:T(8,128)S(1)}, u32[]{:S(2)}, u32[]{:S(2)}) collective-permute-start(f32[4,32,8,1]{3,2,1,0:T(8,128)S(1)} %get-tuple-element.5), channel_id=1, source_target_pairs={{1,0},{2,1},{3,2},{5,4},{6,5},{7,6},{9,8},{10,9},{11,10},{13,12},{... | collective-permute-start | bytes 12296 | tf_op jit(solution)/shard_map/ppermute | solution.py:17
  62.1 9.8 %collective-permute-done.11.refs_3_ = f32[4,32,8,1]{3,2,1,0:T(8,128)S(1)} collective-permute-done((f32[4,32,8,1]{3,2,1,0:T(8,128)S(1)}, f32[4,32,8,1]{3,2,1,0:T(8,128)S(1)}, u32[]{:S(2)}, u32[]{:S(2)}) %collective-permute-start.11) | collective-permute-done | bytes 4128 | tf_op jit(solution)/shard_map/ppermute | solution.py:17
  71.9 12.0 %collective-permute-done.12.refs_4_ = f32[4,32,8,1]{3,2,1,0:T(8,128)S(1)} collective-permute-done((f32[4,32,8,1]{3,2,1,0:T(8,128)S(1)}, f32[4,32,8,1]{3,2,1,0:T(8,128)S(1)}, u32[]{:S(2)}, u32[]{:S(2)}) %collective-permute-start.12) | collective-permute-done | bytes 4128 | tf_op jit(solution)/shard_map/ppermute | solution.py:17
  83.9 0.0 collective-permute-done.10.refs_2_
  83.9 0.8 copy-done.5
  84.7 0.0 copy-done.6
  84.7 0.6 copy-done.7
  85.3 3.7 %shard_map.92 = f32[4,32,8,128]{3,2,1,0:T(8,128)} custom-call(f32[4,32,8,128]{3,2,1,0:T(8,128)} %shard_map.91.refs_0_, f32[4,32,1,128]{3,2,1,0:T(1,128)} %copy-done.7, f32[4,32,1,128]{3,2,1,0:T(1,128)} %copy-done.6, f32[4,32,8,1]{3,2,1,0:T(8,128)} %copy-done.4, f32[4,32,8,1]{3,2,1,0:T(8,128)} %copy-done.5, f32[5,32,1,128]{3,2,1,0:T(1,128)} %copy-done.2, ...), custom_call_target="tpu_custom_call" | custom-call | tf_op jit(solution)/shard_map/pallas_call | solution.py:96
  (31 shorter events, 0.1 us)
Async XLA Ops:
  0.0 0.7 copy-start.14
  0.7 1.0 %copy-start.15 = (s32[1,1,1,32]{3,2,1,0:T(1,128)S(1)}, s32[1,1,1,32]{3,2,1,0:T(1,128)}, u32[]{:S(2)}) copy-start(s32[1,1,1,32]{3,2,1,0:T(1,128)} %param.16) | copy-start | bytes 388
  0.7 1.0 %copy-start.16 = (s32[1,1,1,32,1]{3,4,2,1,0:T(1,128)S(1)}, s32[1,1,1,32,1]{3,4,2,1,0:T(1,128)}, u32[]{:S(2)}) copy-start(s32[1,1,1,32,1]{3,4,2,1,0:T(1,128)} %param.14) | copy-start | bytes 388
  1.6 9.7 %copy-start = (f32[1,4,32,8,128]{4,3,2,1,0:T(8,128)S(1)}, f32[1,4,32,8,128]{4,3,2,1,0:T(8,128)}, u32[]{:S(2)}) copy-start(f32[1,4,32,8,128]{4,3,2,1,0:T(8,128)} %param.9) | copy-start | bytes 1572868
  3.0 23.0 %all-to-all-start = ((f32[16,4,640]{2,1,0:T(4,128)}), f32[16,4,640]{2,1,0:T(4,128)S(1)}, u32[]{:S(2)}, u32[]{:S(2)}) async-start(f32[16,4,640]{2,1,0:T(4,128)} %reshape.47), calls=%async_computation | async-start | bytes 327680 | tf_op jit(solution)/shard_map/all_to_all | solution.py:179
  11.6 0.9 %copy-start.1 = (f32[1,32,8,128]{3,2,1,0:T(8,128)S(1)}, f32[1,32,8,128]{3,2,1,0:T(8,128)}, u32[]{:S(2)}) copy-start(f32[1,32,8,128]{3,2,1,0:T(8,128)} %param.11) | copy-start | bytes 393220
  12.7 12.1 %collective-permute-start.2 = (f32[5,32,8,1]{1,2,3,0:T(8,128)S(1)}, f32[5,32,8,1]{1,2,3,0:T(8,128)S(1)}, u32[]{:S(2)}, u32[]{:S(2)}) collective-permute-start(f32[5,32,8,1]{1,2,3,0:T(8,128)S(1)} %pad_maximum_fusion.2), channel_id=1, source_target_pairs={{0,1},{1,2},{2,3},{4,5},{5,6},{6,7},{8,9},{9,10},{10,11},{12,13},{... | collective-permute-start | bytes 15368 | tf_op jit(solution)/shard_map/ppermute | solution.py:17
  17.0 14.1 %collective-permute-start.3 = (f32[5,32,8,1]{1,2,3,0:T(8,128)S(1)}, f32[5,32,8,1]{1,2,3,0:T(8,128)S(1)}, u32[]{:S(2)}, u32[]{:S(2)}) collective-permute-start(f32[5,32,8,1]{1,2,3,0:T(8,128)S(1)} %pad_maximum_fusion.3), channel_id=1, source_target_pairs={{1,0},{2,1},{3,2},{5,4},{6,5},{7,6},{9,8},{10,9},{11,10},{13,12},{... | collective-permute-start | bytes 15368 | tf_op jit(solution)/shard_map/ppermute | solution.py:17
  19.5 13.0 %collective-permute-start = (f32[5,32,1,128]{3,2,1,0:T(1,128)S(1)}, f32[5,32,1,128]{3,2,1,0:T(1,128)S(1)}, u32[]{:S(2)}, u32[]{:S(2)}) collective-permute-start(f32[5,32,1,128]{3,2,1,0:T(1,128)S(1)} %pad_maximum_fusion), channel_id=1, source_target_pairs={{0,4},{4,8},{8,12},{1,5},{5,9},{9,13},{2,6},{6,10},{10,14},{3,7},{... | collective-permute-start | bytes 245768 | tf_op jit(solution)/shard_map/ppermute | solution.py:17
  22.8 1.4 %copy-start.11 = (s32[1,8,128]{2,1,0:T(8,128)S(1)}, s32[1,8,128]{2,1,0:T(8,128)}, u32[]{:S(2)}) copy-start(s32[1,8,128]{2,1,0:T(8,128)} %param.13) | copy-start | bytes 12292
  22.9 13.7 %collective-permute-start.1 = (f32[5,32,1,128]{3,2,1,0:T(1,128)S(1)}, f32[5,32,1,128]{3,2,1,0:T(1,128)S(1)}, u32[]{:S(2)}, u32[]{:S(2)}) collective-permute-start(f32[5,32,1,128]{3,2,1,0:T(1,128)S(1)} %pad_maximum_fusion.1), channel_id=1, source_target_pairs={{4,0},{8,4},{12,8},{5,1},{9,5},{13,9},{6,2},{10,6},{14,10},{7,3},{... | collective-permute-start | bytes 245768 | tf_op jit(solution)/shard_map/ppermute | solution.py:17
  26.4 16.1 %collective-permute-start.4 = (f32[4,8,128]{2,1,0:T(8,128)S(1)}, f32[4,8,128]{2,1,0:T(8,128)S(1)}, u32[]{:S(2)}, u32[]{:S(2)}) collective-permute-start(f32[4,8,128]{2,1,0:T(8,128)S(1)} %convolution_bitcast_fusion), channel_id=1, source_target_pairs={{0,16},{1,17},{2,18},{3,19},{4,20},{5,21},{6,22},{7,23},{8,24},{9,... | collective-permute-start | bytes 49160 | tf_op jit(solution)/shard_map/ppermute | solution.py:204
  26.5 16.0 %collective-permute-start.5 = (f32[4,1,128]{2,1,0:T(1,128)S(1)}, f32[4,1,128]{2,1,0:T(1,128)S(1)}, u32[]{:S(2)}, u32[]{:S(2)}) collective-permute-start(f32[4,1,128]{2,1,0:T(1,128)S(1)} %get-tuple-element.20), channel_id=1, source_target_pairs={{0,20},{1,21},{2,22},{3,23},{4,24},{5,25},{6,26},{7,27},{8,28},{9,... | collective-permute-start | bytes 6152 | tf_op jit(solution)/shard_map/ppermute | solution.py:204
  31.1 11.4 %collective-permute-start.6 = (f32[4,1,128]{2,1,0:T(1,128)S(1)}, f32[4,1,128]{2,1,0:T(1,128)S(1)}, u32[]{:S(2)}, u32[]{:S(2)}) collective-permute-start(f32[4,1,128]{2,1,0:T(1,128)S(1)} %get-tuple-element.19), channel_id=1, source_target_pairs={{4,16},{5,17},{6,18},{7,19},{8,20},{9,21},{10,22},{11,23},{12,24},... | collective-permute-start | bytes 6152 | tf_op jit(solution)/shard_map/ppermute | solution.py:204
  32.5 6.7 %copy-start.2 = (f32[5,32,1,128]{3,2,1,0:T(1,128)}, f32[5,32,1,128]{3,2,1,0:T(1,128)S(1)}, u32[]{:S(2)}) copy-start(f32[5,32,1,128]{3,2,1,0:T(1,128)S(1)} %collective-permute-done.refs_1_.refs_5_) | copy-start | bytes 245764
  32.5 6.7 %collective-permute-start.7 = (f32[4,8,1]{2,1,0:T(8,128)S(1)}, f32[4,8,1]{2,1,0:T(8,128)S(1)}, u32[]{:S(2)}, u32[]{:S(2)}) collective-permute-start(f32[4,8,1]{2,1,0:T(8,128)S(1)} %get-tuple-element.18), channel_id=1, source_target_pairs={{0,17},{1,18},{2,19},{4,21},{5,22},{6,23},{8,25},{9,26},{10,27},{1... | collective-permute-start | bytes 392 | tf_op jit(solution)/shard_map/ppermute | solution.py:204
  36.7 2.5 %copy-start.3 = (f32[5,32,1,128]{3,2,1,0:T(1,128)}, f32[5,32,1,128]{3,2,1,0:T(1,128)S(1)}, u32[]{:S(2)}) copy-start(f32[5,32,1,128]{3,2,1,0:T(1,128)S(1)} %collective-permute-done.1.refs_2_.refs_6_) | copy-start | bytes 245764
  36.7 5.8 %collective-permute-start.8 = (f32[4,8,1]{2,1,0:T(8,128)S(1)}, f32[4,8,1]{2,1,0:T(8,128)S(1)}, u32[]{:S(2)}, u32[]{:S(2)}) collective-permute-start(f32[4,8,1]{2,1,0:T(8,128)S(1)} %get-tuple-element.17), channel_id=1, source_target_pairs={{1,16},{2,17},{3,18},{5,20},{6,21},{7,22},{9,24},{10,25},{11,26},{... | collective-permute-start | bytes 392 | tf_op jit(solution)/shard_map/ppermute | solution.py:204
  39.2 3.3 %copy-start.9 = (f32[4,8,1]{2,1,0:T(8,128)}, f32[4,8,1]{2,1,0:T(8,128)S(1)}, u32[]{:S(2)}) copy-start(f32[4,8,1]{2,1,0:T(8,128)S(1)} %collective-permute-done.7.refs_16_) | copy-start | bytes 388
  42.5 0.6 copy-start.10
  42.5 0.6 copy-start.12
  42.5 0.6 copy-start.13
  42.5 0.6 copy-start.8
  48.3 35.6 %collective-permute-start.10 = (f32[4,32,1,128]{3,2,1,0:T(1,128)S(1)}, f32[4,32,1,128]{3,2,1,0:T(1,128)S(1)}, u32[]{:S(2)}, u32[]{:S(2)}) collective-permute-start(f32[4,32,1,128]{3,2,1,0:T(1,128)S(1)} %get-tuple-element.7), channel_id=1, source_target_pairs={{4,0},{8,4},{12,8},{5,1},{9,5},{13,9},{6,2},{10,6},{14,10},{7,3},{... | collective-permute-start | bytes 196616 | tf_op jit(solution)/shard_map/ppermute | solution.py:17
  49.6 34.3 %collective-permute-start.9 = (f32[4,32,1,128]{3,2,1,0:T(1,128)S(1)}, f32[4,32,1,128]{3,2,1,0:T(1,128)S(1)}, u32[]{:S(2)}, u32[]{:S(2)}) collective-permute-start(f32[4,32,1,128]{3,2,1,0:T(1,128)S(1)} %get-tuple-element.8), channel_id=1, source_target_pairs={{0,4},{4,8},{8,12},{1,5},{5,9},{9,13},{2,6},{6,10},{10,14},{3,7},{... | collective-permute-start | bytes 196616 | tf_op jit(solution)/shard_map/ppermute | solution.py:17
  55.8 16.1 %collective-permute-start.11 = (f32[4,32,8,1]{3,2,1,0:T(8,128)S(1)}, f32[4,32,8,1]{3,2,1,0:T(8,128)S(1)}, u32[]{:S(2)}, u32[]{:S(2)}) collective-permute-start(f32[4,32,8,1]{3,2,1,0:T(8,128)S(1)} %get-tuple-element.6), channel_id=1, source_target_pairs={{0,1},{1,2},{2,3},{4,5},{5,6},{6,7},{8,9},{9,10},{10,11},{12,13},{... | collective-permute-start | bytes 12296 | tf_op jit(solution)/shard_map/ppermute | solution.py:17
  60.8 23.1 %collective-permute-start.12 = (f32[4,32,8,1]{3,2,1,0:T(8,128)S(1)}, f32[4,32,8,1]{3,2,1,0:T(8,128)S(1)}, u32[]{:S(2)}, u32[]{:S(2)}) collective-permute-start(f32[4,32,8,1]{3,2,1,0:T(8,128)S(1)} %get-tuple-element.5), channel_id=1, source_target_pairs={{1,0},{2,1},{3,2},{5,4},{6,5},{7,6},{9,8},{10,9},{11,10},{13,12},{... | collective-permute-start | bytes 12296 | tf_op jit(solution)/shard_map/ppermute | solution.py:17
  71.9 12.0 %copy-start.4 = (f32[4,32,8,1]{3,2,1,0:T(8,128)}, f32[4,32,8,1]{3,2,1,0:T(8,128)S(1)}, u32[]{:S(2)}) copy-start(f32[4,32,8,1]{3,2,1,0:T(8,128)S(1)} %collective-permute-done.11.refs_3_) | copy-start | bytes 12292
  83.9 0.8 copy-start.5
  83.9 0.8 copy-start.6
  84.7 0.6 copy-start.7

commit v2 on v1

v2 whole, which is shorter than its diff:
```python
import jax
import jax.numpy as jnp
from jax import lax
from jax.experimental import pallas as pl
from jax.experimental.pallas import tpu as pltpu
from jax.sharding import PartitionSpec as P

CAP = 4


diffusion = 0.2


def shift(block, axis, step):
    count = lax.axis_size(axis)
    route = [(i, i + step) for i in range(count) if 0 <= i + step < count]
    return lax.ppermute(block, axis, route)


def step_kernel(fields, levels, rows, cols, coupled, emit):
    planes = fields * levels

    def kernel(*refs):
        refs = list(refs)
        a_ref, up_ref, dn_ref, lf_ref, rt_ref, cu_ref, cd_ref, cl_ref, cr_ref = refs[:9]
        ue_ref, un_ref, k_ref, wet_ref = refs[9:13]
        refs = refs[13:]
        if coupled:
            inc_ref = refs.pop(0)
        out_ref = refs.pop(0)
        if emit:
            eu_ref, ed_ref, el_ref, er_ref = refs[:4]
            refs = refs[4:]
        c_ref = refs[0]
        row = lax.broadcasted_iota(jnp.int32, (rows, cols), 0)
        col = lax.broadcasted_iota(jnp.int32, (rows, cols), 1)
        top = row == 0
        bottom = row == rows - 1
        left = col == 0
        right = col == cols - 1
        cprev = [None] * fields
        dprev = [None] * fields
        for l in range(levels):
            ue = ue_ref[l]
            un = un_ref[l]
            ci = planes + l
            ue_m = jnp.where(top, cu_ref[pl.ds(ci, 1), :], pltpu.roll(ue, 1, 0))
            ue_p = jnp.where(bottom, cd_ref[pl.ds(ci, 1), :], pltpu.roll(ue, rows - 1, 0))
            un_m = jnp.where(left, cl_ref[:, pl.ds(ci, 1)], pltpu.roll(un, 1, 1))
            un_p = jnp.where(right, cr_ref[:, pl.ds(ci, 1)], pltpu.roll(un, cols - 1, 1))
            for f in range(fields):
                k = f * levels + l
                a = a_ref[f, l]
                if coupled and l == 0:
                    a = a + inc_ref[f]
                a_im = jnp.where(top, up_ref[pl.ds(k, 1), :], pltpu.roll(a, 1, 0))
                a_ip = jnp.where(bottom, dn_ref[pl.ds(k, 1), :], pltpu.roll(a, rows - 1, 0))
                a_jm = jnp.where(left, lf_ref[:, pl.ds(k, 1)], pltpu.roll(a, 1, 1))
                a_jp = jnp.where(right, rt_ref[:, pl.ds(k, 1)], pltpu.roll(a, cols - 1, 1))
                laplace = a_ip + a_im + a_jp + a_jm - 4.0 * a
                advect = 0.5 * (ue_m * a_im - ue_p * a_ip) + 0.5 * (un_m * a_jm - un_p * a_jp)
                h = a + diffusion * laplace + advect
                if l < levels - 1:
                    kd = k_ref[f, l]
                    diagonal = 1.0 + kd
                else:
                    diagonal = 1.0
                if l > 0:
                    kp = k_ref[f, l - 1]
                    divisor = diagonal + kp + kp * cprev[f]
                    numerator = h + kp * dprev[f]
                else:
                    divisor = diagonal
                    numerator = h
                if l < levels - 1:
                    cprev[f] = -kd / divisor
                    c_ref[f, l] = cprev[f]
                dprev[f] = numerator / divisor
                out_ref[f, l] = dprev[f]
        wet = wet_ref[...]
        if emit:
            sub = lax.broadcasted_iota(jnp.int32, (8, cols), 0)
            lane = lax.broadcasted_iota(jnp.int32, (rows, planes), 1)
            last_cols = jnp.zeros((rows, planes), jnp.float32)
            first_cols = jnp.zeros((rows, planes), jnp.float32)
            last_rows = jnp.zeros((8, cols), jnp.float32)
            first_rows = jnp.zeros((8, cols), jnp.float32)
        for f in range(fields):
            r = dprev[f]
            for l in range(levels - 1, -1, -1):
                if l < levels - 1:
                    r = out_ref[f, l] - c_ref[f, l] * r
                v = r * wet
                out_ref[f, l] = v
                if emit:
                    k = f * levels + l
                    last_rows = jnp.where(sub == k % 8, v[rows - 1 : rows, :], last_rows)
                    first_rows = jnp.where(sub == k % 8, v[0:1, :], first_rows)
                    last_cols = jnp.where(lane == k, v[:, cols - 1 : cols], last_cols)
                    first_cols = jnp.where(lane == k, v[:, 0:1], first_cols)
                    if k % 8 == 0:
                        eu_ref[pl.ds(k, 8), :] = last_rows
                        ed_ref[pl.ds(k, 8), :] = first_rows
        if emit:
            el_ref[...] = last_cols
            er_ref[...] = first_cols

    return kernel


def run_step(a, halos, coef_halos, ue, un, coeffs, wet, inc=None, emit=False):
    fields, levels, rows, cols = a.shape
    planes = fields * levels
    coupled = inc is not None
    operands = [a, *halos, *coef_halos, ue, un, coeffs, wet]
    if coupled:
        operands.append(inc)
    shapes = [jax.ShapeDtypeStruct(a.shape, jnp.float32)]
    if emit:
        shapes += [jax.ShapeDtypeStruct((planes, cols), jnp.float32)] * 2
        shapes += [jax.ShapeDtypeStruct((rows, planes), jnp.float32)] * 2
    return pl.pallas_call(
        step_kernel(fields, levels, rows, cols, coupled, emit),
        out_shape=shapes,
        scratch_shapes=[pltpu.VMEM(a.shape, jnp.float32)],
    )(*operands)


def shards(
    adjoint_in, u_east, u_north, diffusivity, wet_mask, dest_tile, src_row, dst_row, area_weight
):
    adjoint = adjoint_in[0]
    fields, levels, rows_x, cols_y = adjoint.shape
    planes = fields * levels
    sections = lax.axis_size("comp")
    tiles_x = lax.axis_size("gx")
    tiles_y = lax.axis_size("gy")
    tiles = tiles_x * tiles_y
    section = lax.axis_index("comp")
    east = u_east[0]
    north = u_north[0]
    coeffs = diffusivity[0]
    wet = wet_mask[0].astype(jnp.float32)

    targets = dest_tile[0, 0, 0, :, 0]
    sources = src_row[0, 0, 0]
    landing = dst_row[0, 0, 0]
    weights = area_weight[0, 0, 0]
    count = targets.shape[0]
    surface_rows = jnp.transpose(adjoint[:, 0], (1, 0, 2)).reshape(rows_x, fields * cols_y)
    pick_table = (sources[:, None] == jnp.arange(rows_x, dtype=jnp.int32)[None, :]).astype(
        jnp.float32
    )
    payload = jnp.dot(
        pick_table,
        surface_rows,
        precision=lax.Precision.HIGHEST,
        preferred_element_type=jnp.float32,
    )
    payload = (payload.reshape(count, fields, cols_y) * weights[:, None, :]).reshape(
        count, fields * cols_y
    )
    tag = jnp.broadcast_to((landing + 1).astype(jnp.float32)[:, None], (count, cols_y))
    tagged = jnp.concatenate([payload, tag], axis=1)
    order_ids = jnp.arange(count, dtype=jnp.int32)
    earlier = (targets[:, None] == targets[None, :]) & (order_ids[None, :] < order_ids[:, None])
    rank_in = jnp.sum(earlier.astype(jnp.int32), axis=1)
    slot_ids = ((sections - 1 - section) * tiles + targets) * CAP + rank_in
    placing = slot_ids[:, None] == jnp.arange(sections * tiles * CAP, dtype=jnp.int32)[None, :]
    send_data = jnp.dot(
        placing.astype(jnp.float32).T,
        tagged,
        precision=lax.Precision.HIGHEST,
        preferred_element_type=jnp.float32,
    )
    width = (fields + 1) * cols_y
    got = lax.all_to_all(
        send_data.reshape(sections * tiles, CAP, width),
        ("comp", "gx", "gy"),
        split_axis=0,
        concat_axis=0,
        tiled=True,
    ).reshape(sections * tiles * CAP, width)
    got_rows = got[:, fields * cols_y]
    row_table = (
        got_rows[None, :] == (jnp.arange(rows_x, dtype=jnp.int32) + 1).astype(jnp.float32)[:, None]
    ).astype(jnp.float32)
    increment = jnp.dot(
        row_table,
        got[:, : fields * cols_y],
        precision=lax.Precision.HIGHEST,
        preferred_element_type=jnp.float32,
    )
    increment = jnp.transpose(increment.reshape(rows_x, fields, cols_y), (1, 0, 2))

    def row_edge(index):
        field_rows = adjoint[:, :, index, :].at[:, 0].add(increment[:, index, :])
        return jnp.concatenate([field_rows.reshape(planes, cols_y), east[:, index, :]], 0)

    def col_edge(index):
        field_cols = adjoint[:, :, :, index].at[:, 0].add(increment[:, :, index])
        field_cols = jnp.transpose(field_cols, (2, 0, 1)).reshape(rows_x, planes)
        return jnp.concatenate([field_cols, north[:, :, index].T], 1)

    halos = (
        shift(row_edge(rows_x - 1), "gx", 1),
        shift(row_edge(0), "gx", -1),
        shift(col_edge(cols_y - 1), "gy", 1),
        shift(col_edge(0), "gy", -1),
    )

    middle, last_rows, first_rows, last_cols, first_cols = run_step(
        adjoint, halos, halos, east, north, coeffs, wet, inc=increment, emit=True
    )
    step_halos = (
        shift(last_rows, "gx", 1),
        shift(first_rows, "gx", -1),
        shift(last_cols, "gy", 1),
        shift(first_cols, "gy", -1),
    )
    (result,) = run_step(middle, step_halos, halos, east, north, coeffs, wet)
    return result[None]


def solution(mesh):
    placed = (
        P("comp", None, None, "gx", "gy"),
        P("comp", None, "gx", "gy"),
        P("comp", None, "gx", "gy"),
        P("comp", None, None, "gx", "gy"),
        P("comp", "gx", "gy"),
        P("comp", "gx", "gy", None, None),
        P("comp", "gx", "gy", None),
        P("comp", "gx", "gy", None),
        P("comp", "gx", "gy", None, None),
    )
    return jax.shard_map(
        shards,
        mesh=mesh,
        in_specs=placed,
        out_specs=P("comp", None, None, "gx", "gy"),
        check_vma=False,
    )
```

time: 89.7 us -> 63.1 us (0.70)
  the two profiles are of different devices: /device:TPU:0 before, /device:TPU:10 now
where the time goes in v2:
time: 63.1 us; the launch traced here: 62.5 us
  starting transfers between devices  31.2 us (49%)
  waiting for transfers between devices  11.8 us (19%)
  local copies, waits for them, and re-layouts  11 us (17%)
  Pallas kernels  6.49 us (10%)
  matrix products  0.85 us (1%)
  other arithmetic  0.84 us (1%)
    ppermute x8, starting transfers between devices, shift(): return lax.ppermute(block, axis, route)  25.2 us
    all_to_all x1, waiting for transfers between devices, shards(): lax.all_to_all(send_data.reshape(sections * tiles, CAP, width), ('comp',...  6.9 us
    pallas_call x2, Pallas kernels, run_step(): pl.pallas_call(step_kernel(fields, levels, rows, cols, coupled, emit), ou...  6.49 us
    all_to_all x1, starting transfers between devices, shards(): lax.all_to_all(send_data.reshape(sections * tiles, CAP, width), ('comp',...  6.02 us
    unnamed x34, local copies, waits for them, and re-layouts  5.7 us
    ppermute x8, waiting for transfers between devices, shift(): return lax.ppermute(block, axis, route)  4.87 us
  transfers between devices with their start and end apart: 9, of which 3 were waited for; matrix products, arithmetic and copies ran while one was open for 7% of the time, Pallas kernels for 0%

profile of v2, /device:TPU:10, one launch (start us, length us, event | category | flops | bytes accessed | tf_op | source)
XLA Modules:
  0.0 62.5 jit_solution(2398636739879068576)
XLA Ops:
  0.0 1.4 %copy.110 = f32[1,4,32,8,128]{4,1,3,2,0:T(4,128)S(1)} copy(f32[1,4,32,8,128]{4,3,2,1,0:T(8,128)} %param.17) | data formatting | bytes 1048576 | tf_op args[0]
  1.4 0.0 copy-start.8
  1.4 0.0 copy-start.12
  1.4 0.7 %copy-done.8 = f32[1,1,1,32,128]{4,3,2,1,0:T(8,128)S(1)} copy-done((f32[1,1,1,32,128]{4,3,2,1,0:T(8,128)S(1)}, f32[1,1,1,32,128]{4,3,2,1,0:T(8,128)}, u32[]{:S(2)}) %copy-start.8) | copy-done | bytes 16408
  2.1 0.0 copy-done.12
  2.1 0.2 fusion
  2.3 0.0 copy-start.15
  2.4 0.6 %copy-done.15 = s32[1,1,1,32]{3,2,1,0:T(1,128)S(1)} copy-done((s32[1,1,1,32]{3,2,1,0:T(1,128)S(1)}, s32[1,1,1,32]{3,2,1,0:T(1,128)}, u32[]{:S(2)}) %copy-start.15) | copy-done | bytes 152
  3.0 0.7 %copy-done.13 = s32[1,1,1,32,1]{3,4,2,1,0:T(1,128)S(1)} copy-done((s32[1,1,1,32,1]{3,4,2,1,0:T(1,128)S(1)}, s32[1,1,1,32,1]{3,4,2,1,0:T(1,128)}, u32[]{:S(2)}) %copy-start.13) | copy-done | bytes 152
  3.7 0.2 convert_reduce_fusion
  3.8 0.1 broadcast_in_dim.4
  3.9 0.4 fusion.2
  4.3 0.8 %reshape.219 = f32[32,4,640]{2,1,0:T(4,128)} reshape(f32[128,640]{1,0:T(8,128)S(1)} %fusion.2) | data formatting | bytes 655360 | tf_op jit(solution)/shard_map/reshape | solution.py:178
  5.1 6.0 %all-to-all-start = ((f32[32,4,640]{2,1,0:T(4,128)}), f32[32,4,640]{2,1,0:T(4,128)S(1)}, u32[]{:S(2)}, u32[]{:S(2)}) async-start(f32[32,4,640]{2,1,0:T(4,128)} %reshape.219), calls=%async_computation | async-start | bytes 655360 | tf_op jit(solution)/shard_map/all_to_all | solution.py:177
  11.2 0.0 copy-start
  11.2 0.3 fusion.19
  11.5 0.5 copy-done
  12.1 0.1 fusion.20
  12.2 0.1 fusion.18
  12.3 0.1 copy.91
  12.4 0.1 copy.96
  12.5 0.4 copy.95
  12.8 0.1 copy.99
  13.0 0.4 copy.90
  13.4 0.1 copy.94
  13.5 1.0 %fusion.21 = (f32[32,1,128]{2,1,0:T(1,128)S(1)}, f32[32,1,128]{2,1,0:T(1,128)S(1)}) fusion(f32[32,8,128]{2,1,0:T(8,128)} %bitcast.87), kind=kLoop, calls=%fused_computation.48 | loop fusion | bytes 65536 | tf_op jit(solution)/shard_map/slice | solution.py:198
  14.5 6.9 %all-to-all-done = f32[32,4,640]{2,1,0:T(4,128)S(1)} async-done(((f32[32,4,640]{2,1,0:T(4,128)}), f32[32,4,640]{2,1,0:T(4,128)S(1)}, u32[]{:S(2)}, u32[]{:S(2)}) %all-to-all-start) | async-done | bytes 327712 | tf_op jit(solution)/shard_map/all_to_all | solution.py:177
  21.4 0.1 reshape.220
  21.6 0.1 slice_reduce_fusion
  21.7 0.2 convolution_bitcast_fusion.refs_13_
  21.9 0.1 slice_reduce_fusion.1
  22.0 0.5 copy-done.3
  22.5 3.2 %collective-permute-start.1 = (f32[160,128]{1,0:T(8,128)S(1)}, f32[160,128]{1,0:T(8,128)S(1)}, u32[]{:S(2)}, u32[]{:S(2)}) collective-permute-start(f32[160,128]{1,0:T(8,128)S(1)} %pad_maximum_fusion.1), channel_id=1, source_target_pairs={{4,0},{8,4},{12,8},{5,1},{9,5},{13,9},{6,2},{10,6},{14,10},{7,3},{... | collective-permute-start | bytes 245768 | tf_op jit(solution)/shard_map/ppermute | solution.py:17
  25.8 2.6 %collective-permute-start = (f32[160,128]{1,0:T(8,128)S(1)}, f32[160,128]{1,0:T(8,128)S(1)}, u32[]{:S(2)}, u32[]{:S(2)}) collective-permute-start(f32[160,128]{1,0:T(8,128)S(1)} %pad_maximum_fusion), channel_id=1, source_target_pairs={{0,4},{4,8},{8,12},{1,5},{5,9},{9,13},{2,6},{6,10},{10,14},{3,7},{... | collective-permute-start | bytes 245768 | tf_op jit(solution)/shard_map/ppermute | solution.py:17
  28.4 0.1 copy.97
  28.6 0.1 reshape.230
  28.7 3.0 %collective-permute-start.3 = (f32[8,160]{1,0:T(8,128)S(1)}, f32[8,160]{1,0:T(8,128)S(1)}, u32[]{:S(2)}, u32[]{:S(2)}) collective-permute-start(f32[8,160]{1,0:T(8,128)S(1)} %pad_maximum_fusion.3), channel_id=1, source_target_pairs={{1,0},{2,1},{3,2},{5,4},{6,5},{7,6},{9,8},{10,9},{11,10},{13,12},{... | collective-permute-start | bytes 15368 | tf_op jit(solution)/shard_map/ppermute | solution.py:17
  31.7 0.1 copy.92
  31.9 0.1 reshape.227
  32.0 3.8 %collective-permute-start.2 = (f32[8,160]{1,0:T(8,128)S(1)}, f32[8,160]{1,0:T(8,128)S(1)}, u32[]{:S(2)}, u32[]{:S(2)}) collective-permute-start(f32[8,160]{1,0:T(8,128)S(1)} %pad_maximum_fusion.2), channel_id=1, source_target_pairs={{0,1},{1,2},{2,3},{4,5},{5,6},{6,7},{8,9},{9,10},{10,11},{12,13},{... | collective-permute-start | bytes 15368 | tf_op jit(solution)/shard_map/ppermute | solution.py:17
  35.8 0.6 convert_bitcast_fusion.refs_12_
  36.4 0.8 %copy.100.refs_0_ = f32[4,32,8,128]{3,2,1,0:T(8,128)} copy(f32[4,32,8,128]{3,0,2,1:T(4,128)S(1)} %bitcast.81) | data formatting | bytes 1048576 | tf_op jit(solution)/shard_map/squeeze | solution.py:132
  37.2 0.0 collective-permute-done.3.refs_4_.refs_8_
  37.2 0.4 collective-permute-done.2.refs_3_.refs_7_
  37.6 0.0 collective-permute-done.1.refs_2_.refs_6_
  37.6 0.0 collective-permute-done.refs_1_.refs_5_
  37.7 0.2 copy-done.4
  37.8 0.4 copy-done.5
  38.2 0.1 copy-done.1
  38.3 0.0 copy-done.2
  38.3 3.3 %shard_map.91 = (f32[4,32,8,128]{3,2,1,0:T(8,128)}, f32[128,128]{1,0:T(8,128)}, f32[128,128]{1,0:T(8,128)}, f32[8,128]{1,0:T(8,128)}, f32[8,128]{1,0:T(8,128)}) custom-call(f32[4,32,8,128]{3,2,1,0:T(8,128)} %copy.100.refs_0_, f32[160,128]{1,0:T(8,128)} %copy-done.2, f32[160,128]{1,0:T(8,128)} %copy-done.1, f32[8,160]{1,0:T(8,128)} %copy-done.5, ...), custom_call_target="tpu_custom_call" | custom-call | tf_op jit(solution)/shard_map/pallas_call | solution.py:122
  41.7 2.4 %collective-permute-start.4 = (f32[128,128]{1,0:T(8,128)}, f32[128,128]{1,0:T(8,128)S(1)}, u32[]{:S(2)}, u32[]{:S(2)}) collective-permute-start(f32[128,128]{1,0:T(8,128)} %get-tuple-element.59), channel_id=1, source_target_pairs={{0,4},{4,8},{8,12},{1,5},{5,9},{9,13},{2,6},{6,10},{10,14},{3,7},{... | collective-permute-start | bytes 196616 | tf_op jit(solution)/shard_map/ppermute | solution.py:17
  44.0 3.6 %collective-permute-start.5 = (f32[128,128]{1,0:T(8,128)}, f32[128,128]{1,0:T(8,128)S(1)}, u32[]{:S(2)}, u32[]{:S(2)}) collective-permute-start(f32[128,128]{1,0:T(8,128)} %get-tuple-element.60), channel_id=1, source_target_pairs={{4,0},{8,4},{12,8},{5,1},{9,5},{13,9},{6,2},{10,6},{14,10},{7,3},{... | collective-permute-start | bytes 196616 | tf_op jit(solution)/shard_map/ppermute | solution.py:17
  47.6 4.6 %collective-permute-start.6 = (f32[8,128]{1,0:T(8,128)}, f32[8,128]{1,0:T(8,128)S(1)}, u32[]{:S(2)}, u32[]{:S(2)}) collective-permute-start(f32[8,128]{1,0:T(8,128)} %get-tuple-element.61), channel_id=1, source_target_pairs={{0,1},{1,2},{2,3},{4,5},{5,6},{6,7},{8,9},{9,10},{10,11},{12,13},{... | collective-permute-start | bytes 12296 | tf_op jit(solution)/shard_map/ppermute | solution.py:17
  52.2 0.0 copy-done.14
  52.2 1.9 %collective-permute-start.7 = (f32[8,128]{1,0:T(8,128)S(1)}, f32[8,128]{1,0:T(8,128)S(1)}, u32[]{:S(2)}, u32[]{:S(2)}) collective-permute-start(f32[8,128]{1,0:T(8,128)S(1)} %copy-done.14), channel_id=1, source_target_pairs={{1,0},{2,1},{3,2},{5,4},{6,5},{7,6},{9,8},{10,9},{11,10},{13,12},{... | collective-permute-start | bytes 12296 | tf_op jit(solution)/shard_map/ppermute | solution.py:17
  54.2 0.0 collective-permute-done.6.refs_3_
  54.2 4.5 %collective-permute-done.7.refs_4_ = f32[8,128]{1,0:T(8,128)S(1)} collective-permute-done((f32[8,128]{1,0:T(8,128)S(1)}, f32[8,128]{1,0:T(8,128)S(1)}, u32[]{:S(2)}, u32[]{:S(2)}) %collective-permute-start.7) | collective-permute-done | bytes 4128 | tf_op jit(solution)/shard_map/ppermute | solution.py:17
  58.6 0.0 collective-permute-done.4.refs_1_
  58.7 0.0 collective-permute-done.5.refs_2_
  58.7 0.6 copy-done.10
  59.2 0.0 copy-done.6
  59.3 0.0 copy-done.7
  59.3 3.1 %shard_map.92 = f32[4,32,8,128]{3,2,1,0:T(8,128)} custom-call(f32[4,32,8,128]{3,2,1,0:T(8,128)} %get-tuple-element.58.refs_0_, f32[128,128]{1,0:T(8,128)} %copy-done.6, f32[128,128]{1,0:T(8,128)} %copy-done.7, f32[8,128]{1,0:T(8,128)} %copy-done.9, f32[8,128]{1,0:T(8,128)} %copy-done.10, f32[160,128]{1,0:T(8,128)} %copy-done.2, f32[160,128]{1,0:T(8,128)} %copy-done.1, ...), custom_call_target="tpu_custom_call" | custom-call | tf_op jit(solution)/shard_map/pallas_call | solution.py:122
  (34 shorter events, 0.2 us)
Async XLA Ops:
  1.4 0.7 %copy-start.8 = (f32[1,1,1,32,128]{4,3,2,1,0:T(8,128)S(1)}, f32[1,1,1,32,128]{4,3,2,1,0:T(8,128)}, u32[]{:S(2)}) copy-start(f32[1,1,1,32,128]{4,3,2,1,0:T(8,128)} %param.25) | copy-start | bytes 49156
  1.4 0.7 %copy-start.12 = (s32[1,1,1,32]{3,2,1,0:T(1,128)S(1)}, s32[1,1,1,32]{3,2,1,0:T(1,128)}, u32[]{:S(2)}) copy-start(s32[1,1,1,32]{3,2,1,0:T(1,128)} %param.23) | copy-start | bytes 388
  2.3 0.7 %copy-start.15 = (s32[1,1,1,32]{3,2,1,0:T(1,128)S(1)}, s32[1,1,1,32]{3,2,1,0:T(1,128)}, u32[]{:S(2)}) copy-start(s32[1,1,1,32]{3,2,1,0:T(1,128)} %param.24) | copy-start | bytes 388
  3.0 0.7 %copy-start.13 = (s32[1,1,1,32,1]{3,4,2,1,0:T(1,128)S(1)}, s32[1,1,1,32,1]{3,4,2,1,0:T(1,128)}, u32[]{:S(2)}) copy-start(s32[1,1,1,32,1]{3,4,2,1,0:T(1,128)} %param.22) | copy-start | bytes 388
  5.1 16.3 %all-to-all-start = ((f32[32,4,640]{2,1,0:T(4,128)}), f32[32,4,640]{2,1,0:T(4,128)S(1)}, u32[]{:S(2)}, u32[]{:S(2)}) async-start(f32[32,4,640]{2,1,0:T(4,128)} %reshape.219), calls=%async_computation | async-start | bytes 655360 | tf_op jit(solution)/shard_map/all_to_all | solution.py:177
  11.2 0.9 %copy-start = (f32[1,32,8,128]{3,2,1,0:T(8,128)S(1)}, f32[1,32,8,128]{3,2,1,0:T(8,128)}, u32[]{:S(2)}) copy-start(f32[1,32,8,128]{3,2,1,0:T(8,128)} %param.19) | copy-start | bytes 393220
  21.9 0.6 copy-start.3
  22.5 15.1 %collective-permute-start.1 = (f32[160,128]{1,0:T(8,128)S(1)}, f32[160,128]{1,0:T(8,128)S(1)}, u32[]{:S(2)}, u32[]{:S(2)}) collective-permute-start(f32[160,128]{1,0:T(8,128)S(1)} %pad_maximum_fusion.1), channel_id=1, source_target_pairs={{4,0},{8,4},{12,8},{5,1},{9,5},{13,9},{6,2},{10,6},{14,10},{7,3},{... | collective-permute-start | bytes 245768 | tf_op jit(solution)/shard_map/ppermute | solution.py:17
  25.8 11.8 %collective-permute-start = (f32[160,128]{1,0:T(8,128)S(1)}, f32[160,128]{1,0:T(8,128)S(1)}, u32[]{:S(2)}, u32[]{:S(2)}) collective-permute-start(f32[160,128]{1,0:T(8,128)S(1)} %pad_maximum_fusion), channel_id=1, source_target_pairs={{0,4},{4,8},{8,12},{1,5},{5,9},{9,13},{2,6},{6,10},{10,14},{3,7},{... | collective-permute-start | bytes 245768 | tf_op jit(solution)/shard_map/ppermute | solution.py:17
  28.7 8.5 %collective-permute-start.3 = (f32[8,160]{1,0:T(8,128)S(1)}, f32[8,160]{1,0:T(8,128)S(1)}, u32[]{:S(2)}, u32[]{:S(2)}) collective-permute-start(f32[8,160]{1,0:T(8,128)S(1)} %pad_maximum_fusion.3), channel_id=1, source_target_pairs={{1,0},{2,1},{3,2},{5,4},{6,5},{7,6},{9,8},{10,9},{11,10},{13,12},{... | collective-permute-start | bytes 15368 | tf_op jit(solution)/shard_map/ppermute | solution.py:17
  32.0 3.8 %copy-start.11 = (s32[1,8,128]{2,1,0:T(8,128)S(1)}, s32[1,8,128]{2,1,0:T(8,128)}, u32[]{:S(2)}) copy-start(s32[1,8,128]{2,1,0:T(8,128)} %param.21) | copy-start | bytes 12292
  32.0 5.7 %collective-permute-start.2 = (f32[8,160]{1,0:T(8,128)S(1)}, f32[8,160]{1,0:T(8,128)S(1)}, u32[]{:S(2)}, u32[]{:S(2)}) collective-permute-start(f32[8,160]{1,0:T(8,128)S(1)} %pad_maximum_fusion.2), channel_id=1, source_target_pairs={{0,1},{1,2},{2,3},{4,5},{5,6},{6,7},{8,9},{9,10},{10,11},{12,13},{... | collective-permute-start | bytes 15368 | tf_op jit(solution)/shard_map/ppermute | solution.py:17
  37.2 0.6 copy-start.4
  37.6 0.6 copy-start.5
  37.6 0.6 %copy-start.1 = (f32[160,128]{1,0:T(8,128)}, f32[160,128]{1,0:T(8,128)S(1)}, u32[]{:S(2)}) copy-start(f32[160,128]{1,0:T(8,128)S(1)} %collective-permute-done.1.refs_2_.refs_6_) | copy-start | bytes 245764
  37.6 0.7 %copy-start.2 = (f32[160,128]{1,0:T(8,128)}, f32[160,128]{1,0:T(8,128)S(1)}, u32[]{:S(2)}) copy-start(f32[160,128]{1,0:T(8,128)S(1)} %collective-permute-done.refs_1_.refs_5_) | copy-start | bytes 245764
  41.6 10.6 %copy-start.14 = (f32[8,128]{1,0:T(8,128)S(1)}, f32[8,128]{1,0:T(8,128)}, u32[]{:S(2)}) copy-start(f32[8,128]{1,0:T(8,128)} %get-tuple-element.62) | copy-start | bytes 12292
  41.7 17.0 %collective-permute-start.4 = (f32[128,128]{1,0:T(8,128)}, f32[128,128]{1,0:T(8,128)S(1)}, u32[]{:S(2)}, u32[]{:S(2)}) collective-permute-start(f32[128,128]{1,0:T(8,128)} %get-tuple-element.59), channel_id=1, source_target_pairs={{0,4},{4,8},{8,12},{1,5},{5,9},{9,13},{2,6},{6,10},{10,14},{3,7},{... | collective-permute-start | bytes 196616 | tf_op jit(solution)/shard_map/ppermute | solution.py:17
  44.0 14.6 %collective-permute-start.5 = (f32[128,128]{1,0:T(8,128)}, f32[128,128]{1,0:T(8,128)S(1)}, u32[]{:S(2)}, u32[]{:S(2)}) collective-permute-start(f32[128,128]{1,0:T(8,128)} %get-tuple-element.60), channel_id=1, source_target_pairs={{4,0},{8,4},{12,8},{5,1},{9,5},{13,9},{6,2},{10,6},{14,10},{7,3},{... | collective-permute-start | bytes 196616 | tf_op jit(solution)/shard_map/ppermute | solution.py:17
  47.6 6.6 %collective-permute-start.6 = (f32[8,128]{1,0:T(8,128)}, f32[8,128]{1,0:T(8,128)S(1)}, u32[]{:S(2)}, u32[]{:S(2)}) collective-permute-start(f32[8,128]{1,0:T(8,128)} %get-tuple-element.61), channel_id=1, source_target_pairs={{0,1},{1,2},{2,3},{4,5},{5,6},{6,7},{8,9},{9,10},{10,11},{12,13},{... | collective-permute-start | bytes 12296 | tf_op jit(solution)/shard_map/ppermute | solution.py:17
  52.2 6.4 %collective-permute-start.7 = (f32[8,128]{1,0:T(8,128)S(1)}, f32[8,128]{1,0:T(8,128)S(1)}, u32[]{:S(2)}, u32[]{:S(2)}) collective-permute-start(f32[8,128]{1,0:T(8,128)S(1)} %copy-done.14), channel_id=1, source_target_pairs={{1,0},{2,1},{3,2},{5,4},{6,5},{7,6},{9,8},{10,9},{11,10},{13,12},{... | collective-permute-start | bytes 12296 | tf_op jit(solution)/shard_map/ppermute | solution.py:17
  54.2 4.5 %copy-start.9 = (f32[8,128]{1,0:T(8,128)}, f32[8,128]{1,0:T(8,128)S(1)}, u32[]{:S(2)}) copy-start(f32[8,128]{1,0:T(8,128)S(1)} %collective-permute-done.6.refs_3_) | copy-start | bytes 12292
  58.6 0.6 copy-start.10
  58.7 0.6 copy-start.6
  58.7 0.7 %copy-start.7 = (f32[128,128]{1,0:T(8,128)}, f32[128,128]{1,0:T(8,128)S(1)}, u32[]{:S(2)}) copy-start(f32[128,128]{1,0:T(8,128)S(1)} %collective-permute-done.5.refs_2_) | copy-start | bytes 196612

commit v3 on v2

--- a/solution.py
+++ b/solution.py
@@ -27,6 +27,7 @@
         refs = refs[13:]
         if coupled:
             inc_ref = refs.pop(0)
+            ic_ref = refs.pop(0)
         out_ref = refs.pop(0)
         if emit:
             eu_ref, ed_ref, el_ref, er_ref = refs[:4]
@@ -51,12 +52,21 @@
             for f in range(fields):
                 k = f * levels + l
                 a = a_ref[f, l]
+                up = up_ref[pl.ds(k, 1), :]
+                dn = dn_ref[pl.ds(k, 1), :]
+                lf = lf_ref[:, pl.ds(k, 1)]
+                rt = rt_ref[:, pl.ds(k, 1)]
                 if coupled and l == 0:
-                    a = a + inc_ref[f]
-                a_im = jnp.where(top, up_ref[pl.ds(k, 1), :], pltpu.roll(a, 1, 0))
-                a_ip = jnp.where(bottom, dn_ref[pl.ds(k, 1), :], pltpu.roll(a, rows - 1, 0))
-                a_jm = jnp.where(left, lf_ref[:, pl.ds(k, 1)], pltpu.roll(a, 1, 1))
-                a_jp = jnp.where(right, rt_ref[:, pl.ds(k, 1)], pltpu.roll(a, cols - 1, 1))
+                    lanes = pl.ds(f * cols, cols)
+                    a = a + inc_ref[pl.ds(0, rows), lanes]
+                    up = up + inc_ref[pl.ds(rows, 1), lanes]
+                    dn = dn + inc_ref[pl.ds(rows + 1, 1), lanes]
+                    lf = lf + ic_ref[:, pl.ds(f, 1)]
+                    rt = rt + ic_ref[:, pl.ds(fields + f, 1)]
+                a_im = jnp.where(top, up, pltpu.roll(a, 1, 0))
+                a_ip = jnp.where(bottom, dn, pltpu.roll(a, rows - 1, 0))
+                a_jm = jnp.where(left, lf, pltpu.roll(a, 1, 1))
+                a_jp = jnp.where(right, rt, pltpu.roll(a, cols - 1, 1))
                 laplace = a_ip + a_im + a_jp + a_jm - 4.0 * a
                 advect = 0.5 * (ue_m * a_im - ue_p * a_ip) + 0.5 * (un_m * a_jm - un_p * a_jp)
                 h = a + diffusion * laplace + advect
@@ -114,7 +124,7 @@
     coupled = inc is not None
     operands = [a, *halos, *coef_halos, ue, un, coeffs, wet]
     if coupled:
-        operands.append(inc)
+        operands += list(inc)
     shapes = [jax.ShapeDtypeStruct(a.shape, jnp.float32)]
     if emit:
         shapes += [jax.ShapeDtypeStruct((planes, cols), jnp.float32)] * 2
@@ -142,6 +152,21 @@
     coeffs = diffusivity[0]
     wet = wet_mask[0].astype(jnp.float32)
 
+    def row_edge(index):
+        field_rows = adjoint[:, :, index, :].reshape(planes, cols_y)
+        return jnp.concatenate([field_rows, east[:, index, :]], 0)
+
+    def col_edge(index):
+        field_cols = jnp.transpose(adjoint[:, :, :, index], (2, 0, 1)).reshape(rows_x, planes)
+        return jnp.concatenate([field_cols, north[:, :, index].T], 1)
+
+    halos = (
+        shift(row_edge(rows_x - 1), "gx", 1),
+        shift(row_edge(0), "gx", -1),
+        shift(col_edge(cols_y - 1), "gy", 1),
+        shift(col_edge(0), "gy", -1),
+    )
+
     targets = dest_tile[0, 0, 0, :, 0]
     sources = src_row[0, 0, 0]
     landing = dst_row[0, 0, 0]
@@ -160,57 +185,45 @@
     payload = (payload.reshape(count, fields, cols_y) * weights[:, None, :]).reshape(
         count, fields * cols_y
     )
-    tag = jnp.broadcast_to((landing + 1).astype(jnp.float32)[:, None], (count, cols_y))
-    tagged = jnp.concatenate([payload, tag], axis=1)
-    order_ids = jnp.arange(count, dtype=jnp.int32)
-    earlier = (targets[:, None] == targets[None, :]) & (order_ids[None, :] < order_ids[:, None])
-    rank_in = jnp.sum(earlier.astype(jnp.int32), axis=1)
-    slot_ids = ((sections - 1 - section) * tiles + targets) * CAP + rank_in
-    placing = slot_ids[:, None] == jnp.arange(sections * tiles * CAP, dtype=jnp.int32)[None, :]
-    send_data = jnp.dot(
-        placing.astype(jnp.float32).T,
-        tagged,
-        precision=lax.Precision.HIGHEST,
-        preferred_element_type=jnp.float32,
-    )
-    width = (fields + 1) * cols_y
+    keys = targets * rows_x + landing
+    placing = (
+        keys[None, :] == jnp.arange(tiles * rows_x, dtype=jnp.int32)[:, None]
+    ).astype(jnp.float32)
+    summed = jnp.dot(
+        placing, payload, precision=lax.Precision.HIGHEST, preferred_element_type=jnp.float32
+    ).reshape(tiles_x, tiles_y, rows_x, fields, cols_y)
+    zero_x = jnp.zeros((1, tiles_y, fields, cols_y), jnp.float32)
+    up_rows = jnp.concatenate([zero_x, summed[:-1, :, rows_x - 1]], 0)
+    dn_rows = jnp.concatenate([summed[1:, :, 0], zero_x], 0)
+    zero_y = jnp.zeros((tiles_x, 1, rows_x, fields), jnp.float32)
+    lf_cols = jnp.concatenate([zero_y, summed[:, :-1, :, :, cols_y - 1]], 1)
+    rt_cols = jnp.concatenate([summed[:, 1:, :, :, 0], zero_y], 1)
+    side = jnp.concatenate([lf_cols, rt_cols], 3).reshape(tiles_x, tiles_y, 2 * rows_x * fields)
+    side = jnp.pad(side, ((0, 0), (0, 0), (0, fields * cols_y - 2 * rows_x * fields)))
+    depth = rows_x + 3
+    chunks = jnp.concatenate(
+        [
+            summed.reshape(tiles, rows_x, fields * cols_y),
+            up_rows.reshape(tiles, 1, fields * cols_y),
+            dn_rows.reshape(tiles, 1, fields * cols_y),
+            side.reshape(tiles, 1, fields * cols_y),
+        ],
+        1,
+    )
+    send_data = lax.dynamic_update_slice(
+        jnp.zeros((sections * tiles, depth, fields * cols_y), jnp.float32),
+        chunks,
+        ((sections - 1 - section) * tiles, 0, 0),
+    )
     got = lax.all_to_all(
-        send_data.reshape(sections * tiles, CAP, width),
-        ("comp", "gx", "gy"),
-        split_axis=0,
-        concat_axis=0,
-        tiled=True,
-    ).reshape(sections * tiles * CAP, width)
-    got_rows = got[:, fields * cols_y]
-    row_table = (
-        got_rows[None, :] == (jnp.arange(rows_x, dtype=jnp.int32) + 1).astype(jnp.float32)[:, None]
-    ).astype(jnp.float32)
-    increment = jnp.dot(
-        row_table,
-        got[:, : fields * cols_y],
-        precision=lax.Precision.HIGHEST,
-        preferred_element_type=jnp.float32,
-    )
-    increment = jnp.transpose(increment.reshape(rows_x, fields, cols_y), (1, 0, 2))
-
-    def row_edge(index):
-        field_rows = adjoint[:, :, index, :].at[:, 0].add(increment[:, index, :])
-        return jnp.concatenate([field_rows.reshape(planes, cols_y), east[:, index, :]], 0)
-
-    def col_edge(index):
-        field_cols = adjoint[:, :, :, index].at[:, 0].add(increment[:, :, index])
-        field_cols = jnp.transpose(field_cols, (2, 0, 1)).reshape(rows_x, planes)
-        return jnp.concatenate([field_cols, north[:, :, index].T], 1)
-
-    halos = (
-        shift(row_edge(rows_x - 1), "gx", 1),
-        shift(row_edge(0), "gx", -1),
-        shift(col_edge(cols_y - 1), "gy", 1),
-        shift(col_edge(0), "gy", -1),
-    )
+        send_data, ("comp", "gx", "gy"), split_axis=0, concat_axis=0, tiled=True
+    )
+    got = jnp.sum(got, axis=0)
+    inc_cols = got[rows_x + 2, : 2 * rows_x * fields].reshape(rows_x, 2 * fields)
+    inc = (got[: rows_x + 2], inc_cols)
 
     middle, last_rows, first_rows, last_cols, first_cols = run_step(
-        adjoint, halos, halos, east, north, coeffs, wet, inc=increment, emit=True
+        adjoint, halos, halos, east, north, coeffs, wet, inc=inc, emit=True
     )
     step_halos = (
         shift(last_rows, "gx", 1),

time: 63.1 us -> 62.7 us (level)
  the two profiles are of different devices: /device:TPU:10 before, /device:TPU:0 now
where the time goes in v3:
time: 62.7 us; the launch traced here: 61.7 us
  starting transfers between devices  24 us (38%)
  waiting for transfers between devices  19.6 us (31%)
  local copies, waits for them, and re-layouts  7.73 us (12%)
  Pallas kernels  6.52 us (10%)
  other arithmetic  2.31 us (4%)
  matrix products  1.21 us (2%)
    ppermute x8, starting transfers between devices, shift(): return lax.ppermute(block, axis, route)  16.7 us
    all_to_all x1, waiting for transfers between devices, shards(): lax.all_to_all(send_data, ('comp', 'gx', 'gy'), split_axis=0, concat_axis...  15.3 us
    all_to_all x1, starting transfers between devices, shards(): lax.all_to_all(send_data, ('comp', 'gx', 'gy'), split_axis=0, concat_axis...  7.32 us
    pallas_call x2, Pallas kernels, run_step(): pl.pallas_call(step_kernel(fields, levels, rows, cols, coupled, emit), ou...  6.52 us
    ppermute x8, waiting for transfers between devices, shift(): return lax.ppermute(block, axis, route)  4.21 us
    unnamed x30, local copies, waits for them, and re-layouts  3.16 us
  transfers between devices with their start and end apart: 9, of which 3 were waited for; matrix products, arithmetic and copies ran while one was open for 6% of the time, Pallas kernels for 0%

profile of v3, /device:TPU:0, one launch (start us, length us, event | category | flops | bytes accessed | tf_op | source)
XLA Modules:
  0.0 61.7 jit_solution(11877401888698406658)
XLA Ops:
  0.0 0.7 %bitcast_add_fusion = s32[32]{0:T(128)S(1)} fusion(s32[1,1,1,32]{3,2,1,0:T(1,128)} %param.16, s32[1,1,1,32,1]{3,4,2,1,0:T(1,128)} %param.14), kind=kLoop, calls=%fused_computation.21 | loop fusion | flops 64 | bytes 384 | tf_op jit(solution)/shard_map/add | solution.py:188
  0.7 0.7 %copy-done.12 = s32[1,1,1,32]{3,2,1,0:T(1,128)S(1)} copy-done((s32[1,1,1,32]{3,2,1,0:T(1,128)S(1)}, s32[1,1,1,32]{3,2,1,0:T(1,128)}, u32[]{:S(2)}) %copy-start.12) | copy-done | bytes 152
  1.3 1.0 %fusion = f32[4,4,8,128]{3,2,1,0:T(8,128)S(1)} fusion(f32[32,128]{1,0:T(8,128)} %bitcast.89, f32[4,32,8,128]{3,2,1,0:T(8,128)} %bitcast.59, s32[32]{0:T(128)S(1)} %bitcast.90), kind=kOutput, calls=%fused_computation.1 | convolution fusion | flops 1589504 | bytes 98432 | tf_op jit(solution)/shard_map/dot_general | solution.py:179
  2.3 0.3 fusion.1
  2.6 0.1 fusion.11
  2.7 0.3 copy.30
  3.1 0.4 copy.31
  3.5 0.1 copy.26
  3.5 0.1 reshape.51
  3.6 0.1 reshape.54
  3.7 1.1 %broadcast_in_dim.4 = f32[32,11,512]{2,1,0:T(8,128)} broadcast(f32[]{:T(128)} %constant.8.clone.1), dimensions={} | broadcast | bytes 720900 | tf_op jit(solution)/shard_map/broadcast_in_dim | solution.py:214
  4.9 0.9 %maximum_dynamic-update-slice_fusion = f32[32,11,512]{2,1,0:T(8,128)} fusion(f32[32,11,512]{2,1,0:T(8,128)} %broadcast_in_dim.4, s32[]{:T(128)S(6)} %select_n.3, f32[16,1,512]{2,1,0:T(1,128)S(1)} %reshape.54, f32[16,1,512]{2,1,0:T(1,128)S(1)} %bitcast.77, f32[16,1,512]{2,1,0:T(1,128)S(1)} %bitcast.76, f32[16,8,512]{2,1,0:T(8,128)S(1)} %bitcast.65), kind=kLoop, calls=%fused_computation.2 | loop fusion | flops 270336 | bytes 884740 | tf_op jit(solution)/shard_map/dynamic_update_slice | solution.py:213
  5.8 7.3 %all-to-all-start = ((f32[32,11,512]{2,1,0:T(8,128)}), f32[32,11,512]{2,1,0:T(8,128)S(1)}, u32[]{:S(2)}, u32[]{:S(2)}) async-start(f32[32,11,512]{2,1,0:T(8,128)} %maximum_dynamic-update-slice_fusion), calls=%async_computation | async-start | bytes 2097152 | tf_op jit(solution)/shard_map/all_to_all | solution.py:218
  13.1 0.0 copy-done
  13.1 0.2 fusion.8
  13.3 0.0 copy-start.1
  13.3 0.3 copy.17
  13.6 0.1 reshape.44
  13.7 0.5 copy-done.1
  14.2 0.1 fusion.12
  14.3 0.1 copy.19
  14.5 3.7 %collective-permute-start.2 = (f32[8,160]{1,0:T(8,128)S(1)}, f32[8,160]{1,0:T(8,128)S(1)}, u32[]{:S(2)}, u32[]{:S(2)}) collective-permute-start(f32[8,160]{1,0:T(8,128)S(1)} %pad_maximum_fusion.2), channel_id=1, source_target_pairs={{0,1},{1,2},{2,3},{4,5},{5,6},{6,7},{8,9},{9,10},{10,11},{12,13},{... | collective-permute-start | bytes 15368 | tf_op jit(solution)/shard_map/ppermute | solution.py:17
  18.1 0.3 copy.20
  18.4 0.1 reshape.45
  18.5 0.1 copy.22
  18.6 1.3 %collective-permute-start.3 = (f32[8,160]{1,0:T(8,128)S(1)}, f32[8,160]{1,0:T(8,128)S(1)}, u32[]{:S(2)}, u32[]{:S(2)}) collective-permute-start(f32[8,160]{1,0:T(8,128)S(1)} %pad_maximum_fusion.3), channel_id=1, source_target_pairs={{1,0},{2,1},{3,2},{5,4},{6,5},{7,6},{9,8},{10,9},{11,10},{13,12},{... | collective-permute-start | bytes 15368 | tf_op jit(solution)/shard_map/ppermute | solution.py:17
  19.9 1.0 %fusion.13 = (f32[32,1,128]{2,1,0:T(1,128)S(1)}, f32[32,1,128]{2,1,0:T(1,128)S(1)}) fusion(f32[32,8,128]{2,1,0:T(8,128)} %bitcast.71), kind=kLoop, calls=%fused_computation.27 | loop fusion | bytes 65536 | tf_op jit(solution)/shard_map/slice | solution.py:157
  20.9 0.1 fusion.9
  21.1 3.4 %collective-permute-start = (f32[160,128]{1,0:T(8,128)S(1)}, f32[160,128]{1,0:T(8,128)S(1)}, u32[]{:S(2)}, u32[]{:S(2)}) collective-permute-start(f32[160,128]{1,0:T(8,128)S(1)} %pad_maximum_fusion), channel_id=1, source_target_pairs={{0,4},{4,8},{8,12},{1,5},{5,9},{9,13},{2,6},{6,10},{10,14},{3,7},{... | collective-permute-start | bytes 245768 | tf_op jit(solution)/shard_map/ppermute | solution.py:17
  24.4 0.0 copy-start.11
  24.5 1.3 %collective-permute-start.1 = (f32[160,128]{1,0:T(8,128)S(1)}, f32[160,128]{1,0:T(8,128)S(1)}, u32[]{:S(2)}, u32[]{:S(2)}) collective-permute-start(f32[160,128]{1,0:T(8,128)S(1)} %pad_maximum_fusion.1), channel_id=1, source_target_pairs={{4,0},{8,4},{12,8},{5,1},{9,5},{13,9},{6,2},{10,6},{14,10},{7,3},{... | collective-permute-start | bytes 245768 | tf_op jit(solution)/shard_map/ppermute | solution.py:17
  25.8 0.0 copy-done.11
  25.8 0.6 convert_bitcast_fusion.refs_12_
  26.4 15.3 %all-to-all-done = f32[32,11,512]{2,1,0:T(8,128)S(1)} async-done(((f32[32,11,512]{2,1,0:T(8,128)}), f32[32,11,512]{2,1,0:T(8,128)S(1)}, u32[]{:S(2)}, u32[]{:S(2)}) %all-to-all-start) | async-done | bytes 720928 | tf_op jit(solution)/shard_map/all_to_all | solution.py:218
  41.7 0.1 reduce_sum.9
  41.8 0.0 copy-start.4
  41.8 0.7 %reshape_squeeze.11.refs_14_ = f32[8,8]{1,0:T(8,128)} reshape(f32[64]{0:T(128)S(1)} %slice_reduce_fusion) | data formatting | bytes 512 | tf_op jit(solution)/shard_map/reshape;squeeze | solution.py:222
  42.5 0.0 collective-permute-done.2.refs_3_.refs_7_
  42.5 0.0 collective-permute-done.3.refs_4_.refs_8_
  42.5 0.0 copy-start.6
  42.5 0.0 collective-permute-done.refs_1_.refs_5_
  42.5 0.0 copy-start.2
  42.5 0.0 collective-permute-done.1.refs_2_.refs_6_
  42.5 0.0 copy-start.3
  42.6 0.0 copy-done.4
  42.6 0.5 copy-done.5
  43.1 0.0 copy-done.6
  43.1 0.1 copy-done.2
  43.2 0.0 copy-done.3
  43.2 3.4 %shard_map.91 = (f32[4,32,8,128]{3,2,1,0:T(8,128)}, f32[128,128]{1,0:T(8,128)}, f32[128,128]{1,0:T(8,128)}, f32[8,128]{1,0:T(8,128)}, f32[8,128]{1,0:T(8,128)}) custom-call(f32[4,32,8,128]{3,2,1,0:T(8,128)} %bitcast.60, f32[160,128]{1,0:T(8,128)} %copy-done.2, f32[160,128]{1,0:T(8,128)} %copy-done.3, f32[8,160]{1,0:T(8,128)} %copy-done.5, ...), custom_call_target="tpu_custom_call" | custom-call | tf_op jit(solution)/shard_map/pallas_call | solution.py:132
  46.6 1.4 %collective-permute-start.4 = (f32[128,128]{1,0:T(8,128)}, f32[128,128]{1,0:T(8,128)S(1)}, u32[]{:S(2)}, u32[]{:S(2)}) collective-permute-start(f32[128,128]{1,0:T(8,128)} %get-tuple-element.11), channel_id=1, source_target_pairs={{0,4},{4,8},{8,12},{1,5},{5,9},{9,13},{2,6},{6,10},{10,14},{3,7},{... | collective-permute-start | bytes 196616 | tf_op jit(solution)/shard_map/ppermute | solution.py:17
  48.0 1.3 %collective-permute-start.5 = (f32[128,128]{1,0:T(8,128)}, f32[128,128]{1,0:T(8,128)S(1)}, u32[]{:S(2)}, u32[]{:S(2)}) collective-permute-start(f32[128,128]{1,0:T(8,128)} %get-tuple-element.12), channel_id=1, source_target_pairs={{4,0},{8,4},{12,8},{5,1},{9,5},{13,9},{6,2},{10,6},{14,10},{7,3},{... | collective-permute-start | bytes 196616 | tf_op jit(solution)/shard_map/ppermute | solution.py:17
  49.3 3.0 %collective-permute-start.6 = (f32[8,128]{1,0:T(8,128)}, f32[8,128]{1,0:T(8,128)S(1)}, u32[]{:S(2)}, u32[]{:S(2)}) collective-permute-start(f32[8,128]{1,0:T(8,128)} %get-tuple-element.13), channel_id=1, source_target_pairs={{0,1},{1,2},{2,3},{4,5},{5,6},{6,7},{8,9},{9,10},{10,11},{12,13},{... | collective-permute-start | bytes 12296 | tf_op jit(solution)/shard_map/ppermute | solution.py:17
  52.3 0.0 copy-done.13
  52.4 1.3 %collective-permute-start.7 = (f32[8,128]{1,0:T(8,128)S(1)}, f32[8,128]{1,0:T(8,128)S(1)}, u32[]{:S(2)}, u32[]{:S(2)}) collective-permute-start(f32[8,128]{1,0:T(8,128)S(1)} %copy-done.13), channel_id=1, source_target_pairs={{1,0},{2,1},{3,2},{5,4},{6,5},{7,6},{9,8},{10,9},{11,10},{13,12},{... | collective-permute-start | bytes 12296 | tf_op jit(solution)/shard_map/ppermute | solution.py:17
  53.7 0.2 collective-permute-done.6.refs_3_
  53.9 4.0 %collective-permute-done.7.refs_4_ = f32[8,128]{1,0:T(8,128)S(1)} collective-permute-done((f32[8,128]{1,0:T(8,128)S(1)}, f32[8,128]{1,0:T(8,128)S(1)}, u32[]{:S(2)}, u32[]{:S(2)}) %collective-permute-start.7) | collective-permute-done | bytes 4128 | tf_op jit(solution)/shard_map/ppermute | solution.py:17
  57.9 0.0 collective-permute-done.4.refs_1_
  57.9 0.0 collective-permute-done.5.refs_2_
  57.9 0.0 copy-start.8
  57.9 0.6 copy-done.10
  58.5 0.0 copy-done.7
  58.5 0.0 copy-done.8
  58.5 3.1 %shard_map.92 = f32[4,32,8,128]{3,2,1,0:T(8,128)} custom-call(f32[4,32,8,128]{3,2,1,0:T(8,128)} %get-tuple-element.10.refs_0_, f32[128,128]{1,0:T(8,128)} %copy-done.7, f32[128,128]{1,0:T(8,128)} %copy-done.8, f32[8,128]{1,0:T(8,128)} %copy-done.9, f32[8,128]{1,0:T(8,128)} %copy-done.10, f32[160,128]{1,0:T(8,128)} %copy-done.2, f32[160,128]{1,0:T(8,128)} %copy-done.3, ...), custom_call_target="tpu_custom_call" | custom-call | tf_op jit(solution)/shard_map/pallas_call | solution.py:132
  (20 shorter events, 0.2 us)
Async XLA Ops:
  0.7 0.7 %copy-start.12 = (s32[1,1,1,32]{3,2,1,0:T(1,128)S(1)}, s32[1,1,1,32]{3,2,1,0:T(1,128)}, u32[]{:S(2)}) copy-start(s32[1,1,1,32]{3,2,1,0:T(1,128)} %param.15) | copy-start | bytes 388
  5.8 7.3 %copy-start = (f32[1,4,32,8,128]{4,3,2,1,0:T(8,128)S(1)}, f32[1,4,32,8,128]{4,3,2,1,0:T(8,128)}, u32[]{:S(2)}) copy-start(f32[1,4,32,8,128]{4,3,2,1,0:T(8,128)} %param.9) | copy-start | bytes 1572868
  5.8 35.9 %all-to-all-start = ((f32[32,11,512]{2,1,0:T(8,128)}), f32[32,11,512]{2,1,0:T(8,128)S(1)}, u32[]{:S(2)}, u32[]{:S(2)}) async-start(f32[32,11,512]{2,1,0:T(8,128)} %maximum_dynamic-update-slice_fusion), calls=%async_computation | async-start | bytes 2097152 | tf_op jit(solution)/shard_map/all_to_all | solution.py:218
  13.3 0.9 %copy-start.1 = (f32[1,32,8,128]{3,2,1,0:T(8,128)S(1)}, f32[1,32,8,128]{3,2,1,0:T(8,128)}, u32[]{:S(2)}) copy-start(f32[1,32,8,128]{3,2,1,0:T(8,128)} %param.11) | copy-start | bytes 393220
  14.5 28.0 %collective-permute-start.2 = (f32[8,160]{1,0:T(8,128)S(1)}, f32[8,160]{1,0:T(8,128)S(1)}, u32[]{:S(2)}, u32[]{:S(2)}) collective-permute-start(f32[8,160]{1,0:T(8,128)S(1)} %pad_maximum_fusion.2), channel_id=1, source_target_pairs={{0,1},{1,2},{2,3},{4,5},{5,6},{6,7},{8,9},{9,10},{10,11},{12,13},{... | collective-permute-start | bytes 15368 | tf_op jit(solution)/shard_map/ppermute | solution.py:17
  18.6 23.9 %collective-permute-start.3 = (f32[8,160]{1,0:T(8,128)S(1)}, f32[8,160]{1,0:T(8,128)S(1)}, u32[]{:S(2)}, u32[]{:S(2)}) collective-permute-start(f32[8,160]{1,0:T(8,128)S(1)} %pad_maximum_fusion.3), channel_id=1, source_target_pairs={{1,0},{2,1},{3,2},{5,4},{6,5},{7,6},{9,8},{10,9},{11,10},{13,12},{... | collective-permute-start | bytes 15368 | tf_op jit(solution)/shard_map/ppermute | solution.py:17
  21.1 21.5 %collective-permute-start = (f32[160,128]{1,0:T(8,128)S(1)}, f32[160,128]{1,0:T(8,128)S(1)}, u32[]{:S(2)}, u32[]{:S(2)}) collective-permute-start(f32[160,128]{1,0:T(8,128)S(1)} %pad_maximum_fusion), channel_id=1, source_target_pairs={{0,4},{4,8},{8,12},{1,5},{5,9},{9,13},{2,6},{6,10},{10,14},{3,7},{... | collective-permute-start | bytes 245768 | tf_op jit(solution)/shard_map/ppermute | solution.py:17
  24.4 1.3 %copy-start.11 = (s32[1,8,128]{2,1,0:T(8,128)S(1)}, s32[1,8,128]{2,1,0:T(8,128)}, u32[]{:S(2)}) copy-start(s32[1,8,128]{2,1,0:T(8,128)} %param.13) | copy-start | bytes 12292
  24.5 18.1 %collective-permute-start.1 = (f32[160,128]{1,0:T(8,128)S(1)}, f32[160,128]{1,0:T(8,128)S(1)}, u32[]{:S(2)}, u32[]{:S(2)}) collective-permute-start(f32[160,128]{1,0:T(8,128)S(1)} %pad_maximum_fusion.1), channel_id=1, source_target_pairs={{4,0},{8,4},{12,8},{5,1},{9,5},{13,9},{6,2},{10,6},{14,10},{7,3},{... | collective-permute-start | bytes 245768 | tf_op jit(solution)/shard_map/ppermute | solution.py:17
  41.8 0.8 %copy-start.4 = (f32[11,512]{1,0:T(8,128)}, f32[11,512]{1,0:T(8,128)S(1)}, u32[]{:S(2)}) copy-start(f32[11,512]{1,0:T(8,128)S(1)} %reduce_sum.9) | copy-start | bytes 67588
  42.5 0.6 copy-start.5
  42.5 0.6 copy-start.6
  42.5 0.6 %copy-start.2 = (f32[160,128]{1,0:T(8,128)}, f32[160,128]{1,0:T(8,128)S(1)}, u32[]{:S(2)}) copy-start(f32[160,128]{1,0:T(8,128)S(1)} %collective-permute-done.refs_1_.refs_5_) | copy-start | bytes 245764
  42.5 0.6 %copy-start.3 = (f32[160,128]{1,0:T(8,128)}, f32[160,128]{1,0:T(8,128)S(1)}, u32[]{:S(2)}) copy-start(f32[160,128]{1,0:T(8,128)S(1)} %collective-permute-done.1.refs_2_.refs_6_) | copy-start | bytes 245764
  46.6 5.8 %copy-start.13 = (f32[8,128]{1,0:T(8,128)S(1)}, f32[8,128]{1,0:T(8,128)}, u32[]{:S(2)}) copy-start(f32[8,128]{1,0:T(8,128)} %get-tuple-element.14) | copy-start | bytes 12292
  46.6 11.3 %collective-permute-start.4 = (f32[128,128]{1,0:T(8,128)}, f32[128,128]{1,0:T(8,128)S(1)}, u32[]{:S(2)}, u32[]{:S(2)}) collective-permute-start(f32[128,128]{1,0:T(8,128)} %get-tuple-element.11), channel_id=1, source_target_pairs={{0,4},{4,8},{8,12},{1,5},{5,9},{9,13},{2,6},{6,10},{10,14},{3,7},{... | collective-permute-start | bytes 196616 | tf_op jit(solution)/shard_map/ppermute | solution.py:17
  48.0 9.9 %collective-permute-start.5 = (f32[128,128]{1,0:T(8,128)}, f32[128,128]{1,0:T(8,128)S(1)}, u32[]{:S(2)}, u32[]{:S(2)}) collective-permute-start(f32[128,128]{1,0:T(8,128)} %get-tuple-element.12), channel_id=1, source_target_pairs={{4,0},{8,4},{12,8},{5,1},{9,5},{13,9},{6,2},{10,6},{14,10},{7,3},{... | collective-permute-start | bytes 196616 | tf_op jit(solution)/shard_map/ppermute | solution.py:17
  49.3 4.6 %collective-permute-start.6 = (f32[8,128]{1,0:T(8,128)}, f32[8,128]{1,0:T(8,128)S(1)}, u32[]{:S(2)}, u32[]{:S(2)}) collective-permute-start(f32[8,128]{1,0:T(8,128)} %get-tuple-element.13), channel_id=1, source_target_pairs={{0,1},{1,2},{2,3},{4,5},{5,6},{6,7},{8,9},{9,10},{10,11},{12,13},{... | collective-permute-start | bytes 12296 | tf_op jit(solution)/shard_map/ppermute | solution.py:17
  52.4 5.5 %collective-permute-start.7 = (f32[8,128]{1,0:T(8,128)S(1)}, f32[8,128]{1,0:T(8,128)S(1)}, u32[]{:S(2)}, u32[]{:S(2)}) collective-permute-start(f32[8,128]{1,0:T(8,128)S(1)} %copy-done.13), channel_id=1, source_target_pairs={{1,0},{2,1},{3,2},{5,4},{6,5},{7,6},{9,8},{10,9},{11,10},{13,12},{... | collective-permute-start | bytes 12296 | tf_op jit(solution)/shard_map/ppermute | solution.py:17
  53.9 4.0 %copy-start.9 = (f32[8,128]{1,0:T(8,128)}, f32[8,128]{1,0:T(8,128)S(1)}, u32[]{:S(2)}) copy-start(f32[8,128]{1,0:T(8,128)S(1)} %collective-permute-done.6.refs_3_) | copy-start | bytes 12292
  57.9 0.6 copy-start.10
  57.9 0.6 copy-start.7
  57.9 0.6 %copy-start.8 = (f32[128,128]{1,0:T(8,128)}, f32[128,128]{1,0:T(8,128)S(1)}, u32[]{:S(2)}) copy-start(f32[128,128]{1,0:T(8,128)S(1)} %collective-permute-done.5.refs_2_) | copy-start | bytes 196612

commit v4 on v3

--- a/solution.py
+++ b/solution.py
@@ -192,35 +192,54 @@
     summed = jnp.dot(
         placing, payload, precision=lax.Precision.HIGHEST, preferred_element_type=jnp.float32
     ).reshape(tiles_x, tiles_y, rows_x, fields, cols_y)
+    order_ids = jnp.arange(count, dtype=jnp.int32)
+    earlier = (targets[:, None] == targets[None, :]) & (order_ids[None, :] < order_ids[:, None])
+    rank_in = jnp.sum(earlier.astype(jnp.int32), axis=1)
+    slot_ids = targets * CAP + rank_in
+    slotting = (
+        slot_ids[None, :] == jnp.arange(tiles * CAP, dtype=jnp.int32)[:, None]
+    ).astype(jnp.float32)
+    tagged = jnp.concatenate([payload, (landing + 1).astype(jnp.float32)[:, None]], 1)
+    slots = jnp.dot(
+        slotting, tagged, precision=lax.Precision.HIGHEST, preferred_element_type=jnp.float32
+    )
+    tags = slots[:, fields * cols_y].reshape(tiles_x, tiles_y, CAP)
+    slots = slots[:, : fields * cols_y].reshape(tiles, CAP, fields * cols_y)
     zero_x = jnp.zeros((1, tiles_y, fields, cols_y), jnp.float32)
     up_rows = jnp.concatenate([zero_x, summed[:-1, :, rows_x - 1]], 0)
     dn_rows = jnp.concatenate([summed[1:, :, 0], zero_x], 0)
     zero_y = jnp.zeros((tiles_x, 1, rows_x, fields), jnp.float32)
     lf_cols = jnp.concatenate([zero_y, summed[:, :-1, :, :, cols_y - 1]], 1)
     rt_cols = jnp.concatenate([summed[:, 1:, :, :, 0], zero_y], 1)
-    side = jnp.concatenate([lf_cols, rt_cols], 3).reshape(tiles_x, tiles_y, 2 * rows_x * fields)
-    side = jnp.pad(side, ((0, 0), (0, 0), (0, fields * cols_y - 2 * rows_x * fields)))
-    depth = rows_x + 3
-    chunks = jnp.concatenate(
+    ring = 2 * rows_x * fields
+    side = jnp.concatenate([lf_cols, rt_cols], 3).reshape(tiles_x, tiles_y, ring)
+    side = jnp.concatenate([side, tags], 2)
+    side = jnp.pad(side, ((0, 0), (0, 0), (0, fields * cols_y - ring - CAP)))
+    send_data = jnp.concatenate(
         [
-            summed.reshape(tiles, rows_x, fields * cols_y),
+            slots,
             up_rows.reshape(tiles, 1, fields * cols_y),
             dn_rows.reshape(tiles, 1, fields * cols_y),
             side.reshape(tiles, 1, fields * cols_y),
         ],
         1,
     )
-    send_data = lax.dynamic_update_slice(
-        jnp.zeros((sections * tiles, depth, fields * cols_y), jnp.float32),
-        chunks,
-        ((sections - 1 - section) * tiles, 0, 0),
-    )
-    got = lax.all_to_all(
-        send_data, ("comp", "gx", "gy"), split_axis=0, concat_axis=0, tiled=True
-    )
-    got = jnp.sum(got, axis=0)
-    inc_cols = got[rows_x + 2, : 2 * rows_x * fields].reshape(rows_x, 2 * fields)
-    inc = (got[: rows_x + 2], inc_cols)
+    got = lax.all_to_all(send_data, ("gx", "gy"), split_axis=0, concat_axis=0, tiled=True)
+    got_tags = got[:, CAP + 2, ring : ring + CAP].reshape(tiles * CAP)
+    row_table = (
+        got_tags[None, :] == (jnp.arange(rows_x, dtype=jnp.int32) + 1).astype(jnp.float32)[:, None]
+    ).astype(jnp.float32)
+    increment = jnp.dot(
+        row_table,
+        got[:, :CAP].reshape(tiles * CAP, fields * cols_y),
+        precision=lax.Precision.HIGHEST,
+        preferred_element_type=jnp.float32,
+    )
+    edges_sum = jnp.sum(got[:, CAP:], axis=0)
+    packed = jnp.concatenate([increment, edges_sum], 0)
+    packed = lax.ppermute(packed, "comp", [(c, sections - 1 - c) for c in range(sections)])
+    inc_cols = packed[rows_x + 2, :ring].reshape(rows_x, 2 * fields)
+    inc = (packed[: rows_x + 2], inc_cols)
 
     middle, last_rows, first_rows, last_cols, first_cols = run_step(
         adjoint, halos, halos, east, north, coeffs, wet, inc=inc, emit=True

time: 62.7 us -> 56.6 us (0.903)
  waiting for transfers between devices: 19.6 us -> 6.38 us
  starting transfers between devices: 24 us -> 29.3 us
  local copies, waits for them, and re-layouts: 7.73 us -> 10.6 us
    all_to_all x1, waiting for transfers between devices: 15.3 us -> 2.16 us  [shards(): lax.all_to_all(send_data, ('gx', 'gy'), split_axis=0, concat_axis=0, tile...]
    ppermute x8, starting transfers between devices: 16.7 us -> 21.2 us  [shift(): return lax.ppermute(block, axis, route)]
    slice x1, local copies, waits for them, and re-layouts: 0.08 us -> 1.42 us  [row_edge(): field_rows = adjoint[:, :, index, :].reshape(planes, cols_y)]
    unnamed x30 -> x36, local copies, waits for them, and re-layouts: 3.16 us -> 4.4 us
    broadcast_in_dim x1 -> x0, local copies, waits for them, and re-layouts: 1.13 us -> none  [shards(): jnp.zeros((sections * tiles, depth, fields * cols_y), jnp.float32)]
    concatenate x1 -> x4, other arithmetic: 0.03 us -> 0.93 us  [the longest x1 0.83 us: shards(): jnp.concatenate([slots, up_rows.reshape(tiles, 1, fields * cols_y), dn_ro...]
    dynamic_update_slice x1 -> x0, other arithmetic: 0.9 us -> none  [shards(): lax.dynamic_update_slice(jnp.zeros((sections * tiles, depth, fields * col...]
    slice x1 -> x6, local copies, waits for them, and re-layouts: 0.02 us -> 0.78 us  [the longest x2 0.54 us: shards(): slots = slots[:, :fields * cols_y].reshape(tiles, CAP, fields * cols_y)]
  transfers between devices with their start and end apart: 9 -> 10, of which waited for: 3 -> 3; matrix products, arithmetic and copies ran while one was open for 6% -> 11% of each run, Pallas kernels for 0% -> 0%
where the time goes in v4:
time: 56.6 us; the launch traced here: 55.9 us
  starting transfers between devices  29.3 us (52%)
  local copies, waits for them, and re-layouts  10.6 us (19%)
  Pallas kernels  6.57 us (12%)
  waiting for transfers between devices  6.38 us (11%)
  other arithmetic  1.81 us (3%)
  matrix products  0.92 us (2%)
    ppermute x8, starting transfers between devices, shift(): return lax.ppermute(block, axis, route)  21.2 us
    all_to_all x1, starting transfers between devices, shards(): lax.all_to_all(send_data, ('gx', 'gy'), split_axis=0, concat_axis=0, tile...  7.94 us
    pallas_call x2, Pallas kernels, run_step(): pl.pallas_call(step_kernel(fields, levels, rows, cols, coupled, emit), ou...  6.57 us
    unnamed x36, local copies, waits for them, and re-layouts  4.4 us
    ppermute x8, waiting for transfers between devices, shift(): return lax.ppermute(block, axis, route)  4.21 us
    all_to_all x1, waiting for transfers between devices, shards(): lax.all_to_all(send_data, ('gx', 'gy'), split_axis=0, concat_axis=0, tile...  2.16 us
    slice x1, local copies, waits for them, and re-layouts, row_edge(): field_rows = adjoint[:, :, index, :].reshape(planes, cols_y)  1.42 us
  transfers between devices with their start and end apart: 10, of which 3 were waited for; matrix products, arithmetic and copies ran while one was open for 11% of the time, Pallas kernels for 0%

profile of v4, /device:TPU:0, one launch (start us, length us, event | category | flops | bytes accessed | tf_op | source)
XLA Modules:
  0.0 55.9 jit_solution(17087456871219297346)
XLA Ops:
  0.0 1.0 %fusion.26 = (f32[32,1,128]{2,1,0:T(1,128)S(1)}, f32[32,1,128]{2,1,0:T(1,128)S(1)}) fusion(f32[32,8,128]{2,1,0:T(8,128)} %bitcast.81), kind=kLoop, calls=%fused_computation.55 | loop fusion | bytes 65536 | tf_op jit(solution)/shard_map/slice | solution.py:157
  1.1 1.4 %fusion.23 = (f32[4,32,1,128]{3,2,1,0:T(1,128)S(1)}, f32[4,32,1,128]{3,2,1,0:T(1,128)S(1)}) fusion(f32[4,32,8,128]{3,2,1,0:T(8,128)} %bitcast.72), kind=kLoop, calls=%fused_computation.52 | loop fusion | bytes 262144 | tf_op jit(solution)/shard_map/slice | solution.py:156
  2.5 5.0 %collective-permute-start = (f32[160,128]{1,0:T(8,128)S(1)}, f32[160,128]{1,0:T(8,128)S(1)}, u32[]{:S(2)}, u32[]{:S(2)}) collective-permute-start(f32[160,128]{1,0:T(8,128)S(1)} %pad_maximum_fusion.1), channel_id=1, source_target_pairs={{0,4},{4,8},{8,12},{1,5},{5,9},{9,13},{2,6},{6,10},{10,14},{3,7},{... | collective-permute-start | bytes 245768 | tf_op jit(solution)/shard_map/ppermute | solution.py:17
  7.5 1.3 %collective-permute-start.1 = (f32[160,128]{1,0:T(8,128)S(1)}, f32[160,128]{1,0:T(8,128)S(1)}, u32[]{:S(2)}, u32[]{:S(2)}) collective-permute-start(f32[160,128]{1,0:T(8,128)S(1)} %pad_maximum_fusion.2), channel_id=1, source_target_pairs={{4,0},{8,4},{12,8},{5,1},{9,5},{13,9},{6,2},{10,6},{14,10},{7,3},{... | collective-permute-start | bytes 245768 | tf_op jit(solution)/shard_map/ppermute | solution.py:17
  8.8 0.0 copy-start.16
  8.8 0.0 copy-start.15
  8.8 0.0 copy-start.10
  8.8 0.6 %copy-done.16 = s32[1,1,1,32,1]{3,4,2,1,0:T(1,128)S(1)} copy-done((s32[1,1,1,32,1]{3,4,2,1,0:T(1,128)S(1)}, s32[1,1,1,32,1]{3,4,2,1,0:T(1,128)}, u32[]{:S(2)}) %copy-start.16) | copy-done | bytes 152
  9.4 0.2 convert_reduce_fusion
  9.6 0.1 copy.50
  9.7 0.6 %copy-done.14 = s32[1,1,1,32]{3,2,1,0:T(1,128)S(1)} copy-done((s32[1,1,1,32]{3,2,1,0:T(1,128)S(1)}, s32[1,1,1,32]{3,2,1,0:T(1,128)}, u32[]{:S(2)}) %copy-start.14) | copy-done | bytes 152
  10.4 0.2 fusion
  10.6 0.2 fusion.1
  10.8 0.0 copy-start.4
  10.8 0.1 slice_reduce_fusion.3
  11.0 0.5 copy-done.4
  11.5 0.3 fusion.5
  11.8 0.0 slice-start
  11.9 0.3 slice_reduce_fusion.1
  12.2 0.5 slice-done
  12.8 0.1 reshape_squeeze.14
  12.9 0.1 copy.52
  13.0 0.1 reshape.108
  13.1 0.1 select_maximum_fusion.1
  13.2 0.1 reshape.114
  13.3 0.8 %pad_maximum_fusion = f32[16,7,512]{2,1,0:T(8,128)} fusion(f32[16,1,512]{2,1,0:T(1,128)S(1)} %reshape.114, f32[16,1,512]{2,1,0:T(1,128)S(1)} %bitcast.89, f32[16,1,512]{2,1,0:T(1,128)S(1)} %bitcast.90, f32[16,4,512]{2,1,0:T(4,128)S(1)} %reshape.105), kind=kLoop, calls=%fused_computation.2 | loop fusion | flops 172032 | bytes 458752 | tf_op jit(solution)/shard_map/concatenate | solution.py:218
  14.1 7.9 %all-to-all-start = ((f32[16,7,512]{2,1,0:T(8,128)}), f32[16,7,512]{2,1,0:T(8,128)S(1)}, u32[]{:S(2)}, u32[]{:S(2)}) async-start(f32[16,7,512]{2,1,0:T(8,128)} %pad_maximum_fusion), calls=%async_computation | async-start | bytes 524288 | tf_op jit(solution)/shard_map/all_to_all | solution.py:227
  22.0 0.0 copy-start.1
  22.0 0.2 fusion.22
  22.2 0.7 %copy-done.1 = f32[1,32,8,128]{3,2,1,0:T(8,128)S(1)} copy-done((f32[1,32,8,128]{3,2,1,0:T(8,128)S(1)}, f32[1,32,8,128]{3,2,1,0:T(8,128)}, u32[]{:S(2)}) %copy-start.1) | copy-done | bytes 131096
  22.9 0.1 fusion.25
  23.0 0.1 copy.45
  23.2 0.3 copy.43
  23.5 0.1 reshape.101
  23.5 3.8 %collective-permute-start.2 = (f32[8,160]{1,0:T(8,128)S(1)}, f32[8,160]{1,0:T(8,128)S(1)}, u32[]{:S(2)}, u32[]{:S(2)}) collective-permute-start(f32[8,160]{1,0:T(8,128)S(1)} %pad_maximum_fusion.4), channel_id=1, source_target_pairs={{0,1},{1,2},{2,3},{4,5},{5,6},{6,7},{8,9},{9,10},{10,11},{12,13},{... | collective-permute-start | bytes 15368 | tf_op jit(solution)/shard_map/ppermute | solution.py:17
  27.4 0.1 copy.48
  27.5 0.3 copy.46
  27.8 0.1 reshape.102
  27.9 1.3 %collective-permute-start.3 = (f32[8,160]{1,0:T(8,128)S(1)}, f32[8,160]{1,0:T(8,128)S(1)}, u32[]{:S(2)}, u32[]{:S(2)}) collective-permute-start(f32[8,160]{1,0:T(8,128)S(1)} %pad_maximum_fusion.5), channel_id=1, source_target_pairs={{1,0},{2,1},{3,2},{5,4},{6,5},{7,6},{9,8},{10,9},{11,10},{13,12},{... | collective-permute-start | bytes 15368 | tf_op jit(solution)/shard_map/ppermute | solution.py:17
  29.2 2.2 %all-to-all-done = f32[16,7,512]{2,1,0:T(8,128)S(1)} async-done(((f32[16,7,512]{2,1,0:T(8,128)}), f32[16,7,512]{2,1,0:T(8,128)S(1)}, u32[]{:S(2)}, u32[]{:S(2)}) %all-to-all-start) | async-done | bytes 229408 | tf_op jit(solution)/shard_map/all_to_all | solution.py:227
  31.3 0.1 slice_reduce_fusion.4
  31.4 0.1 eq.105
  31.6 0.2 fusion.15
  31.8 0.1 slice_reduce_fusion.2
  31.9 0.1 collective-permute-start.4
  32.0 0.6 %copy-done.13 = s32[1,8,128]{2,1,0:T(8,128)S(1)} copy-done((s32[1,8,128]{2,1,0:T(8,128)S(1)}, s32[1,8,128]{2,1,0:T(8,128)}, u32[]{:S(2)}) %copy-start.13) | copy-done | bytes 4120
  32.6 0.6 %convert_bitcast_fusion.refs_12_ = f32[8,128]{1,0:T(8,128)} fusion(s32[1,8,128]{2,1,0:T(8,128)S(1)} %copy-done.13), kind=kLoop, calls=%fused_computation.37 | loop fusion | flops 1024 | bytes 8192 | tf_op jit(solution)/shard_map/convert_element_type | solution.py:153
  33.2 0.0 collective-permute-done.4
  33.2 0.7 %reshape_squeeze.15.refs_14_ = f32[8,8]{1,0:T(8,128)} reshape(f32[64]{0:T(128)S(1)} %slice_reduce_fusion.5) | data formatting | bytes 512 | tf_op jit(solution)/shard_map/reshape;squeeze | solution.py:241
  33.9 0.0 collective-permute-done.2.refs_3_.refs_7_
  33.9 0.5 copy-done.5
  34.5 0.1 copy-done.2
  34.5 0.0 copy-done.3
  34.6 3.4 %shard_map.91 = (f32[4,32,8,128]{3,2,1,0:T(8,128)}, f32[128,128]{1,0:T(8,128)}, f32[128,128]{1,0:T(8,128)}, f32[8,128]{1,0:T(8,128)}, f32[8,128]{1,0:T(8,128)}) custom-call(f32[4,32,8,128]{3,2,1,0:T(8,128)} %bitcast.73, f32[160,128]{1,0:T(8,128)} %copy-done.2, f32[160,128]{1,0:T(8,128)} %copy-done.3, f32[8,160]{1,0:T(8,128)} %copy-done.5, ...), custom_call_target="tpu_custom_call" | custom-call | tf_op jit(solution)/shard_map/pallas_call | solution.py:132
  38.0 3.1 %collective-permute-start.5 = (f32[128,128]{1,0:T(8,128)}, f32[128,128]{1,0:T(8,128)S(1)}, u32[]{:S(2)}, u32[]{:S(2)}) collective-permute-start(f32[128,128]{1,0:T(8,128)} %get-tuple-element.11), channel_id=1, source_target_pairs={{0,4},{4,8},{8,12},{1,5},{5,9},{9,13},{2,6},{6,10},{10,14},{3,7},{... | collective-permute-start | bytes 196616 | tf_op jit(solution)/shard_map/ppermute | solution.py:17
  41.1 1.3 %collective-permute-start.6 = (f32[128,128]{1,0:T(8,128)}, f32[128,128]{1,0:T(8,128)S(1)}, u32[]{:S(2)}, u32[]{:S(2)}) collective-permute-start(f32[128,128]{1,0:T(8,128)} %get-tuple-element.12), channel_id=1, source_target_pairs={{4,0},{8,4},{12,8},{5,1},{9,5},{13,9},{6,2},{10,6},{14,10},{7,3},{... | collective-permute-start | bytes 196616 | tf_op jit(solution)/shard_map/ppermute | solution.py:17
  42.4 4.2 %collective-permute-start.7 = (f32[8,128]{1,0:T(8,128)}, f32[8,128]{1,0:T(8,128)S(1)}, u32[]{:S(2)}, u32[]{:S(2)}) collective-permute-start(f32[8,128]{1,0:T(8,128)} %get-tuple-element.13), channel_id=1, source_target_pairs={{0,1},{1,2},{2,3},{4,5},{5,6},{6,7},{8,9},{9,10},{10,11},{12,13},{... | collective-permute-start | bytes 12296 | tf_op jit(solution)/shard_map/ppermute | solution.py:17
  46.6 1.3 %collective-permute-start.8 = (f32[8,128]{1,0:T(8,128)S(1)}, f32[8,128]{1,0:T(8,128)S(1)}, u32[]{:S(2)}, u32[]{:S(2)}) collective-permute-start(f32[8,128]{1,0:T(8,128)S(1)} %copy-done.17), channel_id=1, source_target_pairs={{1,0},{2,1},{3,2},{5,4},{6,5},{7,6},{9,8},{10,9},{11,10},{13,12},{... | collective-permute-start | bytes 12296 | tf_op jit(solution)/shard_map/ppermute | solution.py:17
  47.9 0.2 collective-permute-done.7.refs_3_
  48.1 4.0 %collective-permute-done.8.refs_4_ = f32[8,128]{1,0:T(8,128)S(1)} collective-permute-done((f32[8,128]{1,0:T(8,128)S(1)}, f32[8,128]{1,0:T(8,128)S(1)}, u32[]{:S(2)}, u32[]{:S(2)}) %collective-permute-start.8) | collective-permute-done | bytes 4128 | tf_op jit(solution)/shard_map/ppermute | solution.py:17
  52.2 0.6 copy-done.12
  52.7 0.0 copy-done.7
  52.8 0.0 copy-done.8
  52.8 3.1 %shard_map.92 = f32[4,32,8,128]{3,2,1,0:T(8,128)} custom-call(f32[4,32,8,128]{3,2,1,0:T(8,128)} %get-tuple-element.10.refs_0_, f32[128,128]{1,0:T(8,128)} %copy-done.7, f32[128,128]{1,0:T(8,128)} %copy-done.8, f32[8,128]{1,0:T(8,128)} %copy-done.11, f32[8,128]{1,0:T(8,128)} %copy-done.12, f32[160,128]{1,0:T(8,128)} %copy-done.2, f32[160,128]{1,0:T(8,128)} %copy-done.3, ...), custom_call_target="tpu_custom_call" | custom-call | tf_op jit(solution)/shard_map/pallas_call | solution.py:132
  (46 shorter events, 0.4 us)
Async XLA Ops:
  0.0 9.7 %copy-start = (f32[1,4,32,8,128]{4,3,2,1,0:T(8,128)S(1)}, f32[1,4,32,8,128]{4,3,2,1,0:T(8,128)}, u32[]{:S(2)}) copy-start(f32[1,4,32,8,128]{4,3,2,1,0:T(8,128)} %param.9) | copy-start | bytes 1572868
  2.5 31.4 %collective-permute-start = (f32[160,128]{1,0:T(8,128)S(1)}, f32[160,128]{1,0:T(8,128)S(1)}, u32[]{:S(2)}, u32[]{:S(2)}) collective-permute-start(f32[160,128]{1,0:T(8,128)S(1)} %pad_maximum_fusion.1), channel_id=1, source_target_pairs={{0,4},{4,8},{8,12},{1,5},{5,9},{9,13},{2,6},{6,10},{10,14},{3,7},{... | collective-permute-start | bytes 245768 | tf_op jit(solution)/shard_map/ppermute | solution.py:17
  7.5 26.4 %collective-permute-start.1 = (f32[160,128]{1,0:T(8,128)S(1)}, f32[160,128]{1,0:T(8,128)S(1)}, u32[]{:S(2)}, u32[]{:S(2)}) collective-permute-start(f32[160,128]{1,0:T(8,128)S(1)} %pad_maximum_fusion.2), channel_id=1, source_target_pairs={{4,0},{8,4},{12,8},{5,1},{9,5},{13,9},{6,2},{10,6},{14,10},{7,3},{... | collective-permute-start | bytes 245768 | tf_op jit(solution)/shard_map/ppermute | solution.py:17
  8.8 0.7 %copy-start.16 = (s32[1,1,1,32,1]{3,4,2,1,0:T(1,128)S(1)}, s32[1,1,1,32,1]{3,4,2,1,0:T(1,128)}, u32[]{:S(2)}) copy-start(s32[1,1,1,32,1]{3,4,2,1,0:T(1,128)} %param.14) | copy-start | bytes 388
  8.8 0.8 %copy-start.15 = (s32[1,1,1,32]{3,2,1,0:T(1,128)S(1)}, s32[1,1,1,32]{3,2,1,0:T(1,128)}, u32[]{:S(2)}) copy-start(s32[1,1,1,32]{3,2,1,0:T(1,128)} %param.16) | copy-start | bytes 388
  8.8 0.9 %copy-start.10 = (f32[1,1,1,32,128]{4,3,2,1,0:T(8,128)S(1)}, f32[1,1,1,32,128]{4,3,2,1,0:T(8,128)}, u32[]{:S(2)}) copy-start(f32[1,1,1,32,128]{4,3,2,1,0:T(8,128)} %param.17) | copy-start | bytes 49156
  9.7 0.7 %copy-start.14 = (s32[1,1,1,32]{3,2,1,0:T(1,128)S(1)}, s32[1,1,1,32]{3,2,1,0:T(1,128)}, u32[]{:S(2)}) copy-start(s32[1,1,1,32]{3,2,1,0:T(1,128)} %param.15) | copy-start | bytes 388
  10.8 0.7 %copy-start.4 = (f32[64,513]{1,0:T(8,128)}, f32[64,513]{1,0:T(8,128)S(1)}, u32[]{:S(2)}) copy-start(f32[64,513]{1,0:T(8,128)S(1)} %fusion.1) | copy-start | bytes 393988
  11.8 0.9 %slice-start = ((f32[64,513]{1,0:T(8,128)}), f32[64,512]{1,0:T(8,128)S(1)}, s32[]{:S(2)}) async-start(f32[64,513]{1,0:T(8,128)} %copy-done.4), calls=%async_computation.1 | async-start | bytes 262144 | tf_op jit(solution)/shard_map/slice | solution.py:207
  14.1 17.3 %all-to-all-start = ((f32[16,7,512]{2,1,0:T(8,128)}), f32[16,7,512]{2,1,0:T(8,128)S(1)}, u32[]{:S(2)}, u32[]{:S(2)}) async-start(f32[16,7,512]{2,1,0:T(8,128)} %pad_maximum_fusion), calls=%async_computation | async-start | bytes 524288 | tf_op jit(solution)/shard_map/all_to_all | solution.py:227
  22.0 0.9 %copy-start.1 = (f32[1,32,8,128]{3,2,1,0:T(8,128)S(1)}, f32[1,32,8,128]{3,2,1,0:T(8,128)}, u32[]{:S(2)}) copy-start(f32[1,32,8,128]{3,2,1,0:T(8,128)} %param.11) | copy-start | bytes 393220
  23.5 10.3 %collective-permute-start.2 = (f32[8,160]{1,0:T(8,128)S(1)}, f32[8,160]{1,0:T(8,128)S(1)}, u32[]{:S(2)}, u32[]{:S(2)}) collective-permute-start(f32[8,160]{1,0:T(8,128)S(1)} %pad_maximum_fusion.4), channel_id=1, source_target_pairs={{0,1},{1,2},{2,3},{4,5},{5,6},{6,7},{8,9},{9,10},{10,11},{12,13},{... | collective-permute-start | bytes 15368 | tf_op jit(solution)/shard_map/ppermute | solution.py:17
  27.9 6.0 %collective-permute-start.3 = (f32[8,160]{1,0:T(8,128)S(1)}, f32[8,160]{1,0:T(8,128)S(1)}, u32[]{:S(2)}, u32[]{:S(2)}) collective-permute-start(f32[8,160]{1,0:T(8,128)S(1)} %pad_maximum_fusion.5), channel_id=1, source_target_pairs={{1,0},{2,1},{3,2},{5,4},{6,5},{7,6},{9,8},{10,9},{11,10},{13,12},{... | collective-permute-start | bytes 15368 | tf_op jit(solution)/shard_map/ppermute | solution.py:17
  31.9 0.7 %copy-start.13 = (s32[1,8,128]{2,1,0:T(8,128)S(1)}, s32[1,8,128]{2,1,0:T(8,128)}, u32[]{:S(2)}) copy-start(s32[1,8,128]{2,1,0:T(8,128)} %param.13) | copy-start | bytes 12292
  31.9 1.3 %collective-permute-start.4 = (f32[11,512]{1,0:T(8,128)S(1)}, f32[11,512]{1,0:T(8,128)S(1)}, u32[]{:S(2)}, u32[]{:S(2)}) collective-permute-start(f32[11,512]{1,0:T(8,128)S(1)} %pad_maximum_fusion.3), channel_id=1, source_target_pairs={{0,16},{16,0},{1,17},{17,1},{2,18},{18,2},{3,19},{19,3},{4,20},{20... | collective-permute-start | bytes 67592 | tf_op jit(solution)/shard_map/ppermute | solution.py:240
  33.2 0.8 %copy-start.9 = (f32[11,512]{1,0:T(8,128)}, f32[11,512]{1,0:T(8,128)S(1)}, u32[]{:S(2)}) copy-start(f32[11,512]{1,0:T(8,128)S(1)} %collective-permute-done.4) | copy-start | bytes 67588
  33.9 0.6 %copy-start.5 = (f32[8,160]{1,0:T(8,128)}, f32[8,160]{1,0:T(8,128)S(1)}, u32[]{:S(2)}) copy-start(f32[8,160]{1,0:T(8,128)S(1)} %collective-permute-done.2.refs_3_.refs_7_) | copy-start | bytes 15364
  33.9 0.6 %copy-start.6 = (f32[8,160]{1,0:T(8,128)}, f32[8,160]{1,0:T(8,128)S(1)}, u32[]{:S(2)}) copy-start(f32[8,160]{1,0:T(8,128)S(1)} %collective-permute-done.3.refs_4_.refs_8_) | copy-start | bytes 15364
  33.9 0.6 %copy-start.2 = (f32[160,128]{1,0:T(8,128)}, f32[160,128]{1,0:T(8,128)S(1)}, u32[]{:S(2)}) copy-start(f32[160,128]{1,0:T(8,128)S(1)} %collective-permute-done.refs_1_.refs_5_) | copy-start | bytes 245764
  33.9 0.6 %copy-start.3 = (f32[160,128]{1,0:T(8,128)}, f32[160,128]{1,0:T(8,128)S(1)}, u32[]{:S(2)}) copy-start(f32[160,128]{1,0:T(8,128)S(1)} %collective-permute-done.1.refs_2_.refs_6_) | copy-start | bytes 245764
  38.0 8.6 %copy-start.17 = (f32[8,128]{1,0:T(8,128)S(1)}, f32[8,128]{1,0:T(8,128)}, u32[]{:S(2)}) copy-start(f32[8,128]{1,0:T(8,128)} %get-tuple-element.14) | copy-start | bytes 12292
  38.0 14.1 %collective-permute-start.5 = (f32[128,128]{1,0:T(8,128)}, f32[128,128]{1,0:T(8,128)S(1)}, u32[]{:S(2)}, u32[]{:S(2)}) collective-permute-start(f32[128,128]{1,0:T(8,128)} %get-tuple-element.11), channel_id=1, source_target_pairs={{0,4},{4,8},{8,12},{1,5},{5,9},{9,13},{2,6},{6,10},{10,14},{3,7},{... | collective-permute-start | bytes 196616 | tf_op jit(solution)/shard_map/ppermute | solution.py:17
  41.1 11.0 %collective-permute-start.6 = (f32[128,128]{1,0:T(8,128)}, f32[128,128]{1,0:T(8,128)S(1)}, u32[]{:S(2)}, u32[]{:S(2)}) collective-permute-start(f32[128,128]{1,0:T(8,128)} %get-tuple-element.12), channel_id=1, source_target_pairs={{4,0},{8,4},{12,8},{5,1},{9,5},{13,9},{6,2},{10,6},{14,10},{7,3},{... | collective-permute-start | bytes 196616 | tf_op jit(solution)/shard_map/ppermute | solution.py:17
  42.4 5.7 %collective-permute-start.7 = (f32[8,128]{1,0:T(8,128)}, f32[8,128]{1,0:T(8,128)S(1)}, u32[]{:S(2)}, u32[]{:S(2)}) collective-permute-start(f32[8,128]{1,0:T(8,128)} %get-tuple-element.13), channel_id=1, source_target_pairs={{0,1},{1,2},{2,3},{4,5},{5,6},{6,7},{8,9},{9,10},{10,11},{12,13},{... | collective-permute-start | bytes 12296 | tf_op jit(solution)/shard_map/ppermute | solution.py:17
  46.6 5.5 %collective-permute-start.8 = (f32[8,128]{1,0:T(8,128)S(1)}, f32[8,128]{1,0:T(8,128)S(1)}, u32[]{:S(2)}, u32[]{:S(2)}) collective-permute-start(f32[8,128]{1,0:T(8,128)S(1)} %copy-done.17), channel_id=1, source_target_pairs={{1,0},{2,1},{3,2},{5,4},{6,5},{7,6},{9,8},{10,9},{11,10},{13,12},{... | collective-permute-start | bytes 12296 | tf_op jit(solution)/shard_map/ppermute | solution.py:17
  48.1 4.0 %copy-start.11 = (f32[8,128]{1,0:T(8,128)}, f32[8,128]{1,0:T(8,128)S(1)}, u32[]{:S(2)}) copy-start(f32[8,128]{1,0:T(8,128)S(1)} %collective-permute-done.7.refs_3_) | copy-start | bytes 12292
  52.1 0.6 %copy-start.12 = (f32[8,128]{1,0:T(8,128)}, f32[8,128]{1,0:T(8,128)S(1)}, u32[]{:S(2)}) copy-start(f32[8,128]{1,0:T(8,128)S(1)} %collective-permute-done.8.refs_4_) | copy-start | bytes 12292
  52.1 0.6 %copy-start.7 = (f32[128,128]{1,0:T(8,128)}, f32[128,128]{1,0:T(8,128)S(1)}, u32[]{:S(2)}) copy-start(f32[128,128]{1,0:T(8,128)S(1)} %collective-permute-done.5.refs_1_) | copy-start | bytes 196612
  52.1 0.7 %copy-start.8 = (f32[128,128]{1,0:T(8,128)}, f32[128,128]{1,0:T(8,128)S(1)}, u32[]{:S(2)}) copy-start(f32[128,128]{1,0:T(8,128)S(1)} %collective-permute-done.6.refs_2_) | copy-start | bytes 196612

commit v5 on v4

--- a/solution.py
+++ b/solution.py
@@ -160,12 +160,6 @@
         field_cols = jnp.transpose(adjoint[:, :, :, index], (2, 0, 1)).reshape(rows_x, planes)
         return jnp.concatenate([field_cols, north[:, :, index].T], 1)
 
-    halos = (
-        shift(row_edge(rows_x - 1), "gx", 1),
-        shift(row_edge(0), "gx", -1),
-        shift(col_edge(cols_y - 1), "gy", 1),
-        shift(col_edge(0), "gy", -1),
-    )
 
     targets = dest_tile[0, 0, 0, :, 0]
     sources = src_row[0, 0, 0]
@@ -224,7 +218,16 @@
         ],
         1,
     )
+    send_data, *outgoing = lax.optimization_barrier(
+        (send_data, row_edge(rows_x - 1), row_edge(0), col_edge(cols_y - 1), col_edge(0))
+    )
     got = lax.all_to_all(send_data, ("gx", "gy"), split_axis=0, concat_axis=0, tiled=True)
+    halos = (
+        shift(outgoing[0], "gx", 1),
+        shift(outgoing[1], "gx", -1),
+        shift(outgoing[2], "gy", 1),
+        shift(outgoing[3], "gy", -1),
+    )
     got_tags = got[:, CAP + 2, ring : ring + CAP].reshape(tiles * CAP)
     row_table = (
         got_tags[None, :] == (jnp.arange(rows_x, dtype=jnp.int32) + 1).astype(jnp.float32)[:, None]

time: 56.6 us -> 56.2 us (level)
  local copies, waits for them, and re-layouts: 10.6 us -> 9.65 us
  matrix products: 0.92 us -> 1.65 us
    all_to_all x1, waiting for transfers between devices: 2.16 us -> 0.14 us  [shards(): lax.all_to_all(send_data, ('gx', 'gy'), split_axis=0, concat_axis=0, tile...]
    ppermute x8, waiting for transfers between devices: 4.21 us -> 5.78 us  [shift(): return lax.ppermute(block, axis, route)]
    slice x1, local copies, waits for them, and re-layouts: 1.42 us -> 0.08 us  [row_edge(): field_rows = adjoint[:, :, index, :].reshape(planes, cols_y)]
    dot_general x1, matrix products: 0.22 us -> 0.95 us  [shards(): jnp.dot(pick_table, surface_rows, precision=lax.Precision.HIGHEST, prefer...]
    unnamed x36 -> x34, local copies, waits for them, and re-layouts: 4.4 us -> 4.75 us
  transfers between devices with their start and end apart: 10 -> 10, of which waited for: 3 -> 4; matrix products, arithmetic and copies ran while one was open for 11% -> 3% of each run, Pallas kernels for 0% -> 0%
where the time goes in v5:
time: 56.2 us; the launch traced here: 55.6 us
  starting transfers between devices  29.7 us (53%)
  local copies, waits for them, and re-layouts  9.65 us (17%)
  Pallas kernels  6.52 us (12%)
  waiting for transfers between devices  5.93 us (11%)
  other arithmetic  1.79 us (3%)
  matrix products  1.65 us (3%)
    ppermute x8, starting transfers between devices, shift(): return lax.ppermute(block, axis, route)  21.3 us
    all_to_all x1, starting transfers between devices, shards(): lax.all_to_all(send_data, ('gx', 'gy'), split_axis=0, concat_axis=0, tile...  8.36 us
    pallas_call x2, Pallas kernels, run_step(): pl.pallas_call(step_kernel(fields, levels, rows, cols, coupled, emit), ou...  6.52 us
    ppermute x8, waiting for transfers between devices, shift(): return lax.ppermute(block, axis, route)  5.78 us
    unnamed x34, local copies, waits for them, and re-layouts  4.75 us
  transfers between devices with their start and end apart: 10, of which 4 were waited for; matrix products, arithmetic and copies ran while one was open for 3% of the time, Pallas kernels for 0%

profile of v5, /device:TPU:0, one launch (start us, length us, event | category | flops | bytes accessed | tf_op | source)
XLA Modules:
  0.0 55.6 jit_solution(3313951058090178247)
XLA Ops:
  0.0 0.7 %copy-done.13 = s32[1,1,1,32]{3,2,1,0:T(1,128)S(1)} copy-done((s32[1,1,1,32]{3,2,1,0:T(1,128)S(1)}, s32[1,1,1,32]{3,2,1,0:T(1,128)}, u32[]{:S(2)}) %copy-start.13) | copy-done | bytes 152
  0.7 1.0 %fusion = f32[4,4,8,128]{3,2,1,0:T(8,128)S(1)} fusion(f32[32,128]{1,0:T(8,128)} %bitcast.98, f32[4,32,8,128]{3,2,1,0:T(8,128)} %bitcast.72, s32[32]{0:T(128)S(1)} %bitcast.101), kind=kOutput, calls=%fused_computation.1 | convolution fusion | flops 1589504 | bytes 98432 | tf_op jit(solution)/shard_map/dot_general | solution.py:173
  1.7 0.0 copy-start.15
  1.7 0.6 %copy-done.15 = s32[1,1,1,32,1]{3,4,2,1,0:T(1,128)S(1)} copy-done((s32[1,1,1,32,1]{3,4,2,1,0:T(1,128)S(1)}, s32[1,1,1,32,1]{3,4,2,1,0:T(1,128)}, u32[]{:S(2)}) %copy-start.15) | copy-done | bytes 152
  2.3 0.2 convert_reduce_fusion
  2.5 0.5 copy-done.14
  3.0 0.3 fusion.5
  3.3 0.0 copy-start
  3.3 0.3 slice_reduce_fusion.1
  3.7 0.1 copy.44
  3.8 0.2 fusion.1
  4.0 0.0 copy-start.4
  4.0 0.1 slice_reduce_fusion.3
  4.1 0.5 copy-done.4
  4.6 0.2 fusion.22
  4.8 0.1 fusion.23
  5.0 0.1 copy.46
  5.0 0.1 reshape.106
  5.1 0.0 slice-start
  5.2 0.1 reshape_squeeze.12
  5.2 0.1 select_maximum_fusion.1
  5.3 0.1 reshape.114
  5.4 0.6 %slice-done = f32[64,512]{1,0:T(8,128)S(1)} async-done(((f32[64,513]{1,0:T(8,128)}), f32[64,512]{1,0:T(8,128)S(1)}, s32[]{:S(2)}) %slice-start) | async-done | bytes 131096 | tf_op jit(solution)/shard_map/slice | solution.py:201
  6.1 0.3 copy.50
  6.4 0.1 reshape.108
  6.5 0.3 copy.53
  6.7 0.1 reshape.109
  6.8 0.5 copy-done.1
  7.4 0.1 fusion.25
  7.5 0.1 copy.52
  7.6 0.1 copy.55
  7.7 1.0 %fusion.26 = (f32[32,1,128]{2,1,0:T(1,128)S(1)}, f32[32,1,128]{2,1,0:T(1,128)S(1)}) fusion(f32[32,8,128]{2,1,0:T(8,128)} %bitcast.81), kind=kLoop, calls=%fused_computation.55 | loop fusion | bytes 65536 | tf_op jit(solution)/shard_map/slice | solution.py:157
  8.7 0.8 %pad_maximum_fusion = f32[16,7,512]{2,1,0:T(8,128)} fusion(f32[16,1,512]{2,1,0:T(1,128)S(1)} %reshape.114, f32[16,1,512]{2,1,0:T(1,128)S(1)} %bitcast.90, f32[16,1,512]{2,1,0:T(1,128)S(1)} %bitcast.89, f32[16,4,512]{2,1,0:T(4,128)S(1)} %reshape.103), kind=kLoop, calls=%fused_computation.2 | loop fusion | flops 172032 | bytes 458752 | tf_op jit(solution)/shard_map/concatenate | solution.py:212
  9.6 8.4 %all-to-all-start = ((f32[16,7,512]{2,1,0:T(8,128)}), f32[16,7,512]{2,1,0:T(8,128)S(1)}, u32[]{:S(2)}, u32[]{:S(2)}) async-start(f32[16,7,512]{2,1,0:T(8,128)} %pad_maximum_fusion), calls=%async_computation | async-start | bytes 524288 | tf_op jit(solution)/shard_map/all_to_all | solution.py:224
  18.0 3.8 %collective-permute-start = (f32[160,128]{1,0:T(8,128)S(1)}, f32[160,128]{1,0:T(8,128)S(1)}, u32[]{:S(2)}, u32[]{:S(2)}) collective-permute-start(f32[160,128]{1,0:T(8,128)S(1)} %get-tuple-element.15), channel_id=1, source_target_pairs={{0,4},{4,8},{8,12},{1,5},{5,9},{9,13},{2,6},{6,10},{10,14},{3,7},{... | collective-permute-start | bytes 245768 | tf_op jit(solution)/shard_map/ppermute | solution.py:17
  21.8 1.3 %collective-permute-start.1 = (f32[160,128]{1,0:T(8,128)S(1)}, f32[160,128]{1,0:T(8,128)S(1)}, u32[]{:S(2)}, u32[]{:S(2)}) collective-permute-start(f32[160,128]{1,0:T(8,128)S(1)} %get-tuple-element.16), channel_id=1, source_target_pairs={{4,0},{8,4},{12,8},{5,1},{9,5},{13,9},{6,2},{10,6},{14,10},{7,3},{... | collective-permute-start | bytes 245768 | tf_op jit(solution)/shard_map/ppermute | solution.py:17
  23.1 3.4 %collective-permute-start.2 = (f32[8,160]{1,0:T(8,128)S(1)}, f32[8,160]{1,0:T(8,128)S(1)}, u32[]{:S(2)}, u32[]{:S(2)}) collective-permute-start(f32[8,160]{1,0:T(8,128)S(1)} %get-tuple-element.17), channel_id=1, source_target_pairs={{0,1},{1,2},{2,3},{4,5},{5,6},{6,7},{8,9},{9,10},{10,11},{12,13},{... | collective-permute-start | bytes 15368 | tf_op jit(solution)/shard_map/ppermute | solution.py:17
  26.5 1.3 %collective-permute-start.3 = (f32[8,160]{1,0:T(8,128)S(1)}, f32[8,160]{1,0:T(8,128)S(1)}, u32[]{:S(2)}, u32[]{:S(2)}) collective-permute-start(f32[8,160]{1,0:T(8,128)S(1)} %get-tuple-element.18), channel_id=1, source_target_pairs={{1,0},{2,1},{3,2},{5,4},{6,5},{7,6},{9,8},{10,9},{11,10},{13,12},{... | collective-permute-start | bytes 15368 | tf_op jit(solution)/shard_map/ppermute | solution.py:17
  27.8 0.1 all-to-all-done
  28.0 0.1 slice_reduce_fusion.4
  28.1 0.1 eq.105
  28.2 0.2 fusion.15
  28.4 0.1 slice_reduce_fusion.2
  28.4 0.0 copy-start.12
  28.5 0.1 collective-permute-start.4
  28.5 0.6 %copy-done.12 = s32[1,8,128]{2,1,0:T(8,128)S(1)} copy-done((s32[1,8,128]{2,1,0:T(8,128)S(1)}, s32[1,8,128]{2,1,0:T(8,128)}, u32[]{:S(2)}) %copy-start.12) | copy-done | bytes 4120
  29.1 0.6 %convert_bitcast_fusion.refs_12_ = f32[8,128]{1,0:T(8,128)} fusion(s32[1,8,128]{2,1,0:T(8,128)S(1)} %copy-done.12), kind=kLoop, calls=%fused_computation.36 | loop fusion | flops 1024 | bytes 8192 | tf_op jit(solution)/shard_map/convert_element_type | solution.py:153
  29.7 0.0 collective-permute-done.4
  29.8 0.7 %reshape_squeeze.15.refs_14_ = f32[8,8]{1,0:T(8,128)} reshape(f32[64]{0:T(128)S(1)} %slice_reduce_fusion.5) | data formatting | bytes 512 | tf_op jit(solution)/shard_map/reshape;squeeze | solution.py:244
  30.4 1.6 %collective-permute-done.3.refs_4_.refs_8_ = f32[8,160]{1,0:T(8,128)S(1)} collective-permute-done((f32[8,160]{1,0:T(8,128)S(1)}, f32[8,160]{1,0:T(8,128)S(1)}, u32[]{:S(2)}, u32[]{:S(2)}) %collective-permute-start.3) | collective-permute-done | bytes 5152 | tf_op jit(solution)/shard_map/ppermute | solution.py:17
  32.0 0.6 copy-done.6
  32.6 0.1 copy-done.2
  32.7 0.0 copy-done.3
  32.7 3.4 %shard_map.91 = (f32[4,32,8,128]{3,2,1,0:T(8,128)}, f32[128,128]{1,0:T(8,128)}, f32[128,128]{1,0:T(8,128)}, f32[8,128]{1,0:T(8,128)}, f32[8,128]{1,0:T(8,128)}) custom-call(f32[4,32,8,128]{3,2,1,0:T(8,128)} %bitcast.73, f32[160,128]{1,0:T(8,128)} %copy-done.2, f32[160,128]{1,0:T(8,128)} %copy-done.3, f32[8,160]{1,0:T(8,128)} %copy-done.5, ...), custom_call_target="tpu_custom_call" | custom-call | tf_op jit(solution)/shard_map/pallas_call | solution.py:132
  36.1 4.7 %collective-permute-start.5 = (f32[128,128]{1,0:T(8,128)}, f32[128,128]{1,0:T(8,128)S(1)}, u32[]{:S(2)}, u32[]{:S(2)}) collective-permute-start(f32[128,128]{1,0:T(8,128)} %get-tuple-element.21), channel_id=1, source_target_pairs={{0,4},{4,8},{8,12},{1,5},{5,9},{9,13},{2,6},{6,10},{10,14},{3,7},{... | collective-permute-start | bytes 196616 | tf_op jit(solution)/shard_map/ppermute | solution.py:17
  40.7 1.3 %collective-permute-start.6 = (f32[128,128]{1,0:T(8,128)}, f32[128,128]{1,0:T(8,128)S(1)}, u32[]{:S(2)}, u32[]{:S(2)}) collective-permute-start(f32[128,128]{1,0:T(8,128)} %get-tuple-element.22), channel_id=1, source_target_pairs={{4,0},{8,4},{12,8},{5,1},{9,5},{13,9},{6,2},{10,6},{14,10},{7,3},{... | collective-permute-start | bytes 196616 | tf_op jit(solution)/shard_map/ppermute | solution.py:17
  42.0 4.3 %collective-permute-start.7 = (f32[8,128]{1,0:T(8,128)}, f32[8,128]{1,0:T(8,128)S(1)}, u32[]{:S(2)}, u32[]{:S(2)}) collective-permute-start(f32[8,128]{1,0:T(8,128)} %get-tuple-element.23), channel_id=1, source_target_pairs={{0,1},{1,2},{2,3},{4,5},{5,6},{6,7},{8,9},{9,10},{10,11},{12,13},{... | collective-permute-start | bytes 12296 | tf_op jit(solution)/shard_map/ppermute | solution.py:17
  46.3 1.3 %collective-permute-start.8 = (f32[8,128]{1,0:T(8,128)S(1)}, f32[8,128]{1,0:T(8,128)S(1)}, u32[]{:S(2)}, u32[]{:S(2)}) collective-permute-start(f32[8,128]{1,0:T(8,128)S(1)} %copy-done.16), channel_id=1, source_target_pairs={{1,0},{2,1},{3,2},{5,4},{6,5},{7,6},{9,8},{10,9},{11,10},{13,12},{... | collective-permute-start | bytes 12296 | tf_op jit(solution)/shard_map/ppermute | solution.py:17
  47.6 0.2 collective-permute-done.7.refs_3_
  47.8 4.0 %collective-permute-done.8.refs_4_ = f32[8,128]{1,0:T(8,128)S(1)} collective-permute-done((f32[8,128]{1,0:T(8,128)S(1)}, f32[8,128]{1,0:T(8,128)S(1)}, u32[]{:S(2)}, u32[]{:S(2)}) %collective-permute-start.8) | collective-permute-done | bytes 4128 | tf_op jit(solution)/shard_map/ppermute | solution.py:17
  51.9 0.6 copy-done.11
  52.4 0.0 copy-done.7
  52.4 0.0 copy-done.8
  52.5 3.1 %shard_map.92 = f32[4,32,8,128]{3,2,1,0:T(8,128)} custom-call(f32[4,32,8,128]{3,2,1,0:T(8,128)} %get-tuple-element.20.refs_0_, f32[128,128]{1,0:T(8,128)} %copy-done.7, f32[128,128]{1,0:T(8,128)} %copy-done.8, f32[8,128]{1,0:T(8,128)} %copy-done.10, f32[8,128]{1,0:T(8,128)} %copy-done.11, f32[160,128]{1,0:T(8,128)} %copy-done.2, f32[160,128]{1,0:T(8,128)} %copy-done.3, ...), custom_call_target="tpu_custom_call" | custom-call | tf_op jit(solution)/shard_map/pallas_call | solution.py:132
  (42 shorter events, 0.3 us)
Async XLA Ops:
  0.0 0.7 %copy-start.13 = (s32[1,1,1,32]{3,2,1,0:T(1,128)S(1)}, s32[1,1,1,32]{3,2,1,0:T(1,128)}, u32[]{:S(2)}) copy-start(s32[1,1,1,32]{3,2,1,0:T(1,128)} %param.15) | copy-start | bytes 388
  1.7 0.7 %copy-start.15 = (s32[1,1,1,32,1]{3,4,2,1,0:T(1,128)S(1)}, s32[1,1,1,32,1]{3,4,2,1,0:T(1,128)}, u32[]{:S(2)}) copy-start(s32[1,1,1,32,1]{3,4,2,1,0:T(1,128)} %param.14) | copy-start | bytes 388
  2.3 0.7 %copy-start.14 = (s32[1,1,1,32]{3,2,1,0:T(1,128)S(1)}, s32[1,1,1,32]{3,2,1,0:T(1,128)}, u32[]{:S(2)}) copy-start(s32[1,1,1,32]{3,2,1,0:T(1,128)} %param.16) | copy-start | bytes 388
  3.3 1.3 %copy-start = (f32[1,4,32,8,128]{4,3,2,1,0:T(8,128)S(1)}, f32[1,4,32,8,128]{4,3,2,1,0:T(8,128)}, u32[]{:S(2)}) copy-start(f32[1,4,32,8,128]{4,3,2,1,0:T(8,128)} %param.9) | copy-start | bytes 1572868
  4.0 0.7 %copy-start.4 = (f32[64,513]{1,0:T(8,128)}, f32[64,513]{1,0:T(8,128)S(1)}, u32[]{:S(2)}) copy-start(f32[64,513]{1,0:T(8,128)S(1)} %fusion.1) | copy-start | bytes 393988
  5.1 0.9 %slice-start = ((f32[64,513]{1,0:T(8,128)}), f32[64,512]{1,0:T(8,128)S(1)}, s32[]{:S(2)}) async-start(f32[64,513]{1,0:T(8,128)} %copy-done.4), calls=%async_computation.1 | async-start | bytes 262144 | tf_op jit(solution)/shard_map/slice | solution.py:201
  6.5 0.9 %copy-start.1 = (f32[1,32,8,128]{3,2,1,0:T(8,128)S(1)}, f32[1,32,8,128]{3,2,1,0:T(8,128)}, u32[]{:S(2)}) copy-start(f32[1,32,8,128]{3,2,1,0:T(8,128)} %param.11) | copy-start | bytes 393220
  9.6 18.3 %all-to-all-start = ((f32[16,7,512]{2,1,0:T(8,128)}), f32[16,7,512]{2,1,0:T(8,128)S(1)}, u32[]{:S(2)}, u32[]{:S(2)}) async-start(f32[16,7,512]{2,1,0:T(8,128)} %pad_maximum_fusion), calls=%async_computation | async-start | bytes 524288 | tf_op jit(solution)/shard_map/all_to_all | solution.py:224
  18.0 14.1 %collective-permute-start = (f32[160,128]{1,0:T(8,128)S(1)}, f32[160,128]{1,0:T(8,128)S(1)}, u32[]{:S(2)}, u32[]{:S(2)}) collective-permute-start(f32[160,128]{1,0:T(8,128)S(1)} %get-tuple-element.15), channel_id=1, source_target_pairs={{0,4},{4,8},{8,12},{1,5},{5,9},{9,13},{2,6},{6,10},{10,14},{3,7},{... | collective-permute-start | bytes 245768 | tf_op jit(solution)/shard_map/ppermute | solution.py:17
  21.8 10.2 %collective-permute-start.1 = (f32[160,128]{1,0:T(8,128)S(1)}, f32[160,128]{1,0:T(8,128)S(1)}, u32[]{:S(2)}, u32[]{:S(2)}) collective-permute-start(f32[160,128]{1,0:T(8,128)S(1)} %get-tuple-element.16), channel_id=1, source_target_pairs={{4,0},{8,4},{12,8},{5,1},{9,5},{13,9},{6,2},{10,6},{14,10},{7,3},{... | collective-permute-start | bytes 245768 | tf_op jit(solution)/shard_map/ppermute | solution.py:17
  23.1 7.4 %collective-permute-start.2 = (f32[8,160]{1,0:T(8,128)S(1)}, f32[8,160]{1,0:T(8,128)S(1)}, u32[]{:S(2)}, u32[]{:S(2)}) collective-permute-start(f32[8,160]{1,0:T(8,128)S(1)} %get-tuple-element.17), channel_id=1, source_target_pairs={{0,1},{1,2},{2,3},{4,5},{5,6},{6,7},{8,9},{9,10},{10,11},{12,13},{... | collective-permute-start | bytes 15368 | tf_op jit(solution)/shard_map/ppermute | solution.py:17
  26.5 5.5 %collective-permute-start.3 = (f32[8,160]{1,0:T(8,128)S(1)}, f32[8,160]{1,0:T(8,128)S(1)}, u32[]{:S(2)}, u32[]{:S(2)}) collective-permute-start(f32[8,160]{1,0:T(8,128)S(1)} %get-tuple-element.18), channel_id=1, source_target_pairs={{1,0},{2,1},{3,2},{5,4},{6,5},{7,6},{9,8},{10,9},{11,10},{13,12},{... | collective-permute-start | bytes 15368 | tf_op jit(solution)/shard_map/ppermute | solution.py:17
  28.4 0.7 %copy-start.12 = (s32[1,8,128]{2,1,0:T(8,128)S(1)}, s32[1,8,128]{2,1,0:T(8,128)}, u32[]{:S(2)}) copy-start(s32[1,8,128]{2,1,0:T(8,128)} %param.13) | copy-start | bytes 12292
  28.5 1.3 %collective-permute-start.4 = (f32[11,512]{1,0:T(8,128)S(1)}, f32[11,512]{1,0:T(8,128)S(1)}, u32[]{:S(2)}, u32[]{:S(2)}) collective-permute-start(f32[11,512]{1,0:T(8,128)S(1)} %pad_maximum_fusion.3), channel_id=1, source_target_pairs={{0,16},{16,0},{1,17},{17,1},{2,18},{18,2},{3,19},{19,3},{4,20},{20... | collective-permute-start | bytes 67592 | tf_op jit(solution)/shard_map/ppermute | solution.py:243
  29.7 2.3 %copy-start.9 = (f32[11,512]{1,0:T(8,128)}, f32[11,512]{1,0:T(8,128)S(1)}, u32[]{:S(2)}) copy-start(f32[11,512]{1,0:T(8,128)S(1)} %collective-permute-done.4) | copy-start | bytes 67588
  30.4 1.6 %copy-start.5 = (f32[8,160]{1,0:T(8,128)}, f32[8,160]{1,0:T(8,128)S(1)}, u32[]{:S(2)}) copy-start(f32[8,160]{1,0:T(8,128)S(1)} %collective-permute-done.2.refs_3_.refs_7_) | copy-start | bytes 15364
  32.0 0.6 %copy-start.6 = (f32[8,160]{1,0:T(8,128)}, f32[8,160]{1,0:T(8,128)S(1)}, u32[]{:S(2)}) copy-start(f32[8,160]{1,0:T(8,128)S(1)} %collective-permute-done.3.refs_4_.refs_8_) | copy-start | bytes 15364
  32.0 0.6 %copy-start.2 = (f32[160,128]{1,0:T(8,128)}, f32[160,128]{1,0:T(8,128)S(1)}, u32[]{:S(2)}) copy-start(f32[160,128]{1,0:T(8,128)S(1)} %collective-permute-done.refs_1_.refs_5_) | copy-start | bytes 245764
  32.0 0.7 %copy-start.3 = (f32[160,128]{1,0:T(8,128)}, f32[160,128]{1,0:T(8,128)S(1)}, u32[]{:S(2)}) copy-start(f32[160,128]{1,0:T(8,128)S(1)} %collective-permute-done.1.refs_2_.refs_6_) | copy-start | bytes 245764
  36.1 10.3 %copy-start.16 = (f32[8,128]{1,0:T(8,128)S(1)}, f32[8,128]{1,0:T(8,128)}, u32[]{:S(2)}) copy-start(f32[8,128]{1,0:T(8,128)} %get-tuple-element.24) | copy-start | bytes 12292
  36.1 15.8 %collective-permute-start.5 = (f32[128,128]{1,0:T(8,128)}, f32[128,128]{1,0:T(8,128)S(1)}, u32[]{:S(2)}, u32[]{:S(2)}) collective-permute-start(f32[128,128]{1,0:T(8,128)} %get-tuple-element.21), channel_id=1, source_target_pairs={{0,4},{4,8},{8,12},{1,5},{5,9},{9,13},{2,6},{6,10},{10,14},{3,7},{... | collective-permute-start | bytes 196616 | tf_op jit(solution)/shard_map/ppermute | solution.py:17
  40.7 11.1 %collective-permute-start.6 = (f32[128,128]{1,0:T(8,128)}, f32[128,128]{1,0:T(8,128)S(1)}, u32[]{:S(2)}, u32[]{:S(2)}) collective-permute-start(f32[128,128]{1,0:T(8,128)} %get-tuple-element.22), channel_id=1, source_target_pairs={{4,0},{8,4},{12,8},{5,1},{9,5},{13,9},{6,2},{10,6},{14,10},{7,3},{... | collective-permute-start | bytes 196616 | tf_op jit(solution)/shard_map/ppermute | solution.py:17
  42.0 5.8 %collective-permute-start.7 = (f32[8,128]{1,0:T(8,128)}, f32[8,128]{1,0:T(8,128)S(1)}, u32[]{:S(2)}, u32[]{:S(2)}) collective-permute-start(f32[8,128]{1,0:T(8,128)} %get-tuple-element.23), channel_id=1, source_target_pairs={{0,1},{1,2},{2,3},{4,5},{5,6},{6,7},{8,9},{9,10},{10,11},{12,13},{... | collective-permute-start | bytes 12296 | tf_op jit(solution)/shard_map/ppermute | solution.py:17
  46.3 5.5 %collective-permute-start.8 = (f32[8,128]{1,0:T(8,128)S(1)}, f32[8,128]{1,0:T(8,128)S(1)}, u32[]{:S(2)}, u32[]{:S(2)}) collective-permute-start(f32[8,128]{1,0:T(8,128)S(1)} %copy-done.16), channel_id=1, source_target_pairs={{1,0},{2,1},{3,2},{5,4},{6,5},{7,6},{9,8},{10,9},{11,10},{13,12},{... | collective-permute-start | bytes 12296 | tf_op jit(solution)/shard_map/ppermute | solution.py:17
  47.8 4.0 %copy-start.10 = (f32[8,128]{1,0:T(8,128)}, f32[8,128]{1,0:T(8,128)S(1)}, u32[]{:S(2)}) copy-start(f32[8,128]{1,0:T(8,128)S(1)} %collective-permute-done.7.refs_3_) | copy-start | bytes 12292
  51.8 0.6 %copy-start.11 = (f32[8,128]{1,0:T(8,128)}, f32[8,128]{1,0:T(8,128)S(1)}, u32[]{:S(2)}) copy-start(f32[8,128]{1,0:T(8,128)S(1)} %collective-permute-done.8.refs_4_) | copy-start | bytes 12292
  51.8 0.6 %copy-start.7 = (f32[128,128]{1,0:T(8,128)}, f32[128,128]{1,0:T(8,128)S(1)}, u32[]{:S(2)}) copy-start(f32[128,128]{1,0:T(8,128)S(1)} %collective-permute-done.5.refs_1_) | copy-start | bytes 196612
  51.8 0.7 %copy-start.8 = (f32[128,128]{1,0:T(8,128)}, f32[128,128]{1,0:T(8,128)S(1)}, u32[]{:S(2)}) copy-start(f32[128,128]{1,0:T(8,128)S(1)} %collective-permute-done.6.refs_2_) | copy-start | bytes 196612

commit v6 on v5

--- a/solution.py
+++ b/solution.py
@@ -82,12 +82,13 @@
                 else:
                     divisor = diagonal
                     numerator = h
+                inverse = 1.0 / divisor
                 if l < levels - 1:
-                    cprev[f] = -kd / divisor
+                    cprev[f] = -kd * inverse
                     c_ref[f, l] = cprev[f]
-                dprev[f] = numerator / divisor
+                dprev[f] = numerator * inverse
                 out_ref[f, l] = dprev[f]
-        wet = wet_ref[...]
+        wet = wet_ref[...].astype(jnp.float32)
         if emit:
             sub = lax.broadcasted_iota(jnp.int32, (8, cols), 0)
             lane = lax.broadcasted_iota(jnp.int32, (rows, planes), 1)
@@ -150,7 +151,7 @@
     east = u_east[0]
     north = u_north[0]
     coeffs = diffusivity[0]
-    wet = wet_mask[0].astype(jnp.float32)
+    wet = wet_mask[0]
 
     def row_edge(index):
         field_rows = adjoint[:, :, index, :].reshape(planes, cols_y)
@@ -190,15 +191,15 @@
     earlier = (targets[:, None] == targets[None, :]) & (order_ids[None, :] < order_ids[:, None])
     rank_in = jnp.sum(earlier.astype(jnp.int32), axis=1)
     slot_ids = targets * CAP + rank_in
-    slotting = (
-        slot_ids[None, :] == jnp.arange(tiles * CAP, dtype=jnp.int32)[:, None]
-    ).astype(jnp.float32)
-    tagged = jnp.concatenate([payload, (landing + 1).astype(jnp.float32)[:, None]], 1)
+    slotting = slot_ids[None, :] == jnp.arange(tiles * CAP, dtype=jnp.int32)[:, None]
     slots = jnp.dot(
-        slotting, tagged, precision=lax.Precision.HIGHEST, preferred_element_type=jnp.float32
-    )
-    tags = slots[:, fields * cols_y].reshape(tiles_x, tiles_y, CAP)
-    slots = slots[:, : fields * cols_y].reshape(tiles, CAP, fields * cols_y)
+        slotting.astype(jnp.float32),
+        payload,
+        precision=lax.Precision.HIGHEST,
+        preferred_element_type=jnp.float32,
+    ).reshape(tiles, CAP, fields * cols_y)
+    tags = jnp.sum(slotting.astype(jnp.int32) * (landing + 1)[None, :], axis=1)
+    tags = tags.astype(jnp.float32).reshape(tiles_x, tiles_y, CAP)
     zero_x = jnp.zeros((1, tiles_y, fields, cols_y), jnp.float32)
     up_rows = jnp.concatenate([zero_x, summed[:-1, :, rows_x - 1]], 0)
     dn_rows = jnp.concatenate([summed[1:, :, 0], zero_x], 0)

time: 56.2 us -> 63.5 us (1.13)
  waiting for transfers between devices: 5.93 us -> 17.6 us
  local copies, waits for them, and re-layouts: 9.65 us -> 8.04 us
  starting transfers between devices: 29.7 us -> 28.2 us
  other arithmetic: 1.79 us -> 0.5 us
    all_to_all x1, waiting for transfers between devices: 0.14 us -> 9.86 us  [shards(): lax.all_to_all(send_data, ('gx', 'gy'), split_axis=0, concat_axis=0, tile...]
    ppermute x8, waiting for transfers between devices: 5.78 us -> 7.74 us  [shift(): return lax.ppermute(block, axis, route)]
    unnamed x34 -> x30, local copies, waits for them, and re-layouts: 4.75 us -> 3.08 us
    ppermute x8, starting transfers between devices: 21.3 us -> 19.7 us  [shift(): return lax.ppermute(block, axis, route)]
    optimization_barrier x0 -> x1, local copies, waits for them, and re-layouts: none -> 0.84 us  [shards(): lax.optimization_barrier((send_data, row_edge(rows_x - 1), row_edge(0), c...]
    concatenate x1, other arithmetic: 0.83 us -> 0.02 us  [shards(): jnp.concatenate([slots, up_rows.reshape(tiles, 1, fields * cols_y), dn_ro...]
    slice x3 -> x0, local copies, waits for them, and re-layouts: 0.73 us -> none  [the longest x2 0.63 us: shards(): slots = slots[:, :fields * cols_y].reshape(tiles, CAP, fields * cols_y)]
  transfers between devices with their start and end apart: 10 -> 10, of which waited for: 4 -> 4; matrix products, arithmetic and copies ran while one was open for 3% -> 1% of each run, Pallas kernels for 0% -> 0%
where the time goes in v6:
time: 63.5 us; the launch traced here: 62.9 us
  starting transfers between devices  28.2 us (44%)
  waiting for transfers between devices  17.6 us (28%)
  local copies, waits for them, and re-layouts  8.04 us (13%)
  Pallas kernels  6.51 us (10%)
  matrix products  1.71 us (3%)
    ppermute x8, starting transfers between devices, shift(): return lax.ppermute(block, axis, route)  19.7 us
    all_to_all x1, waiting for transfers between devices, shards(): lax.all_to_all(send_data, ('gx', 'gy'), split_axis=0, concat_axis=0, tile...  9.86 us
    all_to_all x1, starting transfers between devices, shards(): lax.all_to_all(send_data, ('gx', 'gy'), split_axis=0, concat_axis=0, tile...  8.34 us
    ppermute x8, waiting for transfers between devices, shift(): return lax.ppermute(block, axis, route)  7.74 us
    pallas_call x2, Pallas kernels, run_step(): pl.pallas_call(step_kernel(fields, levels, rows, cols, coupled, emit), ou...  6.51 us
    unnamed x30, local copies, waits for them, and re-layouts  3.08 us
  transfers between devices with their start and end apart: 10, of which 4 were waited for; matrix products, arithmetic and copies ran while one was open for 1% of the time, Pallas kernels for 0%

profile of v6, /device:TPU:0, one launch (start us, length us, event | category | flops | bytes accessed | tf_op | source)
XLA Modules:
  0.0 62.9 jit_solution(16797408616947705886)
XLA Ops:
  0.0 0.7 %copy-done.11 = s32[1,1,1,32]{3,2,1,0:T(1,128)S(1)} copy-done((s32[1,1,1,32]{3,2,1,0:T(1,128)S(1)}, s32[1,1,1,32]{3,2,1,0:T(1,128)}, u32[]{:S(2)}) %copy-start.11) | copy-done | bytes 152
  0.7 1.0 %convolution_multiply_fusion = f32[32,4,128]{2,0,1:T(8,128)S(1)} fusion(f32[32,128]{1,0:T(8,128)} %bitcast.90, f32[4,32,8,128]{3,2,1,0:T(8,128)} %bitcast.66, s32[32]{0:T(128)S(1)} %bitcast.93), kind=kOutput, calls=%fused_computation | convolution fusion | flops 1589504 | bytes 98432 | tf_op jit(solution)/shard_map/dot_general | solution.py:174
  1.6 0.0 copy-start.13
  1.7 0.0 copy-start.12
  1.7 0.0 copy-start
  1.7 0.6 copy-done.13
  2.3 0.2 convert_reduce_fusion
  2.5 0.0 copy-done.12
  2.5 0.3 fusion
  2.8 0.3 slice_reduce_fusion.1
  3.2 0.0 copy-done
  3.2 0.2 fusion.18
  3.4 0.1 fusion.19
  3.6 0.1 copy.47
  3.6 0.1 reshape.112
  3.7 0.1 select_reduce_fusion
  3.8 0.1 convert_element_type.26
  3.9 0.1 select_maximum_fusion.1
  4.2 0.3 copy.48
  4.4 0.1 reshape.114
  4.5 0.3 copy.51
  4.8 0.1 reshape.115
  4.9 0.5 copy-done.1
  5.4 0.1 fusion.21
  5.5 0.1 copy.50
  5.7 0.1 copy.53
  5.8 1.0 %fusion.22 = (f32[32,1,128]{2,1,0:T(1,128)S(1)}, f32[32,1,128]{2,1,0:T(1,128)S(1)}) fusion(f32[32,8,128]{2,1,0:T(8,128)} %bitcast.75), kind=kLoop, calls=%fused_computation.51 | loop fusion | bytes 65536 | tf_op jit(solution)/shard_map/slice | solution.py:158
  6.8 0.3 fusion.6
  7.1 0.8 %copy.54 = f32[16,7,512]{2,1,0:T(8,128)} copy(f32[16,7,512]{2,0,1:T(8,128)S(1)} %pad_maximum_fusion) | data formatting | bytes 458752 | tf_op jit(solution)/shard_map/optimization_barrier | solution.py:222
  8.0 8.3 %all-to-all-start = ((f32[16,7,512]{2,1,0:T(8,128)}), f32[16,7,512]{2,1,0:T(8,128)S(1)}, u32[]{:S(2)}, u32[]{:S(2)}) async-start(f32[16,7,512]{2,1,0:T(8,128)} %copy.54), calls=%async_computation | async-start | bytes 524288 | tf_op jit(solution)/shard_map/all_to_all | solution.py:225
  16.3 9.9 %all-to-all-done = f32[16,7,512]{2,1,0:T(8,128)S(1)} async-done(((f32[16,7,512]{2,1,0:T(8,128)}), f32[16,7,512]{2,1,0:T(8,128)S(1)}, u32[]{:S(2)}, u32[]{:S(2)}) %all-to-all-start) | async-done | bytes 229408 | tf_op jit(solution)/shard_map/all_to_all | solution.py:225
  26.3 0.1 slice_reduce_fusion.3
  26.4 0.1 eq.128
  26.5 0.2 fusion.13
  26.7 0.1 slice_reduce_fusion.2
  26.7 0.1 collective-permute-start.4
  26.8 3.0 %collective-permute-start = (f32[160,128]{1,0:T(8,128)S(1)}, f32[160,128]{1,0:T(8,128)S(1)}, u32[]{:S(2)}, u32[]{:S(2)}) collective-permute-start(f32[160,128]{1,0:T(8,128)S(1)} %get-tuple-element.15), channel_id=1, source_target_pairs={{0,4},{4,8},{8,12},{1,5},{5,9},{9,13},{2,6},{6,10},{10,14},{3,7},{... | collective-permute-start | bytes 245768 | tf_op jit(solution)/shard_map/ppermute | solution.py:17
  29.8 1.3 %collective-permute-start.1 = (f32[160,128]{1,0:T(8,128)S(1)}, f32[160,128]{1,0:T(8,128)S(1)}, u32[]{:S(2)}, u32[]{:S(2)}) collective-permute-start(f32[160,128]{1,0:T(8,128)S(1)} %get-tuple-element.16), channel_id=1, source_target_pairs={{4,0},{8,4},{12,8},{5,1},{9,5},{13,9},{6,2},{10,6},{14,10},{7,3},{... | collective-permute-start | bytes 245768 | tf_op jit(solution)/shard_map/ppermute | solution.py:17
  31.1 2.5 %collective-permute-start.2 = (f32[8,160]{1,0:T(8,128)S(1)}, f32[8,160]{1,0:T(8,128)S(1)}, u32[]{:S(2)}, u32[]{:S(2)}) collective-permute-start(f32[8,160]{1,0:T(8,128)S(1)} %get-tuple-element.17), channel_id=1, source_target_pairs={{0,1},{1,2},{2,3},{4,5},{5,6},{6,7},{8,9},{9,10},{10,11},{12,13},{... | collective-permute-start | bytes 15368 | tf_op jit(solution)/shard_map/ppermute | solution.py:17
  33.6 1.3 %collective-permute-start.3 = (f32[8,160]{1,0:T(8,128)S(1)}, f32[8,160]{1,0:T(8,128)S(1)}, u32[]{:S(2)}, u32[]{:S(2)}) collective-permute-start(f32[8,160]{1,0:T(8,128)S(1)} %get-tuple-element.18), channel_id=1, source_target_pairs={{1,0},{2,1},{3,2},{5,4},{6,5},{7,6},{9,8},{10,9},{11,10},{13,12},{... | collective-permute-start | bytes 15368 | tf_op jit(solution)/shard_map/ppermute | solution.py:17
  34.9 0.0 collective-permute-done.4
  34.9 0.0 copy-start.8
  34.9 0.7 %reshape_squeeze.11.refs_14_ = f32[8,8]{1,0:T(8,128)} reshape(f32[64]{0:T(128)S(1)} %slice_reduce_fusion.4) | data formatting | bytes 512 | tf_op jit(solution)/shard_map/reshape;squeeze | solution.py:245
  35.6 0.0 collective-permute-done.2.refs_3_.refs_7_
  35.6 3.5 %collective-permute-done.3.refs_4_.refs_8_ = f32[8,160]{1,0:T(8,128)S(1)} collective-permute-done((f32[8,160]{1,0:T(8,128)S(1)}, f32[8,160]{1,0:T(8,128)S(1)}, u32[]{:S(2)}, u32[]{:S(2)}) %collective-permute-start.3) | collective-permute-done | bytes 5152 | tf_op jit(solution)/shard_map/ppermute | solution.py:17
  39.1 0.0 collective-permute-done.refs_1_.refs_5_
  39.1 0.0 collective-permute-done.1.refs_2_.refs_6_
  39.2 0.6 copy-done.5
  39.7 0.0 copy-done.2
  39.8 0.0 copy-done.3
  39.8 3.4 %shard_map.91 = (f32[4,32,8,128]{3,2,1,0:T(8,128)}, f32[128,128]{1,0:T(8,128)}, f32[128,128]{1,0:T(8,128)}, f32[8,128]{1,0:T(8,128)}, f32[8,128]{1,0:T(8,128)}) custom-call(f32[4,32,8,128]{3,2,1,0:T(8,128)} %bitcast.67, f32[160,128]{1,0:T(8,128)} %copy-done.2, f32[160,128]{1,0:T(8,128)} %copy-done.3, f32[8,160]{1,0:T(8,128)} %copy-done.4, ...), custom_call_target="tpu_custom_call" | custom-call | tf_op jit(solution)/shard_map/pallas_call | solution.py:133
  43.2 4.7 %collective-permute-start.5 = (f32[128,128]{1,0:T(8,128)}, f32[128,128]{1,0:T(8,128)S(1)}, u32[]{:S(2)}, u32[]{:S(2)}) collective-permute-start(f32[128,128]{1,0:T(8,128)} %get-tuple-element.21), channel_id=1, source_target_pairs={{0,4},{4,8},{8,12},{1,5},{5,9},{9,13},{2,6},{6,10},{10,14},{3,7},{... | collective-permute-start | bytes 196616 | tf_op jit(solution)/shard_map/ppermute | solution.py:17
  47.9 1.3 %collective-permute-start.6 = (f32[128,128]{1,0:T(8,128)}, f32[128,128]{1,0:T(8,128)S(1)}, u32[]{:S(2)}, u32[]{:S(2)}) collective-permute-start(f32[128,128]{1,0:T(8,128)} %get-tuple-element.22), channel_id=1, source_target_pairs={{4,0},{8,4},{12,8},{5,1},{9,5},{13,9},{6,2},{10,6},{14,10},{7,3},{... | collective-permute-start | bytes 196616 | tf_op jit(solution)/shard_map/ppermute | solution.py:17
  49.2 4.4 %collective-permute-start.7 = (f32[8,128]{1,0:T(8,128)}, f32[8,128]{1,0:T(8,128)S(1)}, u32[]{:S(2)}, u32[]{:S(2)}) collective-permute-start(f32[8,128]{1,0:T(8,128)} %get-tuple-element.23), channel_id=1, source_target_pairs={{0,1},{1,2},{2,3},{4,5},{5,6},{6,7},{8,9},{9,10},{10,11},{12,13},{... | collective-permute-start | bytes 12296 | tf_op jit(solution)/shard_map/ppermute | solution.py:17
  53.6 0.0 copy-done.14
  53.6 1.3 %collective-permute-start.8 = (f32[8,128]{1,0:T(8,128)S(1)}, f32[8,128]{1,0:T(8,128)S(1)}, u32[]{:S(2)}, u32[]{:S(2)}) collective-permute-start(f32[8,128]{1,0:T(8,128)S(1)} %copy-done.14), channel_id=1, source_target_pairs={{1,0},{2,1},{3,2},{5,4},{6,5},{7,6},{9,8},{10,9},{11,10},{13,12},{... | collective-permute-start | bytes 12296 | tf_op jit(solution)/shard_map/ppermute | solution.py:17
  54.9 0.2 collective-permute-done.7.refs_3_
  55.1 4.0 %collective-permute-done.8.refs_4_ = f32[8,128]{1,0:T(8,128)S(1)} collective-permute-done((f32[8,128]{1,0:T(8,128)S(1)}, f32[8,128]{1,0:T(8,128)S(1)}, u32[]{:S(2)}, u32[]{:S(2)}) %collective-permute-start.8) | collective-permute-done | bytes 4128 | tf_op jit(solution)/shard_map/ppermute | solution.py:17
  59.1 0.0 collective-permute-done.5.refs_1_
  59.1 0.0 collective-permute-done.6.refs_2_
  59.2 0.6 copy-done.10
  59.7 0.0 copy-done.6
  59.8 0.0 copy-done.7
  59.8 3.1 %shard_map.92 = f32[4,32,8,128]{3,2,1,0:T(8,128)} custom-call(f32[4,32,8,128]{3,2,1,0:T(8,128)} %get-tuple-element.20.refs_0_, f32[128,128]{1,0:T(8,128)} %copy-done.6, f32[128,128]{1,0:T(8,128)} %copy-done.7, f32[8,128]{1,0:T(8,128)} %copy-done.9, f32[8,128]{1,0:T(8,128)} %copy-done.10, f32[160,128]{1,0:T(8,128)} %copy-done.2, f32[160,128]{1,0:T(8,128)} %copy-done.3, ...), custom_call_target="tpu_custom_call" | custom-call | tf_op jit(solution)/shard_map/pallas_call | solution.py:133
  (39 shorter events, 0.4 us)
Async XLA Ops:
  0.0 0.7 %copy-start.11 = (s32[1,1,1,32]{3,2,1,0:T(1,128)S(1)}, s32[1,1,1,32]{3,2,1,0:T(1,128)}, u32[]{:S(2)}) copy-start(s32[1,1,1,32]{3,2,1,0:T(1,128)} %param.15) | copy-start | bytes 388
  1.6 0.7 %copy-start.13 = (s32[1,1,1,32,1]{3,4,2,1,0:T(1,128)S(1)}, s32[1,1,1,32,1]{3,4,2,1,0:T(1,128)}, u32[]{:S(2)}) copy-start(s32[1,1,1,32,1]{3,4,2,1,0:T(1,128)} %param.14) | copy-start | bytes 388
  1.7 0.8 %copy-start.12 = (s32[1,1,1,32]{3,2,1,0:T(1,128)S(1)}, s32[1,1,1,32]{3,2,1,0:T(1,128)}, u32[]{:S(2)}) copy-start(s32[1,1,1,32]{3,2,1,0:T(1,128)} %param.16) | copy-start | bytes 388
  1.7 1.5 %copy-start = (f32[1,4,32,8,128]{4,3,2,1,0:T(8,128)S(1)}, f32[1,4,32,8,128]{4,3,2,1,0:T(8,128)}, u32[]{:S(2)}) copy-start(f32[1,4,32,8,128]{4,3,2,1,0:T(8,128)} %param.9) | copy-start | bytes 1572868
  4.5 0.9 %copy-start.1 = (f32[1,32,8,128]{3,2,1,0:T(8,128)S(1)}, f32[1,32,8,128]{3,2,1,0:T(8,128)}, u32[]{:S(2)}) copy-start(f32[1,32,8,128]{3,2,1,0:T(8,128)} %param.11) | copy-start | bytes 393220
  8.0 18.2 %all-to-all-start = ((f32[16,7,512]{2,1,0:T(8,128)}), f32[16,7,512]{2,1,0:T(8,128)S(1)}, u32[]{:S(2)}, u32[]{:S(2)}) async-start(f32[16,7,512]{2,1,0:T(8,128)} %copy.54), calls=%async_computation | async-start | bytes 524288 | tf_op jit(solution)/shard_map/all_to_all | solution.py:225
  26.7 8.2 %collective-permute-start.4 = (f32[11,512]{1,0:T(8,128)S(1)}, f32[11,512]{1,0:T(8,128)S(1)}, u32[]{:S(2)}, u32[]{:S(2)}) collective-permute-start(f32[11,512]{1,0:T(8,128)S(1)} %pad_maximum_fusion.3), channel_id=1, source_target_pairs={{0,16},{16,0},{1,17},{17,1},{2,18},{18,2},{3,19},{19,3},{4,20},{20... | collective-permute-start | bytes 67592 | tf_op jit(solution)/shard_map/ppermute | solution.py:244
  26.8 12.3 %collective-permute-start = (f32[160,128]{1,0:T(8,128)S(1)}, f32[160,128]{1,0:T(8,128)S(1)}, u32[]{:S(2)}, u32[]{:S(2)}) collective-permute-start(f32[160,128]{1,0:T(8,128)S(1)} %get-tuple-element.15), channel_id=1, source_target_pairs={{0,4},{4,8},{8,12},{1,5},{5,9},{9,13},{2,6},{6,10},{10,14},{3,7},{... | collective-permute-start | bytes 245768 | tf_op jit(solution)/shard_map/ppermute | solution.py:17
  29.8 9.3 %collective-permute-start.1 = (f32[160,128]{1,0:T(8,128)S(1)}, f32[160,128]{1,0:T(8,128)S(1)}, u32[]{:S(2)}, u32[]{:S(2)}) collective-permute-start(f32[160,128]{1,0:T(8,128)S(1)} %get-tuple-element.16), channel_id=1, source_target_pairs={{4,0},{8,4},{12,8},{5,1},{9,5},{13,9},{6,2},{10,6},{14,10},{7,3},{... | collective-permute-start | bytes 245768 | tf_op jit(solution)/shard_map/ppermute | solution.py:17
  31.1 4.5 %collective-permute-start.2 = (f32[8,160]{1,0:T(8,128)S(1)}, f32[8,160]{1,0:T(8,128)S(1)}, u32[]{:S(2)}, u32[]{:S(2)}) collective-permute-start(f32[8,160]{1,0:T(8,128)S(1)} %get-tuple-element.17), channel_id=1, source_target_pairs={{0,1},{1,2},{2,3},{4,5},{5,6},{6,7},{8,9},{9,10},{10,11},{12,13},{... | collective-permute-start | bytes 15368 | tf_op jit(solution)/shard_map/ppermute | solution.py:17
  33.6 5.5 %collective-permute-start.3 = (f32[8,160]{1,0:T(8,128)S(1)}, f32[8,160]{1,0:T(8,128)S(1)}, u32[]{:S(2)}, u32[]{:S(2)}) collective-permute-start(f32[8,160]{1,0:T(8,128)S(1)} %get-tuple-element.18), channel_id=1, source_target_pairs={{1,0},{2,1},{3,2},{5,4},{6,5},{7,6},{9,8},{10,9},{11,10},{13,12},{... | collective-permute-start | bytes 15368 | tf_op jit(solution)/shard_map/ppermute | solution.py:17
  34.9 4.3 %copy-start.8 = (f32[11,512]{1,0:T(8,128)}, f32[11,512]{1,0:T(8,128)S(1)}, u32[]{:S(2)}) copy-start(f32[11,512]{1,0:T(8,128)S(1)} %collective-permute-done.4) | copy-start | bytes 67588
  35.6 3.6 %copy-start.4 = (f32[8,160]{1,0:T(8,128)}, f32[8,160]{1,0:T(8,128)S(1)}, u32[]{:S(2)}) copy-start(f32[8,160]{1,0:T(8,128)S(1)} %collective-permute-done.2.refs_3_.refs_7_) | copy-start | bytes 15364
  39.1 0.6 copy-start.5
  39.1 0.6 %copy-start.2 = (f32[160,128]{1,0:T(8,128)}, f32[160,128]{1,0:T(8,128)S(1)}, u32[]{:S(2)}) copy-start(f32[160,128]{1,0:T(8,128)S(1)} %collective-permute-done.refs_1_.refs_5_) | copy-start | bytes 245764
  39.1 0.7 %copy-start.3 = (f32[160,128]{1,0:T(8,128)}, f32[160,128]{1,0:T(8,128)S(1)}, u32[]{:S(2)}) copy-start(f32[160,128]{1,0:T(8,128)S(1)} %collective-permute-done.1.refs_2_.refs_6_) | copy-start | bytes 245764
  43.2 10.4 %copy-start.14 = (f32[8,128]{1,0:T(8,128)S(1)}, f32[8,128]{1,0:T(8,128)}, u32[]{:S(2)}) copy-start(f32[8,128]{1,0:T(8,128)} %get-tuple-element.24) | copy-start | bytes 12292
  43.2 15.9 %collective-permute-start.5 = (f32[128,128]{1,0:T(8,128)}, f32[128,128]{1,0:T(8,128)S(1)}, u32[]{:S(2)}, u32[]{:S(2)}) collective-permute-start(f32[128,128]{1,0:T(8,128)} %get-tuple-element.21), channel_id=1, source_target_pairs={{0,4},{4,8},{8,12},{1,5},{5,9},{9,13},{2,6},{6,10},{10,14},{3,7},{... | collective-permute-start | bytes 196616 | tf_op jit(solution)/shard_map/ppermute | solution.py:17
  47.9 11.3 %collective-permute-start.6 = (f32[128,128]{1,0:T(8,128)}, f32[128,128]{1,0:T(8,128)S(1)}, u32[]{:S(2)}, u32[]{:S(2)}) collective-permute-start(f32[128,128]{1,0:T(8,128)} %get-tuple-element.22), channel_id=1, source_target_pairs={{4,0},{8,4},{12,8},{5,1},{9,5},{13,9},{6,2},{10,6},{14,10},{7,3},{... | collective-permute-start | bytes 196616 | tf_op jit(solution)/shard_map/ppermute | solution.py:17
  49.2 6.0 %collective-permute-start.7 = (f32[8,128]{1,0:T(8,128)}, f32[8,128]{1,0:T(8,128)S(1)}, u32[]{:S(2)}, u32[]{:S(2)}) collective-permute-start(f32[8,128]{1,0:T(8,128)} %get-tuple-element.23), channel_id=1, source_target_pairs={{0,1},{1,2},{2,3},{4,5},{5,6},{6,7},{8,9},{9,10},{10,11},{12,13},{... | collective-permute-start | bytes 12296 | tf_op jit(solution)/shard_map/ppermute | solution.py:17
  53.6 5.5 %collective-permute-start.8 = (f32[8,128]{1,0:T(8,128)S(1)}, f32[8,128]{1,0:T(8,128)S(1)}, u32[]{:S(2)}, u32[]{:S(2)}) collective-permute-start(f32[8,128]{1,0:T(8,128)S(1)} %copy-done.14), channel_id=1, source_target_pairs={{1,0},{2,1},{3,2},{5,4},{6,5},{7,6},{9,8},{10,9},{11,10},{13,12},{... | collective-permute-start | bytes 12296 | tf_op jit(solution)/shard_map/ppermute | solution.py:17
  55.1 4.0 %copy-start.9 = (f32[8,128]{1,0:T(8,128)}, f32[8,128]{1,0:T(8,128)S(1)}, u32[]{:S(2)}) copy-start(f32[8,128]{1,0:T(8,128)S(1)} %collective-permute-done.7.refs_3_) | copy-start | bytes 12292
  59.1 0.6 copy-start.10
  59.1 0.6 %copy-start.6 = (f32[128,128]{1,0:T(8,128)}, f32[128,128]{1,0:T(8,128)S(1)}, u32[]{:S(2)}) copy-start(f32[128,128]{1,0:T(8,128)S(1)} %collective-permute-done.5.refs_1_) | copy-start | bytes 196612
  59.1 0.6 %copy-start.7 = (f32[128,128]{1,0:T(8,128)}, f32[128,128]{1,0:T(8,128)S(1)}, u32[]{:S(2)}) copy-start(f32[128,128]{1,0:T(8,128)S(1)} %collective-permute-done.6.refs_2_) | copy-start | bytes 196612

commit v7 on v6

--- a/solution.py
+++ b/solution.py
@@ -82,13 +82,12 @@
                 else:
                     divisor = diagonal
                     numerator = h
-                inverse = 1.0 / divisor
                 if l < levels - 1:
-                    cprev[f] = -kd * inverse
+                    cprev[f] = -kd / divisor
                     c_ref[f, l] = cprev[f]
-                dprev[f] = numerator * inverse
+                dprev[f] = numerator / divisor
                 out_ref[f, l] = dprev[f]
-        wet = wet_ref[...].astype(jnp.float32)
+        wet = wet_ref[...]
         if emit:
             sub = lax.broadcasted_iota(jnp.int32, (8, cols), 0)
             lane = lax.broadcasted_iota(jnp.int32, (rows, planes), 1)
@@ -151,7 +150,7 @@
     east = u_east[0]
     north = u_north[0]
     coeffs = diffusivity[0]
-    wet = wet_mask[0]
+    wet = wet_mask[0].astype(jnp.float32)
 
     def row_edge(index):
         field_rows = adjoint[:, :, index, :].reshape(planes, cols_y)

time: 63.5 us -> 54.6 us (0.86)
  waiting for transfers between devices: 17.6 us -> 5.93 us
  starting transfers between devices: 28.2 us -> 29.7 us
    all_to_all x1, waiting for transfers between devices: 9.86 us -> 0.15 us  [shards(): lax.all_to_all(send_data, ('gx', 'gy'), split_axis=0, concat_axis=0, tile...]
    ppermute x8, waiting for transfers between devices: 7.74 us -> 5.77 us  [shift(): return lax.ppermute(block, axis, route)]
    ppermute x8, starting transfers between devices: 19.7 us -> 21.3 us  [shift(): return lax.ppermute(block, axis, route)]
    unnamed x30 -> x32, local copies, waits for them, and re-layouts: 3.08 us -> 3.68 us
  transfers between devices with their start and end apart: 10 -> 10, of which waited for: 4 -> 4; matrix products, arithmetic and copies ran while one was open for 1% -> 3% of each run, Pallas kernels for 0% -> 0%
where the time goes in v7:
time: 54.6 us; the launch traced here: 54 us
  starting transfers between devices  29.7 us (54%)
  local copies, waits for them, and re-layouts  8.63 us (16%)
  Pallas kernels  6.52 us (12%)
  waiting for transfers between devices  5.93 us (11%)
  matrix products  1.71 us (3%)
  other arithmetic  1.1 us (2%)
    ppermute x8, starting transfers between devices, shift(): return lax.ppermute(block, axis, route)  21.3 us
    all_to_all x1, starting transfers between devices, shards(): lax.all_to_all(send_data, ('gx', 'gy'), split_axis=0, concat_axis=0, tile...  8.34 us
    pallas_call x2, Pallas kernels, run_step(): pl.pallas_call(step_kernel(fields, levels, rows, cols, coupled, emit), ou...  6.52 us
    ppermute x8, waiting for transfers between devices, shift(): return lax.ppermute(block, axis, route)  5.77 us
    unnamed x32, local copies, waits for them, and re-layouts  3.68 us
  transfers between devices with their start and end apart: 10, of which 4 were waited for; matrix products, arithmetic and copies ran while one was open for 3% of the time, Pallas kernels for 0%

profile of v7, /device:TPU:0, one launch (start us, length us, event | category | flops | bytes accessed | tf_op | source)
XLA Modules:
  0.0 54.0 jit_solution(15803887570706295900)
XLA Ops:
  0.0 0.7 %copy-done.12 = s32[1,1,1,32]{3,2,1,0:T(1,128)S(1)} copy-done((s32[1,1,1,32]{3,2,1,0:T(1,128)S(1)}, s32[1,1,1,32]{3,2,1,0:T(1,128)}, u32[]{:S(2)}) %copy-start.12) | copy-done | bytes 152
  0.7 1.0 %convolution_multiply_fusion = f32[32,4,128]{2,0,1:T(8,128)S(1)} fusion(f32[32,128]{1,0:T(8,128)} %bitcast.89, f32[4,32,8,128]{3,2,1,0:T(8,128)} %bitcast.67, s32[32]{0:T(128)S(1)} %bitcast.92), kind=kOutput, calls=%fused_computation | convolution fusion | flops 1589504 | bytes 98432 | tf_op jit(solution)/shard_map/dot_general | solution.py:173
  1.6 0.0 copy-start.14
  1.7 0.0 copy-start.13
  1.7 0.0 copy-start
  1.7 0.6 %copy-done.14 = s32[1,1,1,32,1]{3,4,2,1,0:T(1,128)S(1)} copy-done((s32[1,1,1,32,1]{3,4,2,1,0:T(1,128)S(1)}, s32[1,1,1,32,1]{3,4,2,1,0:T(1,128)}, u32[]{:S(2)}) %copy-start.14) | copy-done | bytes 152
  2.3 0.2 convert_reduce_fusion
  2.5 0.0 copy-done.13
  2.5 0.3 fusion
  2.8 0.3 slice_reduce_fusion.1
  3.2 0.2 fusion.18
  3.4 0.1 fusion.19
  3.6 0.1 copy.47
  3.6 0.1 reshape.113
  3.7 0.1 select_reduce_fusion
  3.8 0.1 convert_element_type.31
  3.9 0.1 select_maximum_fusion.1
  4.2 0.3 copy.48
  4.4 0.1 reshape.115
  4.5 0.3 copy.51
  4.8 0.1 reshape.116
  4.9 0.5 copy-done.1
  5.4 0.1 fusion.21
  5.5 0.1 copy.50
  5.7 0.1 copy.53
  5.8 1.0 %fusion.22 = (f32[32,1,128]{2,1,0:T(1,128)S(1)}, f32[32,1,128]{2,1,0:T(1,128)S(1)}) fusion(f32[32,8,128]{2,1,0:T(8,128)} %bitcast.76), kind=kLoop, calls=%fused_computation.52 | loop fusion | bytes 65536 | tf_op jit(solution)/shard_map/slice | solution.py:157
  6.8 0.3 fusion.6
  7.1 0.8 %copy.54 = f32[16,7,512]{2,1,0:T(8,128)} copy(f32[16,7,512]{2,0,1:T(8,128)S(1)} %pad_maximum_fusion) | data formatting | bytes 458752 | tf_op jit(solution)/shard_map/optimization_barrier | solution.py:221
  8.0 8.3 %all-to-all-start = ((f32[16,7,512]{2,1,0:T(8,128)}), f32[16,7,512]{2,1,0:T(8,128)S(1)}, u32[]{:S(2)}, u32[]{:S(2)}) async-start(f32[16,7,512]{2,1,0:T(8,128)} %copy.54), calls=%async_computation | async-start | bytes 524288 | tf_op jit(solution)/shard_map/all_to_all | solution.py:224
  16.3 3.8 %collective-permute-start = (f32[160,128]{1,0:T(8,128)S(1)}, f32[160,128]{1,0:T(8,128)S(1)}, u32[]{:S(2)}, u32[]{:S(2)}) collective-permute-start(f32[160,128]{1,0:T(8,128)S(1)} %get-tuple-element.15), channel_id=1, source_target_pairs={{0,4},{4,8},{8,12},{1,5},{5,9},{9,13},{2,6},{6,10},{10,14},{3,7},{... | collective-permute-start | bytes 245768 | tf_op jit(solution)/shard_map/ppermute | solution.py:17
  20.2 1.3 %collective-permute-start.1 = (f32[160,128]{1,0:T(8,128)S(1)}, f32[160,128]{1,0:T(8,128)S(1)}, u32[]{:S(2)}, u32[]{:S(2)}) collective-permute-start(f32[160,128]{1,0:T(8,128)S(1)} %get-tuple-element.16), channel_id=1, source_target_pairs={{4,0},{8,4},{12,8},{5,1},{9,5},{13,9},{6,2},{10,6},{14,10},{7,3},{... | collective-permute-start | bytes 245768 | tf_op jit(solution)/shard_map/ppermute | solution.py:17
  21.5 3.4 %collective-permute-start.2 = (f32[8,160]{1,0:T(8,128)S(1)}, f32[8,160]{1,0:T(8,128)S(1)}, u32[]{:S(2)}, u32[]{:S(2)}) collective-permute-start(f32[8,160]{1,0:T(8,128)S(1)} %get-tuple-element.17), channel_id=1, source_target_pairs={{0,1},{1,2},{2,3},{4,5},{5,6},{6,7},{8,9},{9,10},{10,11},{12,13},{... | collective-permute-start | bytes 15368 | tf_op jit(solution)/shard_map/ppermute | solution.py:17
  24.8 1.3 %collective-permute-start.3 = (f32[8,160]{1,0:T(8,128)S(1)}, f32[8,160]{1,0:T(8,128)S(1)}, u32[]{:S(2)}, u32[]{:S(2)}) collective-permute-start(f32[8,160]{1,0:T(8,128)S(1)} %get-tuple-element.18), channel_id=1, source_target_pairs={{1,0},{2,1},{3,2},{5,4},{6,5},{7,6},{9,8},{10,9},{11,10},{13,12},{... | collective-permute-start | bytes 15368 | tf_op jit(solution)/shard_map/ppermute | solution.py:17
  26.1 0.2 all-to-all-done
  26.4 0.1 slice_reduce_fusion.3
  26.5 0.1 eq.128
  26.6 0.2 fusion.13
  26.8 0.1 slice_reduce_fusion.2
  26.8 0.0 copy-start.11
  26.8 0.1 collective-permute-start.4
  26.9 0.6 %copy-done.11 = s32[1,8,128]{2,1,0:T(8,128)S(1)} copy-done((s32[1,8,128]{2,1,0:T(8,128)S(1)}, s32[1,8,128]{2,1,0:T(8,128)}, u32[]{:S(2)}) %copy-start.11) | copy-done | bytes 4120
  27.5 0.6 %convert_bitcast_fusion.refs_12_ = f32[8,128]{1,0:T(8,128)} fusion(s32[1,8,128]{2,1,0:T(8,128)S(1)} %copy-done.11), kind=kLoop, calls=%fused_computation.34 | loop fusion | flops 1024 | bytes 8192 | tf_op jit(solution)/shard_map/convert_element_type | solution.py:153
  28.1 0.0 collective-permute-done.4
  28.1 0.7 %reshape_squeeze.11.refs_14_ = f32[8,8]{1,0:T(8,128)} reshape(f32[64]{0:T(128)S(1)} %slice_reduce_fusion.4) | data formatting | bytes 512 | tf_op jit(solution)/shard_map/reshape;squeeze | solution.py:244
  28.8 0.0 collective-permute-done.2.refs_3_.refs_7_
  28.8 1.6 %collective-permute-done.3.refs_4_.refs_8_ = f32[8,160]{1,0:T(8,128)S(1)} collective-permute-done((f32[8,160]{1,0:T(8,128)S(1)}, f32[8,160]{1,0:T(8,128)S(1)}, u32[]{:S(2)}, u32[]{:S(2)}) %collective-permute-start.3) | collective-permute-done | bytes 5152 | tf_op jit(solution)/shard_map/ppermute | solution.py:17
  30.4 0.0 collective-permute-done.refs_1_.refs_5_
  30.4 0.0 collective-permute-done.1.refs_2_.refs_6_
  30.4 0.6 %copy-done.5 = f32[8,160]{1,0:T(8,128)} copy-done((f32[8,160]{1,0:T(8,128)}, f32[8,160]{1,0:T(8,128)S(1)}, u32[]{:S(2)}) %copy-start.5) | copy-done | bytes 5144
  31.0 0.0 copy-done.2
  31.0 0.0 copy-done.3
  31.0 3.4 %shard_map.91 = (f32[4,32,8,128]{3,2,1,0:T(8,128)}, f32[128,128]{1,0:T(8,128)}, f32[128,128]{1,0:T(8,128)}, f32[8,128]{1,0:T(8,128)}, f32[8,128]{1,0:T(8,128)}) custom-call(f32[4,32,8,128]{3,2,1,0:T(8,128)} %bitcast.68, f32[160,128]{1,0:T(8,128)} %copy-done.2, f32[160,128]{1,0:T(8,128)} %copy-done.3, f32[8,160]{1,0:T(8,128)} %copy-done.4, ...), custom_call_target="tpu_custom_call" | custom-call | tf_op jit(solution)/shard_map/pallas_call | solution.py:132
  34.4 4.7 %collective-permute-start.5 = (f32[128,128]{1,0:T(8,128)}, f32[128,128]{1,0:T(8,128)S(1)}, u32[]{:S(2)}, u32[]{:S(2)}) collective-permute-start(f32[128,128]{1,0:T(8,128)} %get-tuple-element.21), channel_id=1, source_target_pairs={{0,4},{4,8},{8,12},{1,5},{5,9},{9,13},{2,6},{6,10},{10,14},{3,7},{... | collective-permute-start | bytes 196616 | tf_op jit(solution)/shard_map/ppermute | solution.py:17
  39.1 1.3 %collective-permute-start.6 = (f32[128,128]{1,0:T(8,128)}, f32[128,128]{1,0:T(8,128)S(1)}, u32[]{:S(2)}, u32[]{:S(2)}) collective-permute-start(f32[128,128]{1,0:T(8,128)} %get-tuple-element.22), channel_id=1, source_target_pairs={{4,0},{8,4},{12,8},{5,1},{9,5},{13,9},{6,2},{10,6},{14,10},{7,3},{... | collective-permute-start | bytes 196616 | tf_op jit(solution)/shard_map/ppermute | solution.py:17
  40.4 4.3 %collective-permute-start.7 = (f32[8,128]{1,0:T(8,128)}, f32[8,128]{1,0:T(8,128)S(1)}, u32[]{:S(2)}, u32[]{:S(2)}) collective-permute-start(f32[8,128]{1,0:T(8,128)} %get-tuple-element.23), channel_id=1, source_target_pairs={{0,1},{1,2},{2,3},{4,5},{5,6},{6,7},{8,9},{9,10},{10,11},{12,13},{... | collective-permute-start | bytes 12296 | tf_op jit(solution)/shard_map/ppermute | solution.py:17
  44.7 1.3 %collective-permute-start.8 = (f32[8,128]{1,0:T(8,128)S(1)}, f32[8,128]{1,0:T(8,128)S(1)}, u32[]{:S(2)}, u32[]{:S(2)}) collective-permute-start(f32[8,128]{1,0:T(8,128)S(1)} %copy-done.15), channel_id=1, source_target_pairs={{1,0},{2,1},{3,2},{5,4},{6,5},{7,6},{9,8},{10,9},{11,10},{13,12},{... | collective-permute-start | bytes 12296 | tf_op jit(solution)/shard_map/ppermute | solution.py:17
  46.0 0.2 collective-permute-done.7.refs_3_
  46.2 4.0 %collective-permute-done.8.refs_4_ = f32[8,128]{1,0:T(8,128)S(1)} collective-permute-done((f32[8,128]{1,0:T(8,128)S(1)}, f32[8,128]{1,0:T(8,128)S(1)}, u32[]{:S(2)}, u32[]{:S(2)}) %collective-permute-start.8) | collective-permute-done | bytes 4128 | tf_op jit(solution)/shard_map/ppermute | solution.py:17
  50.2 0.0 collective-permute-done.5.refs_1_
  50.2 0.0 collective-permute-done.6.refs_2_
  50.2 0.6 %copy-done.10 = f32[8,128]{1,0:T(8,128)} copy-done((f32[8,128]{1,0:T(8,128)}, f32[8,128]{1,0:T(8,128)S(1)}, u32[]{:S(2)}) %copy-start.10) | copy-done | bytes 4120
  50.8 0.0 copy-done.6
  50.8 0.0 copy-done.7
  50.9 3.1 %shard_map.92 = f32[4,32,8,128]{3,2,1,0:T(8,128)} custom-call(f32[4,32,8,128]{3,2,1,0:T(8,128)} %get-tuple-element.20.refs_0_, f32[128,128]{1,0:T(8,128)} %copy-done.6, f32[128,128]{1,0:T(8,128)} %copy-done.7, f32[8,128]{1,0:T(8,128)} %copy-done.9, f32[8,128]{1,0:T(8,128)} %copy-done.10, f32[160,128]{1,0:T(8,128)} %copy-done.2, f32[160,128]{1,0:T(8,128)} %copy-done.3, ...), custom_call_target="tpu_custom_call" | custom-call | tf_op jit(solution)/shard_map/pallas_call | solution.py:132
  (42 shorter events, 0.4 us)
Async XLA Ops:
  0.0 0.7 %copy-start.12 = (s32[1,1,1,32]{3,2,1,0:T(1,128)S(1)}, s32[1,1,1,32]{3,2,1,0:T(1,128)}, u32[]{:S(2)}) copy-start(s32[1,1,1,32]{3,2,1,0:T(1,128)} %param.15) | copy-start | bytes 388
  1.6 0.7 %copy-start.14 = (s32[1,1,1,32,1]{3,4,2,1,0:T(1,128)S(1)}, s32[1,1,1,32,1]{3,4,2,1,0:T(1,128)}, u32[]{:S(2)}) copy-start(s32[1,1,1,32,1]{3,4,2,1,0:T(1,128)} %param.14) | copy-start | bytes 388
  1.7 0.8 %copy-start.13 = (s32[1,1,1,32]{3,2,1,0:T(1,128)S(1)}, s32[1,1,1,32]{3,2,1,0:T(1,128)}, u32[]{:S(2)}) copy-start(s32[1,1,1,32]{3,2,1,0:T(1,128)} %param.16) | copy-start | bytes 388
  1.7 1.5 %copy-start = (f32[1,4,32,8,128]{4,3,2,1,0:T(8,128)S(1)}, f32[1,4,32,8,128]{4,3,2,1,0:T(8,128)}, u32[]{:S(2)}) copy-start(f32[1,4,32,8,128]{4,3,2,1,0:T(8,128)} %param.9) | copy-start | bytes 1572868
  4.5 0.9 %copy-start.1 = (f32[1,32,8,128]{3,2,1,0:T(8,128)S(1)}, f32[1,32,8,128]{3,2,1,0:T(8,128)}, u32[]{:S(2)}) copy-start(f32[1,32,8,128]{3,2,1,0:T(8,128)} %param.11) | copy-start | bytes 393220
  8.0 18.3 %all-to-all-start = ((f32[16,7,512]{2,1,0:T(8,128)}), f32[16,7,512]{2,1,0:T(8,128)S(1)}, u32[]{:S(2)}, u32[]{:S(2)}) async-start(f32[16,7,512]{2,1,0:T(8,128)} %copy.54), calls=%async_computation | async-start | bytes 524288 | tf_op jit(solution)/shard_map/all_to_all | solution.py:224
  16.3 14.1 %collective-permute-start = (f32[160,128]{1,0:T(8,128)S(1)}, f32[160,128]{1,0:T(8,128)S(1)}, u32[]{:S(2)}, u32[]{:S(2)}) collective-permute-start(f32[160,128]{1,0:T(8,128)S(1)} %get-tuple-element.15), channel_id=1, source_target_pairs={{0,4},{4,8},{8,12},{1,5},{5,9},{9,13},{2,6},{6,10},{10,14},{3,7},{... | collective-permute-start | bytes 245768 | tf_op jit(solution)/shard_map/ppermute | solution.py:17
  20.2 10.2 %collective-permute-start.1 = (f32[160,128]{1,0:T(8,128)S(1)}, f32[160,128]{1,0:T(8,128)S(1)}, u32[]{:S(2)}, u32[]{:S(2)}) collective-permute-start(f32[160,128]{1,0:T(8,128)S(1)} %get-tuple-element.16), channel_id=1, source_target_pairs={{4,0},{8,4},{12,8},{5,1},{9,5},{13,9},{6,2},{10,6},{14,10},{7,3},{... | collective-permute-start | bytes 245768 | tf_op jit(solution)/shard_map/ppermute | solution.py:17
  21.5 7.4 %collective-permute-start.2 = (f32[8,160]{1,0:T(8,128)S(1)}, f32[8,160]{1,0:T(8,128)S(1)}, u32[]{:S(2)}, u32[]{:S(2)}) collective-permute-start(f32[8,160]{1,0:T(8,128)S(1)} %get-tuple-element.17), channel_id=1, source_target_pairs={{0,1},{1,2},{2,3},{4,5},{5,6},{6,7},{8,9},{9,10},{10,11},{12,13},{... | collective-permute-start | bytes 15368 | tf_op jit(solution)/shard_map/ppermute | solution.py:17
  24.8 5.5 %collective-permute-start.3 = (f32[8,160]{1,0:T(8,128)S(1)}, f32[8,160]{1,0:T(8,128)S(1)}, u32[]{:S(2)}, u32[]{:S(2)}) collective-permute-start(f32[8,160]{1,0:T(8,128)S(1)} %get-tuple-element.18), channel_id=1, source_target_pairs={{1,0},{2,1},{3,2},{5,4},{6,5},{7,6},{9,8},{10,9},{11,10},{13,12},{... | collective-permute-start | bytes 15368 | tf_op jit(solution)/shard_map/ppermute | solution.py:17
  26.8 0.7 %copy-start.11 = (s32[1,8,128]{2,1,0:T(8,128)S(1)}, s32[1,8,128]{2,1,0:T(8,128)}, u32[]{:S(2)}) copy-start(s32[1,8,128]{2,1,0:T(8,128)} %param.13) | copy-start | bytes 12292
  26.8 1.3 %collective-permute-start.4 = (f32[11,512]{1,0:T(8,128)S(1)}, f32[11,512]{1,0:T(8,128)S(1)}, u32[]{:S(2)}, u32[]{:S(2)}) collective-permute-start(f32[11,512]{1,0:T(8,128)S(1)} %pad_maximum_fusion.3), channel_id=1, source_target_pairs={{0,16},{16,0},{1,17},{17,1},{2,18},{18,2},{3,19},{19,3},{4,20},{20... | collective-permute-start | bytes 67592 | tf_op jit(solution)/shard_map/ppermute | solution.py:243
  28.1 2.3 %copy-start.8 = (f32[11,512]{1,0:T(8,128)}, f32[11,512]{1,0:T(8,128)S(1)}, u32[]{:S(2)}) copy-start(f32[11,512]{1,0:T(8,128)S(1)} %collective-permute-done.4) | copy-start | bytes 67588
  28.8 1.6 %copy-start.4 = (f32[8,160]{1,0:T(8,128)}, f32[8,160]{1,0:T(8,128)S(1)}, u32[]{:S(2)}) copy-start(f32[8,160]{1,0:T(8,128)S(1)} %collective-permute-done.2.refs_3_.refs_7_) | copy-start | bytes 15364
  30.4 0.6 %copy-start.5 = (f32[8,160]{1,0:T(8,128)}, f32[8,160]{1,0:T(8,128)S(1)}, u32[]{:S(2)}) copy-start(f32[8,160]{1,0:T(8,128)S(1)} %collective-permute-done.3.refs_4_.refs_8_) | copy-start | bytes 15364
  30.4 0.6 %copy-start.2 = (f32[160,128]{1,0:T(8,128)}, f32[160,128]{1,0:T(8,128)S(1)}, u32[]{:S(2)}) copy-start(f32[160,128]{1,0:T(8,128)S(1)} %collective-permute-done.refs_1_.refs_5_) | copy-start | bytes 245764
  30.4 0.7 %copy-start.3 = (f32[160,128]{1,0:T(8,128)}, f32[160,128]{1,0:T(8,128)S(1)}, u32[]{:S(2)}) copy-start(f32[160,128]{1,0:T(8,128)S(1)} %collective-permute-done.1.refs_2_.refs_6_) | copy-start | bytes 245764
  34.4 10.3 %copy-start.15 = (f32[8,128]{1,0:T(8,128)S(1)}, f32[8,128]{1,0:T(8,128)}, u32[]{:S(2)}) copy-start(f32[8,128]{1,0:T(8,128)} %get-tuple-element.24) | copy-start | bytes 12292
  34.4 15.8 %collective-permute-start.5 = (f32[128,128]{1,0:T(8,128)}, f32[128,128]{1,0:T(8,128)S(1)}, u32[]{:S(2)}, u32[]{:S(2)}) collective-permute-start(f32[128,128]{1,0:T(8,128)} %get-tuple-element.21), channel_id=1, source_target_pairs={{0,4},{4,8},{8,12},{1,5},{5,9},{9,13},{2,6},{6,10},{10,14},{3,7},{... | collective-permute-start | bytes 196616 | tf_op jit(solution)/shard_map/ppermute | solution.py:17
  39.1 11.1 %collective-permute-start.6 = (f32[128,128]{1,0:T(8,128)}, f32[128,128]{1,0:T(8,128)S(1)}, u32[]{:S(2)}, u32[]{:S(2)}) collective-permute-start(f32[128,128]{1,0:T(8,128)} %get-tuple-element.22), channel_id=1, source_target_pairs={{4,0},{8,4},{12,8},{5,1},{9,5},{13,9},{6,2},{10,6},{14,10},{7,3},{... | collective-permute-start | bytes 196616 | tf_op jit(solution)/shard_map/ppermute | solution.py:17
  40.4 5.8 %collective-permute-start.7 = (f32[8,128]{1,0:T(8,128)}, f32[8,128]{1,0:T(8,128)S(1)}, u32[]{:S(2)}, u32[]{:S(2)}) collective-permute-start(f32[8,128]{1,0:T(8,128)} %get-tuple-element.23), channel_id=1, source_target_pairs={{0,1},{1,2},{2,3},{4,5},{5,6},{6,7},{8,9},{9,10},{10,11},{12,13},{... | collective-permute-start | bytes 12296 | tf_op jit(solution)/shard_map/ppermute | solution.py:17
  44.7 5.5 %collective-permute-start.8 = (f32[8,128]{1,0:T(8,128)S(1)}, f32[8,128]{1,0:T(8,128)S(1)}, u32[]{:S(2)}, u32[]{:S(2)}) collective-permute-start(f32[8,128]{1,0:T(8,128)S(1)} %copy-done.15), channel_id=1, source_target_pairs={{1,0},{2,1},{3,2},{5,4},{6,5},{7,6},{9,8},{10,9},{11,10},{13,12},{... | collective-permute-start | bytes 12296 | tf_op jit(solution)/shard_map/ppermute | solution.py:17
  46.2 4.0 %copy-start.9 = (f32[8,128]{1,0:T(8,128)}, f32[8,128]{1,0:T(8,128)S(1)}, u32[]{:S(2)}) copy-start(f32[8,128]{1,0:T(8,128)S(1)} %collective-permute-done.7.refs_3_) | copy-start | bytes 12292
  50.2 0.6 %copy-start.10 = (f32[8,128]{1,0:T(8,128)}, f32[8,128]{1,0:T(8,128)S(1)}, u32[]{:S(2)}) copy-start(f32[8,128]{1,0:T(8,128)S(1)} %collective-permute-done.8.refs_4_) | copy-start | bytes 12292
  50.2 0.6 %copy-start.6 = (f32[128,128]{1,0:T(8,128)}, f32[128,128]{1,0:T(8,128)S(1)}, u32[]{:S(2)}) copy-start(f32[128,128]{1,0:T(8,128)S(1)} %collective-permute-done.5.refs_1_) | copy-start | bytes 196612
  50.2 0.7 %copy-start.7 = (f32[128,128]{1,0:T(8,128)}, f32[128,128]{1,0:T(8,128)S(1)}, u32[]{:S(2)}) copy-start(f32[128,128]{1,0:T(8,128)S(1)} %collective-permute-done.6.refs_2_) | copy-start | bytes 196612

commit v8 on v7

--- a/solution.py
+++ b/solution.py
@@ -15,6 +15,20 @@
     count = lax.axis_size(axis)
     route = [(i, i + step) for i in range(count) if 0 <= i + step < count]
     return lax.ppermute(block, axis, route)
+
+
+def both_ways(last, first, axis):
+    count = lax.axis_size(axis)
+    here = lax.axis_index(axis)
+    target = lax.broadcasted_iota(jnp.int32, (count,) + (1,) * last.ndim, 0)
+    send = jnp.where(target == here + 1, last[None], jnp.where(target == here - 1, first[None], 0.0))
+    got = lax.all_to_all(send, axis, split_axis=0, concat_axis=0, tiled=True)
+    before = lax.dynamic_index_in_dim(got, jnp.maximum(here - 1, 0), 0, keepdims=False)
+    after = lax.dynamic_index_in_dim(got, jnp.minimum(here + 1, count - 1), 0, keepdims=False)
+    return (
+        jnp.where(here > 0, before, 0.0),
+        jnp.where(here < count - 1, after, 0.0),
+    )
 
 
 def step_kernel(fields, levels, rows, cols, coupled, emit):
@@ -247,12 +261,7 @@
     middle, last_rows, first_rows, last_cols, first_cols = run_step(
         adjoint, halos, halos, east, north, coeffs, wet, inc=inc, emit=True
     )
-    step_halos = (
-        shift(last_rows, "gx", 1),
-        shift(first_rows, "gx", -1),
-        shift(last_cols, "gy", 1),
-        shift(first_cols, "gy", -1),
-    )
+    step_halos = both_ways(last_rows, first_rows, "gx") + both_ways(last_cols, first_cols, "gy")
     (result,) = run_step(middle, step_halos, halos, east, north, coeffs, wet)
     return result[None]
 

time: 54.6 us -> 63.1 us (1.16)
  waiting for transfers between devices: 5.93 us -> 12.1 us
  other arithmetic: 1.1 us -> 5.4 us
  starting transfers between devices: 29.7 us -> 28.3 us
    ppermute x8 -> x4, starting transfers between devices: 21.3 us -> 9.78 us  [shift(): return lax.ppermute(block, axis, route)]
    all_to_all x0 -> x2, waiting for transfers between devices: none -> 10.4 us  [both_ways(): got = lax.all_to_all(send, axis, split_axis=0, concat_axis=0, tiled=True)]
    all_to_all x0 -> x2, starting transfers between devices: none -> 10.1 us  [both_ways(): got = lax.all_to_all(send, axis, split_axis=0, concat_axis=0, tiled=True)]
    ppermute x8 -> x4, waiting for transfers between devices: 5.77 us -> 0.44 us  [shift(): return lax.ppermute(block, axis, route)]
    select_n x0 -> x4, other arithmetic: none -> 4.29 us  [the longest x2 3.02 us: both_ways(): jnp.where(target == here + 1, last[None], jnp.where(target == here - 1, f...]
    ppermute x1, waiting for transfers between devices: 0.01 us -> 1.18 us  [shards(): lax.ppermute(packed, 'comp', [(c, sections - 1 - c) for c in range(sectio...]
    unnamed x32 -> x24, local copies, waits for them, and re-layouts: 3.68 us -> 3.11 us
  transfers between devices with their start and end apart: 10 -> 8, of which waited for: 4 -> 4; matrix products, arithmetic and copies ran while one was open for 3% -> 7% of each run, Pallas kernels for 0% -> 0%
where the time goes in v8:
time: 63.1 us; the launch traced here: 62.4 us
  starting transfers between devices  28.3 us (45%)
  waiting for transfers between devices  12.1 us (19%)
  local copies, waits for them, and re-layouts  8.06 us (13%)
  Pallas kernels  6.52 us (10%)
  other arithmetic  5.4 us (9%)
  matrix products  1.71 us (3%)
    all_to_all x2, waiting for transfers between devices, both_ways(): got = lax.all_to_all(send, axis, split_axis=0, concat_axis=0, tiled=True)  10.4 us
    all_to_all x2, starting transfers between devices, both_ways(): got = lax.all_to_all(send, axis, split_axis=0, concat_axis=0, tiled=True)  10.1 us
    ppermute x4, starting transfers between devices, shift(): return lax.ppermute(block, axis, route)  9.78 us
    all_to_all x1, starting transfers between devices, shards(): lax.all_to_all(send_data, ('gx', 'gy'), split_axis=0, concat_axis=0, tile...  8.34 us
    pallas_call x2, Pallas kernels, run_step(): pl.pallas_call(step_kernel(fields, levels, rows, cols, coupled, emit), ou...  6.52 us
    unnamed x24, local copies, waits for them, and re-layouts  3.11 us
    select_n x2, other arithmetic, both_ways(): jnp.where(target == here + 1, last[None], jnp.where(target == here - 1, f...  3.02 us
    select_n x2, other arithmetic, both_ways(): jnp.where(here < count - 1, after, 0.0)  1.27 us
  transfers between devices with their start and end apart: 8, of which 4 were waited for; matrix products, arithmetic and copies ran while one was open for 7% of the time, Pallas kernels for 0%

profile of v8, /device:TPU:0, one launch (start us, length us, event | category | flops | bytes accessed | tf_op | source)
XLA Modules:
  0.0 62.4 jit_solution(224311288304205641)
XLA Ops:
  0.0 0.7 %copy-done.9 = s32[1,1,1,32]{3,2,1,0:T(1,128)S(1)} copy-done((s32[1,1,1,32]{3,2,1,0:T(1,128)S(1)}, s32[1,1,1,32]{3,2,1,0:T(1,128)}, u32[]{:S(2)}) %copy-start.9) | copy-done | bytes 152
  0.7 1.0 %convolution_multiply_fusion = f32[32,4,128]{2,0,1:T(8,128)S(1)} fusion(f32[32,128]{1,0:T(8,128)} %bitcast.97, f32[4,32,8,128]{3,2,1,0:T(8,128)} %bitcast.75, s32[32]{0:T(128)S(1)} %bitcast.100), kind=kOutput, calls=%fused_computation | convolution fusion | flops 1589504 | bytes 98432 | tf_op jit(solution)/shard_map/dot_general | solution.py:187
  1.6 0.0 copy-start.11
  1.7 0.0 copy-start.10
  1.7 0.0 copy-start
  1.7 0.6 copy-done.11
  2.3 0.2 convert_reduce_fusion
  2.5 0.0 copy-done.10
  2.5 0.3 fusion
  2.8 0.3 slice_reduce_fusion.1
  3.2 0.0 copy-done
  3.2 0.2 fusion.18
  3.4 0.1 fusion.19
  3.6 0.1 copy.47
  3.6 0.1 reshape.149
  3.7 0.1 select_reduce_fusion
  3.8 0.1 convert_element_type.31
  3.9 0.1 select_maximum_fusion.1
  4.2 0.3 copy.48
  4.4 0.1 reshape.151
  4.5 0.3 copy.51
  4.8 0.1 reshape.152
  4.9 0.5 copy-done.1
  5.4 0.1 fusion.21
  5.5 0.1 copy.50
  5.7 0.1 copy.53
  5.8 1.0 %fusion.22 = (f32[32,1,128]{2,1,0:T(1,128)S(1)}, f32[32,1,128]{2,1,0:T(1,128)S(1)}) fusion(f32[32,8,128]{2,1,0:T(8,128)} %bitcast.84), kind=kLoop, calls=%fused_computation.62 | loop fusion | bytes 65536 | tf_op jit(solution)/shard_map/slice | solution.py:171
  6.8 0.3 fusion.6
  7.1 0.8 %copy.54 = f32[16,7,512]{2,1,0:T(8,128)} copy(f32[16,7,512]{2,0,1:T(8,128)S(1)} %pad_maximum_fusion) | data formatting | bytes 458752 | tf_op jit(solution)/shard_map/optimization_barrier | solution.py:235
  8.0 8.3 %all-to-all-start = ((f32[16,7,512]{2,1,0:T(8,128)}), f32[16,7,512]{2,1,0:T(8,128)S(1)}, u32[]{:S(2)}, u32[]{:S(2)}) async-start(f32[16,7,512]{2,1,0:T(8,128)} %copy.54), calls=%async_computation | async-start | bytes 524288 | tf_op jit(solution)/shard_map/all_to_all | solution.py:238
  16.3 3.8 %collective-permute-start = (f32[160,128]{1,0:T(8,128)S(1)}, f32[160,128]{1,0:T(8,128)S(1)}, u32[]{:S(2)}, u32[]{:S(2)}) collective-permute-start(f32[160,128]{1,0:T(8,128)S(1)} %get-tuple-element.15), channel_id=1, source_target_pairs={{0,4},{4,8},{8,12},{1,5},{5,9},{9,13},{2,6},{6,10},{10,14},{3,7},{... | collective-permute-start | bytes 245768 | tf_op jit(solution)/shard_map/ppermute | solution.py:17
  20.2 1.3 %collective-permute-start.1 = (f32[160,128]{1,0:T(8,128)S(1)}, f32[160,128]{1,0:T(8,128)S(1)}, u32[]{:S(2)}, u32[]{:S(2)}) collective-permute-start(f32[160,128]{1,0:T(8,128)S(1)} %get-tuple-element.16), channel_id=1, source_target_pairs={{4,0},{8,4},{12,8},{5,1},{9,5},{13,9},{6,2},{10,6},{14,10},{7,3},{... | collective-permute-start | bytes 245768 | tf_op jit(solution)/shard_map/ppermute | solution.py:17
  21.5 3.4 %collective-permute-start.2 = (f32[8,160]{1,0:T(8,128)S(1)}, f32[8,160]{1,0:T(8,128)S(1)}, u32[]{:S(2)}, u32[]{:S(2)}) collective-permute-start(f32[8,160]{1,0:T(8,128)S(1)} %get-tuple-element.17), channel_id=1, source_target_pairs={{0,1},{1,2},{2,3},{4,5},{5,6},{6,7},{8,9},{9,10},{10,11},{12,13},{... | collective-permute-start | bytes 15368 | tf_op jit(solution)/shard_map/ppermute | solution.py:17
  24.8 1.3 %collective-permute-start.3 = (f32[8,160]{1,0:T(8,128)S(1)}, f32[8,160]{1,0:T(8,128)S(1)}, u32[]{:S(2)}, u32[]{:S(2)}) collective-permute-start(f32[8,160]{1,0:T(8,128)S(1)} %get-tuple-element.18), channel_id=1, source_target_pairs={{1,0},{2,1},{3,2},{5,4},{6,5},{7,6},{9,8},{10,9},{11,10},{13,12},{... | collective-permute-start | bytes 15368 | tf_op jit(solution)/shard_map/ppermute | solution.py:17
  26.1 0.0 copy-start.8
  26.2 0.7 %copy-done.8 = s32[1,8,128]{2,1,0:T(8,128)S(1)} copy-done((s32[1,8,128]{2,1,0:T(8,128)S(1)}, s32[1,8,128]{2,1,0:T(8,128)}, u32[]{:S(2)}) %copy-start.8) | copy-done | bytes 4120
  26.8 0.6 convert_bitcast_fusion.refs_12_
  27.4 0.0 all-to-all-done
  27.5 0.1 slice_reduce_fusion.3
  27.6 0.1 eq.172
  27.7 0.2 fusion.13
  27.9 0.1 slice_reduce_fusion.2
  28.0 0.1 collective-permute-start.4
  28.1 1.2 %collective-permute-done.4 = f32[11,512]{1,0:T(8,128)S(1)} collective-permute-done((f32[11,512]{1,0:T(8,128)S(1)}, f32[11,512]{1,0:T(8,128)S(1)}, u32[]{:S(2)}, u32[]{:S(2)}) %collective-permute-start.4) | collective-permute-done | bytes 22560 | tf_op jit(solution)/shard_map/ppermute | solution.py:257
  29.3 0.7 %reshape_squeeze.11.refs_14_ = f32[8,8]{1,0:T(8,128)} reshape(f32[64]{0:T(128)S(1)} %slice_reduce_fusion.4) | data formatting | bytes 512 | tf_op jit(solution)/shard_map/reshape;squeeze | solution.py:258
  29.9 0.0 collective-permute-done.2.refs_3_.refs_7_
  29.9 0.4 collective-permute-done.3.refs_4_.refs_8_
  30.4 0.0 collective-permute-done.refs_1_.refs_5_
  30.4 0.0 collective-permute-done.1.refs_2_.refs_6_
  30.4 0.0 copy-start.3
  30.4 0.1 copy-done.4
  30.5 0.4 copy-done.5
  31.0 0.0 copy-done.2
  31.0 0.0 copy-done.3
  31.0 3.4 %shard_map.91 = (f32[4,32,8,128]{3,2,1,0:T(8,128)}, f32[128,128]{1,0:T(8,128)}, f32[128,128]{1,0:T(8,128)}, f32[8,128]{1,0:T(8,128)}, f32[8,128]{1,0:T(8,128)}) custom-call(f32[4,32,8,128]{3,2,1,0:T(8,128)} %bitcast.76, f32[160,128]{1,0:T(8,128)} %copy-done.2, f32[160,128]{1,0:T(8,128)} %copy-done.3, f32[8,160]{1,0:T(8,128)} %copy-done.4, ...), custom_call_target="tpu_custom_call" | custom-call | tf_op jit(solution)/shard_map/pallas_call | solution.py:146
  34.4 1.4 %select_select_fusion.1 = f32[4,8,128]{2,1,0:T(8,128)} fusion(f32[8,128]{1,0:T(8,128)} %get-tuple-element.24, f32[8,128]{1,0:T(8,128)} %get-tuple-element.23, pred[4]{0:T(512)(128)(4,1)S(1)} %get-tuple-element.50, pred[4]{0:T(512)(128)(4,1)S(1)} %get-tuple-element.51), kind=kLoop, calls=%fused_computation.26 | loop fusion | flops 8192 | bytes 24584 | tf_op jit(solution)/shard_map/jit(_where)/select_n | solution.py:24
  35.8 4.4 %all-to-all-start.2 = ((f32[4,8,128]{2,1,0:T(8,128)}), f32[4,8,128]{2,1,0:T(8,128)S(1)}, u32[]{:S(2)}, u32[]{:S(2)}) async-start(f32[4,8,128]{2,1,0:T(8,128)} %select_select_fusion.1), calls=%async_computation.2 | async-start | bytes 32768 | tf_op jit(solution)/shard_map/all_to_all | solution.py:25
  40.2 1.6 %select_select_fusion = f32[4,128,128]{2,1,0:T(8,128)} fusion(f32[128,128]{1,0:T(8,128)} %get-tuple-element.22, f32[128,128]{1,0:T(8,128)S(1)} %copy-done.6, pred[4]{0:T(512)(128)(4,1)S(1)} %get-tuple-element.48, pred[4]{0:T(512)(128)(4,1)S(1)} %get-tuple-element.49), kind=kLoop, calls=%fused_computation.1 | loop fusion | flops 131072 | bytes 393224 | tf_op jit(solution)/shard_map/jit(_where)/select_n | solution.py:24
  41.9 3.1 %all-to-all-done.2 = f32[4,8,128]{2,1,0:T(8,128)S(1)} async-done(((f32[4,8,128]{2,1,0:T(8,128)}), f32[4,8,128]{2,1,0:T(8,128)S(1)}, u32[]{:S(2)}, u32[]{:S(2)}) %all-to-all-start.2) | async-done | bytes 16416 | tf_op jit(solution)/shard_map/all_to_all | solution.py:25
  44.9 5.7 %all-to-all-start.1 = ((f32[4,128,128]{2,1,0:T(8,128)}), f32[4,128,128]{2,1,0:T(8,128)S(1)}, u32[]{:S(2)}, u32[]{:S(2)}) async-start(f32[4,128,128]{2,1,0:T(8,128)} %select_select_fusion), calls=%async_computation.1 | async-start | bytes 524288 | tf_op jit(solution)/shard_map/all_to_all | solution.py:25
  50.6 0.6 select_bitcast_fusion.2
  51.2 7.4 %all-to-all-done.1 = f32[4,128,128]{2,1,0:T(8,128)S(1)} async-done(((f32[4,128,128]{2,1,0:T(8,128)}), f32[4,128,128]{2,1,0:T(8,128)S(1)}, u32[]{:S(2)}, u32[]{:S(2)}) %all-to-all-start.1) | async-done | bytes 262176 | tf_op jit(solution)/shard_map/all_to_all | solution.py:25
  58.6 0.7 %select_bitcast_fusion = (f32[128,128]{1,0:T(8,128)}, f32[128,128]{1,0:T(8,128)}) fusion(f32[4,128,128]{2,1,0:T(8,128)S(1)} %all-to-all-done.1, s32[]{:T(128)S(6)} %select_n.68, pred[]{:T(512)S(6)} %lt.32, s32[]{:T(128)S(6)} %max.6, pred[]{:T(512)S(6)} %gt.6), kind=kLoop, calls=%fused_computation.14 | loop fusion | flops 32768 | bytes 262154 | tf_op jit(solution)/shard_map/jit(_where)/select_n | solution.py:30
  59.3 3.1 %shard_map.92 = f32[4,32,8,128]{3,2,1,0:T(8,128)} custom-call(f32[4,32,8,128]{3,2,1,0:T(8,128)} %get-tuple-element.20.refs_0_, f32[128,128]{1,0:T(8,128)} %get-tuple-element.32.refs_1_, f32[128,128]{1,0:T(8,128)} %get-tuple-element.31.refs_2_, f32[8,128]{1,0:T(8,128)} %get-tuple-element.40.refs_3_, f32[8,128]{1,0:T(8,128)} %get-tuple-element.39.refs_4_, ...), custom_call_target="tpu_custom_call" | custom-call | tf_op jit(solution)/shard_map/pallas_call | solution.py:146
  (36 shorter events, 0.4 us)
Async XLA Ops:
  0.0 0.7 %copy-start.9 = (s32[1,1,1,32]{3,2,1,0:T(1,128)S(1)}, s32[1,1,1,32]{3,2,1,0:T(1,128)}, u32[]{:S(2)}) copy-start(s32[1,1,1,32]{3,2,1,0:T(1,128)} %param.15) | copy-start | bytes 388
  1.6 0.7 %copy-start.11 = (s32[1,1,1,32,1]{3,4,2,1,0:T(1,128)S(1)}, s32[1,1,1,32,1]{3,4,2,1,0:T(1,128)}, u32[]{:S(2)}) copy-start(s32[1,1,1,32,1]{3,4,2,1,0:T(1,128)} %param.14) | copy-start | bytes 388
  1.7 0.8 %copy-start.10 = (s32[1,1,1,32]{3,2,1,0:T(1,128)S(1)}, s32[1,1,1,32]{3,2,1,0:T(1,128)}, u32[]{:S(2)}) copy-start(s32[1,1,1,32]{3,2,1,0:T(1,128)} %param.16) | copy-start | bytes 388
  1.7 1.5 %copy-start = (f32[1,4,32,8,128]{4,3,2,1,0:T(8,128)S(1)}, f32[1,4,32,8,128]{4,3,2,1,0:T(8,128)}, u32[]{:S(2)}) copy-start(f32[1,4,32,8,128]{4,3,2,1,0:T(8,128)} %param.9) | copy-start | bytes 1572868
  4.5 0.9 %copy-start.1 = (f32[1,32,8,128]{3,2,1,0:T(8,128)S(1)}, f32[1,32,8,128]{3,2,1,0:T(8,128)}, u32[]{:S(2)}) copy-start(f32[1,32,8,128]{3,2,1,0:T(8,128)} %param.11) | copy-start | bytes 393220
  8.0 19.5 %all-to-all-start = ((f32[16,7,512]{2,1,0:T(8,128)}), f32[16,7,512]{2,1,0:T(8,128)S(1)}, u32[]{:S(2)}, u32[]{:S(2)}) async-start(f32[16,7,512]{2,1,0:T(8,128)} %copy.54), calls=%async_computation | async-start | bytes 524288 | tf_op jit(solution)/shard_map/all_to_all | solution.py:238
  16.3 14.1 %collective-permute-start = (f32[160,128]{1,0:T(8,128)S(1)}, f32[160,128]{1,0:T(8,128)S(1)}, u32[]{:S(2)}, u32[]{:S(2)}) collective-permute-start(f32[160,128]{1,0:T(8,128)S(1)} %get-tuple-element.15), channel_id=1, source_target_pairs={{0,4},{4,8},{8,12},{1,5},{5,9},{9,13},{2,6},{6,10},{10,14},{3,7},{... | collective-permute-start | bytes 245768 | tf_op jit(solution)/shard_map/ppermute | solution.py:17
  20.2 10.2 %collective-permute-start.1 = (f32[160,128]{1,0:T(8,128)S(1)}, f32[160,128]{1,0:T(8,128)S(1)}, u32[]{:S(2)}, u32[]{:S(2)}) collective-permute-start(f32[160,128]{1,0:T(8,128)S(1)} %get-tuple-element.16), channel_id=1, source_target_pairs={{4,0},{8,4},{12,8},{5,1},{9,5},{13,9},{6,2},{10,6},{14,10},{7,3},{... | collective-permute-start | bytes 245768 | tf_op jit(solution)/shard_map/ppermute | solution.py:17
  21.5 8.5 %collective-permute-start.2 = (f32[8,160]{1,0:T(8,128)S(1)}, f32[8,160]{1,0:T(8,128)S(1)}, u32[]{:S(2)}, u32[]{:S(2)}) collective-permute-start(f32[8,160]{1,0:T(8,128)S(1)} %get-tuple-element.17), channel_id=1, source_target_pairs={{0,1},{1,2},{2,3},{4,5},{5,6},{6,7},{8,9},{9,10},{10,11},{12,13},{... | collective-permute-start | bytes 15368 | tf_op jit(solution)/shard_map/ppermute | solution.py:17
  24.8 5.5 %collective-permute-start.3 = (f32[8,160]{1,0:T(8,128)S(1)}, f32[8,160]{1,0:T(8,128)S(1)}, u32[]{:S(2)}, u32[]{:S(2)}) collective-permute-start(f32[8,160]{1,0:T(8,128)S(1)} %get-tuple-element.18), channel_id=1, source_target_pairs={{1,0},{2,1},{3,2},{5,4},{6,5},{7,6},{9,8},{10,9},{11,10},{13,12},{... | collective-permute-start | bytes 15368 | tf_op jit(solution)/shard_map/ppermute | solution.py:17
  26.1 0.7 %copy-start.8 = (s32[1,8,128]{2,1,0:T(8,128)S(1)}, s32[1,8,128]{2,1,0:T(8,128)}, u32[]{:S(2)}) copy-start(s32[1,8,128]{2,1,0:T(8,128)} %param.13) | copy-start | bytes 12292
  28.0 1.3 %collective-permute-start.4 = (f32[11,512]{1,0:T(8,128)S(1)}, f32[11,512]{1,0:T(8,128)S(1)}, u32[]{:S(2)}, u32[]{:S(2)}) collective-permute-start(f32[11,512]{1,0:T(8,128)S(1)} %pad_maximum_fusion.3), channel_id=1, source_target_pairs={{0,16},{16,0},{1,17},{17,1},{2,18},{18,2},{3,19},{19,3},{4,20},{20... | collective-permute-start | bytes 67592 | tf_op jit(solution)/shard_map/ppermute | solution.py:257
  29.2 1.2 %copy-start.7 = (f32[11,512]{1,0:T(8,128)}, f32[11,512]{1,0:T(8,128)S(1)}, u32[]{:S(2)}) copy-start(f32[11,512]{1,0:T(8,128)S(1)} %collective-permute-done.4) | copy-start | bytes 67588
  29.9 0.6 copy-start.4
  30.4 0.6 copy-start.5
  30.4 0.6 %copy-start.2 = (f32[160,128]{1,0:T(8,128)}, f32[160,128]{1,0:T(8,128)S(1)}, u32[]{:S(2)}) copy-start(f32[160,128]{1,0:T(8,128)S(1)} %collective-permute-done.refs_1_.refs_5_) | copy-start | bytes 245764
  30.4 0.7 %copy-start.3 = (f32[160,128]{1,0:T(8,128)}, f32[160,128]{1,0:T(8,128)S(1)}, u32[]{:S(2)}) copy-start(f32[160,128]{1,0:T(8,128)S(1)} %collective-permute-done.1.refs_2_.refs_6_) | copy-start | bytes 245764
  34.4 5.8 %copy-start.6 = (f32[128,128]{1,0:T(8,128)S(1)}, f32[128,128]{1,0:T(8,128)}, u32[]{:S(2)}) copy-start(f32[128,128]{1,0:T(8,128)} %get-tuple-element.21) | copy-start | bytes 196612
  35.8 9.1 %all-to-all-start.2 = ((f32[4,8,128]{2,1,0:T(8,128)}), f32[4,8,128]{2,1,0:T(8,128)S(1)}, u32[]{:S(2)}, u32[]{:S(2)}) async-start(f32[4,8,128]{2,1,0:T(8,128)} %select_select_fusion.1), calls=%async_computation.2 | async-start | bytes 32768 | tf_op jit(solution)/shard_map/all_to_all | solution.py:25
  44.9 13.7 %all-to-all-start.1 = ((f32[4,128,128]{2,1,0:T(8,128)}), f32[4,128,128]{2,1,0:T(8,128)S(1)}, u32[]{:S(2)}, u32[]{:S(2)}) async-start(f32[4,128,128]{2,1,0:T(8,128)} %select_select_fusion), calls=%async_computation.1 | async-start | bytes 524288 | tf_op jit(solution)/shard_map/all_to_all | solution.py:25

commit v9 on v7

--- a/solution.py
+++ b/solution.py
@@ -27,7 +27,6 @@
         refs = refs[13:]
         if coupled:
             inc_ref = refs.pop(0)
-            ic_ref = refs.pop(0)
         out_ref = refs.pop(0)
         if emit:
             eu_ref, ed_ref, el_ref, er_ref = refs[:4]
@@ -41,6 +40,14 @@
         right = col == cols - 1
         cprev = [None] * fields
         dprev = [None] * fields
+        if coupled:
+            side = jnp.broadcast_to(inc_ref[pl.ds(rows + 2, 1), :], (rows, fields * cols))
+            place = lax.broadcasted_iota(jnp.int32, (rows, fields * cols), 1)
+            owner = lax.broadcasted_iota(jnp.int32, (rows, fields * cols), 0) * (2 * fields)
+            inc_cols = [
+                jnp.sum(jnp.where(place == owner + c, side, 0.0), axis=1, keepdims=True)
+                for c in range(2 * fields)
+            ]
         for l in range(levels):
             ue = ue_ref[l]
             un = un_ref[l]
@@ -61,8 +68,8 @@
                     a = a + inc_ref[pl.ds(0, rows), lanes]
                     up = up + inc_ref[pl.ds(rows, 1), lanes]
                     dn = dn + inc_ref[pl.ds(rows + 1, 1), lanes]
-                    lf = lf + ic_ref[:, pl.ds(f, 1)]
-                    rt = rt + ic_ref[:, pl.ds(fields + f, 1)]
+                    lf = lf + inc_cols[f]
+                    rt = rt + inc_cols[fields + f]
                 a_im = jnp.where(top, up, pltpu.roll(a, 1, 0))
                 a_ip = jnp.where(bottom, dn, pltpu.roll(a, rows - 1, 0))
                 a_jm = jnp.where(left, lf, pltpu.roll(a, 1, 1))
@@ -241,8 +248,7 @@
     edges_sum = jnp.sum(got[:, CAP:], axis=0)
     packed = jnp.concatenate([increment, edges_sum], 0)
     packed = lax.ppermute(packed, "comp", [(c, sections - 1 - c) for c in range(sections)])
-    inc_cols = packed[rows_x + 2, :ring].reshape(rows_x, 2 * fields)
-    inc = (packed[: rows_x + 2], inc_cols)
+    inc = (packed,)
 
     middle, last_rows, first_rows, last_cols, first_cols = run_step(
         adjoint, halos, halos, east, north, coeffs, wet, inc=inc, emit=True

time: 54.6 us -> 54.6 us (level)
  waiting for transfers between devices: 5.93 us -> 6.63 us
  local copies, waits for them, and re-layouts: 8.63 us -> 7.94 us
    ppermute x8, waiting for transfers between devices: 5.77 us -> 6.48 us  [shift(): return lax.ppermute(block, axis, route)]
    another operation x1 -> x0, local copies, waits for them, and re-layouts: 0.67 us -> none  [shards(): inc_cols = packed[rows_x + 2, :ring].reshape(rows_x, 2 * fields)]
  transfers between devices with their start and end apart: 10 -> 10, of which waited for: 4 -> 4; matrix products, arithmetic and copies ran while one was open for 3% -> 2% of each run, Pallas kernels for 0% -> 0%
where the time goes in v9:
time: 54.6 us; the launch traced here: 54 us
  starting transfers between devices  29.7 us (54%)
  local copies, waits for them, and re-layouts  7.94 us (15%)
  waiting for transfers between devices  6.63 us (12%)
  Pallas kernels  6.53 us (12%)
  matrix products  1.71 us (3%)
  other arithmetic  1.09 us (2%)
    ppermute x8, starting transfers between devices, shift(): return lax.ppermute(block, axis, route)  21.3 us
    all_to_all x1, starting transfers between devices, shards(): lax.all_to_all(send_data, ('gx', 'gy'), split_axis=0, concat_axis=0, tile...  8.34 us
    pallas_call x2, Pallas kernels, run_step(): pl.pallas_call(step_kernel(fields, levels, rows, cols, coupled, emit), ou...  6.53 us
    ppermute x8, waiting for transfers between devices, shift(): return lax.ppermute(block, axis, route)  6.48 us
    unnamed x32, local copies, waits for them, and re-layouts  3.68 us
  transfers between devices with their start and end apart: 10, of which 4 were waited for; matrix products, arithmetic and copies ran while one was open for 2% of the time, Pallas kernels for 0%

profile of v9, /device:TPU:0, one launch (start us, length us, event | category | flops | bytes accessed | tf_op | source)
XLA Modules:
  0.0 54.0 jit_solution(13609663977464064214)
XLA Ops:
  0.0 0.7 %copy-done.12 = s32[1,1,1,32]{3,2,1,0:T(1,128)S(1)} copy-done((s32[1,1,1,32]{3,2,1,0:T(1,128)S(1)}, s32[1,1,1,32]{3,2,1,0:T(1,128)}, u32[]{:S(2)}) %copy-start.12) | copy-done | bytes 152
  0.7 1.0 %convolution_multiply_fusion = f32[32,4,128]{2,0,1:T(8,128)S(1)} fusion(f32[32,128]{1,0:T(8,128)} %bitcast.87, f32[4,32,8,128]{3,2,1,0:T(8,128)} %bitcast.66, s32[32]{0:T(128)S(1)} %bitcast.90), kind=kOutput, calls=%fused_computation | convolution fusion | flops 1589504 | bytes 98432 | tf_op jit(solution)/shard_map/dot_general | solution.py:180
  1.6 0.0 copy-start.14
  1.7 0.0 copy-start.13
  1.7 0.0 copy-start
  1.7 0.6 %copy-done.14 = s32[1,1,1,32,1]{3,4,2,1,0:T(1,128)S(1)} copy-done((s32[1,1,1,32,1]{3,4,2,1,0:T(1,128)S(1)}, s32[1,1,1,32,1]{3,4,2,1,0:T(1,128)}, u32[]{:S(2)}) %copy-start.14) | copy-done | bytes 152
  2.3 0.2 convert_reduce_fusion
  2.5 0.0 copy-done.13
  2.5 0.3 fusion
  2.8 0.3 slice_reduce_fusion.1
  3.2 0.2 fusion.18
  3.4 0.1 fusion.19
  3.6 0.1 copy.47
  3.6 0.1 reshape.113
  3.7 0.1 select_reduce_fusion
  3.8 0.1 convert_element_type.31
  3.9 0.1 select_maximum_fusion.1
  4.2 0.3 copy.48
  4.4 0.1 reshape.115
  4.5 0.3 copy.51
  4.8 0.1 reshape.116
  4.9 0.5 copy-done.1
  5.4 0.1 fusion.21
  5.5 0.1 copy.50
  5.7 0.1 copy.53
  5.8 1.0 %fusion.22 = (f32[32,1,128]{2,1,0:T(1,128)S(1)}, f32[32,1,128]{2,1,0:T(1,128)S(1)}) fusion(f32[32,8,128]{2,1,0:T(8,128)} %bitcast.75), kind=kLoop, calls=%fused_computation.51 | loop fusion | bytes 65536 | tf_op jit(solution)/shard_map/slice | solution.py:164
  6.8 0.3 fusion.6
  7.1 0.8 %copy.54 = f32[16,7,512]{2,1,0:T(8,128)} copy(f32[16,7,512]{2,0,1:T(8,128)S(1)} %pad_maximum_fusion) | data formatting | bytes 458752 | tf_op jit(solution)/shard_map/optimization_barrier | solution.py:228
  8.0 8.3 %all-to-all-start = ((f32[16,7,512]{2,1,0:T(8,128)}), f32[16,7,512]{2,1,0:T(8,128)S(1)}, u32[]{:S(2)}, u32[]{:S(2)}) async-start(f32[16,7,512]{2,1,0:T(8,128)} %copy.54), calls=%async_computation | async-start | bytes 524288 | tf_op jit(solution)/shard_map/all_to_all | solution.py:231
  16.3 3.8 %collective-permute-start = (f32[160,128]{1,0:T(8,128)S(1)}, f32[160,128]{1,0:T(8,128)S(1)}, u32[]{:S(2)}, u32[]{:S(2)}) collective-permute-start(f32[160,128]{1,0:T(8,128)S(1)} %get-tuple-element.15), channel_id=1, source_target_pairs={{0,4},{4,8},{8,12},{1,5},{5,9},{9,13},{2,6},{6,10},{10,14},{3,7},{... | collective-permute-start | bytes 245768 | tf_op jit(solution)/shard_map/ppermute | solution.py:17
  20.2 1.3 %collective-permute-start.1 = (f32[160,128]{1,0:T(8,128)S(1)}, f32[160,128]{1,0:T(8,128)S(1)}, u32[]{:S(2)}, u32[]{:S(2)}) collective-permute-start(f32[160,128]{1,0:T(8,128)S(1)} %get-tuple-element.16), channel_id=1, source_target_pairs={{4,0},{8,4},{12,8},{5,1},{9,5},{13,9},{6,2},{10,6},{14,10},{7,3},{... | collective-permute-start | bytes 245768 | tf_op jit(solution)/shard_map/ppermute | solution.py:17
  21.5 3.4 %collective-permute-start.2 = (f32[8,160]{1,0:T(8,128)S(1)}, f32[8,160]{1,0:T(8,128)S(1)}, u32[]{:S(2)}, u32[]{:S(2)}) collective-permute-start(f32[8,160]{1,0:T(8,128)S(1)} %get-tuple-element.17), channel_id=1, source_target_pairs={{0,1},{1,2},{2,3},{4,5},{5,6},{6,7},{8,9},{9,10},{10,11},{12,13},{... | collective-permute-start | bytes 15368 | tf_op jit(solution)/shard_map/ppermute | solution.py:17
  24.8 1.3 %collective-permute-start.3 = (f32[8,160]{1,0:T(8,128)S(1)}, f32[8,160]{1,0:T(8,128)S(1)}, u32[]{:S(2)}, u32[]{:S(2)}) collective-permute-start(f32[8,160]{1,0:T(8,128)S(1)} %get-tuple-element.18), channel_id=1, source_target_pairs={{1,0},{2,1},{3,2},{5,4},{6,5},{7,6},{9,8},{10,9},{11,10},{13,12},{... | collective-permute-start | bytes 15368 | tf_op jit(solution)/shard_map/ppermute | solution.py:17
  26.1 0.2 all-to-all-done
  26.4 0.1 slice_reduce_fusion.3
  26.5 0.1 eq.128
  26.6 0.2 fusion.13
  26.8 0.1 slice_reduce_fusion.2
  26.8 0.0 copy-start.11
  26.8 0.1 collective-permute-start.4
  26.9 0.6 %copy-done.11 = s32[1,8,128]{2,1,0:T(8,128)S(1)} copy-done((s32[1,8,128]{2,1,0:T(8,128)S(1)}, s32[1,8,128]{2,1,0:T(8,128)}, u32[]{:S(2)}) %copy-start.11) | copy-done | bytes 4120
  27.5 0.6 %convert_bitcast_fusion.refs_12_ = f32[8,128]{1,0:T(8,128)} fusion(s32[1,8,128]{2,1,0:T(8,128)S(1)} %copy-done.11), kind=kLoop, calls=%fused_computation.34 | loop fusion | flops 1024 | bytes 8192 | tf_op jit(solution)/shard_map/convert_element_type | solution.py:160
  28.1 0.0 collective-permute-done.2.refs_3_.refs_7_
  28.1 2.3 %collective-permute-done.3.refs_4_.refs_8_ = f32[8,160]{1,0:T(8,128)S(1)} collective-permute-done((f32[8,160]{1,0:T(8,128)S(1)}, f32[8,160]{1,0:T(8,128)S(1)}, u32[]{:S(2)}, u32[]{:S(2)}) %collective-permute-start.3) | collective-permute-done | bytes 5152 | tf_op jit(solution)/shard_map/ppermute | solution.py:17
  30.4 0.0 collective-permute-done.refs_1_.refs_5_
  30.4 0.0 collective-permute-done.1.refs_2_.refs_6_
  30.4 0.0 collective-permute-done.4.refs_13_
  30.4 0.5 copy-done.5
  31.0 0.1 copy-done.2
  31.0 0.0 copy-done.3
  31.0 0.0 copy-done.8
  31.1 3.4 %shard_map.91 = (f32[4,32,8,128]{3,2,1,0:T(8,128)}, f32[128,128]{1,0:T(8,128)}, f32[128,128]{1,0:T(8,128)}, f32[8,128]{1,0:T(8,128)}, f32[8,128]{1,0:T(8,128)}) custom-call(f32[4,32,8,128]{3,2,1,0:T(8,128)} %bitcast.67, f32[160,128]{1,0:T(8,128)} %copy-done.2, f32[160,128]{1,0:T(8,128)} %copy-done.3, f32[8,160]{1,0:T(8,128)} %copy-done.4, ...), custom_call_target="tpu_custom_call" | custom-call | tf_op jit(solution)/shard_map/pallas_call | solution.py:139
  34.4 4.7 %collective-permute-start.5 = (f32[128,128]{1,0:T(8,128)}, f32[128,128]{1,0:T(8,128)S(1)}, u32[]{:S(2)}, u32[]{:S(2)}) collective-permute-start(f32[128,128]{1,0:T(8,128)} %get-tuple-element.21), channel_id=1, source_target_pairs={{0,4},{4,8},{8,12},{1,5},{5,9},{9,13},{2,6},{6,10},{10,14},{3,7},{... | collective-permute-start | bytes 196616 | tf_op jit(solution)/shard_map/ppermute | solution.py:17
  39.1 1.3 %collective-permute-start.6 = (f32[128,128]{1,0:T(8,128)}, f32[128,128]{1,0:T(8,128)S(1)}, u32[]{:S(2)}, u32[]{:S(2)}) collective-permute-start(f32[128,128]{1,0:T(8,128)} %get-tuple-element.22), channel_id=1, source_target_pairs={{4,0},{8,4},{12,8},{5,1},{9,5},{13,9},{6,2},{10,6},{14,10},{7,3},{... | collective-permute-start | bytes 196616 | tf_op jit(solution)/shard_map/ppermute | solution.py:17
  40.4 4.3 %collective-permute-start.7 = (f32[8,128]{1,0:T(8,128)}, f32[8,128]{1,0:T(8,128)S(1)}, u32[]{:S(2)}, u32[]{:S(2)}) collective-permute-start(f32[8,128]{1,0:T(8,128)} %get-tuple-element.23), channel_id=1, source_target_pairs={{0,1},{1,2},{2,3},{4,5},{5,6},{6,7},{8,9},{9,10},{10,11},{12,13},{... | collective-permute-start | bytes 12296 | tf_op jit(solution)/shard_map/ppermute | solution.py:17
  44.7 1.3 %collective-permute-start.8 = (f32[8,128]{1,0:T(8,128)S(1)}, f32[8,128]{1,0:T(8,128)S(1)}, u32[]{:S(2)}, u32[]{:S(2)}) collective-permute-start(f32[8,128]{1,0:T(8,128)S(1)} %copy-done.15), channel_id=1, source_target_pairs={{1,0},{2,1},{3,2},{5,4},{6,5},{7,6},{9,8},{10,9},{11,10},{13,12},{... | collective-permute-start | bytes 12296 | tf_op jit(solution)/shard_map/ppermute | solution.py:17
  46.0 0.2 collective-permute-done.7.refs_3_
  46.2 4.0 %collective-permute-done.8.refs_4_ = f32[8,128]{1,0:T(8,128)S(1)} collective-permute-done((f32[8,128]{1,0:T(8,128)S(1)}, f32[8,128]{1,0:T(8,128)S(1)}, u32[]{:S(2)}, u32[]{:S(2)}) %collective-permute-start.8) | collective-permute-done | bytes 4128 | tf_op jit(solution)/shard_map/ppermute | solution.py:17
  50.2 0.0 collective-permute-done.5.refs_1_
  50.2 0.0 collective-permute-done.6.refs_2_
  50.2 0.6 %copy-done.10 = f32[8,128]{1,0:T(8,128)} copy-done((f32[8,128]{1,0:T(8,128)}, f32[8,128]{1,0:T(8,128)S(1)}, u32[]{:S(2)}) %copy-start.10) | copy-done | bytes 4120
  50.8 0.0 copy-done.6
  50.8 0.0 copy-done.7
  50.9 3.1 %shard_map.92 = f32[4,32,8,128]{3,2,1,0:T(8,128)} custom-call(f32[4,32,8,128]{3,2,1,0:T(8,128)} %get-tuple-element.20.refs_0_, f32[128,128]{1,0:T(8,128)} %copy-done.6, f32[128,128]{1,0:T(8,128)} %copy-done.7, f32[8,128]{1,0:T(8,128)} %copy-done.9, f32[8,128]{1,0:T(8,128)} %copy-done.10, f32[160,128]{1,0:T(8,128)} %copy-done.2, f32[160,128]{1,0:T(8,128)} %copy-done.3, ...), custom_call_target="tpu_custom_call" | custom-call | tf_op jit(solution)/shard_map/pallas_call | solution.py:139
  (40 shorter events, 0.4 us)
Async XLA Ops:
  0.0 0.7 %copy-start.12 = (s32[1,1,1,32]{3,2,1,0:T(1,128)S(1)}, s32[1,1,1,32]{3,2,1,0:T(1,128)}, u32[]{:S(2)}) copy-start(s32[1,1,1,32]{3,2,1,0:T(1,128)} %param.15) | copy-start | bytes 388
  1.6 0.7 %copy-start.14 = (s32[1,1,1,32,1]{3,4,2,1,0:T(1,128)S(1)}, s32[1,1,1,32,1]{3,4,2,1,0:T(1,128)}, u32[]{:S(2)}) copy-start(s32[1,1,1,32,1]{3,4,2,1,0:T(1,128)} %param.14) | copy-start | bytes 388
  1.7 0.8 %copy-start.13 = (s32[1,1,1,32]{3,2,1,0:T(1,128)S(1)}, s32[1,1,1,32]{3,2,1,0:T(1,128)}, u32[]{:S(2)}) copy-start(s32[1,1,1,32]{3,2,1,0:T(1,128)} %param.16) | copy-start | bytes 388
  1.7 1.5 %copy-start = (f32[1,4,32,8,128]{4,3,2,1,0:T(8,128)S(1)}, f32[1,4,32,8,128]{4,3,2,1,0:T(8,128)}, u32[]{:S(2)}) copy-start(f32[1,4,32,8,128]{4,3,2,1,0:T(8,128)} %param.9) | copy-start | bytes 1572868
  4.5 0.9 %copy-start.1 = (f32[1,32,8,128]{3,2,1,0:T(8,128)S(1)}, f32[1,32,8,128]{3,2,1,0:T(8,128)}, u32[]{:S(2)}) copy-start(f32[1,32,8,128]{3,2,1,0:T(8,128)} %param.11) | copy-start | bytes 393220
  8.0 18.3 %all-to-all-start = ((f32[16,7,512]{2,1,0:T(8,128)}), f32[16,7,512]{2,1,0:T(8,128)S(1)}, u32[]{:S(2)}, u32[]{:S(2)}) async-start(f32[16,7,512]{2,1,0:T(8,128)} %copy.54), calls=%async_computation | async-start | bytes 524288 | tf_op jit(solution)/shard_map/all_to_all | solution.py:231
  16.3 14.1 %collective-permute-start = (f32[160,128]{1,0:T(8,128)S(1)}, f32[160,128]{1,0:T(8,128)S(1)}, u32[]{:S(2)}, u32[]{:S(2)}) collective-permute-start(f32[160,128]{1,0:T(8,128)S(1)} %get-tuple-element.15), channel_id=1, source_target_pairs={{0,4},{4,8},{8,12},{1,5},{5,9},{9,13},{2,6},{6,10},{10,14},{3,7},{... | collective-permute-start | bytes 245768 | tf_op jit(solution)/shard_map/ppermute | solution.py:17
  20.2 10.2 %collective-permute-start.1 = (f32[160,128]{1,0:T(8,128)S(1)}, f32[160,128]{1,0:T(8,128)S(1)}, u32[]{:S(2)}, u32[]{:S(2)}) collective-permute-start(f32[160,128]{1,0:T(8,128)S(1)} %get-tuple-element.16), channel_id=1, source_target_pairs={{4,0},{8,4},{12,8},{5,1},{9,5},{13,9},{6,2},{10,6},{14,10},{7,3},{... | collective-permute-start | bytes 245768 | tf_op jit(solution)/shard_map/ppermute | solution.py:17
  21.5 6.7 %collective-permute-start.2 = (f32[8,160]{1,0:T(8,128)S(1)}, f32[8,160]{1,0:T(8,128)S(1)}, u32[]{:S(2)}, u32[]{:S(2)}) collective-permute-start(f32[8,160]{1,0:T(8,128)S(1)} %get-tuple-element.17), channel_id=1, source_target_pairs={{0,1},{1,2},{2,3},{4,5},{5,6},{6,7},{8,9},{9,10},{10,11},{12,13},{... | collective-permute-start | bytes 15368 | tf_op jit(solution)/shard_map/ppermute | solution.py:17
  24.8 5.5 %collective-permute-start.3 = (f32[8,160]{1,0:T(8,128)S(1)}, f32[8,160]{1,0:T(8,128)S(1)}, u32[]{:S(2)}, u32[]{:S(2)}) collective-permute-start(f32[8,160]{1,0:T(8,128)S(1)} %get-tuple-element.18), channel_id=1, source_target_pairs={{1,0},{2,1},{3,2},{5,4},{6,5},{7,6},{9,8},{10,9},{11,10},{13,12},{... | collective-permute-start | bytes 15368 | tf_op jit(solution)/shard_map/ppermute | solution.py:17
  26.8 0.7 %copy-start.11 = (s32[1,8,128]{2,1,0:T(8,128)S(1)}, s32[1,8,128]{2,1,0:T(8,128)}, u32[]{:S(2)}) copy-start(s32[1,8,128]{2,1,0:T(8,128)} %param.13) | copy-start | bytes 12292
  26.8 3.6 %collective-permute-start.4 = (f32[11,512]{1,0:T(8,128)S(1)}, f32[11,512]{1,0:T(8,128)S(1)}, u32[]{:S(2)}, u32[]{:S(2)}) collective-permute-start(f32[11,512]{1,0:T(8,128)S(1)} %pad_maximum_fusion.3), channel_id=1, source_target_pairs={{0,16},{16,0},{1,17},{17,1},{2,18},{18,2},{3,19},{19,3},{4,20},{20... | collective-permute-start | bytes 67592 | tf_op jit(solution)/shard_map/ppermute | solution.py:250
  28.1 2.3 %copy-start.4 = (f32[8,160]{1,0:T(8,128)}, f32[8,160]{1,0:T(8,128)S(1)}, u32[]{:S(2)}) copy-start(f32[8,160]{1,0:T(8,128)S(1)} %collective-permute-done.2.refs_3_.refs_7_) | copy-start | bytes 15364
  30.4 0.6 %copy-start.5 = (f32[8,160]{1,0:T(8,128)}, f32[8,160]{1,0:T(8,128)S(1)}, u32[]{:S(2)}) copy-start(f32[8,160]{1,0:T(8,128)S(1)} %collective-permute-done.3.refs_4_.refs_8_) | copy-start | bytes 15364
  30.4 0.6 %copy-start.2 = (f32[160,128]{1,0:T(8,128)}, f32[160,128]{1,0:T(8,128)S(1)}, u32[]{:S(2)}) copy-start(f32[160,128]{1,0:T(8,128)S(1)} %collective-permute-done.refs_1_.refs_5_) | copy-start | bytes 245764
  30.4 0.7 %copy-start.3 = (f32[160,128]{1,0:T(8,128)}, f32[160,128]{1,0:T(8,128)S(1)}, u32[]{:S(2)}) copy-start(f32[160,128]{1,0:T(8,128)S(1)} %collective-permute-done.1.refs_2_.refs_6_) | copy-start | bytes 245764
  30.4 0.7 %copy-start.8 = (f32[11,512]{1,0:T(8,128)}, f32[11,512]{1,0:T(8,128)S(1)}, u32[]{:S(2)}) copy-start(f32[11,512]{1,0:T(8,128)S(1)} %collective-permute-done.4.refs_13_) | copy-start | bytes 67588
  34.4 10.3 %copy-start.15 = (f32[8,128]{1,0:T(8,128)S(1)}, f32[8,128]{1,0:T(8,128)}, u32[]{:S(2)}) copy-start(f32[8,128]{1,0:T(8,128)} %get-tuple-element.24) | copy-start | bytes 12292
  34.4 15.8 %collective-permute-start.5 = (f32[128,128]{1,0:T(8,128)}, f32[128,128]{1,0:T(8,128)S(1)}, u32[]{:S(2)}, u32[]{:S(2)}) collective-permute-start(f32[128,128]{1,0:T(8,128)} %get-tuple-element.21), channel_id=1, source_target_pairs={{0,4},{4,8},{8,12},{1,5},{5,9},{9,13},{2,6},{6,10},{10,14},{3,7},{... | collective-permute-start | bytes 196616 | tf_op jit(solution)/shard_map/ppermute | solution.py:17
  39.1 11.1 %collective-permute-start.6 = (f32[128,128]{1,0:T(8,128)}, f32[128,128]{1,0:T(8,128)S(1)}, u32[]{:S(2)}, u32[]{:S(2)}) collective-permute-start(f32[128,128]{1,0:T(8,128)} %get-tuple-element.22), channel_id=1, source_target_pairs={{4,0},{8,4},{12,8},{5,1},{9,5},{13,9},{6,2},{10,6},{14,10},{7,3},{... | collective-permute-start | bytes 196616 | tf_op jit(solution)/shard_map/ppermute | solution.py:17
  40.4 5.8 %collective-permute-start.7 = (f32[8,128]{1,0:T(8,128)}, f32[8,128]{1,0:T(8,128)S(1)}, u32[]{:S(2)}, u32[]{:S(2)}) collective-permute-start(f32[8,128]{1,0:T(8,128)} %get-tuple-element.23), channel_id=1, source_target_pairs={{0,1},{1,2},{2,3},{4,5},{5,6},{6,7},{8,9},{9,10},{10,11},{12,13},{... | collective-permute-start | bytes 12296 | tf_op jit(solution)/shard_map/ppermute | solution.py:17
  44.7 5.5 %collective-permute-start.8 = (f32[8,128]{1,0:T(8,128)S(1)}, f32[8,128]{1,0:T(8,128)S(1)}, u32[]{:S(2)}, u32[]{:S(2)}) collective-permute-start(f32[8,128]{1,0:T(8,128)S(1)} %copy-done.15), channel_id=1, source_target_pairs={{1,0},{2,1},{3,2},{5,4},{6,5},{7,6},{9,8},{10,9},{11,10},{13,12},{... | collective-permute-start | bytes 12296 | tf_op jit(solution)/shard_map/ppermute | solution.py:17
  46.2 4.0 %copy-start.9 = (f32[8,128]{1,0:T(8,128)}, f32[8,128]{1,0:T(8,128)S(1)}, u32[]{:S(2)}) copy-start(f32[8,128]{1,0:T(8,128)S(1)} %collective-permute-done.7.refs_3_) | copy-start | bytes 12292
  50.2 0.6 %copy-start.10 = (f32[8,128]{1,0:T(8,128)}, f32[8,128]{1,0:T(8,128)S(1)}, u32[]{:S(2)}) copy-start(f32[8,128]{1,0:T(8,128)S(1)} %collective-permute-done.8.refs_4_) | copy-start | bytes 12292
  50.2 0.6 %copy-start.6 = (f32[128,128]{1,0:T(8,128)}, f32[128,128]{1,0:T(8,128)S(1)}, u32[]{:S(2)}) copy-start(f32[128,128]{1,0:T(8,128)S(1)} %collective-permute-done.5.refs_1_) | copy-start | bytes 196612
  50.2 0.7 %copy-start.7 = (f32[128,128]{1,0:T(8,128)}, f32[128,128]{1,0:T(8,128)S(1)}, u32[]{:S(2)}) copy-start(f32[128,128]{1,0:T(8,128)S(1)} %collective-permute-done.6.refs_2_) | copy-start | bytes 196612

commit v10 on v9

--- a/solution.py
+++ b/solution.py
@@ -22,8 +22,8 @@
 
     def kernel(*refs):
         refs = list(refs)
-        a_ref, up_ref, dn_ref, lf_ref, rt_ref, cu_ref, cd_ref, cl_ref, cr_ref = refs[:9]
-        ue_ref, un_ref, k_ref, wet_ref = refs[9:13]
+        a_hbm, up_ref, dn_ref, lf_ref, rt_ref, cu_ref, cd_ref, cl_ref, cr_ref = refs[:9]
+        ue_ref, un_ref, k_hbm, wet_ref = refs[9:13]
         refs = refs[13:]
         if coupled:
             inc_ref = refs.pop(0)
@@ -31,7 +31,19 @@
         if emit:
             eu_ref, ed_ref, el_ref, er_ref = refs[:4]
             refs = refs[4:]
-        c_ref = refs[0]
+        c_ref, a_ref, k_ref, sems = refs[:4]
+        chunk = 8
+        pending = []
+        for c in range(levels // chunk):
+            window = pl.ds(c * chunk, chunk)
+            pending.append(
+                (
+                    pltpu.make_async_copy(a_hbm.at[:, window], a_ref.at[:, window], sems.at[0, c]),
+                    pltpu.make_async_copy(k_hbm.at[:, window], k_ref.at[:, window], sems.at[1, c]),
+                )
+            )
+            pending[-1][0].start()
+            pending[-1][1].start()
         row = lax.broadcasted_iota(jnp.int32, (rows, cols), 0)
         col = lax.broadcasted_iota(jnp.int32, (rows, cols), 1)
         top = row == 0
@@ -49,6 +61,9 @@
                 for c in range(2 * fields)
             ]
         for l in range(levels):
+            if l % chunk == 0:
+                pending[l // chunk][0].wait()
+                pending[l // chunk][1].wait()
             ue = ue_ref[l]
             un = un_ref[l]
             ci = planes + l
@@ -136,10 +151,19 @@
     if emit:
         shapes += [jax.ShapeDtypeStruct((planes, cols), jnp.float32)] * 2
         shapes += [jax.ShapeDtypeStruct((rows, planes), jnp.float32)] * 2
+    in_specs = [pl.BlockSpec(memory_space=pltpu.VMEM)] * len(operands)
+    in_specs[0] = pl.BlockSpec(memory_space=pl.ANY)
+    in_specs[11] = pl.BlockSpec(memory_space=pl.ANY)
     return pl.pallas_call(
         step_kernel(fields, levels, rows, cols, coupled, emit),
         out_shape=shapes,
-        scratch_shapes=[pltpu.VMEM(a.shape, jnp.float32)],
+        in_specs=in_specs,
+        scratch_shapes=[
+            pltpu.VMEM(a.shape, jnp.float32),
+            pltpu.VMEM(a.shape, jnp.float32),
+            pltpu.VMEM(coeffs.shape, jnp.float32),
+            pltpu.SemaphoreType.DMA((2, levels // 8)),
+        ],
     )(*operands)
 
 

time: 54.6 us -> 56.5 us (1.035)
  Pallas kernels: 6.53 us -> 8.48 us
    pallas_call x2, Pallas kernels: 6.53 us -> 8.48 us  [run_step(): pl.pallas_call(step_kernel(fields, levels, rows, cols, coupled, emit), ou...]
where the time goes in v10:
time: 56.5 us; the launch traced here: 55.9 us
  starting transfers between devices  29.6 us (52%)
  Pallas kernels  8.48 us (15%)
  local copies, waits for them, and re-layouts  7.94 us (14%)
  waiting for transfers between devices  6.63 us (12%)
  matrix products  1.71 us (3%)
  other arithmetic  1.09 us (2%)
    ppermute x8, starting transfers between devices, shift(): return lax.ppermute(block, axis, route)  21.2 us
    pallas_call x2, Pallas kernels, run_step(): pl.pallas_call(step_kernel(fields, levels, rows, cols, coupled, emit), ou...  8.48 us
    all_to_all x1, starting transfers between devices, shards(): lax.all_to_all(send_data, ('gx', 'gy'), split_axis=0, concat_axis=0, tile...  8.34 us
    ppermute x8, waiting for transfers between devices, shift(): return lax.ppermute(block, axis, route)  6.48 us
    unnamed x32, local copies, waits for them, and re-layouts  3.68 us
  transfers between devices with their start and end apart: 10, of which 4 were waited for; matrix products, arithmetic and copies ran while one was open for 2% of the time, Pallas kernels for 0%

profile of v10, /device:TPU:0, one launch (start us, length us, event | category | flops | bytes accessed | tf_op | source)
XLA Modules:
  0.0 55.9 jit_solution(5267199807230360597)
XLA Ops:
  0.0 0.7 %copy-done.12 = s32[1,1,1,32]{3,2,1,0:T(1,128)S(1)} copy-done((s32[1,1,1,32]{3,2,1,0:T(1,128)S(1)}, s32[1,1,1,32]{3,2,1,0:T(1,128)}, u32[]{:S(2)}) %copy-start.12) | copy-done | bytes 152
  0.7 1.0 %convolution_multiply_fusion = f32[32,4,128]{2,0,1:T(8,128)S(1)} fusion(f32[32,128]{1,0:T(8,128)} %bitcast.87, f32[4,32,8,128]{3,2,1,0:T(8,128)} %bitcast.66, s32[32]{0:T(128)S(1)} %bitcast.90), kind=kOutput, calls=%fused_computation | convolution fusion | flops 1589504 | bytes 98432 | tf_op jit(solution)/shard_map/dot_general | solution.py:204
  1.6 0.0 copy-start.14
  1.7 0.0 copy-start.13
  1.7 0.0 copy-start
  1.7 0.6 %copy-done.14 = s32[1,1,1,32,1]{3,4,2,1,0:T(1,128)S(1)} copy-done((s32[1,1,1,32,1]{3,4,2,1,0:T(1,128)S(1)}, s32[1,1,1,32,1]{3,4,2,1,0:T(1,128)}, u32[]{:S(2)}) %copy-start.14) | copy-done | bytes 152
  2.3 0.2 convert_reduce_fusion
  2.5 0.0 copy-done.13
  2.5 0.3 fusion
  2.8 0.3 slice_reduce_fusion.1
  3.2 0.2 fusion.18
  3.4 0.1 fusion.19
  3.6 0.1 copy.47
  3.6 0.1 reshape.113
  3.7 0.1 select_reduce_fusion
  3.8 0.1 convert_element_type.31
  3.9 0.1 select_maximum_fusion.1
  4.2 0.3 copy.48
  4.4 0.1 reshape.115
  4.5 0.3 copy.51
  4.8 0.1 reshape.116
  4.9 0.5 copy-done.1
  5.4 0.1 fusion.21
  5.5 0.1 copy.50
  5.7 0.1 copy.53
  5.8 1.0 %fusion.22 = (f32[32,1,128]{2,1,0:T(1,128)S(1)}, f32[32,1,128]{2,1,0:T(1,128)S(1)}) fusion(f32[32,8,128]{2,1,0:T(8,128)} %bitcast.75), kind=kLoop, calls=%fused_computation.51 | loop fusion | bytes 65536 | tf_op jit(solution)/shard_map/slice | solution.py:188
  6.8 0.3 fusion.6
  7.1 0.8 %copy.54 = f32[16,7,512]{2,1,0:T(8,128)} copy(f32[16,7,512]{2,0,1:T(8,128)S(1)} %pad_maximum_fusion) | data formatting | bytes 458752 | tf_op jit(solution)/shard_map/optimization_barrier | solution.py:252
  8.0 8.3 %all-to-all-start = ((f32[16,7,512]{2,1,0:T(8,128)}), f32[16,7,512]{2,1,0:T(8,128)S(1)}, u32[]{:S(2)}, u32[]{:S(2)}) async-start(f32[16,7,512]{2,1,0:T(8,128)} %copy.54), calls=%async_computation | async-start | bytes 524288 | tf_op jit(solution)/shard_map/all_to_all | solution.py:255
  16.3 3.8 %collective-permute-start = (f32[160,128]{1,0:T(8,128)S(1)}, f32[160,128]{1,0:T(8,128)S(1)}, u32[]{:S(2)}, u32[]{:S(2)}) collective-permute-start(f32[160,128]{1,0:T(8,128)S(1)} %get-tuple-element.15), channel_id=1, source_target_pairs={{0,4},{4,8},{8,12},{1,5},{5,9},{9,13},{2,6},{6,10},{10,14},{3,7},{... | collective-permute-start | bytes 245768 | tf_op jit(solution)/shard_map/ppermute | solution.py:17
  20.2 1.3 %collective-permute-start.1 = (f32[160,128]{1,0:T(8,128)S(1)}, f32[160,128]{1,0:T(8,128)S(1)}, u32[]{:S(2)}, u32[]{:S(2)}) collective-permute-start(f32[160,128]{1,0:T(8,128)S(1)} %get-tuple-element.16), channel_id=1, source_target_pairs={{4,0},{8,4},{12,8},{5,1},{9,5},{13,9},{6,2},{10,6},{14,10},{7,3},{... | collective-permute-start | bytes 245768 | tf_op jit(solution)/shard_map/ppermute | solution.py:17
  21.5 3.4 %collective-permute-start.2 = (f32[8,160]{1,0:T(8,128)S(1)}, f32[8,160]{1,0:T(8,128)S(1)}, u32[]{:S(2)}, u32[]{:S(2)}) collective-permute-start(f32[8,160]{1,0:T(8,128)S(1)} %get-tuple-element.17), channel_id=1, source_target_pairs={{0,1},{1,2},{2,3},{4,5},{5,6},{6,7},{8,9},{9,10},{10,11},{12,13},{... | collective-permute-start | bytes 15368 | tf_op jit(solution)/shard_map/ppermute | solution.py:17
  24.8 1.3 %collective-permute-start.3 = (f32[8,160]{1,0:T(8,128)S(1)}, f32[8,160]{1,0:T(8,128)S(1)}, u32[]{:S(2)}, u32[]{:S(2)}) collective-permute-start(f32[8,160]{1,0:T(8,128)S(1)} %get-tuple-element.18), channel_id=1, source_target_pairs={{1,0},{2,1},{3,2},{5,4},{6,5},{7,6},{9,8},{10,9},{11,10},{13,12},{... | collective-permute-start | bytes 15368 | tf_op jit(solution)/shard_map/ppermute | solution.py:17
  26.1 0.2 all-to-all-done
  26.4 0.1 slice_reduce_fusion.3
  26.5 0.1 eq.128
  26.6 0.2 fusion.13
  26.8 0.1 slice_reduce_fusion.2
  26.8 0.0 copy-start.11
  26.8 0.1 collective-permute-start.4
  26.9 0.6 %copy-done.11 = s32[1,8,128]{2,1,0:T(8,128)S(1)} copy-done((s32[1,8,128]{2,1,0:T(8,128)S(1)}, s32[1,8,128]{2,1,0:T(8,128)}, u32[]{:S(2)}) %copy-start.11) | copy-done | bytes 4120
  27.5 0.6 %convert_bitcast_fusion.refs_12_ = f32[8,128]{1,0:T(8,128)} fusion(s32[1,8,128]{2,1,0:T(8,128)S(1)} %copy-done.11), kind=kLoop, calls=%fused_computation.34 | loop fusion | flops 1024 | bytes 8192 | tf_op jit(solution)/shard_map/convert_element_type | solution.py:184
  28.1 0.0 collective-permute-done.2.refs_3_.refs_7_
  28.1 2.3 %collective-permute-done.3.refs_4_.refs_8_ = f32[8,160]{1,0:T(8,128)S(1)} collective-permute-done((f32[8,160]{1,0:T(8,128)S(1)}, f32[8,160]{1,0:T(8,128)S(1)}, u32[]{:S(2)}, u32[]{:S(2)}) %collective-permute-start.3) | collective-permute-done | bytes 5152 | tf_op jit(solution)/shard_map/ppermute | solution.py:17
  30.4 0.0 collective-permute-done.refs_1_.refs_5_
  30.4 0.0 collective-permute-done.1.refs_2_.refs_6_
  30.4 0.0 collective-permute-done.4.refs_13_
  30.4 0.5 copy-done.5
  31.0 0.1 copy-done.2
  31.0 0.0 copy-done.3
  31.0 0.0 copy-done.8
  31.1 4.4 %shard_map.91 = (f32[4,32,8,128]{3,2,1,0:T(8,128)}, f32[128,128]{1,0:T(8,128)}, f32[128,128]{1,0:T(8,128)}, f32[8,128]{1,0:T(8,128)}, f32[8,128]{1,0:T(8,128)}) custom-call(f32[4,32,8,128]{3,2,1,0:T(8,128)} %bitcast.67, f32[160,128]{1,0:T(8,128)} %copy-done.2, f32[160,128]{1,0:T(8,128)} %copy-done.3, f32[8,160]{1,0:T(8,128)} %copy-done.4, ...), custom_call_target="tpu_custom_call" | custom-call | tf_op jit(solution)/shard_map/pallas_call | solution.py:157
  35.4 4.5 %collective-permute-start.5 = (f32[128,128]{1,0:T(8,128)}, f32[128,128]{1,0:T(8,128)S(1)}, u32[]{:S(2)}, u32[]{:S(2)}) collective-permute-start(f32[128,128]{1,0:T(8,128)} %get-tuple-element.21), channel_id=1, source_target_pairs={{0,4},{4,8},{8,12},{1,5},{5,9},{9,13},{2,6},{6,10},{10,14},{3,7},{... | collective-permute-start | bytes 196616 | tf_op jit(solution)/shard_map/ppermute | solution.py:17
  40.0 1.3 %collective-permute-start.6 = (f32[128,128]{1,0:T(8,128)}, f32[128,128]{1,0:T(8,128)S(1)}, u32[]{:S(2)}, u32[]{:S(2)}) collective-permute-start(f32[128,128]{1,0:T(8,128)} %get-tuple-element.22), channel_id=1, source_target_pairs={{4,0},{8,4},{12,8},{5,1},{9,5},{13,9},{6,2},{10,6},{14,10},{7,3},{... | collective-permute-start | bytes 196616 | tf_op jit(solution)/shard_map/ppermute | solution.py:17
  41.3 4.3 %collective-permute-start.7 = (f32[8,128]{1,0:T(8,128)}, f32[8,128]{1,0:T(8,128)S(1)}, u32[]{:S(2)}, u32[]{:S(2)}) collective-permute-start(f32[8,128]{1,0:T(8,128)} %get-tuple-element.23), channel_id=1, source_target_pairs={{0,1},{1,2},{2,3},{4,5},{5,6},{6,7},{8,9},{9,10},{10,11},{12,13},{... | collective-permute-start | bytes 12296 | tf_op jit(solution)/shard_map/ppermute | solution.py:17
  45.6 1.3 %collective-permute-start.8 = (f32[8,128]{1,0:T(8,128)S(1)}, f32[8,128]{1,0:T(8,128)S(1)}, u32[]{:S(2)}, u32[]{:S(2)}) collective-permute-start(f32[8,128]{1,0:T(8,128)S(1)} %copy-done.15), channel_id=1, source_target_pairs={{1,0},{2,1},{3,2},{5,4},{6,5},{7,6},{9,8},{10,9},{11,10},{13,12},{... | collective-permute-start | bytes 12296 | tf_op jit(solution)/shard_map/ppermute | solution.py:17
  46.9 0.2 collective-permute-done.7.refs_3_
  47.1 4.0 %collective-permute-done.8.refs_4_ = f32[8,128]{1,0:T(8,128)S(1)} collective-permute-done((f32[8,128]{1,0:T(8,128)S(1)}, f32[8,128]{1,0:T(8,128)S(1)}, u32[]{:S(2)}, u32[]{:S(2)}) %collective-permute-start.8) | collective-permute-done | bytes 4128 | tf_op jit(solution)/shard_map/ppermute | solution.py:17
  51.1 0.0 collective-permute-done.5.refs_1_
  51.1 0.0 collective-permute-done.6.refs_2_
  51.1 0.6 copy-done.10
  51.7 0.0 copy-done.6
  51.7 0.0 copy-done.7
  51.7 4.1 %shard_map.92 = f32[4,32,8,128]{3,2,1,0:T(8,128)} custom-call(f32[4,32,8,128]{3,2,1,0:T(8,128)} %get-tuple-element.20.refs_0_, f32[128,128]{1,0:T(8,128)} %copy-done.6, f32[128,128]{1,0:T(8,128)} %copy-done.7, f32[8,128]{1,0:T(8,128)} %copy-done.9, f32[8,128]{1,0:T(8,128)} %copy-done.10, f32[160,128]{1,0:T(8,128)} %copy-done.2, f32[160,128]{1,0:T(8,128)} %copy-done.3, ...), custom_call_target="tpu_custom_call" | custom-call | tf_op jit(solution)/shard_map/pallas_call | solution.py:157
  (40 shorter events, 0.4 us)
Async XLA Ops:
  0.0 0.7 %copy-start.12 = (s32[1,1,1,32]{3,2,1,0:T(1,128)S(1)}, s32[1,1,1,32]{3,2,1,0:T(1,128)}, u32[]{:S(2)}) copy-start(s32[1,1,1,32]{3,2,1,0:T(1,128)} %param.15) | copy-start | bytes 388
  1.6 0.7 %copy-start.14 = (s32[1,1,1,32,1]{3,4,2,1,0:T(1,128)S(1)}, s32[1,1,1,32,1]{3,4,2,1,0:T(1,128)}, u32[]{:S(2)}) copy-start(s32[1,1,1,32,1]{3,4,2,1,0:T(1,128)} %param.14) | copy-start | bytes 388
  1.7 0.8 %copy-start.13 = (s32[1,1,1,32]{3,2,1,0:T(1,128)S(1)}, s32[1,1,1,32]{3,2,1,0:T(1,128)}, u32[]{:S(2)}) copy-start(s32[1,1,1,32]{3,2,1,0:T(1,128)} %param.16) | copy-start | bytes 388
  1.7 1.5 %copy-start = (f32[1,4,32,8,128]{4,3,2,1,0:T(8,128)S(1)}, f32[1,4,32,8,128]{4,3,2,1,0:T(8,128)}, u32[]{:S(2)}) copy-start(f32[1,4,32,8,128]{4,3,2,1,0:T(8,128)} %param.9) | copy-start | bytes 1572868
  4.5 0.9 %copy-start.1 = (f32[1,32,8,128]{3,2,1,0:T(8,128)S(1)}, f32[1,32,8,128]{3,2,1,0:T(8,128)}, u32[]{:S(2)}) copy-start(f32[1,32,8,128]{3,2,1,0:T(8,128)} %param.11) | copy-start | bytes 393220
  8.0 18.3 %all-to-all-start = ((f32[16,7,512]{2,1,0:T(8,128)}), f32[16,7,512]{2,1,0:T(8,128)S(1)}, u32[]{:S(2)}, u32[]{:S(2)}) async-start(f32[16,7,512]{2,1,0:T(8,128)} %copy.54), calls=%async_computation | async-start | bytes 524288 | tf_op jit(solution)/shard_map/all_to_all | solution.py:255
  16.3 14.1 %collective-permute-start = (f32[160,128]{1,0:T(8,128)S(1)}, f32[160,128]{1,0:T(8,128)S(1)}, u32[]{:S(2)}, u32[]{:S(2)}) collective-permute-start(f32[160,128]{1,0:T(8,128)S(1)} %get-tuple-element.15), channel_id=1, source_target_pairs={{0,4},{4,8},{8,12},{1,5},{5,9},{9,13},{2,6},{6,10},{10,14},{3,7},{... | collective-permute-start | bytes 245768 | tf_op jit(solution)/shard_map/ppermute | solution.py:17
  20.2 10.2 %collective-permute-start.1 = (f32[160,128]{1,0:T(8,128)S(1)}, f32[160,128]{1,0:T(8,128)S(1)}, u32[]{:S(2)}, u32[]{:S(2)}) collective-permute-start(f32[160,128]{1,0:T(8,128)S(1)} %get-tuple-element.16), channel_id=1, source_target_pairs={{4,0},{8,4},{12,8},{5,1},{9,5},{13,9},{6,2},{10,6},{14,10},{7,3},{... | collective-permute-start | bytes 245768 | tf_op jit(solution)/shard_map/ppermute | solution.py:17
  21.5 6.7 %collective-permute-start.2 = (f32[8,160]{1,0:T(8,128)S(1)}, f32[8,160]{1,0:T(8,128)S(1)}, u32[]{:S(2)}, u32[]{:S(2)}) collective-permute-start(f32[8,160]{1,0:T(8,128)S(1)} %get-tuple-element.17), channel_id=1, source_target_pairs={{0,1},{1,2},{2,3},{4,5},{5,6},{6,7},{8,9},{9,10},{10,11},{12,13},{... | collective-permute-start | bytes 15368 | tf_op jit(solution)/shard_map/ppermute | solution.py:17
  24.8 5.5 %collective-permute-start.3 = (f32[8,160]{1,0:T(8,128)S(1)}, f32[8,160]{1,0:T(8,128)S(1)}, u32[]{:S(2)}, u32[]{:S(2)}) collective-permute-start(f32[8,160]{1,0:T(8,128)S(1)} %get-tuple-element.18), channel_id=1, source_target_pairs={{1,0},{2,1},{3,2},{5,4},{6,5},{7,6},{9,8},{10,9},{11,10},{13,12},{... | collective-permute-start | bytes 15368 | tf_op jit(solution)/shard_map/ppermute | solution.py:17
  26.8 0.7 %copy-start.11 = (s32[1,8,128]{2,1,0:T(8,128)S(1)}, s32[1,8,128]{2,1,0:T(8,128)}, u32[]{:S(2)}) copy-start(s32[1,8,128]{2,1,0:T(8,128)} %param.13) | copy-start | bytes 12292
  26.8 3.6 %collective-permute-start.4 = (f32[11,512]{1,0:T(8,128)S(1)}, f32[11,512]{1,0:T(8,128)S(1)}, u32[]{:S(2)}, u32[]{:S(2)}) collective-permute-start(f32[11,512]{1,0:T(8,128)S(1)} %pad_maximum_fusion.3), channel_id=1, source_target_pairs={{0,16},{16,0},{1,17},{17,1},{2,18},{18,2},{3,19},{19,3},{4,20},{20... | collective-permute-start | bytes 67592 | tf_op jit(solution)/shard_map/ppermute | solution.py:274
  28.1 2.3 %copy-start.4 = (f32[8,160]{1,0:T(8,128)}, f32[8,160]{1,0:T(8,128)S(1)}, u32[]{:S(2)}) copy-start(f32[8,160]{1,0:T(8,128)S(1)} %collective-permute-done.2.refs_3_.refs_7_) | copy-start | bytes 15364
  30.4 0.6 %copy-start.5 = (f32[8,160]{1,0:T(8,128)}, f32[8,160]{1,0:T(8,128)S(1)}, u32[]{:S(2)}) copy-start(f32[8,160]{1,0:T(8,128)S(1)} %collective-permute-done.3.refs_4_.refs_8_) | copy-start | bytes 15364
  30.4 0.6 %copy-start.2 = (f32[160,128]{1,0:T(8,128)}, f32[160,128]{1,0:T(8,128)S(1)}, u32[]{:S(2)}) copy-start(f32[160,128]{1,0:T(8,128)S(1)} %collective-permute-done.refs_1_.refs_5_) | copy-start | bytes 245764
  30.4 0.7 %copy-start.3 = (f32[160,128]{1,0:T(8,128)}, f32[160,128]{1,0:T(8,128)S(1)}, u32[]{:S(2)}) copy-start(f32[160,128]{1,0:T(8,128)S(1)} %collective-permute-done.1.refs_2_.refs_6_) | copy-start | bytes 245764
  30.4 0.7 %copy-start.8 = (f32[11,512]{1,0:T(8,128)}, f32[11,512]{1,0:T(8,128)S(1)}, u32[]{:S(2)}) copy-start(f32[11,512]{1,0:T(8,128)S(1)} %collective-permute-done.4.refs_13_) | copy-start | bytes 67588
  35.4 10.1 %copy-start.15 = (f32[8,128]{1,0:T(8,128)S(1)}, f32[8,128]{1,0:T(8,128)}, u32[]{:S(2)}) copy-start(f32[8,128]{1,0:T(8,128)} %get-tuple-element.24) | copy-start | bytes 12292
  35.4 15.7 %collective-permute-start.5 = (f32[128,128]{1,0:T(8,128)}, f32[128,128]{1,0:T(8,128)S(1)}, u32[]{:S(2)}, u32[]{:S(2)}) collective-permute-start(f32[128,128]{1,0:T(8,128)} %get-tuple-element.21), channel_id=1, source_target_pairs={{0,4},{4,8},{8,12},{1,5},{5,9},{9,13},{2,6},{6,10},{10,14},{3,7},{... | collective-permute-start | bytes 196616 | tf_op jit(solution)/shard_map/ppermute | solution.py:17
  40.0 11.1 %collective-permute-start.6 = (f32[128,128]{1,0:T(8,128)}, f32[128,128]{1,0:T(8,128)S(1)}, u32[]{:S(2)}, u32[]{:S(2)}) collective-permute-start(f32[128,128]{1,0:T(8,128)} %get-tuple-element.22), channel_id=1, source_target_pairs={{4,0},{8,4},{12,8},{5,1},{9,5},{13,9},{6,2},{10,6},{14,10},{7,3},{... | collective-permute-start | bytes 196616 | tf_op jit(solution)/shard_map/ppermute | solution.py:17
  41.3 5.8 %collective-permute-start.7 = (f32[8,128]{1,0:T(8,128)}, f32[8,128]{1,0:T(8,128)S(1)}, u32[]{:S(2)}, u32[]{:S(2)}) collective-permute-start(f32[8,128]{1,0:T(8,128)} %get-tuple-element.23), channel_id=1, source_target_pairs={{0,1},{1,2},{2,3},{4,5},{5,6},{6,7},{8,9},{9,10},{10,11},{12,13},{... | collective-permute-start | bytes 12296 | tf_op jit(solution)/shard_map/ppermute | solution.py:17
  45.6 5.5 %collective-permute-start.8 = (f32[8,128]{1,0:T(8,128)S(1)}, f32[8,128]{1,0:T(8,128)S(1)}, u32[]{:S(2)}, u32[]{:S(2)}) collective-permute-start(f32[8,128]{1,0:T(8,128)S(1)} %copy-done.15), channel_id=1, source_target_pairs={{1,0},{2,1},{3,2},{5,4},{6,5},{7,6},{9,8},{10,9},{11,10},{13,12},{... | collective-permute-start | bytes 12296 | tf_op jit(solution)/shard_map/ppermute | solution.py:17
  47.1 4.0 %copy-start.9 = (f32[8,128]{1,0:T(8,128)}, f32[8,128]{1,0:T(8,128)S(1)}, u32[]{:S(2)}) copy-start(f32[8,128]{1,0:T(8,128)S(1)} %collective-permute-done.7.refs_3_) | copy-start | bytes 12292
  51.1 0.6 %copy-start.10 = (f32[8,128]{1,0:T(8,128)}, f32[8,128]{1,0:T(8,128)S(1)}, u32[]{:S(2)}) copy-start(f32[8,128]{1,0:T(8,128)S(1)} %collective-permute-done.8.refs_4_) | copy-start | bytes 12292
  51.1 0.6 %copy-start.6 = (f32[128,128]{1,0:T(8,128)}, f32[128,128]{1,0:T(8,128)S(1)}, u32[]{:S(2)}) copy-start(f32[128,128]{1,0:T(8,128)S(1)} %collective-permute-done.5.refs_1_) | copy-start | bytes 196612
  51.1 0.7 %copy-start.7 = (f32[128,128]{1,0:T(8,128)}, f32[128,128]{1,0:T(8,128)S(1)}, u32[]{:S(2)}) copy-start(f32[128,128]{1,0:T(8,128)S(1)} %collective-permute-done.6.refs_2_) | copy-start | bytes 196612

commit v11 on v9

--- a/solution.py
+++ b/solution.py
@@ -125,6 +125,41 @@
     return kernel
 
 
+def edge_kernel(fields, levels, rows, cols):
+    planes = (fields + 1) * levels
+
+    def kernel(a_ref, ue_ref, un_ref, lr_ref, fr_ref, lc_ref, fc_ref):
+        sub = lax.broadcasted_iota(jnp.int32, (8, cols), 0)
+        lane = lax.broadcasted_iota(jnp.int32, (rows, planes), 1)
+        last_rows = jnp.zeros((8, cols), jnp.float32)
+        first_rows = jnp.zeros((8, cols), jnp.float32)
+        last_cols = jnp.zeros((rows, planes), jnp.float32)
+        first_cols = jnp.zeros((rows, planes), jnp.float32)
+        for k in range(planes):
+            f, l = divmod(k, levels)
+            along_x = a_ref[f, l] if f < fields else ue_ref[l]
+            along_y = a_ref[f, l] if f < fields else un_ref[l]
+            last_rows = jnp.where(sub == k % 8, along_x[rows - 1 : rows, :], last_rows)
+            first_rows = jnp.where(sub == k % 8, along_x[0:1, :], first_rows)
+            last_cols = jnp.where(lane == k, along_y[:, cols - 1 : cols], last_cols)
+            first_cols = jnp.where(lane == k, along_y[:, 0:1], first_cols)
+            if k % 8 == 7:
+                lr_ref[pl.ds(k - 7, 8), :] = last_rows
+                fr_ref[pl.ds(k - 7, 8), :] = first_rows
+        lc_ref[...] = last_cols
+        fc_ref[...] = first_cols
+
+    return kernel
+
+
+def input_edges(a, ue, un):
+    fields, levels, rows, cols = a.shape
+    planes = (fields + 1) * levels
+    shapes = [jax.ShapeDtypeStruct((planes, cols), jnp.float32)] * 2
+    shapes += [jax.ShapeDtypeStruct((rows, planes), jnp.float32)] * 2
+    return pl.pallas_call(edge_kernel(fields, levels, rows, cols), out_shape=shapes)(a, ue, un)
+
+
 def run_step(a, halos, coef_halos, ue, un, coeffs, wet, inc=None, emit=False):
     fields, levels, rows, cols = a.shape
     planes = fields * levels
@@ -226,7 +261,7 @@
         1,
     )
     send_data, *outgoing = lax.optimization_barrier(
-        (send_data, row_edge(rows_x - 1), row_edge(0), col_edge(cols_y - 1), col_edge(0))
+        (send_data, *input_edges(adjoint, east, north))
     )
     got = lax.all_to_all(send_data, ("gx", "gy"), split_axis=0, concat_axis=0, tiled=True)
     halos = (

time: 54.6 us -> 55.8 us (1.022)
  the two profiles are of different devices: /device:TPU:0 before, /device:TPU:10 now
where the time goes in v11:
time: 55.8 us; the launch traced here: 55.2 us
  starting transfers between devices  31.2 us (56%)
  Pallas kernels  8.67 us (16%)
  waiting for transfers between devices  6.45 us (12%)
  local copies, waits for them, and re-layouts  5.69 us (10%)
  matrix products  1.7 us (3%)
  other arithmetic  1.07 us (2%)
    ppermute x8, starting transfers between devices, shift(): return lax.ppermute(block, axis, route)  23.8 us
    all_to_all x1, starting transfers between devices, shards(): lax.all_to_all(send_data, ('gx', 'gy'), split_axis=0, concat_axis=0, tile...  7.34 us
    pallas_call x2, Pallas kernels, run_step(): pl.pallas_call(step_kernel(fields, levels, rows, cols, coupled, emit), ou...  6.53 us
    ppermute x8, waiting for transfers between devices, shift(): return lax.ppermute(block, axis, route)  6.44 us
    unnamed x36, local copies, waits for them, and re-layouts  3.8 us
    pallas_call x1, Pallas kernels, input_edges(): pl.pallas_call(edge_kernel(fields, levels, rows, cols), out_shape=shapes)  2.14 us
  transfers between devices with their start and end apart: 10, of which 2 were waited for; matrix products, arithmetic and copies ran while one was open for 2% of the time, Pallas kernels for 0%

profile of v11, /device:TPU:10, one launch (start us, length us, event | category | flops | bytes accessed | tf_op | source)
XLA Modules:
  0.0 55.2 jit_solution(11631756705896744938)
XLA Ops:
  0.0 0.0 copy-start.10
  0.0 0.6 %copy-done.10 = s32[1,1,1,32]{3,2,1,0:T(1,128)S(1)} copy-done((s32[1,1,1,32]{3,2,1,0:T(1,128)S(1)}, s32[1,1,1,32]{3,2,1,0:T(1,128)}, u32[]{:S(2)}) %copy-start.10) | copy-done | bytes 152
  0.7 1.0 %convolution_multiply_fusion = f32[32,4,128]{2,0,1:T(8,128)S(1)} fusion(f32[32,128]{1,0:T(8,128)} %bitcast.64, f32[4,32,8,128]{3,2,1,0:T(8,128)} %bitcast.50, s32[32]{0:T(128)S(1)} %bitcast.65), kind=kOutput, calls=%fused_computation | convolution fusion | flops 1589504 | bytes 98432 | tf_op jit(solution)/shard_map/dot_general | solution.py:215
  1.7 0.0 copy-start.12
  1.7 0.6 %copy-done.12 = s32[1,1,1,32,1]{3,4,2,1,0:T(1,128)S(1)} copy-done((s32[1,1,1,32,1]{3,4,2,1,0:T(1,128)S(1)}, s32[1,1,1,32,1]{3,4,2,1,0:T(1,128)}, u32[]{:S(2)}) %copy-start.12) | copy-done | bytes 152
  2.4 0.2 convert_reduce_fusion
  2.6 0.6 %copy-done.11 = s32[1,1,1,32]{3,2,1,0:T(1,128)S(1)} copy-done((s32[1,1,1,32]{3,2,1,0:T(1,128)S(1)}, s32[1,1,1,32]{3,2,1,0:T(1,128)}, u32[]{:S(2)}) %copy-start.11) | copy-done | bytes 152
  3.2 0.3 fusion
  3.5 0.3 slice_reduce_fusion.1
  3.9 0.1 select_reduce_fusion
  4.0 0.1 convert_element_type.31
  4.2 0.1 copy.25
  4.3 0.1 reshape.107
  4.4 0.1 select_maximum_fusion.1
  4.5 0.3 fusion.6
  4.8 2.1 %shard_map.91 = (f32[160,128]{1,0:T(8,128)}, f32[160,128]{1,0:T(8,128)}, f32[8,160]{1,0:T(8,128)}, f32[8,160]{1,0:T(8,128)}) custom-call(f32[4,32,8,128]{3,2,1,0:T(8,128)} %bitcast.51, f32[32,8,128]{2,1,0:T(8,128)} %bitcast.55, f32[32,8,128]{2,1,0:T(8,128)} %bitcast.58), custom_call_target="tpu_custom_call" | custom-call | tf_op jit(solution)/shard_map/pallas_call | solution.py:160
  6.9 0.8 %copy.26 = f32[16,7,512]{2,1,0:T(8,128)} copy(f32[16,7,512]{2,0,1:T(8,128)S(1)} %pad_maximum_fusion) | data formatting | bytes 458752 | tf_op jit(solution)/shard_map/optimization_barrier | solution.py:263
  7.8 7.3 %all-to-all-start = ((f32[16,7,512]{2,1,0:T(8,128)}), f32[16,7,512]{2,1,0:T(8,128)S(1)}, u32[]{:S(2)}, u32[]{:S(2)}) async-start(f32[16,7,512]{2,1,0:T(8,128)} %copy.26), calls=%async_computation | async-start | bytes 524288 | tf_op jit(solution)/shard_map/all_to_all | solution.py:266
  15.1 0.0 copy-done.16
  15.1 3.4 %collective-permute-start.2 = (f32[8,160]{1,0:T(8,128)S(1)}, f32[8,160]{1,0:T(8,128)S(1)}, u32[]{:S(2)}, u32[]{:S(2)}) collective-permute-start(f32[8,160]{1,0:T(8,128)S(1)} %copy-done.16), channel_id=1, source_target_pairs={{0,1},{1,2},{2,3},{4,5},{5,6},{6,7},{8,9},{9,10},{10,11},{12,13},{... | collective-permute-start | bytes 15368 | tf_op jit(solution)/shard_map/ppermute | solution.py:17
  18.5 0.0 copy-done.15
  18.5 2.5 %collective-permute-start.3 = (f32[8,160]{1,0:T(8,128)S(1)}, f32[8,160]{1,0:T(8,128)S(1)}, u32[]{:S(2)}, u32[]{:S(2)}) collective-permute-start(f32[8,160]{1,0:T(8,128)S(1)} %copy-done.15), channel_id=1, source_target_pairs={{1,0},{2,1},{3,2},{5,4},{6,5},{7,6},{9,8},{10,9},{11,10},{13,12},{... | collective-permute-start | bytes 15368 | tf_op jit(solution)/shard_map/ppermute | solution.py:17
  21.0 0.0 copy-done.14
  21.0 3.4 %collective-permute-start = (f32[160,128]{1,0:T(8,128)S(1)}, f32[160,128]{1,0:T(8,128)S(1)}, u32[]{:S(2)}, u32[]{:S(2)}) collective-permute-start(f32[160,128]{1,0:T(8,128)S(1)} %copy-done.14), channel_id=1, source_target_pairs={{0,4},{4,8},{8,12},{1,5},{5,9},{9,13},{2,6},{6,10},{10,14},{3,7},{... | collective-permute-start | bytes 245768 | tf_op jit(solution)/shard_map/ppermute | solution.py:17
  24.4 0.0 copy-done.13
  24.4 2.5 %collective-permute-start.1 = (f32[160,128]{1,0:T(8,128)S(1)}, f32[160,128]{1,0:T(8,128)S(1)}, u32[]{:S(2)}, u32[]{:S(2)}) collective-permute-start(f32[160,128]{1,0:T(8,128)S(1)} %copy-done.13), channel_id=1, source_target_pairs={{4,0},{8,4},{12,8},{5,1},{9,5},{13,9},{6,2},{10,6},{14,10},{7,3},{... | collective-permute-start | bytes 245768 | tf_op jit(solution)/shard_map/ppermute | solution.py:17
  26.9 0.0 all-to-all-done
  26.9 0.1 slice_reduce_fusion.3
  27.0 0.1 eq.128
  27.2 0.2 fusion.13
  27.4 0.1 slice_reduce_fusion.2
  27.4 0.0 copy-start.9
  27.4 0.1 collective-permute-start.4
  27.5 0.6 %copy-done.9 = s32[1,8,128]{2,1,0:T(8,128)S(1)} copy-done((s32[1,8,128]{2,1,0:T(8,128)S(1)}, s32[1,8,128]{2,1,0:T(8,128)}, u32[]{:S(2)}) %copy-start.9) | copy-done | bytes 4120
  28.1 0.6 %convert_bitcast_fusion.refs_12_ = f32[8,128]{1,0:T(8,128)} fusion(s32[1,8,128]{2,1,0:T(8,128)S(1)} %copy-done.9), kind=kLoop, calls=%fused_computation.30 | loop fusion | flops 1024 | bytes 8192 | tf_op jit(solution)/shard_map/convert_element_type | solution.py:195
  28.7 0.0 collective-permute-done.2.refs_3_.refs_7_
  28.7 0.0 collective-permute-done.3.refs_4_.refs_8_
  28.7 0.0 copy-start.3
  28.7 0.0 collective-permute-done.refs_1_.refs_5_
  28.7 0.0 copy-start
  28.7 2.0 %collective-permute-done.1.refs_2_.refs_6_ = f32[160,128]{1,0:T(8,128)S(1)} collective-permute-done((f32[160,128]{1,0:T(8,128)S(1)}, f32[160,128]{1,0:T(8,128)S(1)}, u32[]{:S(2)}, u32[]{:S(2)}) %collective-permute-start.1) | collective-permute-done | bytes 81952 | tf_op jit(solution)/shard_map/ppermute | solution.py:17
  30.7 0.0 collective-permute-done.4.refs_13_
  30.7 0.0 copy-done.2
  30.7 0.0 copy-done.3
  30.7 0.0 copy-done
  30.7 0.6 %copy-done.1 = f32[160,128]{1,0:T(8,128)} copy-done((f32[160,128]{1,0:T(8,128)}, f32[160,128]{1,0:T(8,128)S(1)}, u32[]{:S(2)}) %copy-start.1) | copy-done | bytes 81944
  31.3 0.0 copy-done.6
  31.4 3.4 %shard_map.92 = (f32[4,32,8,128]{3,2,1,0:T(8,128)}, f32[128,128]{1,0:T(8,128)}, f32[128,128]{1,0:T(8,128)}, f32[8,128]{1,0:T(8,128)}, f32[8,128]{1,0:T(8,128)}) custom-call(f32[4,32,8,128]{3,2,1,0:T(8,128)} %bitcast.52, f32[160,128]{1,0:T(8,128)} %copy-done, f32[160,128]{1,0:T(8,128)} %copy-done.1, f32[8,160]{1,0:T(8,128)} %copy-done.2, f32[8,160]{1,0:T(8,128)} %copy-done.3, ...), custom_call_target="tpu_custom_call" | custom-call | tf_op jit(solution)/shard_map/pallas_call | solution.py:174
  34.8 3.5 %collective-permute-start.5 = (f32[128,128]{1,0:T(8,128)}, f32[128,128]{1,0:T(8,128)S(1)}, u32[]{:S(2)}, u32[]{:S(2)}) collective-permute-start(f32[128,128]{1,0:T(8,128)} %get-tuple-element.29), channel_id=1, source_target_pairs={{0,4},{4,8},{8,12},{1,5},{5,9},{9,13},{2,6},{6,10},{10,14},{3,7},{... | collective-permute-start | bytes 196616 | tf_op jit(solution)/shard_map/ppermute | solution.py:17
  38.3 2.5 %collective-permute-start.6 = (f32[128,128]{1,0:T(8,128)}, f32[128,128]{1,0:T(8,128)S(1)}, u32[]{:S(2)}, u32[]{:S(2)}) collective-permute-start(f32[128,128]{1,0:T(8,128)} %get-tuple-element.30), channel_id=1, source_target_pairs={{4,0},{8,4},{12,8},{5,1},{9,5},{13,9},{6,2},{10,6},{14,10},{7,3},{... | collective-permute-start | bytes 196616 | tf_op jit(solution)/shard_map/ppermute | solution.py:17
  40.7 4.3 %collective-permute-start.7 = (f32[8,128]{1,0:T(8,128)}, f32[8,128]{1,0:T(8,128)S(1)}, u32[]{:S(2)}, u32[]{:S(2)}) collective-permute-start(f32[8,128]{1,0:T(8,128)} %get-tuple-element.31), channel_id=1, source_target_pairs={{0,1},{1,2},{2,3},{4,5},{5,6},{6,7},{8,9},{9,10},{10,11},{12,13},{... | collective-permute-start | bytes 12296 | tf_op jit(solution)/shard_map/ppermute | solution.py:17
  45.0 0.0 copy-done.17
  45.0 1.9 %collective-permute-start.8 = (f32[8,128]{1,0:T(8,128)S(1)}, f32[8,128]{1,0:T(8,128)S(1)}, u32[]{:S(2)}, u32[]{:S(2)}) collective-permute-start(f32[8,128]{1,0:T(8,128)S(1)} %copy-done.17), channel_id=1, source_target_pairs={{1,0},{2,1},{3,2},{5,4},{6,5},{7,6},{9,8},{10,9},{11,10},{13,12},{... | collective-permute-start | bytes 12296 | tf_op jit(solution)/shard_map/ppermute | solution.py:17
  46.9 0.0 collective-permute-done.7.refs_3_
  47.0 0.0 copy-start.7
  47.0 4.5 %collective-permute-done.8.refs_4_ = f32[8,128]{1,0:T(8,128)S(1)} collective-permute-done((f32[8,128]{1,0:T(8,128)S(1)}, f32[8,128]{1,0:T(8,128)S(1)}, u32[]{:S(2)}, u32[]{:S(2)}) %collective-permute-start.8) | collective-permute-done | bytes 4128 | tf_op jit(solution)/shard_map/ppermute | solution.py:17
  51.4 0.0 collective-permute-done.5.refs_1_
  51.4 0.0 collective-permute-done.6.refs_2_
  51.4 0.0 copy-start.5
  51.4 0.0 copy-done.7
  51.5 0.6 %copy-done.8 = f32[8,128]{1,0:T(8,128)} copy-done((f32[8,128]{1,0:T(8,128)}, f32[8,128]{1,0:T(8,128)S(1)}, u32[]{:S(2)}) %copy-start.8) | copy-done | bytes 4120
  52.0 0.0 copy-done.4
  52.1 0.0 copy-done.5
  52.1 3.1 %shard_map.93 = f32[4,32,8,128]{3,2,1,0:T(8,128)} custom-call(f32[4,32,8,128]{3,2,1,0:T(8,128)} %get-tuple-element.28.refs_0_, f32[128,128]{1,0:T(8,128)} %copy-done.4, f32[128,128]{1,0:T(8,128)} %copy-done.5, f32[8,128]{1,0:T(8,128)} %copy-done.7, f32[8,128]{1,0:T(8,128)} %copy-done.8, f32[160,128]{1,0:T(8,128)} %copy-done, f32[160,128]{1,0:T(8,128)} %copy-done.1, ...), custom_call_target="tpu_custom_call" | custom-call | tf_op jit(solution)/shard_map/pallas_call | solution.py:174
  (31 shorter events, 0.4 us)
Async XLA Ops:
  0.0 0.7 %copy-start.10 = (s32[1,1,1,32]{3,2,1,0:T(1,128)S(1)}, s32[1,1,1,32]{3,2,1,0:T(1,128)}, u32[]{:S(2)}) copy-start(s32[1,1,1,32]{3,2,1,0:T(1,128)} %param.15) | copy-start | bytes 388
  1.7 0.7 %copy-start.12 = (s32[1,1,1,32,1]{3,4,2,1,0:T(1,128)S(1)}, s32[1,1,1,32,1]{3,4,2,1,0:T(1,128)}, u32[]{:S(2)}) copy-start(s32[1,1,1,32,1]{3,4,2,1,0:T(1,128)} %param.14) | copy-start | bytes 388
  2.5 0.7 %copy-start.11 = (s32[1,1,1,32]{3,2,1,0:T(1,128)S(1)}, s32[1,1,1,32]{3,2,1,0:T(1,128)}, u32[]{:S(2)}) copy-start(s32[1,1,1,32]{3,2,1,0:T(1,128)} %param.16) | copy-start | bytes 388
  7.8 7.4 %copy-start.16 = (f32[8,160]{1,0:T(8,128)S(1)}, f32[8,160]{1,0:T(8,128)}, u32[]{:S(2)}) copy-start(f32[8,160]{1,0:T(8,128)} %get-tuple-element.25) | copy-start | bytes 15364
  7.8 10.7 %copy-start.15 = (f32[8,160]{1,0:T(8,128)S(1)}, f32[8,160]{1,0:T(8,128)}, u32[]{:S(2)}) copy-start(f32[8,160]{1,0:T(8,128)} %get-tuple-element.26) | copy-start | bytes 15364
  7.8 13.2 %copy-start.14 = (f32[160,128]{1,0:T(8,128)S(1)}, f32[160,128]{1,0:T(8,128)}, u32[]{:S(2)}) copy-start(f32[160,128]{1,0:T(8,128)} %get-tuple-element.23) | copy-start | bytes 245764
  7.8 16.6 %copy-start.13 = (f32[160,128]{1,0:T(8,128)S(1)}, f32[160,128]{1,0:T(8,128)}, u32[]{:S(2)}) copy-start(f32[160,128]{1,0:T(8,128)} %get-tuple-element.24) | copy-start | bytes 245764
  7.8 19.1 %all-to-all-start = ((f32[16,7,512]{2,1,0:T(8,128)}), f32[16,7,512]{2,1,0:T(8,128)S(1)}, u32[]{:S(2)}, u32[]{:S(2)}) async-start(f32[16,7,512]{2,1,0:T(8,128)} %copy.26), calls=%async_computation | async-start | bytes 524288 | tf_op jit(solution)/shard_map/all_to_all | solution.py:266
  15.1 13.6 %collective-permute-start.2 = (f32[8,160]{1,0:T(8,128)S(1)}, f32[8,160]{1,0:T(8,128)S(1)}, u32[]{:S(2)}, u32[]{:S(2)}) collective-permute-start(f32[8,160]{1,0:T(8,128)S(1)} %copy-done.16), channel_id=1, source_target_pairs={{0,1},{1,2},{2,3},{4,5},{5,6},{6,7},{8,9},{9,10},{10,11},{12,13},{... | collective-permute-start | bytes 15368 | tf_op jit(solution)/shard_map/ppermute | solution.py:17
  18.5 10.2 %collective-permute-start.3 = (f32[8,160]{1,0:T(8,128)S(1)}, f32[8,160]{1,0:T(8,128)S(1)}, u32[]{:S(2)}, u32[]{:S(2)}) collective-permute-start(f32[8,160]{1,0:T(8,128)S(1)} %copy-done.15), channel_id=1, source_target_pairs={{1,0},{2,1},{3,2},{5,4},{6,5},{7,6},{9,8},{10,9},{11,10},{13,12},{... | collective-permute-start | bytes 15368 | tf_op jit(solution)/shard_map/ppermute | solution.py:17
  21.0 7.7 %collective-permute-start = (f32[160,128]{1,0:T(8,128)S(1)}, f32[160,128]{1,0:T(8,128)S(1)}, u32[]{:S(2)}, u32[]{:S(2)}) collective-permute-start(f32[160,128]{1,0:T(8,128)S(1)} %copy-done.14), channel_id=1, source_target_pairs={{0,4},{4,8},{8,12},{1,5},{5,9},{9,13},{2,6},{6,10},{10,14},{3,7},{... | collective-permute-start | bytes 245768 | tf_op jit(solution)/shard_map/ppermute | solution.py:17
  24.4 6.3 %collective-permute-start.1 = (f32[160,128]{1,0:T(8,128)S(1)}, f32[160,128]{1,0:T(8,128)S(1)}, u32[]{:S(2)}, u32[]{:S(2)}) collective-permute-start(f32[160,128]{1,0:T(8,128)S(1)} %copy-done.13), channel_id=1, source_target_pairs={{4,0},{8,4},{12,8},{5,1},{9,5},{13,9},{6,2},{10,6},{14,10},{7,3},{... | collective-permute-start | bytes 245768 | tf_op jit(solution)/shard_map/ppermute | solution.py:17
  27.4 0.7 %copy-start.9 = (s32[1,8,128]{2,1,0:T(8,128)S(1)}, s32[1,8,128]{2,1,0:T(8,128)}, u32[]{:S(2)}) copy-start(s32[1,8,128]{2,1,0:T(8,128)} %param.13) | copy-start | bytes 12292
  27.4 3.3 %collective-permute-start.4 = (f32[11,512]{1,0:T(8,128)S(1)}, f32[11,512]{1,0:T(8,128)S(1)}, u32[]{:S(2)}, u32[]{:S(2)}) collective-permute-start(f32[11,512]{1,0:T(8,128)S(1)} %pad_maximum_fusion.1), channel_id=1, source_target_pairs={{0,16},{16,0},{1,17},{17,1},{2,18},{18,2},{3,19},{19,3},{4,20},{20... | collective-permute-start | bytes 67592 | tf_op jit(solution)/shard_map/ppermute | solution.py:285
  28.7 2.0 %copy-start.2 = (f32[8,160]{1,0:T(8,128)}, f32[8,160]{1,0:T(8,128)S(1)}, u32[]{:S(2)}) copy-start(f32[8,160]{1,0:T(8,128)S(1)} %collective-permute-done.2.refs_3_.refs_7_) | copy-start | bytes 15364
  28.7 2.0 %copy-start.3 = (f32[8,160]{1,0:T(8,128)}, f32[8,160]{1,0:T(8,128)S(1)}, u32[]{:S(2)}) copy-start(f32[8,160]{1,0:T(8,128)S(1)} %collective-permute-done.3.refs_4_.refs_8_) | copy-start | bytes 15364
  28.7 2.0 %copy-start = (f32[160,128]{1,0:T(8,128)}, f32[160,128]{1,0:T(8,128)S(1)}, u32[]{:S(2)}) copy-start(f32[160,128]{1,0:T(8,128)S(1)} %collective-permute-done.refs_1_.refs_5_) | copy-start | bytes 245764
  30.7 0.6 %copy-start.1 = (f32[160,128]{1,0:T(8,128)}, f32[160,128]{1,0:T(8,128)S(1)}, u32[]{:S(2)}) copy-start(f32[160,128]{1,0:T(8,128)S(1)} %collective-permute-done.1.refs_2_.refs_6_) | copy-start | bytes 245764
  30.7 0.6 %copy-start.6 = (f32[11,512]{1,0:T(8,128)}, f32[11,512]{1,0:T(8,128)S(1)}, u32[]{:S(2)}) copy-start(f32[11,512]{1,0:T(8,128)S(1)} %collective-permute-done.4.refs_13_) | copy-start | bytes 67588
  34.7 10.3 %copy-start.17 = (f32[8,128]{1,0:T(8,128)S(1)}, f32[8,128]{1,0:T(8,128)}, u32[]{:S(2)}) copy-start(f32[8,128]{1,0:T(8,128)} %get-tuple-element.32) | copy-start | bytes 12292
  34.8 16.7 %collective-permute-start.5 = (f32[128,128]{1,0:T(8,128)}, f32[128,128]{1,0:T(8,128)S(1)}, u32[]{:S(2)}, u32[]{:S(2)}) collective-permute-start(f32[128,128]{1,0:T(8,128)} %get-tuple-element.29), channel_id=1, source_target_pairs={{0,4},{4,8},{8,12},{1,5},{5,9},{9,13},{2,6},{6,10},{10,14},{3,7},{... | collective-permute-start | bytes 196616 | tf_op jit(solution)/shard_map/ppermute | solution.py:17
  38.3 13.2 %collective-permute-start.6 = (f32[128,128]{1,0:T(8,128)}, f32[128,128]{1,0:T(8,128)S(1)}, u32[]{:S(2)}, u32[]{:S(2)}) collective-permute-start(f32[128,128]{1,0:T(8,128)} %get-tuple-element.30), channel_id=1, source_target_pairs={{4,0},{8,4},{12,8},{5,1},{9,5},{13,9},{6,2},{10,6},{14,10},{7,3},{... | collective-permute-start | bytes 196616 | tf_op jit(solution)/shard_map/ppermute | solution.py:17
  40.7 6.2 %collective-permute-start.7 = (f32[8,128]{1,0:T(8,128)}, f32[8,128]{1,0:T(8,128)S(1)}, u32[]{:S(2)}, u32[]{:S(2)}) collective-permute-start(f32[8,128]{1,0:T(8,128)} %get-tuple-element.31), channel_id=1, source_target_pairs={{0,1},{1,2},{2,3},{4,5},{5,6},{6,7},{8,9},{9,10},{10,11},{12,13},{... | collective-permute-start | bytes 12296 | tf_op jit(solution)/shard_map/ppermute | solution.py:17
  45.0 6.4 %collective-permute-start.8 = (f32[8,128]{1,0:T(8,128)S(1)}, f32[8,128]{1,0:T(8,128)S(1)}, u32[]{:S(2)}, u32[]{:S(2)}) collective-permute-start(f32[8,128]{1,0:T(8,128)S(1)} %copy-done.17), channel_id=1, source_target_pairs={{1,0},{2,1},{3,2},{5,4},{6,5},{7,6},{9,8},{10,9},{11,10},{13,12},{... | collective-permute-start | bytes 12296 | tf_op jit(solution)/shard_map/ppermute | solution.py:17
  47.0 4.5 %copy-start.7 = (f32[8,128]{1,0:T(8,128)}, f32[8,128]{1,0:T(8,128)S(1)}, u32[]{:S(2)}) copy-start(f32[8,128]{1,0:T(8,128)S(1)} %collective-permute-done.7.refs_3_) | copy-start | bytes 12292
  51.4 0.6 %copy-start.8 = (f32[8,128]{1,0:T(8,128)}, f32[8,128]{1,0:T(8,128)S(1)}, u32[]{:S(2)}) copy-start(f32[8,128]{1,0:T(8,128)S(1)} %collective-permute-done.8.refs_4_) | copy-start | bytes 12292
  51.4 0.6 %copy-start.4 = (f32[128,128]{1,0:T(8,128)}, f32[128,128]{1,0:T(8,128)S(1)}, u32[]{:S(2)}) copy-start(f32[128,128]{1,0:T(8,128)S(1)} %collective-permute-done.5.refs_1_) | copy-start | bytes 196612
  51.4 0.7 %copy-start.5 = (f32[128,128]{1,0:T(8,128)}, f32[128,128]{1,0:T(8,128)S(1)}, u32[]{:S(2)}) copy-start(f32[128,128]{1,0:T(8,128)S(1)} %collective-permute-done.6.refs_2_) | copy-start | bytes 196612

commit v12 on v9

--- a/solution.py
+++ b/solution.py
@@ -177,12 +177,7 @@
     pick_table = (sources[:, None] == jnp.arange(rows_x, dtype=jnp.int32)[None, :]).astype(
         jnp.float32
     )
-    payload = jnp.dot(
-        pick_table,
-        surface_rows,
-        precision=lax.Precision.HIGHEST,
-        preferred_element_type=jnp.float32,
-    )
+    payload = jnp.sum(jnp.where(pick_table[:, :, None] > 0, surface_rows[None], 0.0), axis=1)
     payload = (payload.reshape(count, fields, cols_y) * weights[:, None, :]).reshape(
         count, fields * cols_y
     )

time: 54.6 us -> 55.1 us (level)
  local copies, waits for them, and re-layouts: 7.94 us -> 9.06 us
  matrix products: 1.71 us -> 0.76 us
    dot_general x1 -> x0, matrix products: 0.95 us -> none  [shards(): jnp.dot(pick_table, surface_rows, precision=lax.Precision.HIGHEST, prefer...]
    broadcast_in_dim x0 -> x1, local copies, waits for them, and re-layouts: none -> 0.72 us  [shards(): jnp.where(pick_table[:, :, None] > 0, surface_rows[None], 0.0)]
    unnamed x32 -> x34, local copies, waits for them, and re-layouts: 3.68 us -> 4.15 us
where the time goes in v12:
time: 55.1 us; the launch traced here: 54.5 us
  starting transfers between devices  29.7 us (54%)
  local copies, waits for them, and re-layouts  9.06 us (16%)
  waiting for transfers between devices  6.63 us (12%)
  Pallas kernels  6.53 us (12%)
  other arithmetic  1.4 us (3%)
  matrix products  0.76 us (1%)
    ppermute x8, starting transfers between devices, shift(): return lax.ppermute(block, axis, route)  21.3 us
    all_to_all x1, starting transfers between devices, shards(): lax.all_to_all(send_data, ('gx', 'gy'), split_axis=0, concat_axis=0, tile...  8.33 us
    pallas_call x2, Pallas kernels, run_step(): pl.pallas_call(step_kernel(fields, levels, rows, cols, coupled, emit), ou...  6.53 us
    ppermute x8, waiting for transfers between devices, shift(): return lax.ppermute(block, axis, route)  6.47 us
    unnamed x34, local copies, waits for them, and re-layouts  4.15 us
  transfers between devices with their start and end apart: 10, of which 4 were waited for; matrix products, arithmetic and copies ran while one was open for 2% of the time, Pallas kernels for 0%

profile of v12, /device:TPU:0, one launch (start us, length us, event | category | flops | bytes accessed | tf_op | source)
XLA Modules:
  0.0 54.5 jit_solution(14397518358435906016)
XLA Ops:
  0.0 0.7 %slice_bitcast_fusion = f32[8,512]{1,0:T(8,128)S(1)} fusion(f32[4,32,8,128]{3,2,1,0:T(8,128)} %bitcast.63), kind=kLoop, calls=%fused_computation.24 | loop fusion | bytes 32768 | tf_op jit(solution)/shard_map/jit(_where)/broadcast_in_dim | solution.py:180
  0.7 0.7 %copy-done.13 = s32[1,1,1,32]{3,2,1,0:T(1,128)S(1)} copy-done((s32[1,1,1,32]{3,2,1,0:T(1,128)S(1)}, s32[1,1,1,32]{3,2,1,0:T(1,128)}, u32[]{:S(2)}) %copy-start.13) | copy-done | bytes 152
  1.4 0.1 convert_compare_fusion
  1.5 0.2 select_reduce_fusion
  1.7 0.5 copy-done.9
  2.2 0.0 copy-start.15
  2.2 0.0 copy-start.14
  2.2 0.0 copy-start
  2.3 0.6 %copy-done.15 = s32[1,1,1,32,1]{3,4,2,1,0:T(1,128)S(1)} copy-done((s32[1,1,1,32,1]{3,4,2,1,0:T(1,128)S(1)}, s32[1,1,1,32,1]{3,4,2,1,0:T(1,128)}, u32[]{:S(2)}) %copy-start.15) | copy-done | bytes 152
  2.9 0.2 convert_reduce_fusion
  3.0 0.3 fusion
  3.4 0.3 slice_reduce_fusion.1
  3.8 0.2 fusion.17
  4.0 0.1 fusion.18
  4.1 0.1 copy.43
  4.1 0.1 reshape.136
  4.2 0.1 select_reduce_fusion.1
  4.3 0.1 convert_element_type.38
  4.4 0.1 select_maximum_fusion.1
  4.6 0.3 fusion.2
  4.9 0.3 copy.44
  5.2 0.1 reshape.138
  5.3 0.3 copy.47
  5.5 0.1 reshape.139
  5.6 0.5 copy-done.1
  6.2 0.1 fusion.20
  6.3 0.1 copy.46
  6.4 0.1 copy.49
  6.5 1.0 %fusion.21 = (f32[32,1,128]{2,1,0:T(1,128)S(1)}, f32[32,1,128]{2,1,0:T(1,128)S(1)}) fusion(f32[32,8,128]{2,1,0:T(8,128)} %bitcast.72), kind=kLoop, calls=%fused_computation.52 | loop fusion | bytes 65536 | tf_op jit(solution)/shard_map/slice | solution.py:164
  7.6 0.8 %copy.50 = f32[16,7,512]{2,1,0:T(8,128)} copy(f32[16,7,512]{2,0,1:T(8,128)S(1)} %pad_maximum_fusion) | data formatting | bytes 458752 | tf_op jit(solution)/shard_map/optimization_barrier | solution.py:223
  8.4 8.3 %all-to-all-start = ((f32[16,7,512]{2,1,0:T(8,128)}), f32[16,7,512]{2,1,0:T(8,128)S(1)}, u32[]{:S(2)}, u32[]{:S(2)}) async-start(f32[16,7,512]{2,1,0:T(8,128)} %copy.50), calls=%async_computation | async-start | bytes 524288 | tf_op jit(solution)/shard_map/all_to_all | solution.py:226
  16.8 3.8 %collective-permute-start = (f32[160,128]{1,0:T(8,128)S(1)}, f32[160,128]{1,0:T(8,128)S(1)}, u32[]{:S(2)}, u32[]{:S(2)}) collective-permute-start(f32[160,128]{1,0:T(8,128)S(1)} %get-tuple-element.15), channel_id=1, source_target_pairs={{0,4},{4,8},{8,12},{1,5},{5,9},{9,13},{2,6},{6,10},{10,14},{3,7},{... | collective-permute-start | bytes 245768 | tf_op jit(solution)/shard_map/ppermute | solution.py:17
  20.6 1.3 %collective-permute-start.1 = (f32[160,128]{1,0:T(8,128)S(1)}, f32[160,128]{1,0:T(8,128)S(1)}, u32[]{:S(2)}, u32[]{:S(2)}) collective-permute-start(f32[160,128]{1,0:T(8,128)S(1)} %get-tuple-element.16), channel_id=1, source_target_pairs={{4,0},{8,4},{12,8},{5,1},{9,5},{13,9},{6,2},{10,6},{14,10},{7,3},{... | collective-permute-start | bytes 245768 | tf_op jit(solution)/shard_map/ppermute | solution.py:17
  21.9 3.4 %collective-permute-start.2 = (f32[8,160]{1,0:T(8,128)S(1)}, f32[8,160]{1,0:T(8,128)S(1)}, u32[]{:S(2)}, u32[]{:S(2)}) collective-permute-start(f32[8,160]{1,0:T(8,128)S(1)} %get-tuple-element.17), channel_id=1, source_target_pairs={{0,1},{1,2},{2,3},{4,5},{5,6},{6,7},{8,9},{9,10},{10,11},{12,13},{... | collective-permute-start | bytes 15368 | tf_op jit(solution)/shard_map/ppermute | solution.py:17
  25.3 1.3 %collective-permute-start.3 = (f32[8,160]{1,0:T(8,128)S(1)}, f32[8,160]{1,0:T(8,128)S(1)}, u32[]{:S(2)}, u32[]{:S(2)}) collective-permute-start(f32[8,160]{1,0:T(8,128)S(1)} %get-tuple-element.18), channel_id=1, source_target_pairs={{1,0},{2,1},{3,2},{5,4},{6,5},{7,6},{9,8},{10,9},{11,10},{13,12},{... | collective-permute-start | bytes 15368 | tf_op jit(solution)/shard_map/ppermute | solution.py:17
  26.6 0.2 all-to-all-done
  26.8 0.1 slice_reduce_fusion.3
  26.9 0.1 eq.132
  27.0 0.2 fusion.13
  27.2 0.1 slice_reduce_fusion.2
  27.3 0.0 copy-start.12
  27.3 0.1 collective-permute-start.4
  27.4 0.6 %copy-done.12 = s32[1,8,128]{2,1,0:T(8,128)S(1)} copy-done((s32[1,8,128]{2,1,0:T(8,128)S(1)}, s32[1,8,128]{2,1,0:T(8,128)}, u32[]{:S(2)}) %copy-start.12) | copy-done | bytes 4120
  28.0 0.6 %convert_bitcast_fusion.refs_12_ = f32[8,128]{1,0:T(8,128)} fusion(s32[1,8,128]{2,1,0:T(8,128)S(1)} %copy-done.12), kind=kLoop, calls=%fused_computation.38 | loop fusion | flops 1024 | bytes 8192 | tf_op jit(solution)/shard_map/convert_element_type | solution.py:160
  28.6 0.0 collective-permute-done.2.refs_3_.refs_7_
  28.6 2.3 %collective-permute-done.3.refs_4_.refs_8_ = f32[8,160]{1,0:T(8,128)S(1)} collective-permute-done((f32[8,160]{1,0:T(8,128)S(1)}, f32[8,160]{1,0:T(8,128)S(1)}, u32[]{:S(2)}, u32[]{:S(2)}) %collective-permute-start.3) | collective-permute-done | bytes 5152 | tf_op jit(solution)/shard_map/ppermute | solution.py:17
  30.8 0.0 collective-permute-done.refs_1_.refs_5_
  30.8 0.0 collective-permute-done.1.refs_2_.refs_6_
  30.9 0.0 collective-permute-done.4.refs_13_
  30.9 0.5 copy-done.5
  31.4 0.0 copy-done.2
  31.5 0.0 copy-done.3
  31.5 0.0 copy-done.8
  31.5 3.4 %shard_map.91 = (f32[4,32,8,128]{3,2,1,0:T(8,128)}, f32[128,128]{1,0:T(8,128)}, f32[128,128]{1,0:T(8,128)}, f32[8,128]{1,0:T(8,128)}, f32[8,128]{1,0:T(8,128)}) custom-call(f32[4,32,8,128]{3,2,1,0:T(8,128)} %bitcast.64, f32[160,128]{1,0:T(8,128)} %copy-done.2, f32[160,128]{1,0:T(8,128)} %copy-done.3, f32[8,160]{1,0:T(8,128)} %copy-done.4, ...), custom_call_target="tpu_custom_call" | custom-call | tf_op jit(solution)/shard_map/pallas_call | solution.py:139
  34.9 4.7 %collective-permute-start.5 = (f32[128,128]{1,0:T(8,128)}, f32[128,128]{1,0:T(8,128)S(1)}, u32[]{:S(2)}, u32[]{:S(2)}) collective-permute-start(f32[128,128]{1,0:T(8,128)} %get-tuple-element.21), channel_id=1, source_target_pairs={{0,4},{4,8},{8,12},{1,5},{5,9},{9,13},{2,6},{6,10},{10,14},{3,7},{... | collective-permute-start | bytes 196616 | tf_op jit(solution)/shard_map/ppermute | solution.py:17
  39.6 1.3 %collective-permute-start.6 = (f32[128,128]{1,0:T(8,128)}, f32[128,128]{1,0:T(8,128)S(1)}, u32[]{:S(2)}, u32[]{:S(2)}) collective-permute-start(f32[128,128]{1,0:T(8,128)} %get-tuple-element.22), channel_id=1, source_target_pairs={{4,0},{8,4},{12,8},{5,1},{9,5},{13,9},{6,2},{10,6},{14,10},{7,3},{... | collective-permute-start | bytes 196616 | tf_op jit(solution)/shard_map/ppermute | solution.py:17
  40.9 4.3 %collective-permute-start.7 = (f32[8,128]{1,0:T(8,128)}, f32[8,128]{1,0:T(8,128)S(1)}, u32[]{:S(2)}, u32[]{:S(2)}) collective-permute-start(f32[8,128]{1,0:T(8,128)} %get-tuple-element.23), channel_id=1, source_target_pairs={{0,1},{1,2},{2,3},{4,5},{5,6},{6,7},{8,9},{9,10},{10,11},{12,13},{... | collective-permute-start | bytes 12296 | tf_op jit(solution)/shard_map/ppermute | solution.py:17
  45.2 1.3 %collective-permute-start.8 = (f32[8,128]{1,0:T(8,128)S(1)}, f32[8,128]{1,0:T(8,128)S(1)}, u32[]{:S(2)}, u32[]{:S(2)}) collective-permute-start(f32[8,128]{1,0:T(8,128)S(1)} %copy-done.16), channel_id=1, source_target_pairs={{1,0},{2,1},{3,2},{5,4},{6,5},{7,6},{9,8},{10,9},{11,10},{13,12},{... | collective-permute-start | bytes 12296 | tf_op jit(solution)/shard_map/ppermute | solution.py:17
  46.5 0.2 collective-permute-done.7.refs_3_
  46.7 4.0 %collective-permute-done.8.refs_4_ = f32[8,128]{1,0:T(8,128)S(1)} collective-permute-done((f32[8,128]{1,0:T(8,128)S(1)}, f32[8,128]{1,0:T(8,128)S(1)}, u32[]{:S(2)}, u32[]{:S(2)}) %collective-permute-start.8) | collective-permute-done | bytes 4128 | tf_op jit(solution)/shard_map/ppermute | solution.py:17
  50.7 0.6 %copy-done.11 = f32[8,128]{1,0:T(8,128)} copy-done((f32[8,128]{1,0:T(8,128)}, f32[8,128]{1,0:T(8,128)S(1)}, u32[]{:S(2)}) %copy-start.11) | copy-done | bytes 4120
  51.3 0.0 copy-done.6
  51.3 0.0 copy-done.7
  51.3 3.1 %shard_map.92 = f32[4,32,8,128]{3,2,1,0:T(8,128)} custom-call(f32[4,32,8,128]{3,2,1,0:T(8,128)} %get-tuple-element.20.refs_0_, f32[128,128]{1,0:T(8,128)} %copy-done.6, f32[128,128]{1,0:T(8,128)} %copy-done.7, f32[8,128]{1,0:T(8,128)} %copy-done.10, f32[8,128]{1,0:T(8,128)} %copy-done.11, f32[160,128]{1,0:T(8,128)} %copy-done.2, f32[160,128]{1,0:T(8,128)} %copy-done.3, ...), custom_call_target="tpu_custom_call" | custom-call | tf_op jit(solution)/shard_map/pallas_call | solution.py:139
  (43 shorter events, 0.4 us)
Async XLA Ops:
  0.7 0.7 %copy-start.13 = (s32[1,1,1,32]{3,2,1,0:T(1,128)S(1)}, s32[1,1,1,32]{3,2,1,0:T(1,128)}, u32[]{:S(2)}) copy-start(s32[1,1,1,32]{3,2,1,0:T(1,128)} %param.15) | copy-start | bytes 388
  1.5 0.7 %copy-start.9 = (f32[1,1,1,32,128]{4,3,2,1,0:T(8,128)S(1)}, f32[1,1,1,32,128]{4,3,2,1,0:T(8,128)}, u32[]{:S(2)}) copy-start(f32[1,1,1,32,128]{4,3,2,1,0:T(8,128)} %param.17) | copy-start | bytes 49156
  2.2 0.7 %copy-start.15 = (s32[1,1,1,32,1]{3,4,2,1,0:T(1,128)S(1)}, s32[1,1,1,32,1]{3,4,2,1,0:T(1,128)}, u32[]{:S(2)}) copy-start(s32[1,1,1,32,1]{3,4,2,1,0:T(1,128)} %param.14) | copy-start | bytes 388
  2.2 0.8 %copy-start.14 = (s32[1,1,1,32]{3,2,1,0:T(1,128)S(1)}, s32[1,1,1,32]{3,2,1,0:T(1,128)}, u32[]{:S(2)}) copy-start(s32[1,1,1,32]{3,2,1,0:T(1,128)} %param.16) | copy-start | bytes 388
  2.2 1.5 %copy-start = (f32[1,4,32,8,128]{4,3,2,1,0:T(8,128)S(1)}, f32[1,4,32,8,128]{4,3,2,1,0:T(8,128)}, u32[]{:S(2)}) copy-start(f32[1,4,32,8,128]{4,3,2,1,0:T(8,128)} %param.9) | copy-start | bytes 1572868
  5.3 0.9 %copy-start.1 = (f32[1,32,8,128]{3,2,1,0:T(8,128)S(1)}, f32[1,32,8,128]{3,2,1,0:T(8,128)}, u32[]{:S(2)}) copy-start(f32[1,32,8,128]{3,2,1,0:T(8,128)} %param.11) | copy-start | bytes 393220
  8.4 18.3 %all-to-all-start = ((f32[16,7,512]{2,1,0:T(8,128)}), f32[16,7,512]{2,1,0:T(8,128)S(1)}, u32[]{:S(2)}, u32[]{:S(2)}) async-start(f32[16,7,512]{2,1,0:T(8,128)} %copy.50), calls=%async_computation | async-start | bytes 524288 | tf_op jit(solution)/shard_map/all_to_all | solution.py:226
  16.8 14.1 %collective-permute-start = (f32[160,128]{1,0:T(8,128)S(1)}, f32[160,128]{1,0:T(8,128)S(1)}, u32[]{:S(2)}, u32[]{:S(2)}) collective-permute-start(f32[160,128]{1,0:T(8,128)S(1)} %get-tuple-element.15), channel_id=1, source_target_pairs={{0,4},{4,8},{8,12},{1,5},{5,9},{9,13},{2,6},{6,10},{10,14},{3,7},{... | collective-permute-start | bytes 245768 | tf_op jit(solution)/shard_map/ppermute | solution.py:17
  20.6 10.2 %collective-permute-start.1 = (f32[160,128]{1,0:T(8,128)S(1)}, f32[160,128]{1,0:T(8,128)S(1)}, u32[]{:S(2)}, u32[]{:S(2)}) collective-permute-start(f32[160,128]{1,0:T(8,128)S(1)} %get-tuple-element.16), channel_id=1, source_target_pairs={{4,0},{8,4},{12,8},{5,1},{9,5},{13,9},{6,2},{10,6},{14,10},{7,3},{... | collective-permute-start | bytes 245768 | tf_op jit(solution)/shard_map/ppermute | solution.py:17
  21.9 6.7 %collective-permute-start.2 = (f32[8,160]{1,0:T(8,128)S(1)}, f32[8,160]{1,0:T(8,128)S(1)}, u32[]{:S(2)}, u32[]{:S(2)}) collective-permute-start(f32[8,160]{1,0:T(8,128)S(1)} %get-tuple-element.17), channel_id=1, source_target_pairs={{0,1},{1,2},{2,3},{4,5},{5,6},{6,7},{8,9},{9,10},{10,11},{12,13},{... | collective-permute-start | bytes 15368 | tf_op jit(solution)/shard_map/ppermute | solution.py:17
  25.3 5.5 %collective-permute-start.3 = (f32[8,160]{1,0:T(8,128)S(1)}, f32[8,160]{1,0:T(8,128)S(1)}, u32[]{:S(2)}, u32[]{:S(2)}) collective-permute-start(f32[8,160]{1,0:T(8,128)S(1)} %get-tuple-element.18), channel_id=1, source_target_pairs={{1,0},{2,1},{3,2},{5,4},{6,5},{7,6},{9,8},{10,9},{11,10},{13,12},{... | collective-permute-start | bytes 15368 | tf_op jit(solution)/shard_map/ppermute | solution.py:17
  27.3 0.7 %copy-start.12 = (s32[1,8,128]{2,1,0:T(8,128)S(1)}, s32[1,8,128]{2,1,0:T(8,128)}, u32[]{:S(2)}) copy-start(s32[1,8,128]{2,1,0:T(8,128)} %param.13) | copy-start | bytes 12292
  27.3 3.6 %collective-permute-start.4 = (f32[11,512]{1,0:T(8,128)S(1)}, f32[11,512]{1,0:T(8,128)S(1)}, u32[]{:S(2)}, u32[]{:S(2)}) collective-permute-start(f32[11,512]{1,0:T(8,128)S(1)} %pad_maximum_fusion.3), channel_id=1, source_target_pairs={{0,16},{16,0},{1,17},{17,1},{2,18},{18,2},{3,19},{19,3},{4,20},{20... | collective-permute-start | bytes 67592 | tf_op jit(solution)/shard_map/ppermute | solution.py:245
  28.6 2.3 %copy-start.4 = (f32[8,160]{1,0:T(8,128)}, f32[8,160]{1,0:T(8,128)S(1)}, u32[]{:S(2)}) copy-start(f32[8,160]{1,0:T(8,128)S(1)} %collective-permute-done.2.refs_3_.refs_7_) | copy-start | bytes 15364
  30.8 0.6 %copy-start.5 = (f32[8,160]{1,0:T(8,128)}, f32[8,160]{1,0:T(8,128)S(1)}, u32[]{:S(2)}) copy-start(f32[8,160]{1,0:T(8,128)S(1)} %collective-permute-done.3.refs_4_.refs_8_) | copy-start | bytes 15364
  30.8 0.6 %copy-start.2 = (f32[160,128]{1,0:T(8,128)}, f32[160,128]{1,0:T(8,128)S(1)}, u32[]{:S(2)}) copy-start(f32[160,128]{1,0:T(8,128)S(1)} %collective-permute-done.refs_1_.refs_5_) | copy-start | bytes 245764
  30.8 0.7 %copy-start.3 = (f32[160,128]{1,0:T(8,128)}, f32[160,128]{1,0:T(8,128)S(1)}, u32[]{:S(2)}) copy-start(f32[160,128]{1,0:T(8,128)S(1)} %collective-permute-done.1.refs_2_.refs_6_) | copy-start | bytes 245764
  30.9 0.7 %copy-start.8 = (f32[11,512]{1,0:T(8,128)}, f32[11,512]{1,0:T(8,128)S(1)}, u32[]{:S(2)}) copy-start(f32[11,512]{1,0:T(8,128)S(1)} %collective-permute-done.4.refs_13_) | copy-start | bytes 67588
  34.9 10.3 %copy-start.16 = (f32[8,128]{1,0:T(8,128)S(1)}, f32[8,128]{1,0:T(8,128)}, u32[]{:S(2)}) copy-start(f32[8,128]{1,0:T(8,128)} %get-tuple-element.24) | copy-start | bytes 12292
  34.9 15.8 %collective-permute-start.5 = (f32[128,128]{1,0:T(8,128)}, f32[128,128]{1,0:T(8,128)S(1)}, u32[]{:S(2)}, u32[]{:S(2)}) collective-permute-start(f32[128,128]{1,0:T(8,128)} %get-tuple-element.21), channel_id=1, source_target_pairs={{0,4},{4,8},{8,12},{1,5},{5,9},{9,13},{2,6},{6,10},{10,14},{3,7},{... | collective-permute-start | bytes 196616 | tf_op jit(solution)/shard_map/ppermute | solution.py:17
  39.6 11.1 %collective-permute-start.6 = (f32[128,128]{1,0:T(8,128)}, f32[128,128]{1,0:T(8,128)S(1)}, u32[]{:S(2)}, u32[]{:S(2)}) collective-permute-start(f32[128,128]{1,0:T(8,128)} %get-tuple-element.22), channel_id=1, source_target_pairs={{4,0},{8,4},{12,8},{5,1},{9,5},{13,9},{6,2},{10,6},{14,10},{7,3},{... | collective-permute-start | bytes 196616 | tf_op jit(solution)/shard_map/ppermute | solution.py:17
  40.9 5.8 %collective-permute-start.7 = (f32[8,128]{1,0:T(8,128)}, f32[8,128]{1,0:T(8,128)S(1)}, u32[]{:S(2)}, u32[]{:S(2)}) collective-permute-start(f32[8,128]{1,0:T(8,128)} %get-tuple-element.23), channel_id=1, source_target_pairs={{0,1},{1,2},{2,3},{4,5},{5,6},{6,7},{8,9},{9,10},{10,11},{12,13},{... | collective-permute-start | bytes 12296 | tf_op jit(solution)/shard_map/ppermute | solution.py:17
  45.2 5.5 %collective-permute-start.8 = (f32[8,128]{1,0:T(8,128)S(1)}, f32[8,128]{1,0:T(8,128)S(1)}, u32[]{:S(2)}, u32[]{:S(2)}) collective-permute-start(f32[8,128]{1,0:T(8,128)S(1)} %copy-done.16), channel_id=1, source_target_pairs={{1,0},{2,1},{3,2},{5,4},{6,5},{7,6},{9,8},{10,9},{11,10},{13,12},{... | collective-permute-start | bytes 12296 | tf_op jit(solution)/shard_map/ppermute | solution.py:17
  46.7 4.0 %copy-start.10 = (f32[8,128]{1,0:T(8,128)}, f32[8,128]{1,0:T(8,128)S(1)}, u32[]{:S(2)}) copy-start(f32[8,128]{1,0:T(8,128)S(1)} %collective-permute-done.7.refs_3_) | copy-start | bytes 12292
  50.7 0.6 %copy-start.11 = (f32[8,128]{1,0:T(8,128)}, f32[8,128]{1,0:T(8,128)S(1)}, u32[]{:S(2)}) copy-start(f32[8,128]{1,0:T(8,128)S(1)} %collective-permute-done.8.refs_4_) | copy-start | bytes 12292
  50.7 0.6 %copy-start.6 = (f32[128,128]{1,0:T(8,128)}, f32[128,128]{1,0:T(8,128)S(1)}, u32[]{:S(2)}) copy-start(f32[128,128]{1,0:T(8,128)S(1)} %collective-permute-done.5.refs_1_) | copy-start | bytes 196612
  50.7 0.6 %copy-start.7 = (f32[128,128]{1,0:T(8,128)}, f32[128,128]{1,0:T(8,128)S(1)}, u32[]{:S(2)}) copy-start(f32[128,128]{1,0:T(8,128)S(1)} %collective-permute-done.6.refs_2_) | copy-start | bytes 196612

commit v13 on v9

--- a/solution.py
+++ b/solution.py
@@ -186,45 +186,43 @@
     payload = (payload.reshape(count, fields, cols_y) * weights[:, None, :]).reshape(
         count, fields * cols_y
     )
-    keys = targets * rows_x + landing
-    placing = (
-        keys[None, :] == jnp.arange(tiles * rows_x, dtype=jnp.int32)[:, None]
-    ).astype(jnp.float32)
-    summed = jnp.dot(
-        placing, payload, precision=lax.Precision.HIGHEST, preferred_element_type=jnp.float32
-    ).reshape(tiles_x, tiles_y, rows_x, fields, cols_y)
     order_ids = jnp.arange(count, dtype=jnp.int32)
     earlier = (targets[:, None] == targets[None, :]) & (order_ids[None, :] < order_ids[:, None])
     rank_in = jnp.sum(earlier.astype(jnp.int32), axis=1)
-    slot_ids = targets * CAP + rank_in
-    slotting = slot_ids[None, :] == jnp.arange(tiles * CAP, dtype=jnp.int32)[:, None]
-    slots = jnp.dot(
-        slotting.astype(jnp.float32),
-        payload,
-        precision=lax.Precision.HIGHEST,
-        preferred_element_type=jnp.float32,
-    ).reshape(tiles, CAP, fields * cols_y)
-    tags = jnp.sum(slotting.astype(jnp.int32) * (landing + 1)[None, :], axis=1)
-    tags = tags.astype(jnp.float32).reshape(tiles_x, tiles_y, CAP)
-    zero_x = jnp.zeros((1, tiles_y, fields, cols_y), jnp.float32)
-    up_rows = jnp.concatenate([zero_x, summed[:-1, :, rows_x - 1]], 0)
-    dn_rows = jnp.concatenate([summed[1:, :, 0], zero_x], 0)
-    zero_y = jnp.zeros((tiles_x, 1, rows_x, fields), jnp.float32)
-    lf_cols = jnp.concatenate([zero_y, summed[:, :-1, :, :, cols_y - 1]], 1)
-    rt_cols = jnp.concatenate([summed[:, 1:, :, :, 0], zero_y], 1)
+    width = fields * cols_y
     ring = 2 * rows_x * fields
-    side = jnp.concatenate([lf_cols, rt_cols], 3).reshape(tiles_x, tiles_y, ring)
-    side = jnp.concatenate([side, tags], 2)
-    side = jnp.pad(side, ((0, 0), (0, 0), (0, fields * cols_y - ring - CAP)))
-    send_data = jnp.concatenate(
-        [
-            slots,
-            up_rows.reshape(tiles, 1, fields * cols_y),
-            dn_rows.reshape(tiles, 1, fields * cols_y),
-            side.reshape(tiles, 1, fields * cols_y),
-        ],
-        1,
-    )
+    depth = CAP + 3
+    lane = jnp.arange(width, dtype=jnp.int32)[None, :]
+    lf_part = sum(
+        jnp.where(lane == (landing * 2 * fields + f)[:, None], payload[:, f * cols_y + cols_y - 1][:, None], 0.0)
+        for f in range(fields)
+    )
+    rt_part = sum(
+        jnp.where(lane == (landing * 2 * fields + fields + f)[:, None], payload[:, f * cols_y][:, None], 0.0)
+        for f in range(fields)
+    )
+    tag_part = jnp.where(
+        lane == (ring + rank_in)[:, None], (landing + 1).astype(jnp.float32)[:, None], 0.0
+    )
+    sources_all = jnp.concatenate([payload, lf_part, rt_part, tag_part], 0)
+    chunk_row = jnp.arange(tiles * depth, dtype=jnp.int32)[:, None]
+    tile_of = chunk_row // depth
+    part = chunk_row % depth
+    column_of = tile_of % tiles_y
+    to = targets[None, :]
+    blocks = (
+        ((part < CAP) & (to == tile_of) & (rank_in[None, :] == part))
+        | ((part == CAP) & (to == tile_of - tiles_y) & (landing[None, :] == rows_x - 1))
+        | ((part == CAP + 1) & (to == tile_of + tiles_y) & (landing[None, :] == 0))
+    )
+    side_row = part == CAP + 2
+    lf_route = side_row & (to == tile_of - 1) & (column_of > 0)
+    rt_route = side_row & (to == tile_of + 1) & (column_of < tiles_y - 1)
+    tag_route = side_row & (to == tile_of)
+    routing = jnp.concatenate([blocks, lf_route, rt_route, tag_route], 1).astype(jnp.float32)
+    send_data = jnp.dot(
+        routing, sources_all, precision=lax.Precision.HIGHEST, preferred_element_type=jnp.float32
+    ).reshape(tiles, depth, width)
     send_data, *outgoing = lax.optimization_barrier(
         (send_data, row_edge(rows_x - 1), row_edge(0), col_edge(cols_y - 1), col_edge(0))
     )

time: 54.6 us -> 57.3 us (1.049)
  local copies, waits for them, and re-layouts: 7.94 us -> 10 us
  other arithmetic: 1.09 us -> 2.01 us
    slice x1, local copies, waits for them, and re-layouts: 0.08 us -> 1.42 us  [row_edge(): field_rows = adjoint[:, :, index, :].reshape(planes, cols_y)]
    slice x3, local copies, waits for them, and re-layouts: 0.75 us -> 2.07 us  [col_edge(): adjoint[:, :, :, index]]
    add x1 -> x5, other arithmetic: 0.01 us -> 0.97 us  [the longest x1 0.73 us: shards(): landing * 2 * fields + f]
    optimization_barrier x1 -> x0, local copies, waits for them, and re-layouts: 0.84 us -> none  [shards(): lax.optimization_barrier((send_data, row_edge(rows_x - 1), row_edge(0), c...]
    reshape x4 -> x1, local copies, waits for them, and re-layouts: 0.15 us -> 0.73 us  [shards(): send_data = jnp.dot(routing, sources_all, precision=lax.Precision.HIGHEST...]
where the time goes in v13:
time: 57.3 us; the launch traced here: 56.7 us
  starting transfers between devices  29.7 us (52%)
  local copies, waits for them, and re-layouts  10 us (17%)
  waiting for transfers between devices  6.63 us (12%)
  Pallas kernels  6.52 us (11%)
  other arithmetic  2.01 us (4%)
  matrix products  1.43 us (2%)
    ppermute x8, starting transfers between devices, shift(): return lax.ppermute(block, axis, route)  21.3 us
    all_to_all x1, starting transfers between devices, shards(): lax.all_to_all(send_data, ('gx', 'gy'), split_axis=0, concat_axis=0, tile...  8.35 us
    pallas_call x2, Pallas kernels, run_step(): pl.pallas_call(step_kernel(fields, levels, rows, cols, coupled, emit), ou...  6.52 us
    ppermute x8, waiting for transfers between devices, shift(): return lax.ppermute(block, axis, route)  6.48 us
    unnamed x32, local copies, waits for them, and re-layouts  3.72 us
    slice x3, local copies, waits for them, and re-layouts, col_edge(): adjoint[:, :, :, index]  2.07 us
    slice x1, local copies, waits for them, and re-layouts, row_edge(): field_rows = adjoint[:, :, index, :].reshape(planes, cols_y)  1.42 us
  transfers between devices with their start and end apart: 10, of which 4 were waited for; matrix products, arithmetic and copies ran while one was open for 2% of the time, Pallas kernels for 0%

profile of v13, /device:TPU:0, one launch (start us, length us, event | category | flops | bytes accessed | tf_op | source)
XLA Modules:
  0.0 56.7 jit_solution(17565449911842413603)
XLA Ops:
  0.0 0.7 %broadcast_add_fusion.7 = (s32[32]{0:T(128)S(1)}, s32[32]{0:T(128)S(1)}, s32[32]{0:T(128)S(1)}, s32[32]{0:T(128)S(1)}, s32[32]{0:T(128)S(1)}, /*index=5*/s32[32]{0:T(128)S(1)}, s32[32]{0:T(128)S(1)}) fusion(s32[1,1,1,32]{3,2,1,0:T(1,128)} %param.16), kind=kLoop, calls=%fused_computation.85 | loop fusion | flops 256 | bytes 1024 | tf_op jit(solution)/shard_map/add | solution.py:197
  0.9 1.5 %fusion.31 = (f32[4,32,8,1]{3,2,1,0:T(8,128)S(1)}, f32[4,32,8,1]{3,2,1,0:T(8,128)S(1)}) fusion(f32[4,32,8,128]{3,2,1,0:T(8,128)} %bitcast.68), kind=kLoop, calls=%fused_computation.98 | loop fusion | bytes 16384 | tf_op jit(solution)/shard_map/slice | solution.py:167
  2.4 0.0 copy-start.8
  2.4 1.4 %fusion.32 = (f32[4,32,1,128]{3,2,1,0:T(1,128)S(1)}, f32[4,32,1,128]{3,2,1,0:T(1,128)S(1)}) fusion(f32[4,32,8,128]{3,2,1,0:T(8,128)} %bitcast.69), kind=kLoop, calls=%fused_computation.99 | loop fusion | bytes 262144 | tf_op jit(solution)/shard_map/slice | solution.py:163
  3.8 0.0 copy-start.12
  3.8 0.6 %copy-done.12 = s32[1,1,1,32]{3,2,1,0:T(1,128)S(1)} copy-done((s32[1,1,1,32]{3,2,1,0:T(1,128)S(1)}, s32[1,1,1,32]{3,2,1,0:T(1,128)}, u32[]{:S(2)}) %copy-start.12) | copy-done | bytes 152
  4.5 0.9 %fusion = f32[4,4,8,128]{3,2,1,0:T(8,128)S(1)} fusion(f32[32,128]{1,0:T(8,128)S(1)} %bitcast.88, f32[4,32,8,128]{3,2,1,0:T(8,128)} %bitcast.70, s32[32]{0:T(128)S(1)} %bitcast.91), kind=kOutput, calls=%fused_computation.1 | convolution fusion | flops 1589504 | bytes 98432 | tf_op jit(solution)/shard_map/dot_general | solution.py:180
  5.4 0.3 slice_reduce_fusion.8
  5.7 0.0 copy-start.13
  5.7 0.7 %copy-done.13 = s32[1,1,1,32,1]{3,4,2,1,0:T(1,128)S(1)} copy-done((s32[1,1,1,32,1]{3,4,2,1,0:T(1,128)S(1)}, s32[1,1,1,32,1]{3,4,2,1,0:T(1,128)}, u32[]{:S(2)}) %copy-start.13) | copy-done | bytes 152
  6.4 0.2 convert_reduce_fusion
  6.6 0.1 select_add_fusion
  6.7 0.1 select_add_fusion.1
  6.8 0.1 fusion.20
  6.9 0.3 fusion.1
  7.2 0.7 %reshape.181 = f32[16,7,512]{2,1,0:T(8,128)} reshape(f32[112,512]{1,0:T(8,128)S(1)} %fusion.1) | data formatting | bytes 458752 | tf_op jit(solution)/shard_map/reshape | solution.py:225
  7.9 0.3 copy.37
  8.2 0.1 reshape.182
  8.3 0.3 copy.40
  8.6 0.1 reshape.183
  8.7 0.5 copy-done
  9.2 0.1 fusion.33
  9.3 0.1 copy.39
  9.4 0.1 copy.42
  9.6 1.0 %fusion.34 = (f32[32,1,128]{2,1,0:T(1,128)S(1)}, f32[32,1,128]{2,1,0:T(1,128)S(1)}) fusion(f32[32,8,128]{2,1,0:T(8,128)} %bitcast.79), kind=kLoop, calls=%fused_computation.101 | loop fusion | bytes 65536 | tf_op jit(solution)/shard_map/slice | solution.py:164
  10.6 8.4 %all-to-all-start = ((f32[16,7,512]{2,1,0:T(8,128)}), f32[16,7,512]{2,1,0:T(8,128)S(1)}, u32[]{:S(2)}, u32[]{:S(2)}) async-start(f32[16,7,512]{2,1,0:T(8,128)} %reshape.181), calls=%async_computation | async-start | bytes 524288 | tf_op jit(solution)/shard_map/all_to_all | solution.py:229
  19.0 3.8 %collective-permute-start = (f32[160,128]{1,0:T(8,128)S(1)}, f32[160,128]{1,0:T(8,128)S(1)}, u32[]{:S(2)}, u32[]{:S(2)}) collective-permute-start(f32[160,128]{1,0:T(8,128)S(1)} %get-tuple-element.15), channel_id=1, source_target_pairs={{0,4},{4,8},{8,12},{1,5},{5,9},{9,13},{2,6},{6,10},{10,14},{3,7},{... | collective-permute-start | bytes 245768 | tf_op jit(solution)/shard_map/ppermute | solution.py:17
  22.8 1.3 %collective-permute-start.1 = (f32[160,128]{1,0:T(8,128)S(1)}, f32[160,128]{1,0:T(8,128)S(1)}, u32[]{:S(2)}, u32[]{:S(2)}) collective-permute-start(f32[160,128]{1,0:T(8,128)S(1)} %get-tuple-element.16), channel_id=1, source_target_pairs={{4,0},{8,4},{12,8},{5,1},{9,5},{13,9},{6,2},{10,6},{14,10},{7,3},{... | collective-permute-start | bytes 245768 | tf_op jit(solution)/shard_map/ppermute | solution.py:17
  24.1 3.4 %collective-permute-start.2 = (f32[8,160]{1,0:T(8,128)S(1)}, f32[8,160]{1,0:T(8,128)S(1)}, u32[]{:S(2)}, u32[]{:S(2)}) collective-permute-start(f32[8,160]{1,0:T(8,128)S(1)} %get-tuple-element.17), channel_id=1, source_target_pairs={{0,1},{1,2},{2,3},{4,5},{5,6},{6,7},{8,9},{9,10},{10,11},{12,13},{... | collective-permute-start | bytes 15368 | tf_op jit(solution)/shard_map/ppermute | solution.py:17
  27.5 1.3 %collective-permute-start.3 = (f32[8,160]{1,0:T(8,128)S(1)}, f32[8,160]{1,0:T(8,128)S(1)}, u32[]{:S(2)}, u32[]{:S(2)}) collective-permute-start(f32[8,160]{1,0:T(8,128)S(1)} %get-tuple-element.18), channel_id=1, source_target_pairs={{1,0},{2,1},{3,2},{5,4},{6,5},{7,6},{9,8},{10,9},{11,10},{13,12},{... | collective-permute-start | bytes 15368 | tf_op jit(solution)/shard_map/ppermute | solution.py:17
  28.8 0.1 all-to-all-done
  29.0 0.1 slice_reduce_fusion.9
  29.1 0.1 eq.367
  29.2 0.2 fusion.23
  29.4 0.1 slice_reduce_fusion
  29.5 0.0 copy-start.11
  29.5 0.1 collective-permute-start.4
  29.6 0.6 %copy-done.11 = s32[1,8,128]{2,1,0:T(8,128)S(1)} copy-done((s32[1,8,128]{2,1,0:T(8,128)S(1)}, s32[1,8,128]{2,1,0:T(8,128)}, u32[]{:S(2)}) %copy-start.11) | copy-done | bytes 4120
  30.2 0.6 %convert_bitcast_fusion.refs_12_ = f32[8,128]{1,0:T(8,128)} fusion(s32[1,8,128]{2,1,0:T(8,128)S(1)} %copy-done.11), kind=kLoop, calls=%fused_computation.56 | loop fusion | flops 1024 | bytes 8192 | tf_op jit(solution)/shard_map/convert_element_type | solution.py:160
  30.8 0.0 collective-permute-done.2.refs_3_.refs_7_
  30.8 2.3 %collective-permute-done.3.refs_4_.refs_8_ = f32[8,160]{1,0:T(8,128)S(1)} collective-permute-done((f32[8,160]{1,0:T(8,128)S(1)}, f32[8,160]{1,0:T(8,128)S(1)}, u32[]{:S(2)}, u32[]{:S(2)}) %collective-permute-start.3) | collective-permute-done | bytes 5152 | tf_op jit(solution)/shard_map/ppermute | solution.py:17
  33.0 0.0 collective-permute-done.refs_1_.refs_5_
  33.0 0.0 collective-permute-done.1.refs_2_.refs_6_
  33.1 0.0 collective-permute-done.4.refs_13_
  33.1 0.0 copy-start.7
  33.1 0.0 copy-done.3
  33.1 0.5 copy-done.4
  33.6 0.0 copy-done.1
  33.7 0.0 copy-done.2
  33.7 0.0 copy-done.7
  33.7 3.4 %shard_map.91 = (f32[4,32,8,128]{3,2,1,0:T(8,128)}, f32[128,128]{1,0:T(8,128)}, f32[128,128]{1,0:T(8,128)}, f32[8,128]{1,0:T(8,128)}, f32[8,128]{1,0:T(8,128)}) custom-call(f32[4,32,8,128]{3,2,1,0:T(8,128)} %bitcast.71, f32[160,128]{1,0:T(8,128)} %copy-done.1, f32[160,128]{1,0:T(8,128)} %copy-done.2, f32[8,160]{1,0:T(8,128)} %copy-done.3, ...), custom_call_target="tpu_custom_call" | custom-call | tf_op jit(solution)/shard_map/pallas_call | solution.py:139
  37.1 4.7 %collective-permute-start.5 = (f32[128,128]{1,0:T(8,128)}, f32[128,128]{1,0:T(8,128)S(1)}, u32[]{:S(2)}, u32[]{:S(2)}) collective-permute-start(f32[128,128]{1,0:T(8,128)} %get-tuple-element.21), channel_id=1, source_target_pairs={{0,4},{4,8},{8,12},{1,5},{5,9},{9,13},{2,6},{6,10},{10,14},{3,7},{... | collective-permute-start | bytes 196616 | tf_op jit(solution)/shard_map/ppermute | solution.py:17
  41.8 1.3 %collective-permute-start.6 = (f32[128,128]{1,0:T(8,128)}, f32[128,128]{1,0:T(8,128)S(1)}, u32[]{:S(2)}, u32[]{:S(2)}) collective-permute-start(f32[128,128]{1,0:T(8,128)} %get-tuple-element.22), channel_id=1, source_target_pairs={{4,0},{8,4},{12,8},{5,1},{9,5},{13,9},{6,2},{10,6},{14,10},{7,3},{... | collective-permute-start | bytes 196616 | tf_op jit(solution)/shard_map/ppermute | solution.py:17
  43.1 4.3 %collective-permute-start.7 = (f32[8,128]{1,0:T(8,128)}, f32[8,128]{1,0:T(8,128)S(1)}, u32[]{:S(2)}, u32[]{:S(2)}) collective-permute-start(f32[8,128]{1,0:T(8,128)} %get-tuple-element.23), channel_id=1, source_target_pairs={{0,1},{1,2},{2,3},{4,5},{5,6},{6,7},{8,9},{9,10},{10,11},{12,13},{... | collective-permute-start | bytes 12296 | tf_op jit(solution)/shard_map/ppermute | solution.py:17
  47.4 0.0 copy-done.15
  47.4 1.3 %collective-permute-start.8 = (f32[8,128]{1,0:T(8,128)S(1)}, f32[8,128]{1,0:T(8,128)S(1)}, u32[]{:S(2)}, u32[]{:S(2)}) collective-permute-start(f32[8,128]{1,0:T(8,128)S(1)} %copy-done.15), channel_id=1, source_target_pairs={{1,0},{2,1},{3,2},{5,4},{6,5},{7,6},{9,8},{10,9},{11,10},{13,12},{... | collective-permute-start | bytes 12296 | tf_op jit(solution)/shard_map/ppermute | solution.py:17
  48.7 0.2 collective-permute-done.7.refs_3_
  48.9 4.0 %collective-permute-done.8.refs_4_ = f32[8,128]{1,0:T(8,128)S(1)} collective-permute-done((f32[8,128]{1,0:T(8,128)S(1)}, f32[8,128]{1,0:T(8,128)S(1)}, u32[]{:S(2)}, u32[]{:S(2)}) %collective-permute-start.8) | collective-permute-done | bytes 4128 | tf_op jit(solution)/shard_map/ppermute | solution.py:17
  52.9 0.0 collective-permute-done.5.refs_1_
  52.9 0.0 collective-permute-done.6.refs_2_
  52.9 0.6 copy-done.10
  53.5 0.0 copy-done.5
  53.5 0.0 copy-done.6
  53.5 3.1 %shard_map.92 = f32[4,32,8,128]{3,2,1,0:T(8,128)} custom-call(f32[4,32,8,128]{3,2,1,0:T(8,128)} %get-tuple-element.20.refs_0_, f32[128,128]{1,0:T(8,128)} %copy-done.5, f32[128,128]{1,0:T(8,128)} %copy-done.6, f32[8,128]{1,0:T(8,128)} %copy-done.9, f32[8,128]{1,0:T(8,128)} %copy-done.10, f32[160,128]{1,0:T(8,128)} %copy-done.1, f32[160,128]{1,0:T(8,128)} %copy-done.2, ...), custom_call_target="tpu_custom_call" | custom-call | tf_op jit(solution)/shard_map/pallas_call | solution.py:139
  (32 shorter events, 0.3 us)
Async XLA Ops:
  0.0 0.7 %copy-start.14 = (s32[1,1,1,32]{3,2,1,0:T(1,128)S(1)}, s32[1,1,1,32]{3,2,1,0:T(1,128)}, u32[]{:S(2)}) copy-start(s32[1,1,1,32]{3,2,1,0:T(1,128)} %param.16) | copy-start | bytes 388
  2.4 1.4 %copy-start.8 = (f32[1,1,1,32,128]{4,3,2,1,0:T(8,128)S(1)}, f32[1,1,1,32,128]{4,3,2,1,0:T(8,128)}, u32[]{:S(2)}) copy-start(f32[1,1,1,32,128]{4,3,2,1,0:T(8,128)} %param.17) | copy-start | bytes 49156
  3.8 0.7 %copy-start.12 = (s32[1,1,1,32]{3,2,1,0:T(1,128)S(1)}, s32[1,1,1,32]{3,2,1,0:T(1,128)}, u32[]{:S(2)}) copy-start(s32[1,1,1,32]{3,2,1,0:T(1,128)} %param.15) | copy-start | bytes 388
  5.7 0.7 %copy-start.13 = (s32[1,1,1,32,1]{3,4,2,1,0:T(1,128)S(1)}, s32[1,1,1,32,1]{3,4,2,1,0:T(1,128)}, u32[]{:S(2)}) copy-start(s32[1,1,1,32,1]{3,4,2,1,0:T(1,128)} %param.14) | copy-start | bytes 388
  8.3 0.9 %copy-start = (f32[1,32,8,128]{3,2,1,0:T(8,128)S(1)}, f32[1,32,8,128]{3,2,1,0:T(8,128)}, u32[]{:S(2)}) copy-start(f32[1,32,8,128]{3,2,1,0:T(8,128)} %param.11) | copy-start | bytes 393220
  10.6 18.3 %all-to-all-start = ((f32[16,7,512]{2,1,0:T(8,128)}), f32[16,7,512]{2,1,0:T(8,128)S(1)}, u32[]{:S(2)}, u32[]{:S(2)}) async-start(f32[16,7,512]{2,1,0:T(8,128)} %reshape.181), calls=%async_computation | async-start | bytes 524288 | tf_op jit(solution)/shard_map/all_to_all | solution.py:229
  19.0 14.1 %collective-permute-start = (f32[160,128]{1,0:T(8,128)S(1)}, f32[160,128]{1,0:T(8,128)S(1)}, u32[]{:S(2)}, u32[]{:S(2)}) collective-permute-start(f32[160,128]{1,0:T(8,128)S(1)} %get-tuple-element.15), channel_id=1, source_target_pairs={{0,4},{4,8},{8,12},{1,5},{5,9},{9,13},{2,6},{6,10},{10,14},{3,7},{... | collective-permute-start | bytes 245768 | tf_op jit(solution)/shard_map/ppermute | solution.py:17
  22.8 10.2 %collective-permute-start.1 = (f32[160,128]{1,0:T(8,128)S(1)}, f32[160,128]{1,0:T(8,128)S(1)}, u32[]{:S(2)}, u32[]{:S(2)}) collective-permute-start(f32[160,128]{1,0:T(8,128)S(1)} %get-tuple-element.16), channel_id=1, source_target_pairs={{4,0},{8,4},{12,8},{5,1},{9,5},{13,9},{6,2},{10,6},{14,10},{7,3},{... | collective-permute-start | bytes 245768 | tf_op jit(solution)/shard_map/ppermute | solution.py:17
  24.1 6.6 %collective-permute-start.2 = (f32[8,160]{1,0:T(8,128)S(1)}, f32[8,160]{1,0:T(8,128)S(1)}, u32[]{:S(2)}, u32[]{:S(2)}) collective-permute-start(f32[8,160]{1,0:T(8,128)S(1)} %get-tuple-element.17), channel_id=1, source_target_pairs={{0,1},{1,2},{2,3},{4,5},{5,6},{6,7},{8,9},{9,10},{10,11},{12,13},{... | collective-permute-start | bytes 15368 | tf_op jit(solution)/shard_map/ppermute | solution.py:17
  27.5 5.5 %collective-permute-start.3 = (f32[8,160]{1,0:T(8,128)S(1)}, f32[8,160]{1,0:T(8,128)S(1)}, u32[]{:S(2)}, u32[]{:S(2)}) collective-permute-start(f32[8,160]{1,0:T(8,128)S(1)} %get-tuple-element.18), channel_id=1, source_target_pairs={{1,0},{2,1},{3,2},{5,4},{6,5},{7,6},{9,8},{10,9},{11,10},{13,12},{... | collective-permute-start | bytes 15368 | tf_op jit(solution)/shard_map/ppermute | solution.py:17
  29.5 0.7 %copy-start.11 = (s32[1,8,128]{2,1,0:T(8,128)S(1)}, s32[1,8,128]{2,1,0:T(8,128)}, u32[]{:S(2)}) copy-start(s32[1,8,128]{2,1,0:T(8,128)} %param.13) | copy-start | bytes 12292
  29.5 3.6 %collective-permute-start.4 = (f32[11,512]{1,0:T(8,128)S(1)}, f32[11,512]{1,0:T(8,128)S(1)}, u32[]{:S(2)}, u32[]{:S(2)}) collective-permute-start(f32[11,512]{1,0:T(8,128)S(1)} %pad_maximum_fusion.2), channel_id=1, source_target_pairs={{0,16},{16,0},{1,17},{17,1},{2,18},{18,2},{3,19},{19,3},{4,20},{20... | collective-permute-start | bytes 67592 | tf_op jit(solution)/shard_map/ppermute | solution.py:248
  30.8 2.3 %copy-start.3 = (f32[8,160]{1,0:T(8,128)}, f32[8,160]{1,0:T(8,128)S(1)}, u32[]{:S(2)}) copy-start(f32[8,160]{1,0:T(8,128)S(1)} %collective-permute-done.2.refs_3_.refs_7_) | copy-start | bytes 15364
  33.0 0.6 %copy-start.4 = (f32[8,160]{1,0:T(8,128)}, f32[8,160]{1,0:T(8,128)S(1)}, u32[]{:S(2)}) copy-start(f32[8,160]{1,0:T(8,128)S(1)} %collective-permute-done.3.refs_4_.refs_8_) | copy-start | bytes 15364
  33.0 0.6 %copy-start.1 = (f32[160,128]{1,0:T(8,128)}, f32[160,128]{1,0:T(8,128)S(1)}, u32[]{:S(2)}) copy-start(f32[160,128]{1,0:T(8,128)S(1)} %collective-permute-done.refs_1_.refs_5_) | copy-start | bytes 245764
  33.0 0.7 %copy-start.2 = (f32[160,128]{1,0:T(8,128)}, f32[160,128]{1,0:T(8,128)S(1)}, u32[]{:S(2)}) copy-start(f32[160,128]{1,0:T(8,128)S(1)} %collective-permute-done.1.refs_2_.refs_6_) | copy-start | bytes 245764
  33.1 0.7 %copy-start.7 = (f32[11,512]{1,0:T(8,128)}, f32[11,512]{1,0:T(8,128)S(1)}, u32[]{:S(2)}) copy-start(f32[11,512]{1,0:T(8,128)S(1)} %collective-permute-done.4.refs_13_) | copy-start | bytes 67588
  37.1 10.3 %copy-start.15 = (f32[8,128]{1,0:T(8,128)S(1)}, f32[8,128]{1,0:T(8,128)}, u32[]{:S(2)}) copy-start(f32[8,128]{1,0:T(8,128)} %get-tuple-element.24) | copy-start | bytes 12292
  37.1 15.8 %collective-permute-start.5 = (f32[128,128]{1,0:T(8,128)}, f32[128,128]{1,0:T(8,128)S(1)}, u32[]{:S(2)}, u32[]{:S(2)}) collective-permute-start(f32[128,128]{1,0:T(8,128)} %get-tuple-element.21), channel_id=1, source_target_pairs={{0,4},{4,8},{8,12},{1,5},{5,9},{9,13},{2,6},{6,10},{10,14},{3,7},{... | collective-permute-start | bytes 196616 | tf_op jit(solution)/shard_map/ppermute | solution.py:17
  41.8 11.1 %collective-permute-start.6 = (f32[128,128]{1,0:T(8,128)}, f32[128,128]{1,0:T(8,128)S(1)}, u32[]{:S(2)}, u32[]{:S(2)}) collective-permute-start(f32[128,128]{1,0:T(8,128)} %get-tuple-element.22), channel_id=1, source_target_pairs={{4,0},{8,4},{12,8},{5,1},{9,5},{13,9},{6,2},{10,6},{14,10},{7,3},{... | collective-permute-start | bytes 196616 | tf_op jit(solution)/shard_map/ppermute | solution.py:17
  43.1 5.8 %collective-permute-start.7 = (f32[8,128]{1,0:T(8,128)}, f32[8,128]{1,0:T(8,128)S(1)}, u32[]{:S(2)}, u32[]{:S(2)}) collective-permute-start(f32[8,128]{1,0:T(8,128)} %get-tuple-element.23), channel_id=1, source_target_pairs={{0,1},{1,2},{2,3},{4,5},{5,6},{6,7},{8,9},{9,10},{10,11},{12,13},{... | collective-permute-start | bytes 12296 | tf_op jit(solution)/shard_map/ppermute | solution.py:17
  47.4 5.5 %collective-permute-start.8 = (f32[8,128]{1,0:T(8,128)S(1)}, f32[8,128]{1,0:T(8,128)S(1)}, u32[]{:S(2)}, u32[]{:S(2)}) collective-permute-start(f32[8,128]{1,0:T(8,128)S(1)} %copy-done.15), channel_id=1, source_target_pairs={{1,0},{2,1},{3,2},{5,4},{6,5},{7,6},{9,8},{10,9},{11,10},{13,12},{... | collective-permute-start | bytes 12296 | tf_op jit(solution)/shard_map/ppermute | solution.py:17
  48.9 4.0 %copy-start.9 = (f32[8,128]{1,0:T(8,128)}, f32[8,128]{1,0:T(8,128)S(1)}, u32[]{:S(2)}) copy-start(f32[8,128]{1,0:T(8,128)S(1)} %collective-permute-done.7.refs_3_) | copy-start | bytes 12292
  52.9 0.6 %copy-start.10 = (f32[8,128]{1,0:T(8,128)}, f32[8,128]{1,0:T(8,128)S(1)}, u32[]{:S(2)}) copy-start(f32[8,128]{1,0:T(8,128)S(1)} %collective-permute-done.8.refs_4_) | copy-start | bytes 12292
  52.9 0.6 %copy-start.5 = (f32[128,128]{1,0:T(8,128)}, f32[128,128]{1,0:T(8,128)S(1)}, u32[]{:S(2)}) copy-start(f32[128,128]{1,0:T(8,128)S(1)} %collective-permute-done.5.refs_1_) | copy-start | bytes 196612
  52.9 0.7 %copy-start.6 = (f32[128,128]{1,0:T(8,128)}, f32[128,128]{1,0:T(8,128)S(1)}, u32[]{:S(2)}) copy-start(f32[128,128]{1,0:T(8,128)S(1)} %collective-permute-done.6.refs_2_) | copy-start | bytes 196612

commit v14 on v9

--- a/solution.py
+++ b/solution.py
@@ -24,14 +24,16 @@
         refs = list(refs)
         a_ref, up_ref, dn_ref, lf_ref, rt_ref, cu_ref, cd_ref, cl_ref, cr_ref = refs[:9]
         ue_ref, un_ref, k_ref, wet_ref = refs[9:13]
-        refs = refs[13:]
+        refs = refs[13:15] + refs[15:]
+        chain = refs[:2]
+        refs = refs[2:]
         if coupled:
             inc_ref = refs.pop(0)
         out_ref = refs.pop(0)
         if emit:
             eu_ref, ed_ref, el_ref, er_ref = refs[:4]
             refs = refs[4:]
-        c_ref = refs[0]
+        c_ref, inv_ref = chain
         row = lax.broadcasted_iota(jnp.int32, (rows, cols), 0)
         col = lax.broadcasted_iota(jnp.int32, (rows, cols), 1)
         top = row == 0
@@ -77,22 +79,11 @@
                 laplace = a_ip + a_im + a_jp + a_jm - 4.0 * a
                 advect = 0.5 * (ue_m * a_im - ue_p * a_ip) + 0.5 * (un_m * a_jm - un_p * a_jp)
                 h = a + diffusion * laplace + advect
-                if l < levels - 1:
-                    kd = k_ref[f, l]
-                    diagonal = 1.0 + kd
+                if l > 0:
+                    numerator = h + k_ref[f, l - 1] * dprev[f]
                 else:
-                    diagonal = 1.0
-                if l > 0:
-                    kp = k_ref[f, l - 1]
-                    divisor = diagonal + kp + kp * cprev[f]
-                    numerator = h + kp * dprev[f]
-                else:
-                    divisor = diagonal
                     numerator = h
-                if l < levels - 1:
-                    cprev[f] = -kd / divisor
-                    c_ref[f, l] = cprev[f]
-                dprev[f] = numerator / divisor
+                dprev[f] = numerator * inv_ref[f, l]
                 out_ref[f, l] = dprev[f]
         wet = wet_ref[...]
         if emit:
@@ -125,11 +116,43 @@
     return kernel
 
 
-def run_step(a, halos, coef_halos, ue, un, coeffs, wet, inc=None, emit=False):
+def chain_kernel(fields, levels):
+    def kernel(k_ref, c_ref, inv_ref):
+        cprev = [None] * fields
+        for l in range(levels):
+            for f in range(fields):
+                if l < levels - 1:
+                    kd = k_ref[f, l]
+                    diagonal = 1.0 + kd
+                else:
+                    diagonal = 1.0
+                if l > 0:
+                    kp = k_ref[f, l - 1]
+                    divisor = diagonal + kp + kp * cprev[f]
+                else:
+                    divisor = diagonal + jnp.zeros_like(k_ref[f, l])
+                inverse = 1.0 / divisor
+                inv_ref[f, l] = inverse
+                if l < levels - 1:
+                    cprev[f] = -kd * inverse
+                    c_ref[f, l] = cprev[f]
+                else:
+                    c_ref[f, l] = jnp.zeros_like(inverse)
+
+    return kernel
+
+
+def sweep_chain(coeffs):
+    fields, levels = coeffs.shape[:2]
+    shape = jax.ShapeDtypeStruct(coeffs.shape, jnp.float32)
+    return pl.pallas_call(chain_kernel(fields, levels), out_shape=[shape, shape])(coeffs)
+
+
+def run_step(a, halos, coef_halos, ue, un, coeffs, wet, chain, inc=None, emit=False):
     fields, levels, rows, cols = a.shape
     planes = fields * levels
     coupled = inc is not None
-    operands = [a, *halos, *coef_halos, ue, un, coeffs, wet]
+    operands = [a, *halos, *coef_halos, ue, un, coeffs, wet, *chain]
     if coupled:
         operands += list(inc)
     shapes = [jax.ShapeDtypeStruct(a.shape, jnp.float32)]
@@ -139,7 +162,6 @@
     return pl.pallas_call(
         step_kernel(fields, levels, rows, cols, coupled, emit),
         out_shape=shapes,
-        scratch_shapes=[pltpu.VMEM(a.shape, jnp.float32)],
     )(*operands)
 
 
@@ -158,6 +180,7 @@
     north = u_north[0]
     coeffs = diffusivity[0]
     wet = wet_mask[0].astype(jnp.float32)
+    chain = sweep_chain(coeffs)
 
     def row_edge(index):
         field_rows = adjoint[:, :, index, :].reshape(planes, cols_y)
@@ -251,7 +274,7 @@
     inc = (packed,)
 
     middle, last_rows, first_rows, last_cols, first_cols = run_step(
-        adjoint, halos, halos, east, north, coeffs, wet, inc=inc, emit=True
+        adjoint, halos, halos, east, north, coeffs, wet, chain, inc=inc, emit=True
     )
     step_halos = (
         shift(last_rows, "gx", 1),
@@ -259,7 +282,7 @@
         shift(last_cols, "gy", 1),
         shift(first_cols, "gy", -1),
     )
-    (result,) = run_step(middle, step_halos, halos, east, north, coeffs, wet)
+    (result,) = run_step(middle, step_halos, halos, east, north, coeffs, wet, chain)
     return result[None]
 
 

time: 54.6 us -> 57.7 us (1.057)
  the two profiles are of different devices: /device:TPU:0 before, /device:TPU:10 now
where the time goes in v14:
time: 57.7 us; the launch traced here: 57 us
  starting transfers between devices  31 us (54%)
  Pallas kernels  9.51 us (16%)
  local copies, waits for them, and re-layouts  8.77 us (15%)
  waiting for transfers between devices  4.47 us (8%)
  matrix products  1.71 us (3%)
  other arithmetic  1.09 us (2%)
    ppermute x8, starting transfers between devices, shift(): return lax.ppermute(block, axis, route)  23.7 us
    all_to_all x1, starting transfers between devices, shards(): lax.all_to_all(send_data, ('gx', 'gy'), split_axis=0, concat_axis=0, tile...  7.2 us
    pallas_call x2, Pallas kernels, run_step(): pl.pallas_call(step_kernel(fields, levels, rows, cols, coupled, emit), ou...  7.2 us
    ppermute x8, waiting for transfers between devices, shift(): return lax.ppermute(block, axis, route)  4.47 us
    unnamed x32, local copies, waits for them, and re-layouts  3.28 us
    pallas_call x1, Pallas kernels, sweep_chain(): pl.pallas_call(chain_kernel(fields, levels), out_shape=[shape, shape])  2.31 us
    slice x1, local copies, waits for them, and re-layouts, row_edge(): field_rows = adjoint[:, :, index, :].reshape(planes, cols_y)  1.3 us
  transfers between devices with their start and end apart: 10, of which 1 were waited for; matrix products, arithmetic and copies ran while one was open for 2% of the time, Pallas kernels for 4%

profile of v14, /device:TPU:10, one launch (start us, length us, event | category | flops | bytes accessed | tf_op | source)
XLA Modules:
  0.0 57.0 jit_solution(10725571822747880697)
XLA Ops:
  0.0 0.6 %copy-done.12 = s32[1,1,1,32]{3,2,1,0:T(1,128)S(1)} copy-done((s32[1,1,1,32]{3,2,1,0:T(1,128)S(1)}, s32[1,1,1,32]{3,2,1,0:T(1,128)}, u32[]{:S(2)}) %copy-start.12) | copy-done | bytes 152
  0.7 1.0 %convolution_multiply_fusion = f32[32,4,128]{2,0,1:T(8,128)S(1)} fusion(f32[32,128]{1,0:T(8,128)} %bitcast.88, f32[4,32,8,128]{3,2,1,0:T(8,128)} %bitcast.66, s32[32]{0:T(128)S(1)} %bitcast.91), kind=kOutput, calls=%fused_computation | convolution fusion | flops 1589504 | bytes 98432 | tf_op jit(solution)/shard_map/dot_general | solution.py:203
  1.7 0.0 copy-start.14
  1.7 0.0 copy-start.13
  1.7 1.3 %fusion.19 = (f32[4,32,1,128]{3,2,1,0:T(1,128)S(1)}, f32[4,32,1,128]{3,2,1,0:T(1,128)S(1)}) fusion(f32[4,32,8,128]{3,2,1,0:T(8,128)} %bitcast.67), kind=kLoop, calls=%fused_computation.48 | loop fusion | bytes 262144 | tf_op jit(solution)/shard_map/slice | solution.py:186
  3.0 0.0 copy-start
  3.0 0.2 convert_reduce_fusion
  3.3 0.3 fusion
  3.6 0.3 slice_reduce_fusion.1
  4.0 0.1 copy-done
  4.1 0.2 fusion.18
  4.3 0.1 select_reduce_fusion
  4.4 0.1 convert_element_type.31
  4.5 1.0 %fusion.22 = (f32[32,1,128]{2,1,0:T(1,128)S(1)}, f32[32,1,128]{2,1,0:T(1,128)S(1)}) fusion(f32[32,8,128]{2,1,0:T(8,128)} %bitcast.76), kind=kLoop, calls=%fused_computation.51 | loop fusion | bytes 65536 | tf_op jit(solution)/shard_map/slice | solution.py:187
  5.6 0.0 copy-start.1
  5.6 0.1 copy.47
  5.7 0.1 reshape.113
  5.8 0.1 select_maximum_fusion.1
  5.9 0.6 %copy-done.1 = f32[1,32,8,128]{3,2,1,0:T(8,128)S(1)} copy-done((f32[1,32,8,128]{3,2,1,0:T(8,128)S(1)}, f32[1,32,8,128]{3,2,1,0:T(8,128)}, u32[]{:S(2)}) %copy-start.1) | copy-done | bytes 131096
  6.5 0.1 fusion.21
  6.6 0.1 copy.53
  6.8 0.1 copy.50
  6.9 0.3 copy.51
  7.2 0.1 reshape.116
  7.3 0.3 copy.48
  7.6 0.1 reshape.115
  7.6 0.3 fusion.6
  8.0 0.8 %copy.54 = f32[16,7,512]{2,1,0:T(8,128)} copy(f32[16,7,512]{2,0,1:T(8,128)S(1)} %pad_maximum_fusion) | data formatting | bytes 458752 | tf_op jit(solution)/shard_map/optimization_barrier | solution.py:251
  8.8 7.2 %all-to-all-start = ((f32[16,7,512]{2,1,0:T(8,128)}), f32[16,7,512]{2,1,0:T(8,128)S(1)}, u32[]{:S(2)}, u32[]{:S(2)}) async-start(f32[16,7,512]{2,1,0:T(8,128)} %copy.54), calls=%async_computation | async-start | bytes 524288 | tf_op jit(solution)/shard_map/all_to_all | solution.py:254
  16.0 3.4 %collective-permute-start.2 = (f32[8,160]{1,0:T(8,128)S(1)}, f32[8,160]{1,0:T(8,128)S(1)}, u32[]{:S(2)}, u32[]{:S(2)}) collective-permute-start(f32[8,160]{1,0:T(8,128)S(1)} %get-tuple-element.19), channel_id=1, source_target_pairs={{0,1},{1,2},{2,3},{4,5},{5,6},{6,7},{8,9},{9,10},{10,11},{12,13},{... | collective-permute-start | bytes 15368 | tf_op jit(solution)/shard_map/ppermute | solution.py:17
  19.4 2.5 %collective-permute-start.3 = (f32[8,160]{1,0:T(8,128)S(1)}, f32[8,160]{1,0:T(8,128)S(1)}, u32[]{:S(2)}, u32[]{:S(2)}) collective-permute-start(f32[8,160]{1,0:T(8,128)S(1)} %get-tuple-element.20), channel_id=1, source_target_pairs={{1,0},{2,1},{3,2},{5,4},{6,5},{7,6},{9,8},{10,9},{11,10},{13,12},{... | collective-permute-start | bytes 15368 | tf_op jit(solution)/shard_map/ppermute | solution.py:17
  21.8 3.4 %collective-permute-start = (f32[160,128]{1,0:T(8,128)S(1)}, f32[160,128]{1,0:T(8,128)S(1)}, u32[]{:S(2)}, u32[]{:S(2)}) collective-permute-start(f32[160,128]{1,0:T(8,128)S(1)} %get-tuple-element.17), channel_id=1, source_target_pairs={{0,4},{4,8},{8,12},{1,5},{5,9},{9,13},{2,6},{6,10},{10,14},{3,7},{... | collective-permute-start | bytes 245768 | tf_op jit(solution)/shard_map/ppermute | solution.py:17
  25.2 2.5 %collective-permute-start.1 = (f32[160,128]{1,0:T(8,128)S(1)}, f32[160,128]{1,0:T(8,128)S(1)}, u32[]{:S(2)}, u32[]{:S(2)}) collective-permute-start(f32[160,128]{1,0:T(8,128)S(1)} %get-tuple-element.18), channel_id=1, source_target_pairs={{4,0},{8,4},{12,8},{5,1},{9,5},{13,9},{6,2},{10,6},{14,10},{7,3},{... | collective-permute-start | bytes 245768 | tf_op jit(solution)/shard_map/ppermute | solution.py:17
  27.7 0.0 all-to-all-done
  27.7 0.1 slice_reduce_fusion.3
  27.8 0.1 eq.128
  28.0 0.2 fusion.13
  28.2 0.1 slice_reduce_fusion.2
  28.3 0.0 copy-start.11
  28.3 0.1 collective-permute-start.4
  28.4 0.6 %copy-done.11 = s32[1,8,128]{2,1,0:T(8,128)S(1)} copy-done((s32[1,8,128]{2,1,0:T(8,128)S(1)}, s32[1,8,128]{2,1,0:T(8,128)}, u32[]{:S(2)}) %copy-start.11) | copy-done | bytes 4120
  28.9 0.6 %convert_bitcast_fusion.refs_12_ = f32[8,128]{1,0:T(8,128)} fusion(s32[1,8,128]{2,1,0:T(8,128)S(1)} %copy-done.11), kind=kLoop, calls=%fused_computation.34 | loop fusion | flops 1024 | bytes 8192 | tf_op jit(solution)/shard_map/convert_element_type | solution.py:182
  29.5 2.3 %shard_map.91 = (f32[4,32,8,128]{3,2,1,0:T(8,128)}, f32[4,32,8,128]{3,2,1,0:T(8,128)}) custom-call(f32[4,32,8,128]{3,2,1,0:T(8,128)} %bitcast.70), custom_call_target="tpu_custom_call" | custom-call | tf_op jit(solution)/shard_map/pallas_call | solution.py:148
  31.9 0.0 collective-permute-done.2.refs_3_.refs_7_
  31.9 0.0 collective-permute-done.3.refs_4_.refs_8_
  31.9 0.0 collective-permute-done.refs_1_.refs_5_
  31.9 0.0 collective-permute-done.1.refs_2_.refs_6_
  31.9 0.0 collective-permute-done.4.refs_15_
  31.9 0.5 copy-done.4
  32.4 0.0 copy-done.5
  32.5 0.1 copy-done.2
  32.5 0.0 copy-done.3
  32.6 3.7 %shard_map.92 = (f32[4,32,8,128]{3,2,1,0:T(8,128)}, f32[128,128]{1,0:T(8,128)}, f32[128,128]{1,0:T(8,128)}, f32[8,128]{1,0:T(8,128)}, f32[8,128]{1,0:T(8,128)}) custom-call(f32[4,32,8,128]{3,2,1,0:T(8,128)} %bitcast.68, f32[160,128]{1,0:T(8,128)} %copy-done.2, f32[160,128]{1,0:T(8,128)} %copy-done.3, f32[8,160]{1,0:T(8,128)} %copy-done.4, ...), custom_call_target="tpu_custom_call" | custom-call | tf_op jit(solution)/shard_map/pallas_call | solution.py:162
  36.3 3.4 %collective-permute-start.5 = (f32[128,128]{1,0:T(8,128)}, f32[128,128]{1,0:T(8,128)S(1)}, u32[]{:S(2)}, u32[]{:S(2)}) collective-permute-start(f32[128,128]{1,0:T(8,128)} %get-tuple-element.25), channel_id=1, source_target_pairs={{0,4},{4,8},{8,12},{1,5},{5,9},{9,13},{2,6},{6,10},{10,14},{3,7},{... | collective-permute-start | bytes 196616 | tf_op jit(solution)/shard_map/ppermute | solution.py:17
  39.7 2.5 %collective-permute-start.6 = (f32[128,128]{1,0:T(8,128)}, f32[128,128]{1,0:T(8,128)S(1)}, u32[]{:S(2)}, u32[]{:S(2)}) collective-permute-start(f32[128,128]{1,0:T(8,128)} %get-tuple-element.26), channel_id=1, source_target_pairs={{4,0},{8,4},{12,8},{5,1},{9,5},{13,9},{6,2},{10,6},{14,10},{7,3},{... | collective-permute-start | bytes 196616 | tf_op jit(solution)/shard_map/ppermute | solution.py:17
  42.1 4.3 %collective-permute-start.7 = (f32[8,128]{1,0:T(8,128)}, f32[8,128]{1,0:T(8,128)S(1)}, u32[]{:S(2)}, u32[]{:S(2)}) collective-permute-start(f32[8,128]{1,0:T(8,128)} %get-tuple-element.27), channel_id=1, source_target_pairs={{0,1},{1,2},{2,3},{4,5},{5,6},{6,7},{8,9},{9,10},{10,11},{12,13},{... | collective-permute-start | bytes 12296 | tf_op jit(solution)/shard_map/ppermute | solution.py:17
  46.4 1.9 %collective-permute-start.8 = (f32[8,128]{1,0:T(8,128)S(1)}, f32[8,128]{1,0:T(8,128)S(1)}, u32[]{:S(2)}, u32[]{:S(2)}) collective-permute-start(f32[8,128]{1,0:T(8,128)S(1)} %copy-done.15), channel_id=1, source_target_pairs={{1,0},{2,1},{3,2},{5,4},{6,5},{7,6},{9,8},{10,9},{11,10},{13,12},{... | collective-permute-start | bytes 12296 | tf_op jit(solution)/shard_map/ppermute | solution.py:17
  48.4 0.0 collective-permute-done.7.refs_3_
  48.4 4.5 %collective-permute-done.8.refs_4_ = f32[8,128]{1,0:T(8,128)S(1)} collective-permute-done((f32[8,128]{1,0:T(8,128)S(1)}, f32[8,128]{1,0:T(8,128)S(1)}, u32[]{:S(2)}, u32[]{:S(2)}) %collective-permute-start.8) | collective-permute-done | bytes 4128 | tf_op jit(solution)/shard_map/ppermute | solution.py:17
  52.8 0.0 collective-permute-done.5.refs_1_
  52.9 0.6 copy-done.10
  53.4 0.0 copy-done.6
  53.5 0.0 copy-done.7
  53.5 3.5 %shard_map.93 = f32[4,32,8,128]{3,2,1,0:T(8,128)} custom-call(f32[4,32,8,128]{3,2,1,0:T(8,128)} %get-tuple-element.24.refs_0_, f32[128,128]{1,0:T(8,128)} %copy-done.6, f32[128,128]{1,0:T(8,128)} %copy-done.7, f32[8,128]{1,0:T(8,128)} %copy-done.9, f32[8,128]{1,0:T(8,128)} %copy-done.10, f32[160,128]{1,0:T(8,128)} %copy-done.2, f32[160,128]{1,0:T(8,128)} %copy-done.3, ...), custom_call_target="tpu_custom_call" | custom-call | tf_op jit(solution)/shard_map/pallas_call | solution.py:162
  (41 shorter events, 0.4 us)
Async XLA Ops:
  0.0 0.7 %copy-start.12 = (s32[1,1,1,32]{3,2,1,0:T(1,128)S(1)}, s32[1,1,1,32]{3,2,1,0:T(1,128)}, u32[]{:S(2)}) copy-start(s32[1,1,1,32]{3,2,1,0:T(1,128)} %param.15) | copy-start | bytes 388
  1.7 1.3 %copy-start.14 = (s32[1,1,1,32,1]{3,4,2,1,0:T(1,128)S(1)}, s32[1,1,1,32,1]{3,4,2,1,0:T(1,128)}, u32[]{:S(2)}) copy-start(s32[1,1,1,32,1]{3,4,2,1,0:T(1,128)} %param.14) | copy-start | bytes 388
  1.7 1.6 %copy-start.13 = (s32[1,1,1,32]{3,2,1,0:T(1,128)S(1)}, s32[1,1,1,32]{3,2,1,0:T(1,128)}, u32[]{:S(2)}) copy-start(s32[1,1,1,32]{3,2,1,0:T(1,128)} %param.16) | copy-start | bytes 388
  3.0 1.0 %copy-start = (f32[1,4,32,8,128]{4,3,2,1,0:T(8,128)S(1)}, f32[1,4,32,8,128]{4,3,2,1,0:T(8,128)}, u32[]{:S(2)}) copy-start(f32[1,4,32,8,128]{4,3,2,1,0:T(8,128)} %param.9) | copy-start | bytes 1572868
  5.6 0.9 %copy-start.1 = (f32[1,32,8,128]{3,2,1,0:T(8,128)S(1)}, f32[1,32,8,128]{3,2,1,0:T(8,128)}, u32[]{:S(2)}) copy-start(f32[1,32,8,128]{3,2,1,0:T(8,128)} %param.11) | copy-start | bytes 393220
  8.8 18.9 %all-to-all-start = ((f32[16,7,512]{2,1,0:T(8,128)}), f32[16,7,512]{2,1,0:T(8,128)S(1)}, u32[]{:S(2)}, u32[]{:S(2)}) async-start(f32[16,7,512]{2,1,0:T(8,128)} %copy.54), calls=%async_computation | async-start | bytes 524288 | tf_op jit(solution)/shard_map/all_to_all | solution.py:254
  16.0 15.9 %collective-permute-start.2 = (f32[8,160]{1,0:T(8,128)S(1)}, f32[8,160]{1,0:T(8,128)S(1)}, u32[]{:S(2)}, u32[]{:S(2)}) collective-permute-start(f32[8,160]{1,0:T(8,128)S(1)} %get-tuple-element.19), channel_id=1, source_target_pairs={{0,1},{1,2},{2,3},{4,5},{5,6},{6,7},{8,9},{9,10},{10,11},{12,13},{... | collective-permute-start | bytes 15368 | tf_op jit(solution)/shard_map/ppermute | solution.py:17
  19.4 12.5 %collective-permute-start.3 = (f32[8,160]{1,0:T(8,128)S(1)}, f32[8,160]{1,0:T(8,128)S(1)}, u32[]{:S(2)}, u32[]{:S(2)}) collective-permute-start(f32[8,160]{1,0:T(8,128)S(1)} %get-tuple-element.20), channel_id=1, source_target_pairs={{1,0},{2,1},{3,2},{5,4},{6,5},{7,6},{9,8},{10,9},{11,10},{13,12},{... | collective-permute-start | bytes 15368 | tf_op jit(solution)/shard_map/ppermute | solution.py:17
  21.8 10.0 %collective-permute-start = (f32[160,128]{1,0:T(8,128)S(1)}, f32[160,128]{1,0:T(8,128)S(1)}, u32[]{:S(2)}, u32[]{:S(2)}) collective-permute-start(f32[160,128]{1,0:T(8,128)S(1)} %get-tuple-element.17), channel_id=1, source_target_pairs={{0,4},{4,8},{8,12},{1,5},{5,9},{9,13},{2,6},{6,10},{10,14},{3,7},{... | collective-permute-start | bytes 245768 | tf_op jit(solution)/shard_map/ppermute | solution.py:17
  25.2 6.7 %collective-permute-start.1 = (f32[160,128]{1,0:T(8,128)S(1)}, f32[160,128]{1,0:T(8,128)S(1)}, u32[]{:S(2)}, u32[]{:S(2)}) collective-permute-start(f32[160,128]{1,0:T(8,128)S(1)} %get-tuple-element.18), channel_id=1, source_target_pairs={{4,0},{8,4},{12,8},{5,1},{9,5},{13,9},{6,2},{10,6},{14,10},{7,3},{... | collective-permute-start | bytes 245768 | tf_op jit(solution)/shard_map/ppermute | solution.py:17
  28.3 0.7 %copy-start.11 = (s32[1,8,128]{2,1,0:T(8,128)S(1)}, s32[1,8,128]{2,1,0:T(8,128)}, u32[]{:S(2)}) copy-start(s32[1,8,128]{2,1,0:T(8,128)} %param.13) | copy-start | bytes 12292
  28.3 3.6 %collective-permute-start.4 = (f32[11,512]{1,0:T(8,128)S(1)}, f32[11,512]{1,0:T(8,128)S(1)}, u32[]{:S(2)}, u32[]{:S(2)}) collective-permute-start(f32[11,512]{1,0:T(8,128)S(1)} %pad_maximum_fusion.3), channel_id=1, source_target_pairs={{0,16},{16,0},{1,17},{17,1},{2,18},{18,2},{3,19},{19,3},{4,20},{20... | collective-permute-start | bytes 67592 | tf_op jit(solution)/shard_map/ppermute | solution.py:273
  31.9 0.6 %copy-start.4 = (f32[8,160]{1,0:T(8,128)}, f32[8,160]{1,0:T(8,128)S(1)}, u32[]{:S(2)}) copy-start(f32[8,160]{1,0:T(8,128)S(1)} %collective-permute-done.2.refs_3_.refs_7_) | copy-start | bytes 15364
  31.9 0.6 %copy-start.5 = (f32[8,160]{1,0:T(8,128)}, f32[8,160]{1,0:T(8,128)S(1)}, u32[]{:S(2)}) copy-start(f32[8,160]{1,0:T(8,128)S(1)} %collective-permute-done.3.refs_4_.refs_8_) | copy-start | bytes 15364
  31.9 0.6 %copy-start.2 = (f32[160,128]{1,0:T(8,128)}, f32[160,128]{1,0:T(8,128)S(1)}, u32[]{:S(2)}) copy-start(f32[160,128]{1,0:T(8,128)S(1)} %collective-permute-done.refs_1_.refs_5_) | copy-start | bytes 245764
  31.9 0.7 %copy-start.3 = (f32[160,128]{1,0:T(8,128)}, f32[160,128]{1,0:T(8,128)S(1)}, u32[]{:S(2)}) copy-start(f32[160,128]{1,0:T(8,128)S(1)} %collective-permute-done.1.refs_2_.refs_6_) | copy-start | bytes 245764
  31.9 0.6 %copy-start.8 = (f32[11,512]{1,0:T(8,128)}, f32[11,512]{1,0:T(8,128)S(1)}, u32[]{:S(2)}) copy-start(f32[11,512]{1,0:T(8,128)S(1)} %collective-permute-done.4.refs_15_) | copy-start | bytes 67588
  36.3 10.1 %copy-start.15 = (f32[8,128]{1,0:T(8,128)S(1)}, f32[8,128]{1,0:T(8,128)}, u32[]{:S(2)}) copy-start(f32[8,128]{1,0:T(8,128)} %get-tuple-element.28) | copy-start | bytes 12292
  36.3 16.5 %collective-permute-start.5 = (f32[128,128]{1,0:T(8,128)}, f32[128,128]{1,0:T(8,128)S(1)}, u32[]{:S(2)}, u32[]{:S(2)}) collective-permute-start(f32[128,128]{1,0:T(8,128)} %get-tuple-element.25), channel_id=1, source_target_pairs={{0,4},{4,8},{8,12},{1,5},{5,9},{9,13},{2,6},{6,10},{10,14},{3,7},{... | collective-permute-start | bytes 196616 | tf_op jit(solution)/shard_map/ppermute | solution.py:17
  39.7 13.2 %collective-permute-start.6 = (f32[128,128]{1,0:T(8,128)}, f32[128,128]{1,0:T(8,128)S(1)}, u32[]{:S(2)}, u32[]{:S(2)}) collective-permute-start(f32[128,128]{1,0:T(8,128)} %get-tuple-element.26), channel_id=1, source_target_pairs={{4,0},{8,4},{12,8},{5,1},{9,5},{13,9},{6,2},{10,6},{14,10},{7,3},{... | collective-permute-start | bytes 196616 | tf_op jit(solution)/shard_map/ppermute | solution.py:17
  42.1 6.2 %collective-permute-start.7 = (f32[8,128]{1,0:T(8,128)}, f32[8,128]{1,0:T(8,128)S(1)}, u32[]{:S(2)}, u32[]{:S(2)}) collective-permute-start(f32[8,128]{1,0:T(8,128)} %get-tuple-element.27), channel_id=1, source_target_pairs={{0,1},{1,2},{2,3},{4,5},{5,6},{6,7},{8,9},{9,10},{10,11},{12,13},{... | collective-permute-start | bytes 12296 | tf_op jit(solution)/shard_map/ppermute | solution.py:17
  46.4 6.4 %collective-permute-start.8 = (f32[8,128]{1,0:T(8,128)S(1)}, f32[8,128]{1,0:T(8,128)S(1)}, u32[]{:S(2)}, u32[]{:S(2)}) collective-permute-start(f32[8,128]{1,0:T(8,128)S(1)} %copy-done.15), channel_id=1, source_target_pairs={{1,0},{2,1},{3,2},{5,4},{6,5},{7,6},{9,8},{10,9},{11,10},{13,12},{... | collective-permute-start | bytes 12296 | tf_op jit(solution)/shard_map/ppermute | solution.py:17
  48.4 4.5 %copy-start.9 = (f32[8,128]{1,0:T(8,128)}, f32[8,128]{1,0:T(8,128)S(1)}, u32[]{:S(2)}) copy-start(f32[8,128]{1,0:T(8,128)S(1)} %collective-permute-done.7.refs_3_) | copy-start | bytes 12292
  52.8 0.6 %copy-start.10 = (f32[8,128]{1,0:T(8,128)}, f32[8,128]{1,0:T(8,128)S(1)}, u32[]{:S(2)}) copy-start(f32[8,128]{1,0:T(8,128)S(1)} %collective-permute-done.8.refs_4_) | copy-start | bytes 12292
  52.8 0.6 %copy-start.6 = (f32[128,128]{1,0:T(8,128)}, f32[128,128]{1,0:T(8,128)S(1)}, u32[]{:S(2)}) copy-start(f32[128,128]{1,0:T(8,128)S(1)} %collective-permute-done.5.refs_1_) | copy-start | bytes 196612
  52.8 0.7 %copy-start.7 = (f32[128,128]{1,0:T(8,128)}, f32[128,128]{1,0:T(8,128)S(1)}, u32[]{:S(2)}) copy-start(f32[128,128]{1,0:T(8,128)S(1)} %collective-permute-done.6.refs_2_) | copy-start | bytes 196612

commit v15 on v9

--- a/solution.py
+++ b/solution.py
@@ -125,6 +125,56 @@
     return kernel
 
 
+def fix_kernel(fields, levels, rows, cols):
+    planes = fields * levels
+
+    def kernel(z_ref, rt_ref, cr_ref, k_ref, wet_ref, out_ref, c_ref):
+        col = lax.broadcasted_iota(jnp.int32, (rows, cols), 1)
+        right = col == cols - 1
+        cprev = [None] * fields
+        dprev = [None] * fields
+        for l in range(levels):
+            un_p = cr_ref[:, pl.ds(planes + l, 1)]
+            for f in range(fields):
+                rt = rt_ref[:, pl.ds(f * levels + l, 1)]
+                h = jnp.where(right, diffusion * rt - 0.5 * (un_p * rt), 0.0)
+                if l < levels - 1:
+                    kd = k_ref[f, l]
+                    diagonal = 1.0 + kd
+                else:
+                    diagonal = 1.0
+                if l > 0:
+                    kp = k_ref[f, l - 1]
+                    divisor = diagonal + kp + kp * cprev[f]
+                    numerator = h + kp * dprev[f]
+                else:
+                    divisor = diagonal
+                    numerator = h
+                if l < levels - 1:
+                    cprev[f] = -kd / divisor
+                    c_ref[f, l] = cprev[f]
+                dprev[f] = numerator / divisor
+                out_ref[f, l] = dprev[f]
+        wet = wet_ref[...]
+        for f in range(fields):
+            r = dprev[f]
+            for l in range(levels - 1, -1, -1):
+                if l < levels - 1:
+                    r = out_ref[f, l] - c_ref[f, l] * r
+                out_ref[f, l] = z_ref[f, l] + r * wet
+
+    return kernel
+
+
+def add_right_halo(z, rt, coef_rt, coeffs, wet):
+    fields, levels, rows, cols = z.shape
+    return pl.pallas_call(
+        fix_kernel(fields, levels, rows, cols),
+        out_shape=jax.ShapeDtypeStruct(z.shape, jnp.float32),
+        scratch_shapes=[pltpu.VMEM(z.shape, jnp.float32)],
+    )(z, rt, coef_rt, coeffs, wet)
+
+
 def run_step(a, halos, coef_halos, ue, un, coeffs, wet, inc=None, emit=False):
     fields, levels, rows, cols = a.shape
     planes = fields * levels
@@ -259,7 +309,9 @@
         shift(last_cols, "gy", 1),
         shift(first_cols, "gy", -1),
     )
-    (result,) = run_step(middle, step_halos, halos, east, north, coeffs, wet)
+    partial_halos = step_halos[:3] + (jnp.zeros_like(step_halos[3]),)
+    (partial,) = run_step(middle, partial_halos, halos, east, north, coeffs, wet)
+    result = add_right_halo(partial, step_halos[3], halos[3], coeffs, wet)
     return result[None]
 
 

time: 54.6 us -> 56.9 us (1.042)
  the two profiles are of different devices: /device:TPU:0 before, /device:TPU:12 now
where the time goes in v15:
time: 56.9 us; the launch traced here: 56.3 us
  starting transfers between devices  31.6 us (56%)
  Pallas kernels  10.8 us (19%)
  local copies, waits for them, and re-layouts  8.42 us (15%)
  waiting for transfers between devices  2.15 us (4%)
  matrix products  1.7 us (3%)
  other arithmetic  1.09 us (2%)
    ppermute x8, starting transfers between devices, shift(): return lax.ppermute(block, axis, route)  24.4 us
    all_to_all x1, starting transfers between devices, shards(): lax.all_to_all(send_data, ('gx', 'gy'), split_axis=0, concat_axis=0, tile...  7.17 us
    pallas_call x2, Pallas kernels, run_step(): pl.pallas_call(step_kernel(fields, levels, rows, cols, coupled, emit), ou...  6.53 us
    pallas_call x1, Pallas kernels, add_right_halo(): pl.pallas_call(fix_kernel(fields, levels, rows, cols), out_shape=jax.Shap...  4.31 us
    unnamed x33, local copies, waits for them, and re-layouts  3.91 us
    ppermute x8, waiting for transfers between devices, shift(): return lax.ppermute(block, axis, route)  2.14 us
  transfers between devices with their start and end apart: 10, of which 1 were waited for; matrix products, arithmetic and copies ran while one was open for 3% of the time, Pallas kernels for 6%

profile of v15, /device:TPU:12, one launch (start us, length us, event | category | flops | bytes accessed | tf_op | source)
XLA Modules:
  0.0 56.3 jit_solution(5916672345782503253)
XLA Ops:
  0.0 0.7 %copy-done.12 = s32[1,1,1,32]{3,2,1,0:T(1,128)S(1)} copy-done((s32[1,1,1,32]{3,2,1,0:T(1,128)S(1)}, s32[1,1,1,32]{3,2,1,0:T(1,128)}, u32[]{:S(2)}) %copy-start.12) | copy-done | bytes 152
  0.7 1.0 %convolution_multiply_fusion = f32[32,4,128]{2,0,1:T(8,128)S(1)} fusion(f32[32,128]{1,0:T(8,128)} %bitcast.92, f32[4,32,8,128]{3,2,1,0:T(8,128)} %bitcast.70, s32[32]{0:T(128)S(1)} %bitcast.93), kind=kOutput, calls=%fused_computation | convolution fusion | flops 1589504 | bytes 98432 | tf_op jit(solution)/shard_map/dot_general | solution.py:230
  1.6 0.0 copy-start.14
  1.7 0.0 copy-start.13
  1.7 0.0 copy-start
  1.7 0.6 %copy-done.14 = s32[1,1,1,32,1]{3,4,2,1,0:T(1,128)S(1)} copy-done((s32[1,1,1,32,1]{3,4,2,1,0:T(1,128)S(1)}, s32[1,1,1,32,1]{3,4,2,1,0:T(1,128)}, u32[]{:S(2)}) %copy-start.14) | copy-done | bytes 152
  2.3 0.2 convert_reduce_fusion
  2.5 0.3 fusion
  2.8 0.3 slice_reduce_fusion.1
  3.2 0.1 fusion.19
  3.3 0.2 fusion.18
  3.6 0.1 copy.51
  3.6 0.1 reshape.113
  3.7 0.1 select_reduce_fusion
  3.8 0.1 convert_element_type.31
  3.9 0.1 select_maximum_fusion.1
  4.2 1.0 %fusion.21 = (f32[32,1,128]{2,1,0:T(1,128)S(1)}, f32[32,1,128]{2,1,0:T(1,128)S(1)}) fusion(f32[32,8,128]{2,1,0:T(8,128)} %bitcast.79), kind=kLoop, calls=%fused_computation.52 | loop fusion | bytes 65536 | tf_op jit(solution)/shard_map/slice | solution.py:214
  5.2 0.3 copy.52
  5.4 0.1 reshape.115
  5.5 0.3 copy.55
  5.8 0.1 reshape.116
  5.9 0.5 copy-done.1
  6.4 0.2 copy.54
  6.7 0.3 fusion.6
  7.0 0.8 %copy.57 = f32[16,7,512]{2,1,0:T(8,128)} copy(f32[16,7,512]{2,0,1:T(8,128)S(1)} %pad_maximum_fusion) | data formatting | bytes 458752 | tf_op jit(solution)/shard_map/optimization_barrier | solution.py:278
  7.9 7.2 %all-to-all-start = ((f32[16,7,512]{2,1,0:T(8,128)}), f32[16,7,512]{2,1,0:T(8,128)S(1)}, u32[]{:S(2)}, u32[]{:S(2)}) async-start(f32[16,7,512]{2,1,0:T(8,128)} %copy.57), calls=%async_computation | async-start | bytes 524288 | tf_op jit(solution)/shard_map/all_to_all | solution.py:281
  15.0 3.4 %collective-permute-start.3 = (f32[8,160]{1,0:T(8,128)S(1)}, f32[8,160]{1,0:T(8,128)S(1)}, u32[]{:S(2)}, u32[]{:S(2)}) collective-permute-start(f32[8,160]{1,0:T(8,128)S(1)} %get-tuple-element.18), channel_id=1, source_target_pairs={{1,0},{2,1},{3,2},{5,4},{6,5},{7,6},{9,8},{10,9},{11,10},{13,12},{... | collective-permute-start | bytes 15368 | tf_op jit(solution)/shard_map/ppermute | solution.py:17
  18.4 3.4 %collective-permute-start = (f32[160,128]{1,0:T(8,128)S(1)}, f32[160,128]{1,0:T(8,128)S(1)}, u32[]{:S(2)}, u32[]{:S(2)}) collective-permute-start(f32[160,128]{1,0:T(8,128)S(1)} %get-tuple-element.15), channel_id=1, source_target_pairs={{0,4},{4,8},{8,12},{1,5},{5,9},{9,13},{2,6},{6,10},{10,14},{3,7},{... | collective-permute-start | bytes 245768 | tf_op jit(solution)/shard_map/ppermute | solution.py:17
  21.8 2.5 %collective-permute-start.1 = (f32[160,128]{1,0:T(8,128)S(1)}, f32[160,128]{1,0:T(8,128)S(1)}, u32[]{:S(2)}, u32[]{:S(2)}) collective-permute-start(f32[160,128]{1,0:T(8,128)S(1)} %get-tuple-element.16), channel_id=1, source_target_pairs={{4,0},{8,4},{12,8},{5,1},{9,5},{13,9},{6,2},{10,6},{14,10},{7,3},{... | collective-permute-start | bytes 245768 | tf_op jit(solution)/shard_map/ppermute | solution.py:17
  24.3 2.5 %collective-permute-start.2 = (f32[8,160]{1,0:T(8,128)S(1)}, f32[8,160]{1,0:T(8,128)S(1)}, u32[]{:S(2)}, u32[]{:S(2)}) collective-permute-start(f32[8,160]{1,0:T(8,128)S(1)} %get-tuple-element.17), channel_id=1, source_target_pairs={{0,1},{1,2},{2,3},{4,5},{5,6},{6,7},{8,9},{9,10},{10,11},{12,13},{... | collective-permute-start | bytes 15368 | tf_op jit(solution)/shard_map/ppermute | solution.py:17
  26.7 0.0 all-to-all-done
  26.8 0.1 slice_reduce_fusion.3
  26.9 0.1 eq.128
  27.0 0.2 fusion.13
  27.2 0.1 slice_reduce_fusion.2
  27.3 0.0 copy-start.11
  27.3 0.1 collective-permute-start.4
  27.4 0.6 %copy-done.11 = s32[1,8,128]{2,1,0:T(8,128)S(1)} copy-done((s32[1,8,128]{2,1,0:T(8,128)S(1)}, s32[1,8,128]{2,1,0:T(8,128)}, u32[]{:S(2)}) %copy-start.11) | copy-done | bytes 4120
  28.0 0.6 %convert_bitcast_fusion.refs_12_.wet_ref = f32[8,128]{1,0:T(8,128)} fusion(s32[1,8,128]{2,1,0:T(8,128)S(1)} %copy-done.11), kind=kLoop, calls=%fused_computation.36 | loop fusion | flops 1024 | bytes 8192 | tf_op jit(solution)/shard_map/convert_element_type | solution.py:210
  28.6 0.0 collective-permute-done.3.refs_4_.refs_8_.cr_ref
  28.6 2.1 %collective-permute-done.2.refs_3_.refs_7_ = f32[8,160]{1,0:T(8,128)S(1)} collective-permute-done((f32[8,160]{1,0:T(8,128)S(1)}, f32[8,160]{1,0:T(8,128)S(1)}, u32[]{:S(2)}, u32[]{:S(2)}) %collective-permute-start.2) | collective-permute-done | bytes 5152 | tf_op jit(solution)/shard_map/ppermute | solution.py:17
  30.7 0.0 collective-permute-done.refs_1_.refs_5_
  30.7 0.0 collective-permute-done.1.refs_2_.refs_6_
  30.7 0.0 collective-permute-done.4.refs_13_
  30.7 0.0 copy-start.8
  30.8 0.0 copy-done.4
  30.8 0.5 copy-done.5
  31.3 0.1 copy-done.2
  31.4 0.0 copy-done.3
  31.4 0.0 copy-done.8
  31.4 3.4 %shard_map.91 = (f32[4,32,8,128]{3,2,1,0:T(8,128)}, f32[128,128]{1,0:T(8,128)}, f32[128,128]{1,0:T(8,128)}, f32[8,128]{1,0:T(8,128)}, f32[8,128]{1,0:T(8,128)}) custom-call(f32[4,32,8,128]{3,2,1,0:T(8,128)} %bitcast.71, f32[160,128]{1,0:T(8,128)} %copy-done.2, f32[160,128]{1,0:T(8,128)} %copy-done.3, f32[8,160]{1,0:T(8,128)} %copy-done.5, ...), custom_call_target="tpu_custom_call" | custom-call | tf_op jit(solution)/shard_map/pallas_call | solution.py:189
  34.8 3.5 %collective-permute-start.5 = (f32[128,128]{1,0:T(8,128)}, f32[128,128]{1,0:T(8,128)S(1)}, u32[]{:S(2)}, u32[]{:S(2)}) collective-permute-start(f32[128,128]{1,0:T(8,128)} %get-tuple-element.21), channel_id=1, source_target_pairs={{0,4},{4,8},{8,12},{1,5},{5,9},{9,13},{2,6},{6,10},{10,14},{3,7},{... | collective-permute-start | bytes 196616 | tf_op jit(solution)/shard_map/ppermute | solution.py:17
  38.3 2.5 %collective-permute-start.6 = (f32[128,128]{1,0:T(8,128)}, f32[128,128]{1,0:T(8,128)S(1)}, u32[]{:S(2)}, u32[]{:S(2)}) collective-permute-start(f32[128,128]{1,0:T(8,128)} %get-tuple-element.22), channel_id=1, source_target_pairs={{4,0},{8,4},{12,8},{5,1},{9,5},{13,9},{6,2},{10,6},{14,10},{7,3},{... | collective-permute-start | bytes 196616 | tf_op jit(solution)/shard_map/ppermute | solution.py:17
  40.8 1.9 %collective-permute-start.7 = (f32[8,128]{1,0:T(8,128)}, f32[8,128]{1,0:T(8,128)S(1)}, u32[]{:S(2)}, u32[]{:S(2)}) collective-permute-start(f32[8,128]{1,0:T(8,128)} %get-tuple-element.23), channel_id=1, source_target_pairs={{0,1},{1,2},{2,3},{4,5},{5,6},{6,7},{8,9},{9,10},{10,11},{12,13},{... | collective-permute-start | bytes 12296 | tf_op jit(solution)/shard_map/ppermute | solution.py:17
  42.7 4.8 %collective-permute-start.8 = (f32[8,128]{1,0:T(8,128)S(1)}, f32[8,128]{1,0:T(8,128)S(1)}, u32[]{:S(2)}, u32[]{:S(2)}) collective-permute-start(f32[8,128]{1,0:T(8,128)S(1)} %copy-done.15), channel_id=1, source_target_pairs={{1,0},{2,1},{3,2},{5,4},{6,5},{7,6},{9,8},{10,9},{11,10},{13,12},{... | collective-permute-start | bytes 12296 | tf_op jit(solution)/shard_map/ppermute | solution.py:17
  47.5 0.0 collective-permute-done.7.refs_3_
  47.5 0.0 collective-permute-done.5.refs_1_
  47.6 0.0 collective-permute-done.6.refs_2_
  47.6 0.6 %broadcast_in_dim.4.refs_4_ = f32[8,128]{1,0:T(8,128)} broadcast(f32[]{:T(128)} %constant.18.clone.1), dimensions={} | broadcast | bytes 4100 | tf_op jit(solution)/shard_map/broadcast_in_dim | solution.py:312
  48.2 0.0 copy-done.7
  48.2 3.1 %shard_map.92.z_ref = f32[4,32,8,128]{3,2,1,0:T(8,128)} custom-call(f32[4,32,8,128]{3,2,1,0:T(8,128)} %get-tuple-element.20.refs_0_, f32[128,128]{1,0:T(8,128)} %copy-done.6, f32[128,128]{1,0:T(8,128)} %copy-done.7, f32[8,128]{1,0:T(8,128)} %copy-done.10, f32[8,128]{1,0:T(8,128)} %broadcast_in_dim.4.refs_4_, f32[160,128]{1,0:T(8,128)} %copy-done.2, ...), custom_call_target="tpu_custom_call" | custom-call | tf_op jit(solution)/shard_map/pallas_call | solution.py:189
  51.4 0.0 collective-permute-done.8.rt_ref
  51.4 0.6 %copy-done.9 = f32[8,128]{1,0:T(8,128)} copy-done((f32[8,128]{1,0:T(8,128)}, f32[8,128]{1,0:T(8,128)S(1)}, u32[]{:S(2)}) %copy-start.9) | copy-done | bytes 4120
  52.0 4.3 %shard_map.93 = f32[4,32,8,128]{3,2,1,0:T(8,128)} custom-call(f32[4,32,8,128]{3,2,1,0:T(8,128)} %shard_map.92.z_ref, f32[8,128]{1,0:T(8,128)} %copy-done.9, f32[8,160]{1,0:T(8,128)} %copy-done.4, f32[4,32,8,128]{3,2,1,0:T(8,128)} %bitcast.76, f32[8,128]{1,0:T(8,128)} %convert_bitcast_fusion.refs_12_.wet_ref), custom_call_target="tpu_custom_call" | custom-call | tf_op jit(solution)/shard_map/pallas_call | solution.py:171
  (41 shorter events, 0.4 us)
Async XLA Ops:
  0.0 0.7 %copy-start.12 = (s32[1,1,1,32]{3,2,1,0:T(1,128)S(1)}, s32[1,1,1,32]{3,2,1,0:T(1,128)}, u32[]{:S(2)}) copy-start(s32[1,1,1,32]{3,2,1,0:T(1,128)} %param.15) | copy-start | bytes 388
  1.6 0.7 %copy-start.14 = (s32[1,1,1,32,1]{3,4,2,1,0:T(1,128)S(1)}, s32[1,1,1,32,1]{3,4,2,1,0:T(1,128)}, u32[]{:S(2)}) copy-start(s32[1,1,1,32,1]{3,4,2,1,0:T(1,128)} %param.14) | copy-start | bytes 388
  1.7 0.8 %copy-start.13 = (s32[1,1,1,32]{3,2,1,0:T(1,128)S(1)}, s32[1,1,1,32]{3,2,1,0:T(1,128)}, u32[]{:S(2)}) copy-start(s32[1,1,1,32]{3,2,1,0:T(1,128)} %param.16) | copy-start | bytes 388
  1.7 1.5 %copy-start = (f32[1,4,32,8,128]{4,3,2,1,0:T(8,128)S(1)}, f32[1,4,32,8,128]{4,3,2,1,0:T(8,128)}, u32[]{:S(2)}) copy-start(f32[1,4,32,8,128]{4,3,2,1,0:T(8,128)} %param.9) | copy-start | bytes 1572868
  5.5 0.9 %copy-start.1 = (f32[1,32,8,128]{3,2,1,0:T(8,128)S(1)}, f32[1,32,8,128]{3,2,1,0:T(8,128)}, u32[]{:S(2)}) copy-start(f32[1,32,8,128]{3,2,1,0:T(8,128)} %param.11) | copy-start | bytes 393220
  7.9 18.9 %all-to-all-start = ((f32[16,7,512]{2,1,0:T(8,128)}), f32[16,7,512]{2,1,0:T(8,128)S(1)}, u32[]{:S(2)}, u32[]{:S(2)}) async-start(f32[16,7,512]{2,1,0:T(8,128)} %copy.57), calls=%async_computation | async-start | bytes 524288 | tf_op jit(solution)/shard_map/all_to_all | solution.py:281
  15.0 13.5 %collective-permute-start.3 = (f32[8,160]{1,0:T(8,128)S(1)}, f32[8,160]{1,0:T(8,128)S(1)}, u32[]{:S(2)}, u32[]{:S(2)}) collective-permute-start(f32[8,160]{1,0:T(8,128)S(1)} %get-tuple-element.18), channel_id=1, source_target_pairs={{1,0},{2,1},{3,2},{5,4},{6,5},{7,6},{9,8},{10,9},{11,10},{13,12},{... | collective-permute-start | bytes 15368 | tf_op jit(solution)/shard_map/ppermute | solution.py:17
  18.4 12.3 %collective-permute-start = (f32[160,128]{1,0:T(8,128)S(1)}, f32[160,128]{1,0:T(8,128)S(1)}, u32[]{:S(2)}, u32[]{:S(2)}) collective-permute-start(f32[160,128]{1,0:T(8,128)S(1)} %get-tuple-element.15), channel_id=1, source_target_pairs={{0,4},{4,8},{8,12},{1,5},{5,9},{9,13},{2,6},{6,10},{10,14},{3,7},{... | collective-permute-start | bytes 245768 | tf_op jit(solution)/shard_map/ppermute | solution.py:17
  21.8 8.9 %collective-permute-start.1 = (f32[160,128]{1,0:T(8,128)S(1)}, f32[160,128]{1,0:T(8,128)S(1)}, u32[]{:S(2)}, u32[]{:S(2)}) collective-permute-start(f32[160,128]{1,0:T(8,128)S(1)} %get-tuple-element.16), channel_id=1, source_target_pairs={{4,0},{8,4},{12,8},{5,1},{9,5},{13,9},{6,2},{10,6},{14,10},{7,3},{... | collective-permute-start | bytes 245768 | tf_op jit(solution)/shard_map/ppermute | solution.py:17
  24.3 6.4 %collective-permute-start.2 = (f32[8,160]{1,0:T(8,128)S(1)}, f32[8,160]{1,0:T(8,128)S(1)}, u32[]{:S(2)}, u32[]{:S(2)}) collective-permute-start(f32[8,160]{1,0:T(8,128)S(1)} %get-tuple-element.17), channel_id=1, source_target_pairs={{0,1},{1,2},{2,3},{4,5},{5,6},{6,7},{8,9},{9,10},{10,11},{12,13},{... | collective-permute-start | bytes 15368 | tf_op jit(solution)/shard_map/ppermute | solution.py:17
  27.3 0.7 %copy-start.11 = (s32[1,8,128]{2,1,0:T(8,128)S(1)}, s32[1,8,128]{2,1,0:T(8,128)}, u32[]{:S(2)}) copy-start(s32[1,8,128]{2,1,0:T(8,128)} %param.13) | copy-start | bytes 12292
  27.3 3.4 %collective-permute-start.4 = (f32[11,512]{1,0:T(8,128)S(1)}, f32[11,512]{1,0:T(8,128)S(1)}, u32[]{:S(2)}, u32[]{:S(2)}) collective-permute-start(f32[11,512]{1,0:T(8,128)S(1)} %pad_maximum_fusion.3), channel_id=1, source_target_pairs={{0,16},{16,0},{1,17},{17,1},{2,18},{18,2},{3,19},{19,3},{4,20},{20... | collective-permute-start | bytes 67592 | tf_op jit(solution)/shard_map/ppermute | solution.py:300
  28.6 2.2 %copy-start.4 = (f32[8,160]{1,0:T(8,128)}, f32[8,160]{1,0:T(8,128)S(1)}, u32[]{:S(2)}) copy-start(f32[8,160]{1,0:T(8,128)S(1)} %collective-permute-done.3.refs_4_.refs_8_.cr_ref) | copy-start | bytes 15364
  30.7 0.6 %copy-start.5 = (f32[8,160]{1,0:T(8,128)}, f32[8,160]{1,0:T(8,128)S(1)}, u32[]{:S(2)}) copy-start(f32[8,160]{1,0:T(8,128)S(1)} %collective-permute-done.2.refs_3_.refs_7_) | copy-start | bytes 15364
  30.7 0.6 %copy-start.2 = (f32[160,128]{1,0:T(8,128)}, f32[160,128]{1,0:T(8,128)S(1)}, u32[]{:S(2)}) copy-start(f32[160,128]{1,0:T(8,128)S(1)} %collective-permute-done.refs_1_.refs_5_) | copy-start | bytes 245764
  30.7 0.7 %copy-start.3 = (f32[160,128]{1,0:T(8,128)}, f32[160,128]{1,0:T(8,128)S(1)}, u32[]{:S(2)}) copy-start(f32[160,128]{1,0:T(8,128)S(1)} %collective-permute-done.1.refs_2_.refs_6_) | copy-start | bytes 245764
  30.7 0.7 %copy-start.8 = (f32[11,512]{1,0:T(8,128)}, f32[11,512]{1,0:T(8,128)S(1)}, u32[]{:S(2)}) copy-start(f32[11,512]{1,0:T(8,128)S(1)} %collective-permute-done.4.refs_13_) | copy-start | bytes 67588
  34.8 7.9 %copy-start.15 = (f32[8,128]{1,0:T(8,128)S(1)}, f32[8,128]{1,0:T(8,128)}, u32[]{:S(2)}) copy-start(f32[8,128]{1,0:T(8,128)} %get-tuple-element.24) | copy-start | bytes 12292
  34.8 12.8 %collective-permute-start.5 = (f32[128,128]{1,0:T(8,128)}, f32[128,128]{1,0:T(8,128)S(1)}, u32[]{:S(2)}, u32[]{:S(2)}) collective-permute-start(f32[128,128]{1,0:T(8,128)} %get-tuple-element.21), channel_id=1, source_target_pairs={{0,4},{4,8},{8,12},{1,5},{5,9},{9,13},{2,6},{6,10},{10,14},{3,7},{... | collective-permute-start | bytes 196616 | tf_op jit(solution)/shard_map/ppermute | solution.py:17
  38.3 9.3 %collective-permute-start.6 = (f32[128,128]{1,0:T(8,128)}, f32[128,128]{1,0:T(8,128)S(1)}, u32[]{:S(2)}, u32[]{:S(2)}) collective-permute-start(f32[128,128]{1,0:T(8,128)} %get-tuple-element.22), channel_id=1, source_target_pairs={{4,0},{8,4},{12,8},{5,1},{9,5},{13,9},{6,2},{10,6},{14,10},{7,3},{... | collective-permute-start | bytes 196616 | tf_op jit(solution)/shard_map/ppermute | solution.py:17
  40.8 6.8 %collective-permute-start.7 = (f32[8,128]{1,0:T(8,128)}, f32[8,128]{1,0:T(8,128)S(1)}, u32[]{:S(2)}, u32[]{:S(2)}) collective-permute-start(f32[8,128]{1,0:T(8,128)} %get-tuple-element.23), channel_id=1, source_target_pairs={{0,1},{1,2},{2,3},{4,5},{5,6},{6,7},{8,9},{9,10},{10,11},{12,13},{... | collective-permute-start | bytes 12296 | tf_op jit(solution)/shard_map/ppermute | solution.py:17
  42.7 8.7 %collective-permute-start.8 = (f32[8,128]{1,0:T(8,128)S(1)}, f32[8,128]{1,0:T(8,128)S(1)}, u32[]{:S(2)}, u32[]{:S(2)}) collective-permute-start(f32[8,128]{1,0:T(8,128)S(1)} %copy-done.15), channel_id=1, source_target_pairs={{1,0},{2,1},{3,2},{5,4},{6,5},{7,6},{9,8},{10,9},{11,10},{13,12},{... | collective-permute-start | bytes 12296 | tf_op jit(solution)/shard_map/ppermute | solution.py:17
  47.5 0.7 %copy-start.10 = (f32[8,128]{1,0:T(8,128)}, f32[8,128]{1,0:T(8,128)S(1)}, u32[]{:S(2)}) copy-start(f32[8,128]{1,0:T(8,128)S(1)} %collective-permute-done.7.refs_3_) | copy-start | bytes 12292
  47.6 0.6 %copy-start.6 = (f32[128,128]{1,0:T(8,128)}, f32[128,128]{1,0:T(8,128)S(1)}, u32[]{:S(2)}) copy-start(f32[128,128]{1,0:T(8,128)S(1)} %collective-permute-done.5.refs_1_) | copy-start | bytes 196612
  47.6 0.6 %copy-start.7 = (f32[128,128]{1,0:T(8,128)}, f32[128,128]{1,0:T(8,128)S(1)}, u32[]{:S(2)}) copy-start(f32[128,128]{1,0:T(8,128)S(1)} %collective-permute-done.6.refs_2_) | copy-start | bytes 196612
  51.4 0.6 %copy-start.9 = (f32[8,128]{1,0:T(8,128)}, f32[8,128]{1,0:T(8,128)S(1)}, u32[]{:S(2)}) copy-start(f32[8,128]{1,0:T(8,128)S(1)} %collective-permute-done.8.rt_ref) | copy-start | bytes 12292

commit v16 on v9

--- a/solution.py
+++ b/solution.py
@@ -17,14 +17,20 @@
     return lax.ppermute(block, axis, route)
 
 
-def step_kernel(fields, levels, rows, cols, coupled, emit):
+def step_kernel(fields, levels, rows, cols, coupled, emit, shared):
     planes = fields * levels
 
     def kernel(*refs):
         refs = list(refs)
-        a_ref, up_ref, dn_ref, lf_ref, rt_ref, cu_ref, cd_ref, cl_ref, cr_ref = refs[:9]
-        ue_ref, un_ref, k_ref, wet_ref = refs[9:13]
-        refs = refs[13:]
+        a_ref, up_ref, dn_ref, lf_ref, rt_ref = refs[:5]
+        refs = refs[5:]
+        if shared:
+            cu_ref, cd_ref, cl_ref, cr_ref = up_ref, dn_ref, lf_ref, rt_ref
+        else:
+            cu_ref, cd_ref, cl_ref, cr_ref = refs[:4]
+            refs = refs[4:]
+        ue_ref, un_ref, k_ref, wet_ref = refs[:4]
+        refs = refs[4:]
         if coupled:
             inc_ref = refs.pop(0)
         out_ref = refs.pop(0)
@@ -129,7 +135,8 @@
     fields, levels, rows, cols = a.shape
     planes = fields * levels
     coupled = inc is not None
-    operands = [a, *halos, *coef_halos, ue, un, coeffs, wet]
+    shared = coef_halos is halos
+    operands = [a, *halos, *([] if shared else coef_halos), ue, un, coeffs, wet]
     if coupled:
         operands += list(inc)
     shapes = [jax.ShapeDtypeStruct(a.shape, jnp.float32)]
@@ -137,7 +144,7 @@
         shapes += [jax.ShapeDtypeStruct((planes, cols), jnp.float32)] * 2
         shapes += [jax.ShapeDtypeStruct((rows, planes), jnp.float32)] * 2
     return pl.pallas_call(
-        step_kernel(fields, levels, rows, cols, coupled, emit),
+        step_kernel(fields, levels, rows, cols, coupled, emit, shared),
         out_shape=shapes,
         scratch_shapes=[pltpu.VMEM(a.shape, jnp.float32)],
     )(*operands)

time: 54.6 us -> 54.5 us (level)
  no operation moved by 1% of the time
where the time goes in v16:
time: 54.5 us; the launch traced here: 53.9 us
  starting transfers between devices  29.7 us (54%)
  local copies, waits for them, and re-layouts  7.94 us (15%)
  waiting for transfers between devices  6.63 us (12%)
  Pallas kernels  6.45 us (12%)
  matrix products  1.71 us (3%)
  other arithmetic  1.09 us (2%)
    ppermute x8, starting transfers between devices, shift(): return lax.ppermute(block, axis, route)  21.3 us
    all_to_all x1, starting transfers between devices, shards(): lax.all_to_all(send_data, ('gx', 'gy'), split_axis=0, concat_axis=0, tile...  8.34 us
    ppermute x8, waiting for transfers between devices, shift(): return lax.ppermute(block, axis, route)  6.48 us
    pallas_call x2, Pallas kernels, run_step(): pl.pallas_call(step_kernel(fields, levels, rows, cols, coupled, emit, sha...  6.45 us
    unnamed x32, local copies, waits for them, and re-layouts  3.68 us
  transfers between devices with their start and end apart: 10, of which 4 were waited for; matrix products, arithmetic and copies ran while one was open for 2% of the time, Pallas kernels for 0%

profile of v16, /device:TPU:0, one launch (start us, length us, event | category | flops | bytes accessed | tf_op | source)
XLA Modules:
  0.0 53.9 jit_solution(9738021081976298587)
XLA Ops:
  0.0 0.7 %copy-done.12 = s32[1,1,1,32]{3,2,1,0:T(1,128)S(1)} copy-done((s32[1,1,1,32]{3,2,1,0:T(1,128)S(1)}, s32[1,1,1,32]{3,2,1,0:T(1,128)}, u32[]{:S(2)}) %copy-start.12) | copy-done | bytes 152
  0.7 1.0 %convolution_multiply_fusion = f32[32,4,128]{2,0,1:T(8,128)S(1)} fusion(f32[32,128]{1,0:T(8,128)} %bitcast.87, f32[4,32,8,128]{3,2,1,0:T(8,128)} %bitcast.66, s32[32]{0:T(128)S(1)} %bitcast.90), kind=kOutput, calls=%fused_computation | convolution fusion | flops 1589504 | bytes 98432 | tf_op jit(solution)/shard_map/dot_general | solution.py:187
  1.6 0.0 copy-start.14
  1.7 0.0 copy-start.13
  1.7 0.0 copy-start
  1.7 0.6 %copy-done.14 = s32[1,1,1,32,1]{3,4,2,1,0:T(1,128)S(1)} copy-done((s32[1,1,1,32,1]{3,4,2,1,0:T(1,128)S(1)}, s32[1,1,1,32,1]{3,4,2,1,0:T(1,128)}, u32[]{:S(2)}) %copy-start.14) | copy-done | bytes 152
  2.3 0.2 convert_reduce_fusion
  2.5 0.0 copy-done.13
  2.5 0.3 fusion
  2.8 0.3 slice_reduce_fusion.1
  3.2 0.2 fusion.18
  3.4 0.1 fusion.19
  3.6 0.1 copy.47
  3.6 0.1 reshape.113
  3.7 0.1 select_reduce_fusion
  3.8 0.1 convert_element_type.31
  3.9 0.1 select_maximum_fusion.1
  4.2 0.3 copy.48
  4.4 0.1 reshape.115
  4.5 0.3 copy.51
  4.8 0.1 reshape.116
  4.9 0.5 copy-done.1
  5.4 0.1 fusion.21
  5.5 0.1 copy.50
  5.7 0.1 copy.53
  5.8 1.0 %fusion.22 = (f32[32,1,128]{2,1,0:T(1,128)S(1)}, f32[32,1,128]{2,1,0:T(1,128)S(1)}) fusion(f32[32,8,128]{2,1,0:T(8,128)} %bitcast.75), kind=kLoop, calls=%fused_computation.51 | loop fusion | bytes 65536 | tf_op jit(solution)/shard_map/slice | solution.py:171
  6.8 0.3 fusion.6
  7.1 0.8 %copy.54 = f32[16,7,512]{2,1,0:T(8,128)} copy(f32[16,7,512]{2,0,1:T(8,128)S(1)} %pad_maximum_fusion) | data formatting | bytes 458752 | tf_op jit(solution)/shard_map/optimization_barrier | solution.py:235
  8.0 8.3 %all-to-all-start = ((f32[16,7,512]{2,1,0:T(8,128)}), f32[16,7,512]{2,1,0:T(8,128)S(1)}, u32[]{:S(2)}, u32[]{:S(2)}) async-start(f32[16,7,512]{2,1,0:T(8,128)} %copy.54), calls=%async_computation | async-start | bytes 524288 | tf_op jit(solution)/shard_map/all_to_all | solution.py:238
  16.3 3.8 %collective-permute-start = (f32[160,128]{1,0:T(8,128)S(1)}, f32[160,128]{1,0:T(8,128)S(1)}, u32[]{:S(2)}, u32[]{:S(2)}) collective-permute-start(f32[160,128]{1,0:T(8,128)S(1)} %get-tuple-element.15), channel_id=1, source_target_pairs={{0,4},{4,8},{8,12},{1,5},{5,9},{9,13},{2,6},{6,10},{10,14},{3,7},{... | collective-permute-start | bytes 245768 | tf_op jit(solution)/shard_map/ppermute | solution.py:17
  20.2 1.3 %collective-permute-start.1 = (f32[160,128]{1,0:T(8,128)S(1)}, f32[160,128]{1,0:T(8,128)S(1)}, u32[]{:S(2)}, u32[]{:S(2)}) collective-permute-start(f32[160,128]{1,0:T(8,128)S(1)} %get-tuple-element.16), channel_id=1, source_target_pairs={{4,0},{8,4},{12,8},{5,1},{9,5},{13,9},{6,2},{10,6},{14,10},{7,3},{... | collective-permute-start | bytes 245768 | tf_op jit(solution)/shard_map/ppermute | solution.py:17
  21.5 3.4 %collective-permute-start.2 = (f32[8,160]{1,0:T(8,128)S(1)}, f32[8,160]{1,0:T(8,128)S(1)}, u32[]{:S(2)}, u32[]{:S(2)}) collective-permute-start(f32[8,160]{1,0:T(8,128)S(1)} %get-tuple-element.17), channel_id=1, source_target_pairs={{0,1},{1,2},{2,3},{4,5},{5,6},{6,7},{8,9},{9,10},{10,11},{12,13},{... | collective-permute-start | bytes 15368 | tf_op jit(solution)/shard_map/ppermute | solution.py:17
  24.8 1.3 %collective-permute-start.3 = (f32[8,160]{1,0:T(8,128)S(1)}, f32[8,160]{1,0:T(8,128)S(1)}, u32[]{:S(2)}, u32[]{:S(2)}) collective-permute-start(f32[8,160]{1,0:T(8,128)S(1)} %get-tuple-element.18), channel_id=1, source_target_pairs={{1,0},{2,1},{3,2},{5,4},{6,5},{7,6},{9,8},{10,9},{11,10},{13,12},{... | collective-permute-start | bytes 15368 | tf_op jit(solution)/shard_map/ppermute | solution.py:17
  26.1 0.2 all-to-all-done
  26.4 0.1 slice_reduce_fusion.3
  26.5 0.1 eq.128
  26.6 0.2 fusion.13
  26.8 0.1 slice_reduce_fusion.2
  26.8 0.0 copy-start.11
  26.8 0.1 collective-permute-start.4
  26.9 0.6 %copy-done.11 = s32[1,8,128]{2,1,0:T(8,128)S(1)} copy-done((s32[1,8,128]{2,1,0:T(8,128)S(1)}, s32[1,8,128]{2,1,0:T(8,128)}, u32[]{:S(2)}) %copy-start.11) | copy-done | bytes 4120
  27.5 0.6 %convert_bitcast_fusion.refs_8_.refs_12_ = f32[8,128]{1,0:T(8,128)} fusion(s32[1,8,128]{2,1,0:T(8,128)S(1)} %copy-done.11), kind=kLoop, calls=%fused_computation.34 | loop fusion | flops 1024 | bytes 8192 | tf_op jit(solution)/shard_map/convert_element_type | solution.py:167
  28.1 0.0 collective-permute-done.2.refs_3_.refs_7_
  28.1 2.3 %collective-permute-done.3.refs_4_.refs_8_ = f32[8,160]{1,0:T(8,128)S(1)} collective-permute-done((f32[8,160]{1,0:T(8,128)S(1)}, f32[8,160]{1,0:T(8,128)S(1)}, u32[]{:S(2)}, u32[]{:S(2)}) %collective-permute-start.3) | collective-permute-done | bytes 5152 | tf_op jit(solution)/shard_map/ppermute | solution.py:17
  30.4 0.0 collective-permute-done.refs_1_.refs_5_
  30.4 0.0 collective-permute-done.1.refs_2_.refs_6_
  30.4 0.0 collective-permute-done.4.refs_9_
  30.4 0.5 %copy-done.7 = f32[8,160]{1,0:T(8,128)} copy-done((f32[8,160]{1,0:T(8,128)}, f32[8,160]{1,0:T(8,128)S(1)}, u32[]{:S(2)}) %copy-start.7) | copy-done | bytes 5144
  31.0 0.1 copy-done.2
  31.0 0.0 copy-done.3
  31.0 0.0 copy-done.8
  31.1 3.3 %shard_map.91 = (f32[4,32,8,128]{3,2,1,0:T(8,128)}, f32[128,128]{1,0:T(8,128)}, f32[128,128]{1,0:T(8,128)}, f32[8,128]{1,0:T(8,128)}, f32[8,128]{1,0:T(8,128)}) custom-call(f32[4,32,8,128]{3,2,1,0:T(8,128)} %bitcast.67, f32[160,128]{1,0:T(8,128)} %copy-done.2, f32[160,128]{1,0:T(8,128)} %copy-done.3, f32[8,160]{1,0:T(8,128)} %copy-done.6, ...), custom_call_target="tpu_custom_call" | custom-call | tf_op jit(solution)/shard_map/pallas_call | solution.py:146
  34.4 4.7 %collective-permute-start.5 = (f32[128,128]{1,0:T(8,128)}, f32[128,128]{1,0:T(8,128)S(1)}, u32[]{:S(2)}, u32[]{:S(2)}) collective-permute-start(f32[128,128]{1,0:T(8,128)} %get-tuple-element.21), channel_id=1, source_target_pairs={{0,4},{4,8},{8,12},{1,5},{5,9},{9,13},{2,6},{6,10},{10,14},{3,7},{... | collective-permute-start | bytes 196616 | tf_op jit(solution)/shard_map/ppermute | solution.py:17
  39.0 1.3 %collective-permute-start.6 = (f32[128,128]{1,0:T(8,128)}, f32[128,128]{1,0:T(8,128)S(1)}, u32[]{:S(2)}, u32[]{:S(2)}) collective-permute-start(f32[128,128]{1,0:T(8,128)} %get-tuple-element.22), channel_id=1, source_target_pairs={{4,0},{8,4},{12,8},{5,1},{9,5},{13,9},{6,2},{10,6},{14,10},{7,3},{... | collective-permute-start | bytes 196616 | tf_op jit(solution)/shard_map/ppermute | solution.py:17
  40.3 4.3 %collective-permute-start.7 = (f32[8,128]{1,0:T(8,128)}, f32[8,128]{1,0:T(8,128)S(1)}, u32[]{:S(2)}, u32[]{:S(2)}) collective-permute-start(f32[8,128]{1,0:T(8,128)} %get-tuple-element.23), channel_id=1, source_target_pairs={{0,1},{1,2},{2,3},{4,5},{5,6},{6,7},{8,9},{9,10},{10,11},{12,13},{... | collective-permute-start | bytes 12296 | tf_op jit(solution)/shard_map/ppermute | solution.py:17
  44.6 1.3 %collective-permute-start.8 = (f32[8,128]{1,0:T(8,128)S(1)}, f32[8,128]{1,0:T(8,128)S(1)}, u32[]{:S(2)}, u32[]{:S(2)}) collective-permute-start(f32[8,128]{1,0:T(8,128)S(1)} %copy-done.15), channel_id=1, source_target_pairs={{1,0},{2,1},{3,2},{5,4},{6,5},{7,6},{9,8},{10,9},{11,10},{13,12},{... | collective-permute-start | bytes 12296 | tf_op jit(solution)/shard_map/ppermute | solution.py:17
  45.9 0.2 collective-permute-done.7.refs_3_
  46.1 4.0 %collective-permute-done.8.refs_4_ = f32[8,128]{1,0:T(8,128)S(1)} collective-permute-done((f32[8,128]{1,0:T(8,128)S(1)}, f32[8,128]{1,0:T(8,128)S(1)}, u32[]{:S(2)}, u32[]{:S(2)}) %collective-permute-start.8) | collective-permute-done | bytes 4128 | tf_op jit(solution)/shard_map/ppermute | solution.py:17
  50.1 0.0 collective-permute-done.5.refs_1_
  50.1 0.0 collective-permute-done.6.refs_2_
  50.2 0.6 %copy-done.10 = f32[8,128]{1,0:T(8,128)} copy-done((f32[8,128]{1,0:T(8,128)}, f32[8,128]{1,0:T(8,128)S(1)}, u32[]{:S(2)}) %copy-start.10) | copy-done | bytes 4120
  50.7 0.0 copy-done.4
  50.8 0.0 copy-done.5
  50.8 3.1 %shard_map.92 = f32[4,32,8,128]{3,2,1,0:T(8,128)} custom-call(f32[4,32,8,128]{3,2,1,0:T(8,128)} %get-tuple-element.20.refs_0_, f32[128,128]{1,0:T(8,128)} %copy-done.4, f32[128,128]{1,0:T(8,128)} %copy-done.5, f32[8,128]{1,0:T(8,128)} %copy-done.9, f32[8,128]{1,0:T(8,128)} %copy-done.10, f32[160,128]{1,0:T(8,128)} %copy-done.2, f32[160,128]{1,0:T(8,128)} %copy-done.3, ...), custom_call_target="tpu_custom_call" | custom-call | tf_op jit(solution)/shard_map/pallas_call | solution.py:146
  (40 shorter events, 0.4 us)
Async XLA Ops:
  0.0 0.7 %copy-start.12 = (s32[1,1,1,32]{3,2,1,0:T(1,128)S(1)}, s32[1,1,1,32]{3,2,1,0:T(1,128)}, u32[]{:S(2)}) copy-start(s32[1,1,1,32]{3,2,1,0:T(1,128)} %param.15) | copy-start | bytes 388
  1.6 0.7 %copy-start.14 = (s32[1,1,1,32,1]{3,4,2,1,0:T(1,128)S(1)}, s32[1,1,1,32,1]{3,4,2,1,0:T(1,128)}, u32[]{:S(2)}) copy-start(s32[1,1,1,32,1]{3,4,2,1,0:T(1,128)} %param.14) | copy-start | bytes 388
  1.7 0.8 %copy-start.13 = (s32[1,1,1,32]{3,2,1,0:T(1,128)S(1)}, s32[1,1,1,32]{3,2,1,0:T(1,128)}, u32[]{:S(2)}) copy-start(s32[1,1,1,32]{3,2,1,0:T(1,128)} %param.16) | copy-start | bytes 388
  1.7 1.5 %copy-start = (f32[1,4,32,8,128]{4,3,2,1,0:T(8,128)S(1)}, f32[1,4,32,8,128]{4,3,2,1,0:T(8,128)}, u32[]{:S(2)}) copy-start(f32[1,4,32,8,128]{4,3,2,1,0:T(8,128)} %param.9) | copy-start | bytes 1572868
  4.5 0.9 %copy-start.1 = (f32[1,32,8,128]{3,2,1,0:T(8,128)S(1)}, f32[1,32,8,128]{3,2,1,0:T(8,128)}, u32[]{:S(2)}) copy-start(f32[1,32,8,128]{3,2,1,0:T(8,128)} %param.11) | copy-start | bytes 393220
  8.0 18.3 %all-to-all-start = ((f32[16,7,512]{2,1,0:T(8,128)}), f32[16,7,512]{2,1,0:T(8,128)S(1)}, u32[]{:S(2)}, u32[]{:S(2)}) async-start(f32[16,7,512]{2,1,0:T(8,128)} %copy.54), calls=%async_computation | async-start | bytes 524288 | tf_op jit(solution)/shard_map/all_to_all | solution.py:238
  16.3 14.1 %collective-permute-start = (f32[160,128]{1,0:T(8,128)S(1)}, f32[160,128]{1,0:T(8,128)S(1)}, u32[]{:S(2)}, u32[]{:S(2)}) collective-permute-start(f32[160,128]{1,0:T(8,128)S(1)} %get-tuple-element.15), channel_id=1, source_target_pairs={{0,4},{4,8},{8,12},{1,5},{5,9},{9,13},{2,6},{6,10},{10,14},{3,7},{... | collective-permute-start | bytes 245768 | tf_op jit(solution)/shard_map/ppermute | solution.py:17
  20.2 10.2 %collective-permute-start.1 = (f32[160,128]{1,0:T(8,128)S(1)}, f32[160,128]{1,0:T(8,128)S(1)}, u32[]{:S(2)}, u32[]{:S(2)}) collective-permute-start(f32[160,128]{1,0:T(8,128)S(1)} %get-tuple-element.16), channel_id=1, source_target_pairs={{4,0},{8,4},{12,8},{5,1},{9,5},{13,9},{6,2},{10,6},{14,10},{7,3},{... | collective-permute-start | bytes 245768 | tf_op jit(solution)/shard_map/ppermute | solution.py:17
  21.5 6.7 %collective-permute-start.2 = (f32[8,160]{1,0:T(8,128)S(1)}, f32[8,160]{1,0:T(8,128)S(1)}, u32[]{:S(2)}, u32[]{:S(2)}) collective-permute-start(f32[8,160]{1,0:T(8,128)S(1)} %get-tuple-element.17), channel_id=1, source_target_pairs={{0,1},{1,2},{2,3},{4,5},{5,6},{6,7},{8,9},{9,10},{10,11},{12,13},{... | collective-permute-start | bytes 15368 | tf_op jit(solution)/shard_map/ppermute | solution.py:17
  24.8 5.5 %collective-permute-start.3 = (f32[8,160]{1,0:T(8,128)S(1)}, f32[8,160]{1,0:T(8,128)S(1)}, u32[]{:S(2)}, u32[]{:S(2)}) collective-permute-start(f32[8,160]{1,0:T(8,128)S(1)} %get-tuple-element.18), channel_id=1, source_target_pairs={{1,0},{2,1},{3,2},{5,4},{6,5},{7,6},{9,8},{10,9},{11,10},{13,12},{... | collective-permute-start | bytes 15368 | tf_op jit(solution)/shard_map/ppermute | solution.py:17
  26.8 0.7 %copy-start.11 = (s32[1,8,128]{2,1,0:T(8,128)S(1)}, s32[1,8,128]{2,1,0:T(8,128)}, u32[]{:S(2)}) copy-start(s32[1,8,128]{2,1,0:T(8,128)} %param.13) | copy-start | bytes 12292
  26.8 3.6 %collective-permute-start.4 = (f32[11,512]{1,0:T(8,128)S(1)}, f32[11,512]{1,0:T(8,128)S(1)}, u32[]{:S(2)}, u32[]{:S(2)}) collective-permute-start(f32[11,512]{1,0:T(8,128)S(1)} %pad_maximum_fusion.3), channel_id=1, source_target_pairs={{0,16},{16,0},{1,17},{17,1},{2,18},{18,2},{3,19},{19,3},{4,20},{20... | collective-permute-start | bytes 67592 | tf_op jit(solution)/shard_map/ppermute | solution.py:257
  28.1 2.3 %copy-start.6 = (f32[8,160]{1,0:T(8,128)}, f32[8,160]{1,0:T(8,128)S(1)}, u32[]{:S(2)}) copy-start(f32[8,160]{1,0:T(8,128)S(1)} %collective-permute-done.2.refs_3_.refs_7_) | copy-start | bytes 15364
  30.4 0.6 %copy-start.7 = (f32[8,160]{1,0:T(8,128)}, f32[8,160]{1,0:T(8,128)S(1)}, u32[]{:S(2)}) copy-start(f32[8,160]{1,0:T(8,128)S(1)} %collective-permute-done.3.refs_4_.refs_8_) | copy-start | bytes 15364
  30.4 0.6 %copy-start.2 = (f32[160,128]{1,0:T(8,128)}, f32[160,128]{1,0:T(8,128)S(1)}, u32[]{:S(2)}) copy-start(f32[160,128]{1,0:T(8,128)S(1)} %collective-permute-done.refs_1_.refs_5_) | copy-start | bytes 245764
  30.4 0.7 %copy-start.3 = (f32[160,128]{1,0:T(8,128)}, f32[160,128]{1,0:T(8,128)S(1)}, u32[]{:S(2)}) copy-start(f32[160,128]{1,0:T(8,128)S(1)} %collective-permute-done.1.refs_2_.refs_6_) | copy-start | bytes 245764
  30.4 0.7 %copy-start.8 = (f32[11,512]{1,0:T(8,128)}, f32[11,512]{1,0:T(8,128)S(1)}, u32[]{:S(2)}) copy-start(f32[11,512]{1,0:T(8,128)S(1)} %collective-permute-done.4.refs_9_) | copy-start | bytes 67588
  34.4 10.3 %copy-start.15 = (f32[8,128]{1,0:T(8,128)S(1)}, f32[8,128]{1,0:T(8,128)}, u32[]{:S(2)}) copy-start(f32[8,128]{1,0:T(8,128)} %get-tuple-element.24) | copy-start | bytes 12292
  34.4 15.8 %collective-permute-start.5 = (f32[128,128]{1,0:T(8,128)}, f32[128,128]{1,0:T(8,128)S(1)}, u32[]{:S(2)}, u32[]{:S(2)}) collective-permute-start(f32[128,128]{1,0:T(8,128)} %get-tuple-element.21), channel_id=1, source_target_pairs={{0,4},{4,8},{8,12},{1,5},{5,9},{9,13},{2,6},{6,10},{10,14},{3,7},{... | collective-permute-start | bytes 196616 | tf_op jit(solution)/shard_map/ppermute | solution.py:17
  39.0 11.1 %collective-permute-start.6 = (f32[128,128]{1,0:T(8,128)}, f32[128,128]{1,0:T(8,128)S(1)}, u32[]{:S(2)}, u32[]{:S(2)}) collective-permute-start(f32[128,128]{1,0:T(8,128)} %get-tuple-element.22), channel_id=1, source_target_pairs={{4,0},{8,4},{12,8},{5,1},{9,5},{13,9},{6,2},{10,6},{14,10},{7,3},{... | collective-permute-start | bytes 196616 | tf_op jit(solution)/shard_map/ppermute | solution.py:17
  40.3 5.8 %collective-permute-start.7 = (f32[8,128]{1,0:T(8,128)}, f32[8,128]{1,0:T(8,128)S(1)}, u32[]{:S(2)}, u32[]{:S(2)}) collective-permute-start(f32[8,128]{1,0:T(8,128)} %get-tuple-element.23), channel_id=1, source_target_pairs={{0,1},{1,2},{2,3},{4,5},{5,6},{6,7},{8,9},{9,10},{10,11},{12,13},{... | collective-permute-start | bytes 12296 | tf_op jit(solution)/shard_map/ppermute | solution.py:17
  44.6 5.5 %collective-permute-start.8 = (f32[8,128]{1,0:T(8,128)S(1)}, f32[8,128]{1,0:T(8,128)S(1)}, u32[]{:S(2)}, u32[]{:S(2)}) collective-permute-start(f32[8,128]{1,0:T(8,128)S(1)} %copy-done.15), channel_id=1, source_target_pairs={{1,0},{2,1},{3,2},{5,4},{6,5},{7,6},{9,8},{10,9},{11,10},{13,12},{... | collective-permute-start | bytes 12296 | tf_op jit(solution)/shard_map/ppermute | solution.py:17
  46.1 4.0 %copy-start.9 = (f32[8,128]{1,0:T(8,128)}, f32[8,128]{1,0:T(8,128)S(1)}, u32[]{:S(2)}) copy-start(f32[8,128]{1,0:T(8,128)S(1)} %collective-permute-done.7.refs_3_) | copy-start | bytes 12292
  50.1 0.6 %copy-start.10 = (f32[8,128]{1,0:T(8,128)}, f32[8,128]{1,0:T(8,128)S(1)}, u32[]{:S(2)}) copy-start(f32[8,128]{1,0:T(8,128)S(1)} %collective-permute-done.8.refs_4_) | copy-start | bytes 12292
  50.1 0.6 %copy-start.4 = (f32[128,128]{1,0:T(8,128)}, f32[128,128]{1,0:T(8,128)S(1)}, u32[]{:S(2)}) copy-start(f32[128,128]{1,0:T(8,128)S(1)} %collective-permute-done.5.refs_1_) | copy-start | bytes 196612
  50.1 0.7 %copy-start.5 = (f32[128,128]{1,0:T(8,128)}, f32[128,128]{1,0:T(8,128)S(1)}, u32[]{:S(2)}) copy-start(f32[128,128]{1,0:T(8,128)S(1)} %collective-permute-done.6.refs_2_) | copy-start | bytes 196612
